TPU v7x, 32 devices: a whole 2x2x4 slice. The times are simulated.
32 devices in a mesh: gx: 16 (over z, y, x), gy: 2 (over core).
Axes of the slice: x: 2, y: 2, z: 4, core: 2. Of those that a mesh axis runs over, the one named last changes fastest.
Arguments:
- load_parts: bfloat16 [16, 2, 4, 192, 384], P('gx', 'gy'), may hold values from -6 to 6
- schur: bfloat16 [16, 2, 4, 384, 384], P('gx', 'gy'), may hold values from -4 to 4
- deluxe: bfloat16 [16, 2, 4, 384, 384], P('gx', 'gy'), may hold values from -4 to 4
- panels: bfloat16 [16, 2, 4, 384, 384], P('gx', 'gy'), may hold values from -4 to 4
- coarse_inverse: float32 [128, 128], P(('gx', 'gy')), may hold values from -1 to 1
- primal_dofs: int32 [16, 2, 4], P('gx', 'gy'), may hold values from 0 to 1535
- damage_flags: int32 [16, 2, 4], P('gx', 'gy'), may hold values 0 or 1
Outputs:
- increment: bfloat16 [16, 2, 4, 192, 384], P('gx', 'gy')
Inputs may be any that keep to these rules, and one draw needn't show every extreme that they name: `primal_dofs`: each entry names a face times 384 plus a position on that face.
All inputs are finite; a program needn't handle non-finite values. No bound on the sum of `damage_flags` on one device may be relied on, other than what follows from the above.
Results may differ from a plain program's by a relative error of at most 0.003.
The roundings to bfloat16 on the way count: a program that leaves them out, or rounds other values in their place, can miss the bound.
Values may be sent and summed in bfloat16 or wider, within the bound.
No kernel may reach another device: no remote copies, remote signals or barrier semaphores. Data moves between devices by JAX's collectives and lax.ppermute only.
A program may use at most 64 MiB of HBM per device.

v0:
```python
import jax
import jax.numpy as jnp
from jax import lax
from jax.sharding import PartitionSpec as P


def with_halo(block, sides, width):
    for axis, dim in sides:
        count = lax.axis_size(axis)
        forward = [(i, i + 1) for i in range(count - 1)]
        backward = [(target, source) for source, target in forward]
        low = lax.ppermute(
            lax.slice_in_dim(block, block.shape[dim] - width, None, axis=dim), axis, forward
        )
        high = lax.ppermute(lax.slice_in_dim(block, 0, width, axis=dim), axis, backward)
        block = jnp.concatenate([low, block, high], axis=dim)
    return block


def face_mul(vectors, matrices):
    return jnp.einsum("fry,fyx->frx", vectors, matrices, preferred_element_type=jnp.float32)


def face_mul_turned(vectors, matrices):
    return jnp.einsum("fry,fxy->frx", vectors, matrices, preferred_element_type=jnp.float32)


def face_pairs(values):
    along_first = with_halo(values[0:2], (("gx", 0),), 1)
    along_second = with_halo(values[2:4], (("gy", 0),), 1)
    return jnp.stack([along_first[0], along_first[3], along_second[0], along_second[3]], axis=0)


def image_pairs(values):
    along_first = with_halo(values[0:2], (("gx", 0),), 1)
    along_second = with_halo(values[2:4], (("gy", 0),), 1)
    return jnp.stack([along_first[0], along_first[3], along_second[0], along_second[3]], axis=0)


def per_device(load_parts, schur, deluxe, panels, coarse_inverse, primal_dofs, damage_flags):
    loads_here = load_parts[0, 0]
    schur_panel = schur[0, 0]
    deluxe_panel = deluxe[0, 0]
    inverse_panel = panels[0, 0]
    primal_slots = primal_dofs[0, 0]
    flag_values = damage_flags[0, 0]
    width = loads_here.shape[2]
    primal_count = primal_slots.shape[0]
    positions = jnp.arange(4 * width, dtype=jnp.int32)
    picks = (primal_slots[:, None] == positions[None, :]).reshape(primal_count, 4, width)
    picks_half = picks.astype(jnp.bfloat16)
    picks_full = picks.astype(jnp.float32)
    flags_full = flag_values.astype(jnp.float32)

    def add_coarse(piece):
        return jnp.dot(coarse_inverse, piece.astype(jnp.float32), precision=lax.Precision.HIGHEST)

    def precondition(resid):
        scaled = face_mul_turned(resid.astype(jnp.bfloat16), deluxe_panel).astype(jnp.bfloat16)
        local_part = face_mul(scaled, inverse_panel)
        extra = face_mul(local_part.astype(jnp.bfloat16), inverse_panel)
        softened = local_part + 0.5 * flags_full[:, None, None] * extra
        primal = jnp.einsum(
            "kfx,frx->kr", picks_half, scaled, preferred_element_type=jnp.float32
        ).astype(jnp.bfloat16)
        coarse = add_coarse(lax.all_gather(primal, ("gx", "gy"), axis=0, tiled=True))
        placed = jnp.einsum("kfx,kr->frx", picks_full, coarse, precision=lax.Precision.HIGHEST)
        weighted = (softened + placed).astype(jnp.bfloat16)
        spread = face_mul(weighted, deluxe_panel).astype(jnp.bfloat16)
        return spread.astype(jnp.float32) + face_pairs(spread).astype(jnp.float32)

    def apply_operator(field):
        bent = face_mul(field.astype(jnp.bfloat16), schur_panel).astype(jnp.bfloat16)
        return bent.astype(jnp.float32) + image_pairs(bent).astype(jnp.float32)

    resid0 = loads_here.astype(jnp.float32) + face_pairs(loads_here).astype(jnp.float32)
    first = precondition(resid0)
    resid1 = resid0 - apply_operator(first)
    second = precondition(resid1)
    top = lax.psum(jnp.sum(resid1 * second, axis=(0, 2)), ("gx", "gy"))
    curved = apply_operator(second)
    bottom = lax.psum(jnp.sum(second * curved, axis=(0, 2)), ("gx", "gy"))
    step_len = top / bottom
    result = (first + step_len[:, None] * second).astype(jnp.bfloat16)
    return result[None, None]


def solution(mesh):
    return jax.shard_map(
        per_device,
        mesh=mesh,
        in_specs=(
            P("gx", "gy", None, None, None),
            P("gx", "gy", None, None, None),
            P("gx", "gy", None, None, None),
            P("gx", "gy", None, None, None),
            P(("gx", "gy"), None),
            P("gx", "gy", None),
            P("gx", "gy", None),
        ),
        out_specs=P("gx", "gy", None, None, None),
        check_vma=False,
    )
```

profile of v0, /device:TPU:0, one launch (start us, length us, event | category | flops | bytes accessed | tf_op | source)
XLA Modules:
  0.0 210.2 jit_solution(9755467577524988544)
XLA Ops:
  1.3 4.9 %collective-permute-start = (bf16[1,192,384]{2,1,0:T(8,128)(2,1)S(1)}, bf16[1,192,384]{2,1,0:T(8,128)(2,1)S(1)}, u32[]{:S(2)}, u32[]{:S(2)}) collective-permute-start(bf16[1,192,384]{2,1,0:T(8,128)(2,1)S(1)} %get-tuple-element.23), channel_id=1, source_target_pairs={{0,2},{2,4},{4,6},{6,8},{8,10},{10,12},{12,14},{14,16},{16,18},{18... | collective-permute-start | bytes 442376 | tf_op jit(solution)/shard_map/ppermute | solution.py:12
  8.8 3.0 %collective-permute-start.2 = (bf16[1,192,384]{2,1,0:T(8,128)(2,1)S(1)}, bf16[1,192,384]{2,1,0:T(8,128)(2,1)S(1)}, u32[]{:S(2)}, u32[]{:S(2)}) collective-permute-start(bf16[1,192,384]{2,1,0:T(8,128)(2,1)S(1)} %get-tuple-element.26), channel_id=1, source_target_pairs={{0,1},{2,3},{4,5},{6,7},{8,9},{10,11},{12,13},{14,15},{16,17},{18,... | collective-permute-start | bytes 442376 | tf_op jit(solution)/shard_map/ppermute | solution.py:12
  12.5 1.9 collective-permute-done.1
  15.4 44.1 %all-gather = bf16[32,4,192]{2,1,0:T(4,128)(2,1)} all-gather(bf16[1,4,192]{2,1,0:T(4,128)(2,1)S(1)} %fusion.25), channel_id=1, replica_groups=mesh['gx'=16,'gy'=2] {'gx','gy'}, dimensions={0}, use_global_device_ids=true | all-gather | bytes 50688 | tf_op jit(solution)/shard_map/all_gather | solution.py:66
  61.1 1.5 fusion.14
  62.7 1.8 convolution_bitcast_fusion.1
  64.5 2.9 %convolution_convert_fusion.4 = bf16[4,192,384]{2,1,0:T(8,128)(2,1)S(1)} fusion(f32[4,192,384]{2,1,0:T(8,128)} %convolution_bitcast_fusion.1, f32[4,192,384]{2,1,0:T(8,128)} %fusion.14, bf16[1,1,4,384,384]{4,3,2,1,0:T(8,128)(2,1)S(1)} %copy-done.1, bf16[1,1,4,384,384]{4,3,2,1,0:T(8,128)(2,1)S(1)} %copy-done, f32[4]{0:T(128)} %multiply_bitcast_fusion), kind=kOutput, calls=%fused_computation.14 | convolution fusion | flops 454754304 | bytes 5308432 | tf_op jit(solution)/shard_map/fry,fyx->frx/dot_general | solution.py:21
  70.2 3.0 %collective-permute-start.6 = (bf16[1,192,384]{2,1,0:T(8,128)(2,1)S(1)}, bf16[1,192,384]{2,1,0:T(8,128)(2,1)S(1)}, u32[]{:S(2)}, u32[]{:S(2)}) collective-permute-start(bf16[1,192,384]{2,1,0:T(8,128)(2,1)S(1)} %get-tuple-element.21), channel_id=1, source_target_pairs={{0,1},{2,3},{4,5},{6,7},{8,9},{10,11},{12,13},{14,15},{16,17},{18,... | collective-permute-start | bytes 442376 | tf_op jit(solution)/shard_map/ppermute | solution.py:12
  74.7 5.7 %collective-permute-done.5 = bf16[1,192,384]{2,1,0:T(8,128)(2,1)S(1)} collective-permute-done((bf16[1,192,384]{2,1,0:T(8,128)(2,1)S(1)}, bf16[1,192,384]{2,1,0:T(8,128)(2,1)S(1)}, u32[]{:S(2)}, u32[]{:S(2)}) %collective-permute-start.5) | collective-permute-done | bytes 147488 | tf_op jit(solution)/shard_map/ppermute | solution.py:15
  81.1 2.9 %collective-permute-start.8 = (bf16[1,192,384]{2,1,0:T(8,128)(2,1)S(1)}, bf16[1,192,384]{2,1,0:T(8,128)(2,1)S(1)}, u32[]{:S(2)}, u32[]{:S(2)}) collective-permute-start(bf16[1,192,384]{2,1,0:T(8,128)(2,1)S(1)} %get-tuple-element.15), channel_id=1, source_target_pairs={{0,2},{2,4},{4,6},{6,8},{8,10},{10,12},{12,14},{14,16},{16,18},{18... | collective-permute-start | bytes 442376 | tf_op jit(solution)/shard_map/ppermute | solution.py:12
  85.3 3.0 %collective-permute-start.10 = (bf16[1,192,384]{2,1,0:T(8,128)(2,1)S(1)}, bf16[1,192,384]{2,1,0:T(8,128)(2,1)S(1)}, u32[]{:S(2)}, u32[]{:S(2)}) collective-permute-start(bf16[1,192,384]{2,1,0:T(8,128)(2,1)S(1)} %get-tuple-element.17), channel_id=1, source_target_pairs={{0,1},{2,3},{4,5},{6,7},{8,9},{10,11},{12,13},{14,15},{16,17},{18,... | collective-permute-start | bytes 442376 | tf_op jit(solution)/shard_map/ppermute | solution.py:12
  89.7 5.7 %collective-permute-done.9 = bf16[1,192,384]{2,1,0:T(8,128)(2,1)S(1)} collective-permute-done((bf16[1,192,384]{2,1,0:T(8,128)(2,1)S(1)}, bf16[1,192,384]{2,1,0:T(8,128)(2,1)S(1)}, u32[]{:S(2)}, u32[]{:S(2)}) %collective-permute-start.9) | collective-permute-done | bytes 147488 | tf_op jit(solution)/shard_map/ppermute | solution.py:15
  96.4 1.6 fusion.10
  98.0 37.4 %all-gather.1 = bf16[32,4,192]{2,1,0:T(4,128)(2,1)S(1)} all-gather(bf16[1,4,192]{2,1,0:T(4,128)(2,1)S(1)} %fusion.24), channel_id=1, replica_groups=mesh['gx'=16,'gy'=2] {'gx','gy'}, dimensions={0}, use_global_device_ids=true | all-gather | bytes 50688 | tf_op jit(solution)/shard_map/all_gather | solution.py:66
  135.5 1.8 convolution_bitcast_fusion
  137.3 2.9 %convolution_convert_fusion.1 = bf16[4,192,384]{2,1,0:T(8,128)(2,1)S(1)} fusion(f32[4,192,384]{2,1,0:T(8,128)} %convolution_bitcast_fusion, f32[4,192,384]{2,1,0:T(8,128)} %fusion.10, bf16[1,1,4,384,384]{4,3,2,1,0:T(8,128)(2,1)S(1)} %copy-done.1, bf16[1,1,4,384,384]{4,3,2,1,0:T(8,128)(2,1)S(1)} %copy-done, f32[4]{0:T(128)} %multiply_bitcast_fusion), kind=kOutput, calls=%fused_computation.11 | convolution fusion | flops 454754304 | bytes 5308432 | tf_op jit(solution)/shard_map/fry,fyx->frx/dot_general | solution.py:21
  140.3 3.1 %collective-permute-start.12 = (bf16[1,192,384]{2,1,0:T(8,128)(2,1)S(1)}, bf16[1,192,384]{2,1,0:T(8,128)(2,1)S(1)}, u32[]{:S(2)}, u32[]{:S(2)}) collective-permute-start(bf16[1,192,384]{2,1,0:T(8,128)(2,1)S(1)} %get-tuple-element.11), channel_id=1, source_target_pairs={{0,2},{2,4},{4,6},{6,8},{8,10},{10,12},{12,14},{14,16},{16,18},{18... | collective-permute-start | bytes 442376 | tf_op jit(solution)/shard_map/ppermute | solution.py:12
  144.7 3.0 %collective-permute-start.14 = (bf16[1,192,384]{2,1,0:T(8,128)(2,1)S(1)}, bf16[1,192,384]{2,1,0:T(8,128)(2,1)S(1)}, u32[]{:S(2)}, u32[]{:S(2)}) collective-permute-start(bf16[1,192,384]{2,1,0:T(8,128)(2,1)S(1)} %get-tuple-element.13), channel_id=1, source_target_pairs={{0,1},{2,3},{4,5},{6,7},{8,9},{10,11},{12,13},{14,15},{16,17},{18,... | collective-permute-start | bytes 442376 | tf_op jit(solution)/shard_map/ppermute | solution.py:12
  149.1 5.7 %collective-permute-done.13 = bf16[1,192,384]{2,1,0:T(8,128)(2,1)S(1)} collective-permute-done((bf16[1,192,384]{2,1,0:T(8,128)(2,1)S(1)}, bf16[1,192,384]{2,1,0:T(8,128)(2,1)S(1)}, u32[]{:S(2)}, u32[]{:S(2)}) %collective-permute-start.13) | collective-permute-done | bytes 147488 | tf_op jit(solution)/shard_map/ppermute | solution.py:15
  155.5 2.9 %collective-permute-start.16 = (bf16[1,192,384]{2,1,0:T(8,128)(2,1)S(1)}, bf16[1,192,384]{2,1,0:T(8,128)(2,1)S(1)}, u32[]{:S(2)}, u32[]{:S(2)}) collective-permute-start(bf16[1,192,384]{2,1,0:T(8,128)(2,1)S(1)} %get-tuple-element.7), channel_id=1, source_target_pairs={{0,2},{2,4},{4,6},{6,8},{8,10},{10,12},{12,14},{14,16},{16,18},{18... | collective-permute-start | bytes 442376 | tf_op jit(solution)/shard_map/ppermute | solution.py:12
  159.8 3.0 %collective-permute-start.18 = (bf16[1,192,384]{2,1,0:T(8,128)(2,1)S(1)}, bf16[1,192,384]{2,1,0:T(8,128)(2,1)S(1)}, u32[]{:S(2)}, u32[]{:S(2)}) collective-permute-start(bf16[1,192,384]{2,1,0:T(8,128)(2,1)S(1)} %get-tuple-element.9), channel_id=1, source_target_pairs={{0,1},{2,3},{4,5},{6,7},{8,9},{10,11},{12,13},{14,15},{16,17},{18,... | collective-permute-start | bytes 442376 | tf_op jit(solution)/shard_map/ppermute | solution.py:12
  164.9 5.0 %collective-permute-done.17 = bf16[1,192,384]{2,1,0:T(8,128)(2,1)S(1)} collective-permute-done((bf16[1,192,384]{2,1,0:T(8,128)(2,1)S(1)}, bf16[1,192,384]{2,1,0:T(8,128)(2,1)S(1)}, u32[]{:S(2)}, u32[]{:S(2)}) %collective-permute-start.17) | collective-permute-done | bytes 147488 | tf_op jit(solution)/shard_map/ppermute | solution.py:15
  170.3 37.5 %all-reduce = (f32[192]{0:T(256)S(1)}, f32[192]{0:T(256)S(1)}) all-reduce(f32[192]{0:T(256)S(1)} %multiply_reduce_fusion.1, f32[192]{0:T(256)S(1)} %multiply_reduce_fusion), channel_id=1, replica_groups=mesh['gx'=16,'gy'=2] {'gx','gy'}, use_global_device_ids=true, to_apply=%region_1.0 | all-reduce | flops 384 | bytes 3072 | tf_op jit(solution)/shard_map/psum | solution.py:80
  207.9 2.3 %fusion.30 = bf16[1,1,4,192,384]{4,3,2,1,0:T(8,128)(2,1)} fusion(bf16[4,192,384]{2,1,0:T(8,128)(2,1)S(1)} %convolution_convert_fusion.1, bf16[4,192,384]{2,1,0:T(8,128)(2,1)S(1)} %convolution_convert_fusion.4, f32[192]{0:T(256)S(1)} %div.3, bf16[1,192,384]{2,1,0:T(8,128)(2,1)S(1)} %copy-done.26, bf16[1,192,384]{2,1,0:T(8,128)(2,1)S(1)} %copy-done.28, ...), kind=kLoop, calls=%fused_computation.46 | loop fusion | flops 4423680 | bytes 2949888 | tf_op jit(solution)/shard_map/broadcast_in_dim | solution.py:85
  (134 shorter events, 22.5 us)
Async XLA Ops:
  1.3 11.1 %collective-permute-start = (bf16[1,192,384]{2,1,0:T(8,128)(2,1)S(1)}, bf16[1,192,384]{2,1,0:T(8,128)(2,1)S(1)}, u32[]{:S(2)}, u32[]{:S(2)}) collective-permute-start(bf16[1,192,384]{2,1,0:T(8,128)(2,1)S(1)} %get-tuple-element.23), channel_id=1, source_target_pairs={{0,2},{2,4},{4,6},{6,8},{8,10},{10,12},{12,14},{14,16},{16,18},{18... | collective-permute-start | bytes 442376 | tf_op jit(solution)/shard_map/ppermute | solution.py:12
  6.2 8.2 %collective-permute-start.1 = (bf16[1,192,384]{2,1,0:T(8,128)(2,1)S(1)}, bf16[1,192,384]{2,1,0:T(8,128)(2,1)S(1)}, u32[]{:S(2)}, u32[]{:S(2)}) collective-permute-start(bf16[1,192,384]{2,1,0:T(8,128)(2,1)S(1)} %get-tuple-element.24), channel_id=1, source_target_pairs={{2,0},{4,2},{6,4},{8,6},{10,8},{12,10},{14,12},{16,14},{18,16},{20... | collective-permute-start | bytes 442376 | tf_op jit(solution)/shard_map/ppermute | solution.py:15
  7.5 6.9 %collective-permute-start.3 = (bf16[1,192,384]{2,1,0:T(8,128)(2,1)S(1)}, bf16[1,192,384]{2,1,0:T(8,128)(2,1)S(1)}, u32[]{:S(2)}, u32[]{:S(2)}) collective-permute-start(bf16[1,192,384]{2,1,0:T(8,128)(2,1)S(1)} %get-tuple-element.25), channel_id=1, source_target_pairs={{1,0},{3,2},{5,4},{7,6},{9,8},{11,10},{13,12},{15,14},{17,16},{19,... | collective-permute-start | bytes 442376 | tf_op jit(solution)/shard_map/ppermute | solution.py:15
  8.8 5.6 %collective-permute-start.2 = (bf16[1,192,384]{2,1,0:T(8,128)(2,1)S(1)}, bf16[1,192,384]{2,1,0:T(8,128)(2,1)S(1)}, u32[]{:S(2)}, u32[]{:S(2)}) collective-permute-start(bf16[1,192,384]{2,1,0:T(8,128)(2,1)S(1)} %get-tuple-element.26), channel_id=1, source_target_pairs={{0,1},{2,3},{4,5},{6,7},{8,9},{10,11},{12,13},{14,15},{16,17},{18,... | collective-permute-start | bytes 442376 | tf_op jit(solution)/shard_map/ppermute | solution.py:12
  14.4 46.6 %copy-start.1 = (bf16[1,1,4,384,384]{4,3,2,1,0:T(8,128)(2,1)S(1)}, bf16[1,1,4,384,384]{4,3,2,1,0:T(8,128)(2,1)}, u32[]{:S(2)}) copy-start(bf16[1,1,4,384,384]{4,3,2,1,0:T(8,128)(2,1)} %param.10) | copy-start | bytes 3538948
  67.5 7.1 %collective-permute-start.4 = (bf16[1,192,384]{2,1,0:T(8,128)(2,1)S(1)}, bf16[1,192,384]{2,1,0:T(8,128)(2,1)S(1)}, u32[]{:S(2)}, u32[]{:S(2)}) collective-permute-start(bf16[1,192,384]{2,1,0:T(8,128)(2,1)S(1)} %get-tuple-element.19), channel_id=1, source_target_pairs={{0,2},{2,4},{4,6},{6,8},{8,10},{10,12},{12,14},{14,16},{16,18},{18... | collective-permute-start | bytes 442376 | tf_op jit(solution)/shard_map/ppermute | solution.py:12
  69.0 5.7 %collective-permute-start.7 = (bf16[1,192,384]{2,1,0:T(8,128)(2,1)S(1)}, bf16[1,192,384]{2,1,0:T(8,128)(2,1)S(1)}, u32[]{:S(2)}, u32[]{:S(2)}) collective-permute-start(bf16[1,192,384]{2,1,0:T(8,128)(2,1)S(1)} %get-tuple-element.20), channel_id=1, source_target_pairs={{1,0},{3,2},{5,4},{7,6},{9,8},{11,10},{13,12},{15,14},{17,16},{19,... | collective-permute-start | bytes 442376 | tf_op jit(solution)/shard_map/ppermute | solution.py:15
  70.2 4.4 %collective-permute-start.6 = (bf16[1,192,384]{2,1,0:T(8,128)(2,1)S(1)}, bf16[1,192,384]{2,1,0:T(8,128)(2,1)S(1)}, u32[]{:S(2)}, u32[]{:S(2)}) collective-permute-start(bf16[1,192,384]{2,1,0:T(8,128)(2,1)S(1)} %get-tuple-element.21), channel_id=1, source_target_pairs={{0,1},{2,3},{4,5},{6,7},{8,9},{10,11},{12,13},{14,15},{16,17},{18,... | collective-permute-start | bytes 442376 | tf_op jit(solution)/shard_map/ppermute | solution.py:12
  73.3 7.0 %collective-permute-start.5 = (bf16[1,192,384]{2,1,0:T(8,128)(2,1)S(1)}, bf16[1,192,384]{2,1,0:T(8,128)(2,1)S(1)}, u32[]{:S(2)}, u32[]{:S(2)}) collective-permute-start(bf16[1,192,384]{2,1,0:T(8,128)(2,1)S(1)} %get-tuple-element.22), channel_id=1, source_target_pairs={{2,0},{4,2},{6,4},{8,6},{10,8},{12,10},{14,12},{16,14},{18,16},{20... | collective-permute-start | bytes 442376 | tf_op jit(solution)/shard_map/ppermute | solution.py:15
  81.1 8.5 %collective-permute-start.8 = (bf16[1,192,384]{2,1,0:T(8,128)(2,1)S(1)}, bf16[1,192,384]{2,1,0:T(8,128)(2,1)S(1)}, u32[]{:S(2)}, u32[]{:S(2)}) collective-permute-start(bf16[1,192,384]{2,1,0:T(8,128)(2,1)S(1)} %get-tuple-element.15), channel_id=1, source_target_pairs={{0,2},{2,4},{4,6},{6,8},{8,10},{10,12},{12,14},{14,16},{16,18},{18... | collective-permute-start | bytes 442376 | tf_op jit(solution)/shard_map/ppermute | solution.py:12
  84.0 5.7 %collective-permute-start.11 = (bf16[1,192,384]{2,1,0:T(8,128)(2,1)S(1)}, bf16[1,192,384]{2,1,0:T(8,128)(2,1)S(1)}, u32[]{:S(2)}, u32[]{:S(2)}) collective-permute-start(bf16[1,192,384]{2,1,0:T(8,128)(2,1)S(1)} %get-tuple-element.16), channel_id=1, source_target_pairs={{1,0},{3,2},{5,4},{7,6},{9,8},{11,10},{13,12},{15,14},{17,16},{19,... | collective-permute-start | bytes 442376 | tf_op jit(solution)/shard_map/ppermute | solution.py:15
  85.3 4.4 %collective-permute-start.10 = (bf16[1,192,384]{2,1,0:T(8,128)(2,1)S(1)}, bf16[1,192,384]{2,1,0:T(8,128)(2,1)S(1)}, u32[]{:S(2)}, u32[]{:S(2)}) collective-permute-start(bf16[1,192,384]{2,1,0:T(8,128)(2,1)S(1)} %get-tuple-element.17), channel_id=1, source_target_pairs={{0,1},{2,3},{4,5},{6,7},{8,9},{10,11},{12,13},{14,15},{16,17},{18,... | collective-permute-start | bytes 442376 | tf_op jit(solution)/shard_map/ppermute | solution.py:12
  88.3 7.0 %collective-permute-start.9 = (bf16[1,192,384]{2,1,0:T(8,128)(2,1)S(1)}, bf16[1,192,384]{2,1,0:T(8,128)(2,1)S(1)}, u32[]{:S(2)}, u32[]{:S(2)}) collective-permute-start(bf16[1,192,384]{2,1,0:T(8,128)(2,1)S(1)} %get-tuple-element.18), channel_id=1, source_target_pairs={{2,0},{4,2},{6,4},{8,6},{10,8},{12,10},{14,12},{16,14},{18,16},{20... | collective-permute-start | bytes 442376 | tf_op jit(solution)/shard_map/ppermute | solution.py:15
  140.3 8.8 %collective-permute-start.12 = (bf16[1,192,384]{2,1,0:T(8,128)(2,1)S(1)}, bf16[1,192,384]{2,1,0:T(8,128)(2,1)S(1)}, u32[]{:S(2)}, u32[]{:S(2)}) collective-permute-start(bf16[1,192,384]{2,1,0:T(8,128)(2,1)S(1)} %get-tuple-element.11), channel_id=1, source_target_pairs={{0,2},{2,4},{4,6},{6,8},{8,10},{10,12},{12,14},{14,16},{16,18},{18... | collective-permute-start | bytes 442376 | tf_op jit(solution)/shard_map/ppermute | solution.py:12
  143.4 5.7 %collective-permute-start.15 = (bf16[1,192,384]{2,1,0:T(8,128)(2,1)S(1)}, bf16[1,192,384]{2,1,0:T(8,128)(2,1)S(1)}, u32[]{:S(2)}, u32[]{:S(2)}) collective-permute-start(bf16[1,192,384]{2,1,0:T(8,128)(2,1)S(1)} %get-tuple-element.12), channel_id=1, source_target_pairs={{1,0},{3,2},{5,4},{7,6},{9,8},{11,10},{13,12},{15,14},{17,16},{19,... | collective-permute-start | bytes 442376 | tf_op jit(solution)/shard_map/ppermute | solution.py:15
  144.7 4.4 %collective-permute-start.14 = (bf16[1,192,384]{2,1,0:T(8,128)(2,1)S(1)}, bf16[1,192,384]{2,1,0:T(8,128)(2,1)S(1)}, u32[]{:S(2)}, u32[]{:S(2)}) collective-permute-start(bf16[1,192,384]{2,1,0:T(8,128)(2,1)S(1)} %get-tuple-element.13), channel_id=1, source_target_pairs={{0,1},{2,3},{4,5},{6,7},{8,9},{10,11},{12,13},{14,15},{16,17},{18,... | collective-permute-start | bytes 442376 | tf_op jit(solution)/shard_map/ppermute | solution.py:12
  147.8 7.0 %collective-permute-start.13 = (bf16[1,192,384]{2,1,0:T(8,128)(2,1)S(1)}, bf16[1,192,384]{2,1,0:T(8,128)(2,1)S(1)}, u32[]{:S(2)}, u32[]{:S(2)}) collective-permute-start(bf16[1,192,384]{2,1,0:T(8,128)(2,1)S(1)} %get-tuple-element.14), channel_id=1, source_target_pairs={{2,0},{4,2},{6,4},{8,6},{10,8},{12,10},{14,12},{16,14},{18,16},{20... | collective-permute-start | bytes 442376 | tf_op jit(solution)/shard_map/ppermute | solution.py:15
  155.5 9.3 %collective-permute-start.16 = (bf16[1,192,384]{2,1,0:T(8,128)(2,1)S(1)}, bf16[1,192,384]{2,1,0:T(8,128)(2,1)S(1)}, u32[]{:S(2)}, u32[]{:S(2)}) collective-permute-start(bf16[1,192,384]{2,1,0:T(8,128)(2,1)S(1)} %get-tuple-element.7), channel_id=1, source_target_pairs={{0,2},{2,4},{4,6},{6,8},{8,10},{10,12},{12,14},{14,16},{16,18},{18... | collective-permute-start | bytes 442376 | tf_op jit(solution)/shard_map/ppermute | solution.py:12
  158.5 6.4 %collective-permute-start.19 = (bf16[1,192,384]{2,1,0:T(8,128)(2,1)S(1)}, bf16[1,192,384]{2,1,0:T(8,128)(2,1)S(1)}, u32[]{:S(2)}, u32[]{:S(2)}) collective-permute-start(bf16[1,192,384]{2,1,0:T(8,128)(2,1)S(1)} %get-tuple-element.8), channel_id=1, source_target_pairs={{1,0},{3,2},{5,4},{7,6},{9,8},{11,10},{13,12},{15,14},{17,16},{19,... | collective-permute-start | bytes 442376 | tf_op jit(solution)/shard_map/ppermute | solution.py:15
  159.8 5.1 %collective-permute-start.18 = (bf16[1,192,384]{2,1,0:T(8,128)(2,1)S(1)}, bf16[1,192,384]{2,1,0:T(8,128)(2,1)S(1)}, u32[]{:S(2)}, u32[]{:S(2)}) collective-permute-start(bf16[1,192,384]{2,1,0:T(8,128)(2,1)S(1)} %get-tuple-element.9), channel_id=1, source_target_pairs={{0,1},{2,3},{4,5},{6,7},{8,9},{10,11},{12,13},{14,15},{16,17},{18,... | collective-permute-start | bytes 442376 | tf_op jit(solution)/shard_map/ppermute | solution.py:12
  162.8 7.0 %collective-permute-start.17 = (bf16[1,192,384]{2,1,0:T(8,128)(2,1)S(1)}, bf16[1,192,384]{2,1,0:T(8,128)(2,1)S(1)}, u32[]{:S(2)}, u32[]{:S(2)}) collective-permute-start(bf16[1,192,384]{2,1,0:T(8,128)(2,1)S(1)} %get-tuple-element.10), channel_id=1, source_target_pairs={{2,0},{4,2},{6,4},{8,6},{10,8},{12,10},{14,12},{16,14},{18,16},{20... | collective-permute-start | bytes 442376 | tf_op jit(solution)/shard_map/ppermute | solution.py:15
  164.8 43.0 %copy-start.24 = (bf16[1,192,384]{2,1,0:T(8,128)(2,1)S(1)}, bf16[1,192,384]{2,1,0:T(8,128)(2,1)}, u32[]{:S(2)}) copy-start(bf16[1,192,384]{2,1,0:T(8,128)(2,1)} %copy-done.23) | copy-start | bytes 442372
  164.8 43.0 %copy-start.26 = (bf16[1,192,384]{2,1,0:T(8,128)(2,1)S(1)}, bf16[1,192,384]{2,1,0:T(8,128)(2,1)}, u32[]{:S(2)}) copy-start(bf16[1,192,384]{2,1,0:T(8,128)(2,1)} %copy-done.25) | copy-start | bytes 442372
  164.8 43.0 %copy-start.28 = (bf16[1,192,384]{2,1,0:T(8,128)(2,1)S(1)}, bf16[1,192,384]{2,1,0:T(8,128)(2,1)}, u32[]{:S(2)}) copy-start(bf16[1,192,384]{2,1,0:T(8,128)(2,1)} %copy-done.27) | copy-start | bytes 442372
  (40 other events, 403.3 us)
where the time goes:
time: 211 us; the launch traced here: 210 us
  blocking collectives  119 us (56%)
  starting transfers between devices  43.4 us (21%)
  waiting for transfers between devices  24 us (11%)
  matrix products  15.6 us (7%)
  other arithmetic  3.87 us (2%)
  local copies, waits for them, and re-layouts  3.46 us (2%)
    all_gather x2, blocking collectives, precondition(): lax.all_gather(primal, ('gx', 'gy'), axis=0, tiled=True)  81.5 us
    psum x1, blocking collectives, per_device(): top = lax.psum(jnp.sum(resid1 * second, axis=(0, 2)), ('gx', 'gy'))  37.5 us
    ppermute x10, starting transfers between devices, with_halo(): lax.ppermute(lax.slice_in_dim(block, block.shape[dim] - width, None, axis...  30.5 us
    ppermute x10, waiting for transfers between devices, with_halo(): lax.ppermute(lax.slice_in_dim(block, 0, width, axis=dim), axis, backward)  24 us
    ppermute x10, starting transfers between devices, with_halo(): lax.ppermute(lax.slice_in_dim(block, 0, width, axis=dim), axis, backward)  12.9 us
    dot_general x6, matrix products, face_mul(): jnp.einsum('fry,fyx->frx', vectors, matrices, preferred_element_type=jnp....  9.97 us
  transfers between devices with their start and end apart: 20, of which 5 were waited for; matrix products, arithmetic and copies ran while one was open for 1% of the time, Pallas kernels for 0%

commit v1 on v0

--- a/solution.py
+++ b/solution.py
@@ -15,6 +15,17 @@
         high = lax.ppermute(lax.slice_in_dim(block, 0, width, axis=dim), axis, backward)
         block = jnp.concatenate([low, block, high], axis=dim)
     return block
+
+
+def gather_rows(block, axes):
+    count = lax.axis_size(axes)
+    spread = jnp.broadcast_to(block[None], (count,) + block.shape)
+    swapped = lax.all_to_all(spread, axes, 0, 0, tiled=False)
+    return swapped.reshape((count * block.shape[0],) + block.shape[1:])
+
+
+def sum_over(block, axes):
+    return jnp.sum(gather_rows(block[None], axes), axis=0)
 
 
 def face_mul(vectors, matrices):
@@ -63,7 +74,7 @@
         primal = jnp.einsum(
             "kfx,frx->kr", picks_half, scaled, preferred_element_type=jnp.float32
         ).astype(jnp.bfloat16)
-        coarse = add_coarse(lax.all_gather(primal, ("gx", "gy"), axis=0, tiled=True))
+        coarse = add_coarse(gather_rows(primal, ("gx", "gy")))
         placed = jnp.einsum("kfx,kr->frx", picks_full, coarse, precision=lax.Precision.HIGHEST)
         weighted = (softened + placed).astype(jnp.bfloat16)
         spread = face_mul(weighted, deluxe_panel).astype(jnp.bfloat16)
@@ -77,9 +88,11 @@
     first = precondition(resid0)
     resid1 = resid0 - apply_operator(first)
     second = precondition(resid1)
-    top = lax.psum(jnp.sum(resid1 * second, axis=(0, 2)), ("gx", "gy"))
     curved = apply_operator(second)
-    bottom = lax.psum(jnp.sum(second * curved, axis=(0, 2)), ("gx", "gy"))
+    partial = jnp.stack(
+        [jnp.sum(resid1 * second, axis=(0, 2)), jnp.sum(second * curved, axis=(0, 2))]
+    )
+    top, bottom = sum_over(partial, ("gx", "gy"))
     step_len = top / bottom
     result = (first + step_len[:, None] * second).astype(jnp.bfloat16)
     return result[None, None]

time: 211 us -> 130 us (0.62)
  blocking collectives: 119 us -> 11.5 us
  starting transfers between devices: 43.4 us -> 57.1 us
  waiting for transfers between devices: 24 us -> 34.6 us
    all_gather x2 -> x0, blocking collectives: 81.5 us -> none  [precondition(): lax.all_gather(primal, ('gx', 'gy'), axis=0, tiled=True)]
    psum x1 -> x0, blocking collectives: 37.5 us -> none  [per_device(): top = lax.psum(jnp.sum(resid1 * second, axis=(0, 2)), ('gx', 'gy'))]
    all_to_all x0 -> x1, blocking collectives: none -> 11.5 us  [gather_rows(): swapped = lax.all_to_all(spread, axes, 0, 0, tiled=False)]
    all_to_all x0 -> x2, waiting for transfers between devices: none -> 10.5 us  [gather_rows(): swapped = lax.all_to_all(spread, axes, 0, 0, tiled=False)]
    all_to_all x0 -> x2, starting transfers between devices: none -> 10.1 us  [gather_rows(): swapped = lax.all_to_all(spread, axes, 0, 0, tiled=False)]
    ppermute x10, starting transfers between devices: 30.5 us -> 34.1 us  [with_halo(): lax.ppermute(lax.slice_in_dim(block, block.shape[dim] - width, None, axis...]
  transfers between devices with their start and end apart: 20 -> 22, of which waited for: 5 -> 7; matrix products, arithmetic and copies ran while one was open for 1% -> 4% of each run, Pallas kernels for 0% -> 0%
where the time goes in v1:
time: 130 us; the launch traced here: 129 us
  starting transfers between devices  57.1 us (44%)
  waiting for transfers between devices  34.6 us (27%)
  matrix products  16.8 us (13%)
  blocking collectives  11.5 us (9%)
  local copies, waits for them, and re-layouts  4.7 us (4%)
  other arithmetic  3.85 us (3%)
    ppermute x10, starting transfers between devices, with_halo(): lax.ppermute(lax.slice_in_dim(block, block.shape[dim] - width, None, axis...  34.1 us
    ppermute x10, waiting for transfers between devices, with_halo(): lax.ppermute(lax.slice_in_dim(block, 0, width, axis=dim), axis, backward)  24.1 us
    ppermute x10, starting transfers between devices, with_halo(): lax.ppermute(lax.slice_in_dim(block, 0, width, axis=dim), axis, backward)  12.9 us
    all_to_all x1, blocking collectives, gather_rows(): swapped = lax.all_to_all(spread, axes, 0, 0, tiled=False)  11.5 us
    dot_general x6, matrix products, face_mul(): jnp.einsum('fry,fyx->frx', vectors, matrices, preferred_element_type=jnp....  11.2 us
    all_to_all x2, waiting for transfers between devices, gather_rows(): swapped = lax.all_to_all(spread, axes, 0, 0, tiled=False)  10.5 us
    all_to_all x2, starting transfers between devices, gather_rows(): swapped = lax.all_to_all(spread, axes, 0, 0, tiled=False)  10.1 us
    dot_general x2, matrix products, precondition(): jnp.einsum('kfx,kr->frx', picks_full, coarse, precision=lax.Precision.HIG...  3.54 us
  transfers between devices with their start and end apart: 22, of which 7 were waited for; matrix products, arithmetic and copies ran while one was open for 4% of the time, Pallas kernels for 0%

profile of v1, /device:TPU:0, one launch (start us, length us, event | category | flops | bytes accessed | tf_op | source)
XLA Modules:
  0.0 129.3 jit_solution(1721538463541319501)
XLA Ops:
  1.3 4.9 %collective-permute-start = (bf16[1,192,384]{2,1,0:T(8,128)(2,1)S(1)}, bf16[1,192,384]{2,1,0:T(8,128)(2,1)S(1)}, u32[]{:S(2)}, u32[]{:S(2)}) collective-permute-start(bf16[1,192,384]{2,1,0:T(8,128)(2,1)S(1)} %get-tuple-element.21), channel_id=1, source_target_pairs={{0,2},{2,4},{4,6},{6,8},{8,10},{10,12},{12,14},{14,16},{16,18},{18... | collective-permute-start | bytes 442376 | tf_op jit(solution)/shard_map/ppermute | solution.py:12
  8.8 3.0 %collective-permute-start.2 = (bf16[1,192,384]{2,1,0:T(8,128)(2,1)S(1)}, bf16[1,192,384]{2,1,0:T(8,128)(2,1)S(1)}, u32[]{:S(2)}, u32[]{:S(2)}) collective-permute-start(bf16[1,192,384]{2,1,0:T(8,128)(2,1)S(1)} %get-tuple-element.24), channel_id=1, source_target_pairs={{0,1},{2,3},{4,5},{6,7},{8,9},{10,11},{12,13},{14,15},{16,17},{18,... | collective-permute-start | bytes 442376 | tf_op jit(solution)/shard_map/ppermute | solution.py:12
  12.4 2.0 %collective-permute-done.1 = bf16[1,192,384]{2,1,0:T(8,128)(2,1)S(1)} collective-permute-done((bf16[1,192,384]{2,1,0:T(8,128)(2,1)S(1)}, bf16[1,192,384]{2,1,0:T(8,128)(2,1)S(1)}, u32[]{:S(2)}, u32[]{:S(2)}) %collective-permute-start.1) | collective-permute-done | bytes 147488 | tf_op jit(solution)/shard_map/ppermute | solution.py:15
  16.1 5.8 %all-to-all-start = ((bf16[32,4,192]{2,1,0:T(4,128)(2,1)}), bf16[32,4,192]{2,1,0:T(4,128)(2,1)}, u32[]{:S(2)}, u32[]{:S(2)}) async-start(bf16[32,4,192]{2,1,0:T(4,128)(2,1)} %broadcast_in_dim.8), calls=%async_computation | async-start | bytes 131072 | tf_op jit(solution)/shard_map/all_to_all | solution.py:23
  23.5 5.8 %all-to-all-done = bf16[32,4,192]{2,1,0:T(4,128)(2,1)} async-done(((bf16[32,4,192]{2,1,0:T(4,128)(2,1)}), bf16[32,4,192]{2,1,0:T(4,128)(2,1)}, u32[]{:S(2)}, u32[]{:S(2)}) %all-to-all-start) | async-done | bytes 49184 | tf_op jit(solution)/shard_map/all_to_all | solution.py:23
  32.1 2.9 %convolution_convert_fusion.4 = bf16[4,192,384]{2,1,0:T(8,128)(2,1)S(1)} fusion(f32[4,192,384]{2,1,0:T(8,128)} %convolution_bitcast_fusion.1, f32[4,192,384]{2,1,0:T(8,128)} %fusion.14, bf16[1,1,4,384,384]{4,3,2,1,0:T(8,128)(2,1)S(1)} %copy-done.1, bf16[1,1,4,384,384]{4,3,2,1,0:T(8,128)(2,1)S(1)} %copy-done, f32[4]{0:T(128)} %multiply_bitcast_fusion), kind=kOutput, calls=%fused_computation.14 | convolution fusion | flops 454754304 | bytes 5308432 | tf_op jit(solution)/shard_map/fry,fyx->frx/dot_general | solution.py:32
  35.1 2.5 %collective-permute-start.4 = (bf16[1,192,384]{2,1,0:T(8,128)(2,1)S(1)}, bf16[1,192,384]{2,1,0:T(8,128)(2,1)S(1)}, u32[]{:S(2)}, u32[]{:S(2)}) collective-permute-start(bf16[1,192,384]{2,1,0:T(8,128)(2,1)S(1)} %get-tuple-element.17), channel_id=1, source_target_pairs={{0,2},{2,4},{4,6},{6,8},{8,10},{10,12},{12,14},{14,16},{16,18},{18... | collective-permute-start | bytes 442376 | tf_op jit(solution)/shard_map/ppermute | solution.py:12
  38.9 3.0 %collective-permute-start.6 = (bf16[1,192,384]{2,1,0:T(8,128)(2,1)S(1)}, bf16[1,192,384]{2,1,0:T(8,128)(2,1)S(1)}, u32[]{:S(2)}, u32[]{:S(2)}) collective-permute-start(bf16[1,192,384]{2,1,0:T(8,128)(2,1)S(1)} %get-tuple-element.19), channel_id=1, source_target_pairs={{0,1},{2,3},{4,5},{6,7},{8,9},{10,11},{12,13},{14,15},{16,17},{18,... | collective-permute-start | bytes 442376 | tf_op jit(solution)/shard_map/ppermute | solution.py:12
  43.3 5.7 %collective-permute-done.5 = bf16[1,192,384]{2,1,0:T(8,128)(2,1)S(1)} collective-permute-done((bf16[1,192,384]{2,1,0:T(8,128)(2,1)S(1)}, bf16[1,192,384]{2,1,0:T(8,128)(2,1)S(1)}, u32[]{:S(2)}, u32[]{:S(2)}) %collective-permute-start.5) | collective-permute-done | bytes 147488 | tf_op jit(solution)/shard_map/ppermute | solution.py:15
  49.7 4.6 %collective-permute-start.8 = (bf16[1,192,384]{2,1,0:T(8,128)(2,1)S(1)}, bf16[1,192,384]{2,1,0:T(8,128)(2,1)S(1)}, u32[]{:S(2)}, u32[]{:S(2)}) collective-permute-start(bf16[1,192,384]{2,1,0:T(8,128)(2,1)S(1)} %get-tuple-element.13), channel_id=1, source_target_pairs={{0,2},{2,4},{4,6},{6,8},{8,10},{10,12},{12,14},{14,16},{16,18},{18... | collective-permute-start | bytes 442376 | tf_op jit(solution)/shard_map/ppermute | solution.py:12
  55.6 3.0 %collective-permute-start.10 = (bf16[1,192,384]{2,1,0:T(8,128)(2,1)S(1)}, bf16[1,192,384]{2,1,0:T(8,128)(2,1)S(1)}, u32[]{:S(2)}, u32[]{:S(2)}) collective-permute-start(bf16[1,192,384]{2,1,0:T(8,128)(2,1)S(1)} %get-tuple-element.15), channel_id=1, source_target_pairs={{0,1},{2,3},{4,5},{6,7},{8,9},{10,11},{12,13},{14,15},{16,17},{18,... | collective-permute-start | bytes 442376 | tf_op jit(solution)/shard_map/ppermute | solution.py:12
  60.0 5.7 %collective-permute-done.9 = bf16[1,192,384]{2,1,0:T(8,128)(2,1)S(1)} collective-permute-done((bf16[1,192,384]{2,1,0:T(8,128)(2,1)S(1)}, bf16[1,192,384]{2,1,0:T(8,128)(2,1)S(1)}, u32[]{:S(2)}, u32[]{:S(2)}) %collective-permute-start.9) | collective-permute-done | bytes 147488 | tf_op jit(solution)/shard_map/ppermute | solution.py:15
  67.9 4.3 %all-to-all-start.1 = ((bf16[32,4,192]{2,1,0:T(4,128)(2,1)}), bf16[32,4,192]{2,1,0:T(4,128)(2,1)S(1)}, u32[]{:S(2)}, u32[]{:S(2)}) async-start(bf16[32,4,192]{2,1,0:T(4,128)(2,1)} %broadcast_in_dim.9), calls=%async_computation.1 | async-start | bytes 131072 | tf_op jit(solution)/shard_map/all_to_all | solution.py:23
  72.2 2.7 %fusion.10 = f32[4,192,384]{2,1,0:T(8,128)} fusion(bf16[4,192,384]{2,1,0:T(8,128)(2,1)} %copy-done.6, bf16[1,1,4,384,384]{4,3,2,1,0:T(8,128)(2,1)S(1)} %copy-done.1), kind=kOutput, calls=%fused_computation.20 | convolution fusion | flops 226492416 | bytes 2949120 | tf_op jit(solution)/shard_map/fry,fyx->frx/dot_general | solution.py:32
  74.8 4.7 %all-to-all-done.1 = bf16[32,4,192]{2,1,0:T(4,128)(2,1)S(1)} async-done(((bf16[32,4,192]{2,1,0:T(4,128)(2,1)}), bf16[32,4,192]{2,1,0:T(4,128)(2,1)S(1)}, u32[]{:S(2)}, u32[]{:S(2)}) %all-to-all-start.1) | async-done | bytes 49184 | tf_op jit(solution)/shard_map/all_to_all | solution.py:23
  81.5 2.9 %convolution_convert_fusion.1 = bf16[4,192,384]{2,1,0:T(8,128)(2,1)S(1)} fusion(f32[4,192,384]{2,1,0:T(8,128)} %convolution_bitcast_fusion, f32[4,192,384]{2,1,0:T(8,128)} %fusion.10, bf16[1,1,4,384,384]{4,3,2,1,0:T(8,128)(2,1)S(1)} %copy-done.1, bf16[1,1,4,384,384]{4,3,2,1,0:T(8,128)(2,1)S(1)} %copy-done, f32[4]{0:T(128)} %multiply_bitcast_fusion), kind=kOutput, calls=%fused_computation.11 | convolution fusion | flops 454754304 | bytes 5308432 | tf_op jit(solution)/shard_map/fry,fyx->frx/dot_general | solution.py:32
  84.5 2.5 %collective-permute-start.12 = (bf16[1,192,384]{2,1,0:T(8,128)(2,1)S(1)}, bf16[1,192,384]{2,1,0:T(8,128)(2,1)S(1)}, u32[]{:S(2)}, u32[]{:S(2)}) collective-permute-start(bf16[1,192,384]{2,1,0:T(8,128)(2,1)S(1)} %get-tuple-element.9), channel_id=1, source_target_pairs={{0,2},{2,4},{4,6},{6,8},{8,10},{10,12},{12,14},{14,16},{16,18},{18... | collective-permute-start | bytes 442376 | tf_op jit(solution)/shard_map/ppermute | solution.py:12
  88.3 3.0 %collective-permute-start.14 = (bf16[1,192,384]{2,1,0:T(8,128)(2,1)S(1)}, bf16[1,192,384]{2,1,0:T(8,128)(2,1)S(1)}, u32[]{:S(2)}, u32[]{:S(2)}) collective-permute-start(bf16[1,192,384]{2,1,0:T(8,128)(2,1)S(1)} %get-tuple-element.11), channel_id=1, source_target_pairs={{0,1},{2,3},{4,5},{6,7},{8,9},{10,11},{12,13},{14,15},{16,17},{18,... | collective-permute-start | bytes 442376 | tf_op jit(solution)/shard_map/ppermute | solution.py:12
  92.7 5.7 %collective-permute-done.13 = bf16[1,192,384]{2,1,0:T(8,128)(2,1)S(1)} collective-permute-done((bf16[1,192,384]{2,1,0:T(8,128)(2,1)S(1)}, bf16[1,192,384]{2,1,0:T(8,128)(2,1)S(1)}, u32[]{:S(2)}, u32[]{:S(2)}) %collective-permute-start.13) | collective-permute-done | bytes 147488 | tf_op jit(solution)/shard_map/ppermute | solution.py:15
  99.1 4.6 %collective-permute-start.16 = (bf16[1,192,384]{2,1,0:T(8,128)(2,1)S(1)}, bf16[1,192,384]{2,1,0:T(8,128)(2,1)S(1)}, u32[]{:S(2)}, u32[]{:S(2)}) collective-permute-start(bf16[1,192,384]{2,1,0:T(8,128)(2,1)S(1)} %get-tuple-element.5), channel_id=1, source_target_pairs={{0,2},{2,4},{4,6},{6,8},{8,10},{10,12},{12,14},{14,16},{16,18},{18... | collective-permute-start | bytes 442376 | tf_op jit(solution)/shard_map/ppermute | solution.py:12
  105.0 3.0 %collective-permute-start.18 = (bf16[1,192,384]{2,1,0:T(8,128)(2,1)S(1)}, bf16[1,192,384]{2,1,0:T(8,128)(2,1)S(1)}, u32[]{:S(2)}, u32[]{:S(2)}) collective-permute-start(bf16[1,192,384]{2,1,0:T(8,128)(2,1)S(1)} %get-tuple-element.7), channel_id=1, source_target_pairs={{0,1},{2,3},{4,5},{6,7},{8,9},{10,11},{12,13},{14,15},{16,17},{18,... | collective-permute-start | bytes 442376 | tf_op jit(solution)/shard_map/ppermute | solution.py:12
  110.0 5.0 %collective-permute-done.17 = bf16[1,192,384]{2,1,0:T(8,128)(2,1)S(1)} collective-permute-done((bf16[1,192,384]{2,1,0:T(8,128)(2,1)S(1)}, bf16[1,192,384]{2,1,0:T(8,128)(2,1)S(1)}, u32[]{:S(2)}, u32[]{:S(2)}) %collective-permute-start.17) | collective-permute-done | bytes 147488 | tf_op jit(solution)/shard_map/ppermute | solution.py:15
  115.5 11.5 %all_to_all.15 = f32[32,1,2,192]{3,2,1,0:T(2,128)S(1)} all-to-all(f32[32,1,2,192]{3,2,1,0:T(2,128)S(1)} %broadcast_in_dim.10), channel_id=1, replica_groups=mesh['gx'=16,'gy'=2] {'gx','gy'}, dimensions={0} | all-to-all | bytes 98304 | tf_op jit(solution)/shard_map/all_to_all | solution.py:23
  127.0 2.3 %fusion.28 = bf16[1,1,4,192,384]{4,3,2,1,0:T(8,128)(2,1)} fusion(bf16[4,192,384]{2,1,0:T(8,128)(2,1)S(1)} %convolution_convert_fusion.1, bf16[4,192,384]{2,1,0:T(8,128)(2,1)S(1)} %convolution_convert_fusion.4, f32[192]{0:T(256)S(1)} %bitcast.83, bf16[1,192,384]{2,1,0:T(8,128)(2,1)} %copy-done.20, bf16[1,192,384]{2,1,0:T(8,128)(2,1)} %copy-done.21, ...), kind=kLoop, calls=%fused_computation.44 | loop fusion | flops 4423680 | bytes 2949888 | tf_op jit(solution)/shard_map/broadcast_in_dim | solution.py:98
  (125 shorter events, 27.5 us)
Async XLA Ops:
  1.3 11.0 %collective-permute-start = (bf16[1,192,384]{2,1,0:T(8,128)(2,1)S(1)}, bf16[1,192,384]{2,1,0:T(8,128)(2,1)S(1)}, u32[]{:S(2)}, u32[]{:S(2)}) collective-permute-start(bf16[1,192,384]{2,1,0:T(8,128)(2,1)S(1)} %get-tuple-element.21), channel_id=1, source_target_pairs={{0,2},{2,4},{4,6},{6,8},{8,10},{10,12},{12,14},{14,16},{16,18},{18... | collective-permute-start | bytes 442376 | tf_op jit(solution)/shard_map/ppermute | solution.py:12
  6.2 8.2 %collective-permute-start.1 = (bf16[1,192,384]{2,1,0:T(8,128)(2,1)S(1)}, bf16[1,192,384]{2,1,0:T(8,128)(2,1)S(1)}, u32[]{:S(2)}, u32[]{:S(2)}) collective-permute-start(bf16[1,192,384]{2,1,0:T(8,128)(2,1)S(1)} %get-tuple-element.22), channel_id=1, source_target_pairs={{2,0},{4,2},{6,4},{8,6},{10,8},{12,10},{14,12},{16,14},{18,16},{20... | collective-permute-start | bytes 442376 | tf_op jit(solution)/shard_map/ppermute | solution.py:15
  7.5 6.9 %collective-permute-start.3 = (bf16[1,192,384]{2,1,0:T(8,128)(2,1)S(1)}, bf16[1,192,384]{2,1,0:T(8,128)(2,1)S(1)}, u32[]{:S(2)}, u32[]{:S(2)}) collective-permute-start(bf16[1,192,384]{2,1,0:T(8,128)(2,1)S(1)} %get-tuple-element.23), channel_id=1, source_target_pairs={{1,0},{3,2},{5,4},{7,6},{9,8},{11,10},{13,12},{15,14},{17,16},{19,... | collective-permute-start | bytes 442376 | tf_op jit(solution)/shard_map/ppermute | solution.py:15
  8.8 5.6 %collective-permute-start.2 = (bf16[1,192,384]{2,1,0:T(8,128)(2,1)S(1)}, bf16[1,192,384]{2,1,0:T(8,128)(2,1)S(1)}, u32[]{:S(2)}, u32[]{:S(2)}) collective-permute-start(bf16[1,192,384]{2,1,0:T(8,128)(2,1)S(1)} %get-tuple-element.24), channel_id=1, source_target_pairs={{0,1},{2,3},{4,5},{6,7},{8,9},{10,11},{12,13},{14,15},{16,17},{18,... | collective-permute-start | bytes 442376 | tf_op jit(solution)/shard_map/ppermute | solution.py:12
  16.1 13.2 %all-to-all-start = ((bf16[32,4,192]{2,1,0:T(4,128)(2,1)}), bf16[32,4,192]{2,1,0:T(4,128)(2,1)}, u32[]{:S(2)}, u32[]{:S(2)}) async-start(bf16[32,4,192]{2,1,0:T(4,128)(2,1)} %broadcast_in_dim.8), calls=%async_computation | async-start | bytes 131072 | tf_op jit(solution)/shard_map/all_to_all | solution.py:23
  35.1 8.1 %collective-permute-start.4 = (bf16[1,192,384]{2,1,0:T(8,128)(2,1)S(1)}, bf16[1,192,384]{2,1,0:T(8,128)(2,1)S(1)}, u32[]{:S(2)}, u32[]{:S(2)}) collective-permute-start(bf16[1,192,384]{2,1,0:T(8,128)(2,1)S(1)} %get-tuple-element.17), channel_id=1, source_target_pairs={{0,2},{2,4},{4,6},{6,8},{8,10},{10,12},{12,14},{14,16},{16,18},{18... | collective-permute-start | bytes 442376 | tf_op jit(solution)/shard_map/ppermute | solution.py:12
  37.6 5.7 %collective-permute-start.7 = (bf16[1,192,384]{2,1,0:T(8,128)(2,1)S(1)}, bf16[1,192,384]{2,1,0:T(8,128)(2,1)S(1)}, u32[]{:S(2)}, u32[]{:S(2)}) collective-permute-start(bf16[1,192,384]{2,1,0:T(8,128)(2,1)S(1)} %get-tuple-element.18), channel_id=1, source_target_pairs={{1,0},{3,2},{5,4},{7,6},{9,8},{11,10},{13,12},{15,14},{17,16},{19,... | collective-permute-start | bytes 442376 | tf_op jit(solution)/shard_map/ppermute | solution.py:15
  38.9 4.4 %collective-permute-start.6 = (bf16[1,192,384]{2,1,0:T(8,128)(2,1)S(1)}, bf16[1,192,384]{2,1,0:T(8,128)(2,1)S(1)}, u32[]{:S(2)}, u32[]{:S(2)}) collective-permute-start(bf16[1,192,384]{2,1,0:T(8,128)(2,1)S(1)} %get-tuple-element.19), channel_id=1, source_target_pairs={{0,1},{2,3},{4,5},{6,7},{8,9},{10,11},{12,13},{14,15},{16,17},{18,... | collective-permute-start | bytes 442376 | tf_op jit(solution)/shard_map/ppermute | solution.py:12
  41.9 7.0 %collective-permute-start.5 = (bf16[1,192,384]{2,1,0:T(8,128)(2,1)S(1)}, bf16[1,192,384]{2,1,0:T(8,128)(2,1)S(1)}, u32[]{:S(2)}, u32[]{:S(2)}) collective-permute-start(bf16[1,192,384]{2,1,0:T(8,128)(2,1)S(1)} %get-tuple-element.20), channel_id=1, source_target_pairs={{2,0},{4,2},{6,4},{8,6},{10,8},{12,10},{14,12},{16,14},{18,16},{20... | collective-permute-start | bytes 442376 | tf_op jit(solution)/shard_map/ppermute | solution.py:15
  49.6 16.7 %copy-start.4 = (bf16[4,192,384]{2,1,0:T(8,128)(2,1)}, bf16[4,192,384]{2,1,0:T(8,128)(2,1)S(1)}, u32[]{:S(2)}) copy-start(bf16[4,192,384]{2,1,0:T(8,128)(2,1)S(1)} %convolution_convert_fusion.3) | copy-start | bytes 1769476
  49.6 16.1 %copy-start.17 = (bf16[1,192,384]{2,1,0:T(8,128)(2,1)S(1)}, bf16[1,192,384]{2,1,0:T(8,128)(2,1)}, u32[]{:S(2)}) copy-start(bf16[1,192,384]{2,1,0:T(8,128)(2,1)} %copy-done.16) | copy-start | bytes 442372
  49.7 10.2 %collective-permute-start.8 = (bf16[1,192,384]{2,1,0:T(8,128)(2,1)S(1)}, bf16[1,192,384]{2,1,0:T(8,128)(2,1)S(1)}, u32[]{:S(2)}, u32[]{:S(2)}) collective-permute-start(bf16[1,192,384]{2,1,0:T(8,128)(2,1)S(1)} %get-tuple-element.13), channel_id=1, source_target_pairs={{0,2},{2,4},{4,6},{6,8},{8,10},{10,12},{12,14},{14,16},{16,18},{18... | collective-permute-start | bytes 442376 | tf_op jit(solution)/shard_map/ppermute | solution.py:12
  54.3 5.7 %collective-permute-start.11 = (bf16[1,192,384]{2,1,0:T(8,128)(2,1)S(1)}, bf16[1,192,384]{2,1,0:T(8,128)(2,1)S(1)}, u32[]{:S(2)}, u32[]{:S(2)}) collective-permute-start(bf16[1,192,384]{2,1,0:T(8,128)(2,1)S(1)} %get-tuple-element.14), channel_id=1, source_target_pairs={{1,0},{3,2},{5,4},{7,6},{9,8},{11,10},{13,12},{15,14},{17,16},{19,... | collective-permute-start | bytes 442376 | tf_op jit(solution)/shard_map/ppermute | solution.py:15
  55.6 4.4 %collective-permute-start.10 = (bf16[1,192,384]{2,1,0:T(8,128)(2,1)S(1)}, bf16[1,192,384]{2,1,0:T(8,128)(2,1)S(1)}, u32[]{:S(2)}, u32[]{:S(2)}) collective-permute-start(bf16[1,192,384]{2,1,0:T(8,128)(2,1)S(1)} %get-tuple-element.15), channel_id=1, source_target_pairs={{0,1},{2,3},{4,5},{6,7},{8,9},{10,11},{12,13},{14,15},{16,17},{18,... | collective-permute-start | bytes 442376 | tf_op jit(solution)/shard_map/ppermute | solution.py:12
  58.6 7.0 %collective-permute-start.9 = (bf16[1,192,384]{2,1,0:T(8,128)(2,1)S(1)}, bf16[1,192,384]{2,1,0:T(8,128)(2,1)S(1)}, u32[]{:S(2)}, u32[]{:S(2)}) collective-permute-start(bf16[1,192,384]{2,1,0:T(8,128)(2,1)S(1)} %get-tuple-element.16), channel_id=1, source_target_pairs={{2,0},{4,2},{6,4},{8,6},{10,8},{12,10},{14,12},{16,14},{18,16},{20... | collective-permute-start | bytes 442376 | tf_op jit(solution)/shard_map/ppermute | solution.py:15
  67.9 11.7 %all-to-all-start.1 = ((bf16[32,4,192]{2,1,0:T(4,128)(2,1)}), bf16[32,4,192]{2,1,0:T(4,128)(2,1)S(1)}, u32[]{:S(2)}, u32[]{:S(2)}) async-start(bf16[32,4,192]{2,1,0:T(4,128)(2,1)} %broadcast_in_dim.9), calls=%async_computation.1 | async-start | bytes 131072 | tf_op jit(solution)/shard_map/all_to_all | solution.py:23
  84.5 8.1 %collective-permute-start.12 = (bf16[1,192,384]{2,1,0:T(8,128)(2,1)S(1)}, bf16[1,192,384]{2,1,0:T(8,128)(2,1)S(1)}, u32[]{:S(2)}, u32[]{:S(2)}) collective-permute-start(bf16[1,192,384]{2,1,0:T(8,128)(2,1)S(1)} %get-tuple-element.9), channel_id=1, source_target_pairs={{0,2},{2,4},{4,6},{6,8},{8,10},{10,12},{12,14},{14,16},{16,18},{18... | collective-permute-start | bytes 442376 | tf_op jit(solution)/shard_map/ppermute | solution.py:12
  87.0 5.7 %collective-permute-start.15 = (bf16[1,192,384]{2,1,0:T(8,128)(2,1)S(1)}, bf16[1,192,384]{2,1,0:T(8,128)(2,1)S(1)}, u32[]{:S(2)}, u32[]{:S(2)}) collective-permute-start(bf16[1,192,384]{2,1,0:T(8,128)(2,1)S(1)} %get-tuple-element.10), channel_id=1, source_target_pairs={{1,0},{3,2},{5,4},{7,6},{9,8},{11,10},{13,12},{15,14},{17,16},{19,... | collective-permute-start | bytes 442376 | tf_op jit(solution)/shard_map/ppermute | solution.py:15
  88.3 4.4 %collective-permute-start.14 = (bf16[1,192,384]{2,1,0:T(8,128)(2,1)S(1)}, bf16[1,192,384]{2,1,0:T(8,128)(2,1)S(1)}, u32[]{:S(2)}, u32[]{:S(2)}) collective-permute-start(bf16[1,192,384]{2,1,0:T(8,128)(2,1)S(1)} %get-tuple-element.11), channel_id=1, source_target_pairs={{0,1},{2,3},{4,5},{6,7},{8,9},{10,11},{12,13},{14,15},{16,17},{18,... | collective-permute-start | bytes 442376 | tf_op jit(solution)/shard_map/ppermute | solution.py:12
  91.3 7.0 %collective-permute-start.13 = (bf16[1,192,384]{2,1,0:T(8,128)(2,1)S(1)}, bf16[1,192,384]{2,1,0:T(8,128)(2,1)S(1)}, u32[]{:S(2)}, u32[]{:S(2)}) collective-permute-start(bf16[1,192,384]{2,1,0:T(8,128)(2,1)S(1)} %get-tuple-element.12), channel_id=1, source_target_pairs={{2,0},{4,2},{6,4},{8,6},{10,8},{12,10},{14,12},{16,14},{18,16},{20... | collective-permute-start | bytes 442376 | tf_op jit(solution)/shard_map/ppermute | solution.py:15
  99.1 10.9 %collective-permute-start.16 = (bf16[1,192,384]{2,1,0:T(8,128)(2,1)S(1)}, bf16[1,192,384]{2,1,0:T(8,128)(2,1)S(1)}, u32[]{:S(2)}, u32[]{:S(2)}) collective-permute-start(bf16[1,192,384]{2,1,0:T(8,128)(2,1)S(1)} %get-tuple-element.5), channel_id=1, source_target_pairs={{0,2},{2,4},{4,6},{6,8},{8,10},{10,12},{12,14},{14,16},{16,18},{18... | collective-permute-start | bytes 442376 | tf_op jit(solution)/shard_map/ppermute | solution.py:12
  103.7 6.3 %collective-permute-start.19 = (bf16[1,192,384]{2,1,0:T(8,128)(2,1)S(1)}, bf16[1,192,384]{2,1,0:T(8,128)(2,1)S(1)}, u32[]{:S(2)}, u32[]{:S(2)}) collective-permute-start(bf16[1,192,384]{2,1,0:T(8,128)(2,1)S(1)} %get-tuple-element.6), channel_id=1, source_target_pairs={{1,0},{3,2},{5,4},{7,6},{9,8},{11,10},{13,12},{15,14},{17,16},{19,... | collective-permute-start | bytes 442376 | tf_op jit(solution)/shard_map/ppermute | solution.py:15
  105.0 5.0 %collective-permute-start.18 = (bf16[1,192,384]{2,1,0:T(8,128)(2,1)S(1)}, bf16[1,192,384]{2,1,0:T(8,128)(2,1)S(1)}, u32[]{:S(2)}, u32[]{:S(2)}) collective-permute-start(bf16[1,192,384]{2,1,0:T(8,128)(2,1)S(1)} %get-tuple-element.7), channel_id=1, source_target_pairs={{0,1},{2,3},{4,5},{6,7},{8,9},{10,11},{12,13},{14,15},{16,17},{18,... | collective-permute-start | bytes 442376 | tf_op jit(solution)/shard_map/ppermute | solution.py:12
  108.0 7.0 %collective-permute-start.17 = (bf16[1,192,384]{2,1,0:T(8,128)(2,1)S(1)}, bf16[1,192,384]{2,1,0:T(8,128)(2,1)S(1)}, u32[]{:S(2)}, u32[]{:S(2)}) collective-permute-start(bf16[1,192,384]{2,1,0:T(8,128)(2,1)S(1)} %get-tuple-element.8), channel_id=1, source_target_pairs={{2,0},{4,2},{6,4},{8,6},{10,8},{12,10},{14,12},{16,14},{18,16},{20... | collective-permute-start | bytes 442376 | tf_op jit(solution)/shard_map/ppermute | solution.py:15
  (34 other events, 288.5 us)

commit v2 on v1

v2 whole, which is shorter than its diff:
```python
import jax
import jax.numpy as jnp
from jax import lax
from jax.sharding import PartitionSpec as P

PARTNERS = (("gx", True, 1), ("gx", False, 0), ("gy", True, 3), ("gy", False, 2))


def from_partner(values, axis, from_lower):
    count = lax.axis_size(axis)
    if from_lower:
        pairs = [(i, i + 1) for i in range(count - 1)]
    else:
        pairs = [(i + 1, i) for i in range(count - 1)]
    return lax.ppermute(values, axis, pairs)


def gather_rows(block, axes):
    count = lax.axis_size(axes)
    spread = jnp.broadcast_to(block[None], (count,) + block.shape)
    swapped = lax.all_to_all(spread, axes, 0, 0, tiled=False)
    return swapped.reshape((count * block.shape[0],) + block.shape[1:])


def sum_over(block, axes):
    return jnp.sum(gather_rows(block[None], axes), axis=0)


def face_mul(vectors, matrices):
    return jnp.einsum("fry,fyx->frx", vectors, matrices, preferred_element_type=jnp.float32)


def to_half(values):
    return lax.reduce_precision(values, exponent_bits=8, mantissa_bits=7)


def face_mul_turned(vectors, matrices):
    return jnp.einsum("fry,fxy->frx", vectors, matrices, preferred_element_type=jnp.float32)


def per_device(load_parts, schur, deluxe, panels, coarse_inverse, primal_dofs, damage_flags):
    loads_here = load_parts[0, 0]
    schur_own = schur[0, 0]
    deluxe_own = deluxe[0, 0]
    panels_own = panels[0, 0]
    primal_slots = primal_dofs[0, 0]
    flag_values = damage_flags[0, 0]
    width = loads_here.shape[2]
    primal_count = primal_slots.shape[0]
    rows = coarse_inverse.shape[1]

    small = jnp.concatenate(
        [
            coarse_inverse,
            jnp.pad(
                jnp.concatenate([primal_slots, flag_values]).astype(jnp.float32)[None],
                ((0, 0), (0, rows - 2 * primal_count)),
            ),
        ]
    )
    load_partner, mats_partner, small_partner = [], [], []
    for axis, from_lower, face in PARTNERS:
        load_partner.append(from_partner(loads_here[face], axis, from_lower))
        small_partner.append(from_partner(small, axis, from_lower))
        mats = jnp.stack([deluxe_own[face], panels_own[face], schur_own[face]])
        mats_partner.append(from_partner(mats, axis, from_lower))
    load_partner = jnp.stack(load_partner)
    mats_partner = jnp.stack(mats_partner)
    small_partner = jnp.stack(small_partner)
    deluxe_partner = mats_partner[:, 0]
    panels_partner = mats_partner[:, 1]
    schur_partner = mats_partner[:, 2]

    coarse_rows = jnp.concatenate(
        [coarse_inverse, small_partner[:, :primal_count].reshape(-1, small_partner.shape[2])]
    )
    partner_slots = small_partner[:, primal_count, :primal_count].astype(jnp.int32)
    partner_flags = jnp.stack(
        [small_partner[p, primal_count, primal_count + face] for p, (_, _, face) in enumerate(PARTNERS)]
    )
    partner_offsets = jnp.array([face * width for _, _, face in PARTNERS], jnp.int32)

    positions = jnp.arange(4 * width, dtype=jnp.int32)
    picks = (primal_slots[:, None] == positions[None, :]).reshape(primal_count, 4, width)
    picks_half = picks.astype(jnp.bfloat16)
    picks_full = picks.astype(jnp.float32)
    flags_full = flag_values.astype(jnp.float32)
    face_positions = jnp.arange(width, dtype=jnp.int32)
    partner_picks = (
        partner_slots[:, :, None] == (partner_offsets[:, None, None] + face_positions[None, None, :])
    ).astype(jnp.float32)

    def local_side(resid_half, deluxe_panel, inverse_panel, flags):
        scaled = face_mul_turned(resid_half, deluxe_panel).astype(jnp.bfloat16)
        local_part = face_mul(scaled, inverse_panel)
        extra = face_mul(local_part.astype(jnp.bfloat16), inverse_panel)
        return scaled, local_part + 0.5 * flags[:, None, None] * extra

    def precondition(resid):
        resid_half = resid.astype(jnp.bfloat16)
        scaled, softened_own = local_side(resid_half, deluxe_own, panels_own, flags_full)
        _, softened_partner = local_side(resid_half, deluxe_partner, panels_partner, partner_flags)
        primal = jnp.einsum(
            "kfx,frx->kr", picks_half, scaled, preferred_element_type=jnp.float32
        ).astype(jnp.bfloat16)
        primal_all = gather_rows(primal, ("gx", "gy")).astype(jnp.float32)
        coarse = jnp.dot(coarse_rows, primal_all, precision=lax.Precision.HIGHEST)
        coarse_own = coarse[:primal_count]
        coarse_partner = coarse[primal_count:].reshape(4, primal_count, -1)
        placed_own = jnp.einsum("kfx,kr->frx", picks_full, coarse_own, precision=lax.Precision.HIGHEST)
        placed_partner = jnp.einsum(
            "pkx,pkr->prx", partner_picks, coarse_partner, precision=lax.Precision.HIGHEST
        )
        weighted_own = (softened_own + placed_own).astype(jnp.bfloat16)
        weighted_partner = (softened_partner + placed_partner).astype(jnp.bfloat16)
        spread_own = to_half(face_mul(weighted_own, deluxe_own))
        spread_partner = to_half(face_mul(weighted_partner, deluxe_partner))
        return spread_own + spread_partner

    def apply_operator(field):
        field_half = field.astype(jnp.bfloat16)
        bent_own = to_half(face_mul(field_half, schur_own))
        bent_partner = to_half(face_mul(field_half, schur_partner))
        return bent_own + bent_partner

    resid0 = loads_here.astype(jnp.float32) + load_partner.astype(jnp.float32)
    first = precondition(resid0)
    resid1 = resid0 - apply_operator(first)
    second = precondition(resid1)
    curved = apply_operator(second)
    partial = jnp.stack(
        [jnp.sum(resid1 * second, axis=(0, 2)), jnp.sum(second * curved, axis=(0, 2))]
    )
    top, bottom = sum_over(partial, ("gx", "gy"))
    step_len = top / bottom
    result = (first + step_len[:, None] * second).astype(jnp.bfloat16)
    return result[None, None]


def solution(mesh):
    return jax.shard_map(
        per_device,
        mesh=mesh,
        in_specs=(
            P("gx", "gy", None, None, None),
            P("gx", "gy", None, None, None),
            P("gx", "gy", None, None, None),
            P("gx", "gy", None, None, None),
            P(("gx", "gy"), None),
            P("gx", "gy", None),
            P("gx", "gy", None),
        ),
        out_specs=P("gx", "gy", None, None, None),
        check_vma=False,
    )
```

time: 130 us -> 165 us (1.27)
  matrix products: 16.8 us -> 50.2 us
  other arithmetic: 3.85 us -> 15.7 us
  starting transfers between devices: 57.1 us -> 47.9 us
  local copies, waits for them, and re-layouts: 4.7 us -> 11.1 us
  waiting for transfers between devices: 34.6 us -> 29 us
  blocking collectives: 11.5 us -> 9.1 us
    ppermute x20 -> x12, waiting for transfers between devices: 24.1 us -> 0.03 us  [from_partner(): return lax.ppermute(values, axis, pairs)]
    dot_general x6 -> x12, matrix products: 11.2 us -> 35.1 us  [face_mul(): jnp.einsum('fry,fyx->frx', vectors, matrices, preferred_element_type=jnp....]
    all_to_all x2, waiting for transfers between devices: 10.5 us -> 29 us  [gather_rows(): swapped = lax.all_to_all(spread, axes, 0, 0, tiled=False)]
    ppermute x20 -> x12, starting transfers between devices: 47.1 us -> 35 us  [from_partner(): return lax.ppermute(values, axis, pairs)]
    another operation x0 -> x6, other arithmetic: none -> 6.49 us  [the longest x4 4.22 us: per_device(): mats = jnp.stack([deluxe_own[face], panels_own[face], schur_own[face]])]
    dot_general x4 -> x6, matrix products: 3.78 us -> 10.2 us  [the longest x2 5.15 us: precondition(): jnp.einsum('pkx,pkr->prx', partner_picks, coarse_partner, precision=lax.P...]
    mul x1 -> x2, other arithmetic: 0.51 us -> 3.82 us  [local_side(): return (scaled, local_part + 0.5 * flags[:, None, None] * extra)]
    all_to_all x2, starting transfers between devices: 10.1 us -> 12.9 us  [gather_rows(): swapped = lax.all_to_all(spread, axes, 0, 0, tiled=False)]
  transfers between devices with their start and end apart: 22 -> 14, of which waited for: 7 -> 2; matrix products, arithmetic and copies ran while one was open for 4% -> 17% of each run, Pallas kernels for 0% -> 0%
where the time goes in v2:
time: 165 us; the launch traced here: 164 us
  matrix products  50.2 us (30%)
  starting transfers between devices  47.9 us (29%)
  waiting for transfers between devices  29 us (18%)
  other arithmetic  15.7 us (10%)
  local copies, waits for them, and re-layouts  11.1 us (7%)
  blocking collectives  9.1 us (6%)
    dot_general x12, matrix products, face_mul(): jnp.einsum('fry,fyx->frx', vectors, matrices, preferred_element_type=jnp....  35.1 us
    ppermute x12, starting transfers between devices, from_partner(): return lax.ppermute(values, axis, pairs)  35 us
    all_to_all x2, waiting for transfers between devices, gather_rows(): swapped = lax.all_to_all(spread, axes, 0, 0, tiled=False)  29 us
    all_to_all x2, starting transfers between devices, gather_rows(): swapped = lax.all_to_all(spread, axes, 0, 0, tiled=False)  12.9 us
    all_to_all x1, blocking collectives, gather_rows(): swapped = lax.all_to_all(spread, axes, 0, 0, tiled=False)  9.1 us
    dot_general x2, matrix products, precondition(): jnp.einsum('pkx,pkr->prx', partner_picks, coarse_partner, precision=lax.P...  5.15 us
    another operation x4, other arithmetic, per_device(): mats = jnp.stack([deluxe_own[face], panels_own[face], schur_own[face]])  4.22 us
    dot_general x2, matrix products, precondition(): jnp.einsum('kfx,kr->frx', picks_full, coarse_own, precision=lax.Precision...  3.89 us
  transfers between devices with their start and end apart: 14, of which 2 were waited for; matrix products, arithmetic and copies ran while one was open for 17% of the time, Pallas kernels for 0%

profile of v2, /device:TPU:0, one launch (start us, length us, event | category | flops | bytes accessed | tf_op | source)
XLA Modules:
  0.0 163.5 jit_solution(1190861123004753170)
XLA Ops:
  2.8 3.0 %collective-permute-start.6 = (f32[5,128]{1,0:T(8,128)S(1)}, f32[5,128]{1,0:T(8,128)S(1)}, u32[]{:S(2)}, u32[]{:S(2)}) collective-permute-start(f32[5,128]{1,0:T(8,128)S(1)} %select_maximum_fusion), channel_id=1, source_target_pairs={{0,1},{2,3},{4,5},{6,7},{8,9},{10,11},{12,13},{14,15},{16,17},{18,... | collective-permute-start | bytes 7688 | tf_op jit(solution)/shard_map/ppermute | solution.py:15
  7.2 5.5 %collective-permute-start.4 = (f32[5,128]{1,0:T(8,128)S(1)}, f32[5,128]{1,0:T(8,128)S(1)}, u32[]{:S(2)}, u32[]{:S(2)}) collective-permute-start(f32[5,128]{1,0:T(8,128)S(1)} %select_maximum_fusion), channel_id=1, source_target_pairs={{0,2},{2,4},{4,6},{6,8},{8,10},{10,12},{12,14},{14,16},{16,18},{18... | collective-permute-start | bytes 7688 | tf_op jit(solution)/shard_map/ppermute | solution.py:15
  13.8 4.8 %collective-permute-start = (bf16[192,384]{1,0:T(8,128)(2,1)S(1)}, bf16[192,384]{1,0:T(8,128)(2,1)S(1)}, u32[]{:S(2)}, u32[]{:S(2)}) collective-permute-start(bf16[192,384]{1,0:T(8,128)(2,1)S(1)} %get-tuple-element.17), channel_id=1, source_target_pairs={{0,2},{2,4},{4,6},{6,8},{8,10},{10,12},{12,14},{14,16},{16,18},{18... | collective-permute-start | bytes 442376 | tf_op jit(solution)/shard_map/ppermute | solution.py:15
  29.8 3.0 %collective-permute-start.2 = (bf16[192,384]{1,0:T(8,128)(2,1)S(1)}, bf16[192,384]{1,0:T(8,128)(2,1)S(1)}, u32[]{:S(2)}, u32[]{:S(2)}) collective-permute-start(bf16[192,384]{1,0:T(8,128)(2,1)S(1)} %get-tuple-element.20), channel_id=1, source_target_pairs={{0,1},{2,3},{4,5},{6,7},{8,9},{10,11},{12,13},{14,15},{16,17},{18,... | collective-permute-start | bytes 442376 | tf_op jit(solution)/shard_map/ppermute | solution.py:15
  35.4 3.3 %maximum_multiply_fusion = f32[4]{0:T(128)} fusion(f32[1]{0:T(128)} %bitcast.44, f32[1]{0:T(128)} %bitcast.43, f32[1]{0:T(128)} %bitcast.42, f32[1]{0:T(128)} %bitcast.41), kind=kLoop, calls=%fused_computation.133 | loop fusion | flops 16 | bytes 32 | tf_op jit(solution)/shard_map/mul | solution.py:97
  40.5 4.9 %collective-permute-start.10 = (bf16[3,384,384]{2,1,0:T(8,128)(2,1)}, bf16[3,384,384]{2,1,0:T(8,128)(2,1)}, u32[]{:S(2)}, u32[]{:S(2)}) collective-permute-start(bf16[3,384,384]{2,1,0:T(8,128)(2,1)} %pad_maximum_fusion.3), channel_id=1, source_target_pairs={{0,1},{2,3},{4,5},{6,7},{8,9},{10,11},{12,13},{14,15},{16,17},{18,... | collective-permute-start | bytes 2654216 | tf_op jit(solution)/shard_map/ppermute | solution.py:15
  45.4 6.1 %collective-permute-start.8 = (bf16[3,384,384]{2,1,0:T(8,128)(2,1)}, bf16[3,384,384]{2,1,0:T(8,128)(2,1)}, u32[]{:S(2)}, u32[]{:S(2)}) collective-permute-start(bf16[3,384,384]{2,1,0:T(8,128)(2,1)} %pad_maximum_fusion.1), channel_id=1, source_target_pairs={{0,2},{2,4},{4,6},{6,8},{8,10},{10,12},{12,14},{14,16},{16,18},{18... | collective-permute-start | bytes 2654216 | tf_op jit(solution)/shard_map/ppermute | solution.py:15
  53.1 6.9 %all-to-all-start = ((bf16[32,4,192]{2,1,0:T(4,128)(2,1)}), bf16[32,4,192]{2,1,0:T(4,128)(2,1)S(1)}, u32[]{:S(2)}, u32[]{:S(2)}) async-start(bf16[32,4,192]{2,1,0:T(4,128)(2,1)} %broadcast_in_dim.8), calls=%async_computation | async-start | bytes 131072 | tf_op jit(solution)/shard_map/all_to_all | solution.py:21
  61.6 24.8 %all-to-all-done = bf16[32,4,192]{2,1,0:T(4,128)(2,1)S(1)} async-done(((bf16[32,4,192]{2,1,0:T(4,128)(2,1)}), bf16[32,4,192]{2,1,0:T(4,128)(2,1)S(1)}, u32[]{:S(2)}, u32[]{:S(2)}) %all-to-all-start) | async-done | bytes 49184 | tf_op jit(solution)/shard_map/all_to_all | solution.py:21
  89.3 2.6 %fusion.67 = f32[4,192,384]{2,1,0:T(8,128)} fusion(f32[4,4,192]{2,1,0:T(4,128)S(1)} %copy-done.17, s32[4,384]{1,0:T(4,128)} %iota_add_fusion, s32[4,4]{1,0:T(4,128)} %bitcast.156), kind=kOutput, calls=%fused_computation.105 | convolution fusion | flops 14161920 | bytes 1198144 | tf_op jit(solution)/shard_map/pkx,pkr->prx/dot_general | solution.py:111
  91.9 3.5 %convolution_reduce-precision_fusion.7 = f32[4,192,384]{2,1,0:T(8,128)} fusion(f32[4,192,384]{2,1,0:T(8,128)S(1)} %convolution_bitcast_fusion.1, f32[4,192,384]{2,1,0:T(8,128)} %fusion.29, bf16[1,1,4,384,384]{4,3,2,1,0:T(8,128)(2,1)S(1)} %copy-done, bf16[1,1,4,384,384]{4,3,2,1,0:T(8,128)(2,1)S(1)} %copy-done.3, f32[4]{0:T(128)} %multiply_bitcast_fusion), kind=kOutput, calls=%fused_computation.23 | convolution fusion | flops 454754304 | bytes 5898256 | tf_op jit(solution)/shard_map/fry,fyx->frx/dot_general | solution.py:30
  97.7 3.3 %fusion.19 = f32[4,192,384]{2,1,0:T(8,128)} fusion(bf16[4,3,384,384]{3,2,0,1:T(8,128)(2,1)S(1)} %pad_maximum_fusion, bf16[1,1,4,192,384]{4,3,2,1,0:T(8,128)(2,1)} %param.8, bf16[1,192,384]{2,1,0:T(8,128)(2,1)} %bitcast.149, bf16[1,192,384]{2,1,0:T(8,128)(2,1)} %bitcast.152, bf16[1,192,384]{2,1,0:T(8,128)(2,1)} %bitcast.146, bf16[1,192,384]{2,1,0:T(8,128)(2,1)} %bitcast.143), kind=kOutput, calls=%fused_computation.38 | convolution fusion | flops 455344128 | bytes 4718592 | tf_op jit(solution)/shard_map/fry,fyx->frx/dot_general | solution.py:30
  101.0 4.3 %fusion.9 = f32[4,192,384]{2,1,0:T(8,128)} fusion(f32[4,192,384]{2,1,0:T(8,128)} %convolution_reduce-precision_fusion.7, f32[4,192,384]{2,1,0:T(8,128)} %fusion.67, f32[4,192,384]{2,1,0:T(8,128)} %fusion.19, bf16[4,3,384,384]{3,2,0,1:T(8,128)(2,1)S(1)} %pad_maximum_fusion, f32[4]{0:T(128)} %maximum_multiply_fusion), kind=kOutput, calls=%fused_computation.19 | convolution fusion | flops 455049216 | bytes 8258048 | tf_op jit(solution)/shard_map/fry,fyx->frx/dot_general | solution.py:30
  109.3 2.7 %convolution_convert_fusion.1 = bf16[4,192,384]{2,1,0:T(8,128)(2,1)} fusion(bf16[1,1,4,384,384]{4,3,2,1,0:T(8,128)(2,1)S(1)} %copy-done.4, f32[4,192,384]{2,1,0:T(8,128)} %fusion.8), kind=kOutput, calls=%fused_computation.34 | convolution fusion | flops 227082240 | bytes 2949120 | tf_op jit(solution)/shard_map/fry,fxy->frx/dot_general | solution.py:38
  112.1 3.3 %fusion.20 = f32[4,192,384]{2,1,0:T(8,128)} fusion(bf16[4,3,384,384]{3,2,0,1:T(8,128)(2,1)S(1)} %pad_maximum_fusion, f32[4,192,384]{2,1,0:T(8,128)} %fusion.8), kind=kOutput, calls=%fused_computation.39 | convolution fusion | flops 453574656 | bytes 4718592 | tf_op jit(solution)/shard_map/fry,fyx->frx/dot_general | solution.py:30
  117.4 6.0 %all-to-all-start.1 = ((bf16[32,4,192]{2,1,0:T(4,128)(2,1)}), bf16[32,4,192]{2,1,0:T(4,128)(2,1)}, u32[]{:S(2)}, u32[]{:S(2)}) async-start(bf16[32,4,192]{2,1,0:T(4,128)(2,1)} %broadcast_in_dim.9), calls=%async_computation.1 | async-start | bytes 131072 | tf_op jit(solution)/shard_map/all_to_all | solution.py:21
  123.4 3.0 %fusion.25 = f32[4,192,384]{2,1,0:T(8,128)} fusion(bf16[4,192,384]{2,1,0:T(8,128)(2,1)} %convolution_convert_fusion.1, bf16[1,1,4,384,384]{4,3,2,1,0:T(8,128)(2,1)} %param.11), kind=kOutput, calls=%fused_computation.47 | convolution fusion | flops 226492416 | bytes 2949120 | tf_op jit(solution)/shard_map/fry,fyx->frx/dot_general | solution.py:30
  126.4 4.2 %all-to-all-done.1 = bf16[32,4,192]{2,1,0:T(4,128)(2,1)} async-done(((bf16[32,4,192]{2,1,0:T(4,128)(2,1)}), bf16[32,4,192]{2,1,0:T(4,128)(2,1)}, u32[]{:S(2)}, u32[]{:S(2)}) %all-to-all-start.1) | async-done | bytes 49184 | tf_op jit(solution)/shard_map/all_to_all | solution.py:21
  133.7 2.5 %convolution_bitcast_fusion = f32[4,192,384]{2,1,0:T(8,128)} fusion(s32[4,384]{1,0:T(4,128)S(1)} %multiply_add_fusion, s32[4]{0:T(128)} %bitcast.173, f32[20,192]{1,0:T(8,128)S(1)} %fusion.81), kind=kOutput, calls=%fused_computation.27 | convolution fusion | flops 14161920 | bytes 1189904 | tf_op jit(solution)/shard_map/kfx,kr->frx/dot_general | solution.py:110
  136.9 2.6 %fusion.65 = f32[4,192,384]{2,1,0:T(8,128)} fusion(f32[4,4,192]{2,1,0:T(4,128)S(1)} %reshape.171, s32[4,384]{1,0:T(4,128)} %iota_add_fusion, s32[4,4]{1,0:T(4,128)} %bitcast.157), kind=kOutput, calls=%fused_computation.103 | convolution fusion | flops 14161920 | bytes 1198144 | tf_op jit(solution)/shard_map/pkx,pkr->prx/dot_general | solution.py:111
  139.5 4.6 %convolution_reduce-precision_fusion.3 = f32[4,192,384]{2,1,0:T(8,128)} fusion(f32[4,192,384]{2,1,0:T(8,128)} %convolution_bitcast_fusion, f32[4,192,384]{2,1,0:T(8,128)} %fusion.25, bf16[1,1,4,384,384]{4,3,2,1,0:T(8,128)(2,1)} %param.11, bf16[1,1,4,384,384]{4,3,2,1,0:T(8,128)(2,1)} %param.10, f32[4]{0:T(128)} %multiply_bitcast_fusion), kind=kOutput, calls=%fused_computation.10 | convolution fusion | flops 454754304 | bytes 5898256 | tf_op jit(solution)/shard_map/fry,fyx->frx/dot_general | solution.py:30
  144.1 4.6 %multiply_reduce_fusion = (f32[192]{0:T(256)S(1)}, f32[4,192,384]{2,1,0:T(8,128)}) fusion(f32[4,192,384]{2,1,0:T(8,128)} %fusion.8, f32[4,192,384]{2,1,0:T(8,128)} %convolution_reduce-precision_fusion.3, bf16[4,3,384,384]{3,2,0,1:T(8,128)(2,1)S(1)} %pad_maximum_fusion, f32[4,192,384]{2,1,0:T(8,128)} %fusion.65, f32[4,192,384]{2,1,0:T(8,128)} %fusion.20, ...), kind=kOutput, calls=%fused_computation.57 | convolution fusion | flops 455638848 | bytes 9438464 | tf_op jit(solution)/shard_map/fry,fyx->frx/dot_general | solution.py:30
  151.8 9.1 %all_to_all.15 = f32[32,1,2,192]{3,2,1,0:T(2,128)S(1)} all-to-all(f32[32,1,2,192]{3,2,1,0:T(2,128)S(1)} %broadcast_in_dim.10), channel_id=1, replica_groups=mesh['gx'=16,'gy'=2] {'gx','gy'}, dimensions={0} | all-to-all | bytes 98304 | tf_op jit(solution)/shard_map/all_to_all | solution.py:21
  160.9 2.6 %fusion.38 = bf16[1,1,4,192,384]{4,3,2,1,0:T(8,128)(2,1)} fusion(f32[4,192,384]{2,1,0:T(8,128)} %fusion.9, f32[4,192,384]{2,1,0:T(8,128)} %get-tuple-element.22, f32[192]{0:T(256)S(1)} %bitcast.175), kind=kLoop, calls=%fused_computation.67 | loop fusion | flops 884736 | bytes 2949888 | tf_op jit(solution)/shard_map/broadcast_in_dim | solution.py:137
  (107 shorter events, 41.9 us)
Async XLA Ops:
  0.0 19.3 %copy-start.21 = (s32[4]{0:T(128)S(1)}, s32[4]{0:T(128)}, u32[]{:S(2)}) copy-start(s32[4]{0:T(128)} %constant.10.clone) | copy-start | bytes 52
  0.0 18.7 %copy-start.22 = (s32[1,1,4]{2,1,0:T(1,128)S(1)}, s32[1,1,4]{2,1,0:T(1,128)}, u32[]{:S(2)}) copy-start(s32[1,1,4]{2,1,0:T(1,128)} %param.14) | copy-start | bytes 52
  0.0 19.9 %copy-start.3 = (bf16[1,1,4,384,384]{4,3,2,1,0:T(8,128)(2,1)S(1)}, bf16[1,1,4,384,384]{4,3,2,1,0:T(8,128)(2,1)}, u32[]{:S(2)}) copy-start(bf16[1,1,4,384,384]{4,3,2,1,0:T(8,128)(2,1)} %param.10) | copy-start | bytes 3538948
  1.5 24.5 %collective-permute-start.7 = (f32[5,128]{1,0:T(8,128)S(1)}, f32[5,128]{1,0:T(8,128)S(1)}, u32[]{:S(2)}, u32[]{:S(2)}) collective-permute-start(f32[5,128]{1,0:T(8,128)S(1)} %select_maximum_fusion), channel_id=1, source_target_pairs={{1,0},{3,2},{5,4},{7,6},{9,8},{11,10},{13,12},{15,14},{17,16},{19,... | collective-permute-start | bytes 7688 | tf_op jit(solution)/shard_map/ppermute | solution.py:15
  2.8 25.1 %collective-permute-start.6 = (f32[5,128]{1,0:T(8,128)S(1)}, f32[5,128]{1,0:T(8,128)S(1)}, u32[]{:S(2)}, u32[]{:S(2)}) collective-permute-start(f32[5,128]{1,0:T(8,128)S(1)} %select_maximum_fusion), channel_id=1, source_target_pairs={{0,1},{2,3},{4,5},{6,7},{8,9},{10,11},{12,13},{14,15},{16,17},{18,... | collective-permute-start | bytes 7688 | tf_op jit(solution)/shard_map/ppermute | solution.py:15
  5.9 24.0 %collective-permute-start.5 = (f32[5,128]{1,0:T(8,128)S(1)}, f32[5,128]{1,0:T(8,128)S(1)}, u32[]{:S(2)}, u32[]{:S(2)}) collective-permute-start(f32[5,128]{1,0:T(8,128)S(1)} %select_maximum_fusion), channel_id=1, source_target_pairs={{2,0},{4,2},{6,4},{8,6},{10,8},{12,10},{14,12},{16,14},{18,16},{20... | collective-permute-start | bytes 7688 | tf_op jit(solution)/shard_map/ppermute | solution.py:15
  7.2 26.3 %collective-permute-start.4 = (f32[5,128]{1,0:T(8,128)S(1)}, f32[5,128]{1,0:T(8,128)S(1)}, u32[]{:S(2)}, u32[]{:S(2)}) collective-permute-start(f32[5,128]{1,0:T(8,128)S(1)} %select_maximum_fusion), channel_id=1, source_target_pairs={{0,2},{2,4},{4,6},{6,8},{8,10},{10,12},{12,14},{14,16},{16,18},{18... | collective-permute-start | bytes 7688 | tf_op jit(solution)/shard_map/ppermute | solution.py:15
  13.8 25.4 %collective-permute-start = (bf16[192,384]{1,0:T(8,128)(2,1)S(1)}, bf16[192,384]{1,0:T(8,128)(2,1)S(1)}, u32[]{:S(2)}, u32[]{:S(2)}) collective-permute-start(bf16[192,384]{1,0:T(8,128)(2,1)S(1)} %get-tuple-element.17), channel_id=1, source_target_pairs={{0,2},{2,4},{4,6},{6,8},{8,10},{10,12},{12,14},{14,16},{16,18},{18... | collective-permute-start | bytes 442376 | tf_op jit(solution)/shard_map/ppermute | solution.py:15
  25.0 26.6 %copy-start.6 = (bf16[1,1,4,192,384]{4,3,2,1,0:T(8,128)(2,1)S(1)}, bf16[1,1,4,192,384]{4,3,2,1,0:T(8,128)(2,1)}, u32[]{:S(2)}) copy-start(bf16[1,1,4,192,384]{4,3,2,1,0:T(8,128)(2,1)} %param.8) | copy-start | bytes 1769476
  26.0 14.5 %collective-permute-start.1 = (bf16[192,384]{1,0:T(8,128)(2,1)S(1)}, bf16[192,384]{1,0:T(8,128)(2,1)S(1)}, u32[]{:S(2)}, u32[]{:S(2)}) collective-permute-start(bf16[192,384]{1,0:T(8,128)(2,1)S(1)} %get-tuple-element.18), channel_id=1, source_target_pairs={{2,0},{4,2},{6,4},{8,6},{10,8},{12,10},{14,12},{16,14},{18,16},{20... | collective-permute-start | bytes 442376 | tf_op jit(solution)/shard_map/ppermute | solution.py:15
  27.9 17.5 %collective-permute-start.3 = (bf16[192,384]{1,0:T(8,128)(2,1)S(1)}, bf16[192,384]{1,0:T(8,128)(2,1)S(1)}, u32[]{:S(2)}, u32[]{:S(2)}) collective-permute-start(bf16[192,384]{1,0:T(8,128)(2,1)S(1)} %get-tuple-element.19), channel_id=1, source_target_pairs={{1,0},{3,2},{5,4},{7,6},{9,8},{11,10},{13,12},{15,14},{17,16},{19,... | collective-permute-start | bytes 442376 | tf_op jit(solution)/shard_map/ppermute | solution.py:15
  29.8 21.7 %collective-permute-start.2 = (bf16[192,384]{1,0:T(8,128)(2,1)S(1)}, bf16[192,384]{1,0:T(8,128)(2,1)S(1)}, u32[]{:S(2)}, u32[]{:S(2)}) collective-permute-start(bf16[192,384]{1,0:T(8,128)(2,1)S(1)} %get-tuple-element.20), channel_id=1, source_target_pairs={{0,1},{2,3},{4,5},{6,7},{8,9},{10,11},{12,13},{14,15},{16,17},{18,... | collective-permute-start | bytes 442376 | tf_op jit(solution)/shard_map/ppermute | solution.py:15
  33.5 62.0 %collective-permute-start.11 = (bf16[3,384,384]{2,1,0:T(8,128)(2,1)}, bf16[3,384,384]{2,1,0:T(8,128)(2,1)}, u32[]{:S(2)}, u32[]{:S(2)}) collective-permute-start(bf16[3,384,384]{2,1,0:T(8,128)(2,1)} %pad_maximum_fusion.4), channel_id=1, source_target_pairs={{1,0},{3,2},{5,4},{7,6},{9,8},{11,10},{13,12},{15,14},{17,16},{19,... | collective-permute-start | bytes 2654216 | tf_op jit(solution)/shard_map/ppermute | solution.py:15
  39.2 12.9 %copy-start.8 = (bf16[192,384]{1,0:T(8,128)(2,1)}, bf16[192,384]{1,0:T(8,128)(2,1)S(1)}, u32[]{:S(2)}) copy-start(bf16[192,384]{1,0:T(8,128)(2,1)S(1)} %collective-permute-done) | copy-start | bytes 442372
  39.2 56.2 %collective-permute-start.9 = (bf16[3,384,384]{2,1,0:T(8,128)(2,1)}, bf16[3,384,384]{2,1,0:T(8,128)(2,1)}, u32[]{:S(2)}, u32[]{:S(2)}) collective-permute-start(bf16[3,384,384]{2,1,0:T(8,128)(2,1)} %pad_maximum_fusion.2), channel_id=1, source_target_pairs={{2,0},{4,2},{6,4},{8,6},{10,8},{12,10},{14,12},{16,14},{18,16},{20... | collective-permute-start | bytes 2654216 | tf_op jit(solution)/shard_map/ppermute | solution.py:15
  40.5 11.6 %copy-start.10 = (bf16[192,384]{1,0:T(8,128)(2,1)}, bf16[192,384]{1,0:T(8,128)(2,1)S(1)}, u32[]{:S(2)}) copy-start(bf16[192,384]{1,0:T(8,128)(2,1)S(1)} %collective-permute-done.1) | copy-start | bytes 442372
  40.5 54.9 %collective-permute-start.10 = (bf16[3,384,384]{2,1,0:T(8,128)(2,1)}, bf16[3,384,384]{2,1,0:T(8,128)(2,1)}, u32[]{:S(2)}, u32[]{:S(2)}) collective-permute-start(bf16[3,384,384]{2,1,0:T(8,128)(2,1)} %pad_maximum_fusion.3), channel_id=1, source_target_pairs={{0,1},{2,3},{4,5},{6,7},{8,9},{10,11},{12,13},{14,15},{16,17},{18,... | collective-permute-start | bytes 2654216 | tf_op jit(solution)/shard_map/ppermute | solution.py:15
  45.4 6.8 %copy-start.12 = (bf16[192,384]{1,0:T(8,128)(2,1)}, bf16[192,384]{1,0:T(8,128)(2,1)S(1)}, u32[]{:S(2)}) copy-start(bf16[192,384]{1,0:T(8,128)(2,1)S(1)} %collective-permute-done.3) | copy-start | bytes 442372
  45.4 50.1 %collective-permute-start.8 = (bf16[3,384,384]{2,1,0:T(8,128)(2,1)}, bf16[3,384,384]{2,1,0:T(8,128)(2,1)}, u32[]{:S(2)}, u32[]{:S(2)}) collective-permute-start(bf16[3,384,384]{2,1,0:T(8,128)(2,1)} %pad_maximum_fusion.1), channel_id=1, source_target_pairs={{0,2},{2,4},{4,6},{6,8},{8,10},{10,12},{12,14},{14,16},{16,18},{18... | collective-permute-start | bytes 2654216 | tf_op jit(solution)/shard_map/ppermute | solution.py:15
  53.1 33.3 %all-to-all-start = ((bf16[32,4,192]{2,1,0:T(4,128)(2,1)}), bf16[32,4,192]{2,1,0:T(4,128)(2,1)S(1)}, u32[]{:S(2)}, u32[]{:S(2)}) async-start(bf16[32,4,192]{2,1,0:T(4,128)(2,1)} %broadcast_in_dim.8), calls=%async_computation | async-start | bytes 131072 | tf_op jit(solution)/shard_map/all_to_all | solution.py:21
  60.0 26.4 %copy-start.18 = (f32[4,128]{1,0:T(4,128)S(1)}, f32[4,128]{1,0:T(4,128)}, u32[]{:S(2)}) copy-start(f32[4,128]{1,0:T(4,128)} %param.12) | copy-start | bytes 6148
  105.3 2.4 %copy-start.13 = (bf16[192,384]{1,0:T(8,128)(2,1)S(1)}, bf16[192,384]{1,0:T(8,128)(2,1)}, u32[]{:S(2)}) copy-start(bf16[192,384]{1,0:T(8,128)(2,1)} %copy-done.12) | copy-start | bytes 442372
  117.4 13.2 %all-to-all-start.1 = ((bf16[32,4,192]{2,1,0:T(4,128)(2,1)}), bf16[32,4,192]{2,1,0:T(4,128)(2,1)}, u32[]{:S(2)}, u32[]{:S(2)}) async-start(bf16[32,4,192]{2,1,0:T(4,128)(2,1)} %broadcast_in_dim.9), calls=%async_computation.1 | async-start | bytes 131072 | tf_op jit(solution)/shard_map/all_to_all | solution.py:21
  139.5 4.6 %copy-start.20 = (f32[4]{0:T(128)S(1)}, f32[4]{0:T(128)}, u32[]{:S(2)}) copy-start(f32[4]{0:T(128)} %maximum_multiply_fusion) | copy-start | bytes 52
  (13 other events, 21.9 us)

commit v3 on v1

--- a/solution.py
+++ b/solution.py
@@ -28,6 +28,22 @@
     return jnp.sum(gather_rows(block[None], axes), axis=0)
 
 
+PARTNERS = (("gx", True, 1), ("gx", False, 0), ("gy", True, 3), ("gy", False, 2))
+
+
+def from_partner(values, axis, from_lower):
+    count = lax.axis_size(axis)
+    if from_lower:
+        pairs = [(i, i + 1) for i in range(count - 1)]
+    else:
+        pairs = [(i + 1, i) for i in range(count - 1)]
+    return lax.ppermute(values, axis, pairs)
+
+
+def to_half(values):
+    return lax.reduce_precision(values, exponent_bits=8, mantissa_bits=7)
+
+
 def face_mul(vectors, matrices):
     return jnp.einsum("fry,fyx->frx", vectors, matrices, preferred_element_type=jnp.float32)
 
@@ -37,12 +53,6 @@
 
 
 def face_pairs(values):
-    along_first = with_halo(values[0:2], (("gx", 0),), 1)
-    along_second = with_halo(values[2:4], (("gy", 0),), 1)
-    return jnp.stack([along_first[0], along_first[3], along_second[0], along_second[3]], axis=0)
-
-
-def image_pairs(values):
     along_first = with_halo(values[0:2], (("gx", 0),), 1)
     along_second = with_halo(values[2:4], (("gy", 0),), 1)
     return jnp.stack([along_first[0], along_first[3], along_second[0], along_second[3]], axis=0)
@@ -80,9 +90,15 @@
         spread = face_mul(weighted, deluxe_panel).astype(jnp.bfloat16)
         return spread.astype(jnp.float32) + face_pairs(spread).astype(jnp.float32)
 
+    schur_partner = jnp.stack(
+        [from_partner(schur_panel[face], axis, from_lower) for axis, from_lower, face in PARTNERS]
+    )
+
     def apply_operator(field):
-        bent = face_mul(field.astype(jnp.bfloat16), schur_panel).astype(jnp.bfloat16)
-        return bent.astype(jnp.float32) + image_pairs(bent).astype(jnp.float32)
+        field_half = field.astype(jnp.bfloat16)
+        bent_own = to_half(face_mul(field_half, schur_panel))
+        bent_partner = to_half(face_mul(field_half, schur_partner))
+        return bent_own + bent_partner
 
     resid0 = loads_here.astype(jnp.float32) + face_pairs(loads_here).astype(jnp.float32)
     first = precondition(resid0)

time: 130 us -> 114 us (0.88)
  starting transfers between devices: 57.1 us -> 46.8 us
  waiting for transfers between devices: 34.6 us -> 27.5 us
  local copies, waits for them, and re-layouts: 4.7 us -> 6.08 us
    ppermute x10 -> x6, waiting for transfers between devices: 24.1 us -> 7.6 us  [with_halo(): lax.ppermute(lax.slice_in_dim(block, 0, width, axis=dim), axis, backward)]
    ppermute x10 -> x6, starting transfers between devices: 34.1 us -> 18.9 us  [with_halo(): lax.ppermute(lax.slice_in_dim(block, block.shape[dim] - width, None, axis...]
    ppermute x0 -> x4, starting transfers between devices: none -> 10.3 us  [from_partner(): return lax.ppermute(values, axis, pairs)]
    ppermute x0 -> x4, waiting for transfers between devices: none -> 8.32 us  [from_partner(): return lax.ppermute(values, axis, pairs)]
    ppermute x10 -> x6, starting transfers between devices: 12.9 us -> 7.88 us  [with_halo(): lax.ppermute(lax.slice_in_dim(block, 0, width, axis=dim), axis, backward)]
    dot_general x6 -> x8, matrix products: 11.2 us -> 11.5 us  [face_mul(): jnp.einsum('fry,fyx->frx', vectors, matrices, preferred_element_type=jnp....]
  transfers between devices with their start and end apart: 22 -> 18, of which waited for: 7 -> 6; matrix products, arithmetic and copies ran while one was open for 4% -> 4% of each run, Pallas kernels for 0% -> 0%
where the time goes in v3:
time: 114 us
  starting transfers between devices  46.8 us (41%)
  waiting for transfers between devices  27.5 us (24%)
  matrix products  17 us (15%)
  blocking collectives  12.2 us (11%)
  local copies, waits for them, and re-layouts  6.08 us (5%)
  other arithmetic  3.28 us (3%)
    ppermute x6, starting transfers between devices, with_halo(): lax.ppermute(lax.slice_in_dim(block, block.shape[dim] - width, None, axis...  18.9 us
    all_to_all x1, blocking collectives, gather_rows(): swapped = lax.all_to_all(spread, axes, 0, 0, tiled=False)  12.2 us
    all_to_all x2, waiting for transfers between devices, gather_rows(): swapped = lax.all_to_all(spread, axes, 0, 0, tiled=False)  11.6 us
    dot_general x8, matrix products, face_mul(): jnp.einsum('fry,fyx->frx', vectors, matrices, preferred_element_type=jnp....  11.5 us
    ppermute x4, starting transfers between devices, from_partner(): return lax.ppermute(values, axis, pairs)  10.3 us
    all_to_all x2, starting transfers between devices, gather_rows(): swapped = lax.all_to_all(spread, axes, 0, 0, tiled=False)  9.61 us
    ppermute x4, waiting for transfers between devices, from_partner(): return lax.ppermute(values, axis, pairs)  8.32 us
    ppermute x6, starting transfers between devices, with_halo(): lax.ppermute(lax.slice_in_dim(block, 0, width, axis=dim), axis, backward)  7.88 us
  transfers between devices with their start and end apart: 18, of which 6 were waited for; matrix products, arithmetic and copies ran while one was open for 4% of the time, Pallas kernels for 0%

profile of v3, /device:TPU:0, one launch (start us, length us, event | category | flops | bytes accessed | tf_op | source)
XLA Modules:
  0.0 113.6 jit_solution(6419505584537263526)
XLA Ops:
  1.3 4.9 %collective-permute-start = (bf16[1,192,384]{2,1,0:T(8,128)(2,1)S(1)}, bf16[1,192,384]{2,1,0:T(8,128)(2,1)S(1)}, u32[]{:S(2)}, u32[]{:S(2)}) collective-permute-start(bf16[1,192,384]{2,1,0:T(8,128)(2,1)S(1)} %get-tuple-element.17), channel_id=1, source_target_pairs={{0,2},{2,4},{4,6},{6,8},{8,10},{10,12},{12,14},{14,16},{16,18},{18... | collective-permute-start | bytes 442376 | tf_op jit(solution)/shard_map/ppermute | solution.py:12
  8.8 3.0 %collective-permute-start.2 = (bf16[1,192,384]{2,1,0:T(8,128)(2,1)S(1)}, bf16[1,192,384]{2,1,0:T(8,128)(2,1)S(1)}, u32[]{:S(2)}, u32[]{:S(2)}) collective-permute-start(bf16[1,192,384]{2,1,0:T(8,128)(2,1)S(1)} %get-tuple-element.20), channel_id=1, source_target_pairs={{0,1},{2,3},{4,5},{6,7},{8,9},{10,11},{12,13},{14,15},{16,17},{18,... | collective-permute-start | bytes 442376 | tf_op jit(solution)/shard_map/ppermute | solution.py:12
  12.5 1.9 %collective-permute-done.1 = bf16[1,192,384]{2,1,0:T(8,128)(2,1)S(1)} collective-permute-done((bf16[1,192,384]{2,1,0:T(8,128)(2,1)S(1)}, bf16[1,192,384]{2,1,0:T(8,128)(2,1)S(1)}, u32[]{:S(2)}, u32[]{:S(2)}) %collective-permute-start.1) | collective-permute-done | bytes 147488 | tf_op jit(solution)/shard_map/ppermute | solution.py:15
  16.1 5.8 %all-to-all-start = ((bf16[32,4,192]{2,1,0:T(4,128)(2,1)}), bf16[32,4,192]{2,1,0:T(4,128)(2,1)}, u32[]{:S(2)}, u32[]{:S(2)}) async-start(bf16[32,4,192]{2,1,0:T(4,128)(2,1)} %broadcast_in_dim.8), calls=%async_computation | async-start | bytes 131072 | tf_op jit(solution)/shard_map/all_to_all | solution.py:23
  21.9 1.6 %fusion.19 = f32[4,192,384]{2,1,0:T(8,128)} fusion(bf16[4,192,384]{2,1,0:T(8,128)(2,1)S(1)} %convolution_convert_fusion.3, bf16[1,1,4,384,384]{4,3,2,1,0:T(8,128)(2,1)S(1)} %copy-done.1), kind=kOutput, calls=%fused_computation.31 | convolution fusion | flops 226492416 | bytes 2949120 | tf_op jit(solution)/shard_map/fry,fyx->frx/dot_general | solution.py:48
  23.5 5.8 %all-to-all-done = bf16[32,4,192]{2,1,0:T(4,128)(2,1)} async-done(((bf16[32,4,192]{2,1,0:T(4,128)(2,1)}), bf16[32,4,192]{2,1,0:T(4,128)(2,1)}, u32[]{:S(2)}, u32[]{:S(2)}) %all-to-all-start) | async-done | bytes 49184 | tf_op jit(solution)/shard_map/all_to_all | solution.py:23
  30.3 1.8 %convolution_bitcast_fusion.1 = f32[4,192,384]{2,1,0:T(8,128)} fusion(f32[192,4,1]{0,1,2:T(4,128)S(1)} %convolution_bitcast_fusion.5, s32[4,384]{1,0:T(4,128)S(1)} %multiply_add_fusion, s32[4]{0:T(128)S(1)} %bitcast.87), kind=kOutput, calls=%fused_computation.15 | convolution fusion | flops 14161920 | bytes 1188880 | tf_op jit(solution)/shard_map/kfx,kr->frx/dot_general | solution.py:88
  32.1 2.9 %convolution_convert_fusion.2 = bf16[4,192,384]{2,1,0:T(8,128)(2,1)S(1)} fusion(f32[4,192,384]{2,1,0:T(8,128)} %convolution_bitcast_fusion.1, f32[4,192,384]{2,1,0:T(8,128)} %fusion.19, bf16[1,1,4,384,384]{4,3,2,1,0:T(8,128)(2,1)S(1)} %copy-done.1, bf16[1,1,4,384,384]{4,3,2,1,0:T(8,128)(2,1)S(1)} %copy-done, f32[4]{0:T(128)} %multiply_bitcast_fusion), kind=kOutput, calls=%fused_computation.20 | convolution fusion | flops 454754304 | bytes 5308432 | tf_op jit(solution)/shard_map/fry,fyx->frx/dot_general | solution.py:48
  35.0 2.5 %collective-permute-start.4 = (bf16[1,192,384]{2,1,0:T(8,128)(2,1)S(1)}, bf16[1,192,384]{2,1,0:T(8,128)(2,1)S(1)}, u32[]{:S(2)}, u32[]{:S(2)}) collective-permute-start(bf16[1,192,384]{2,1,0:T(8,128)(2,1)S(1)} %get-tuple-element.13), channel_id=1, source_target_pairs={{0,2},{2,4},{4,6},{6,8},{8,10},{10,12},{12,14},{14,16},{16,18},{18... | collective-permute-start | bytes 442376 | tf_op jit(solution)/shard_map/ppermute | solution.py:12
  38.8 3.0 %collective-permute-start.6 = (bf16[1,192,384]{2,1,0:T(8,128)(2,1)S(1)}, bf16[1,192,384]{2,1,0:T(8,128)(2,1)S(1)}, u32[]{:S(2)}, u32[]{:S(2)}) collective-permute-start(bf16[1,192,384]{2,1,0:T(8,128)(2,1)S(1)} %get-tuple-element.15), channel_id=1, source_target_pairs={{0,1},{2,3},{4,5},{6,7},{8,9},{10,11},{12,13},{14,15},{16,17},{18,... | collective-permute-start | bytes 442376 | tf_op jit(solution)/shard_map/ppermute | solution.py:12
  43.3 4.6 %collective-permute-start.8 = (bf16[384,384]{1,0:T(8,128)(2,1)S(1)}, bf16[384,384]{1,0:T(8,128)(2,1)S(1)}, u32[]{:S(2)}, u32[]{:S(2)}) collective-permute-start(bf16[384,384]{1,0:T(8,128)(2,1)S(1)} %get-tuple-element.5), channel_id=1, source_target_pairs={{0,2},{2,4},{4,6},{6,8},{8,10},{10,12},{12,14},{14,16},{16,18},{18... | collective-permute-start | bytes 884744 | tf_op jit(solution)/shard_map/ppermute | solution.py:40
  50.6 3.2 %collective-permute-start.10 = (bf16[384,384]{1,0:T(8,128)(2,1)S(1)}, bf16[384,384]{1,0:T(8,128)(2,1)S(1)}, u32[]{:S(2)}, u32[]{:S(2)}) collective-permute-start(bf16[384,384]{1,0:T(8,128)(2,1)S(1)} %get-tuple-element.8), channel_id=1, source_target_pairs={{0,1},{2,3},{4,5},{6,7},{8,9},{10,11},{12,13},{14,15},{16,17},{18,... | collective-permute-start | bytes 884744 | tf_op jit(solution)/shard_map/ppermute | solution.py:40
  54.4 8.1 %collective-permute-done.8 = bf16[384,384]{1,0:T(8,128)(2,1)S(1)} collective-permute-done((bf16[384,384]{1,0:T(8,128)(2,1)S(1)}, bf16[384,384]{1,0:T(8,128)(2,1)S(1)}, u32[]{:S(2)}, u32[]{:S(2)}) %collective-permute-start.8) | collective-permute-done | bytes 294944 | tf_op jit(solution)/shard_map/ppermute | solution.py:40
  65.6 3.8 %all-to-all-start.1 = ((bf16[32,4,192]{2,1,0:T(4,128)(2,1)}), bf16[32,4,192]{2,1,0:T(4,128)(2,1)}, u32[]{:S(2)}, u32[]{:S(2)}) async-start(bf16[32,4,192]{2,1,0:T(4,128)(2,1)} %broadcast_in_dim.9), calls=%async_computation.1 | async-start | bytes 131072 | tf_op jit(solution)/shard_map/all_to_all | solution.py:23
  69.4 1.6 %fusion.15 = f32[4,192,384]{2,1,0:T(8,128)} fusion(bf16[4,192,384]{2,1,0:T(8,128)(2,1)S(1)} %convolution_convert_fusion.1, bf16[1,1,4,384,384]{4,3,2,1,0:T(8,128)(2,1)S(1)} %copy-done.1), kind=kOutput, calls=%fused_computation.28 | convolution fusion | flops 226492416 | bytes 2949120 | tf_op jit(solution)/shard_map/fry,fyx->frx/dot_general | solution.py:48
  71.0 5.8 %all-to-all-done.1 = bf16[32,4,192]{2,1,0:T(4,128)(2,1)} async-done(((bf16[32,4,192]{2,1,0:T(4,128)(2,1)}), bf16[32,4,192]{2,1,0:T(4,128)(2,1)}, u32[]{:S(2)}, u32[]{:S(2)}) %all-to-all-start.1) | async-done | bytes 49184 | tf_op jit(solution)/shard_map/all_to_all | solution.py:23
  77.8 1.8 %convolution_bitcast_fusion = f32[4,192,384]{2,1,0:T(8,128)} fusion(f32[192,4,1]{0,1,2:T(4,128)S(1)} %convolution_bitcast_fusion.4, s32[4,384]{1,0:T(4,128)S(1)} %multiply_add_fusion, s32[4]{0:T(128)S(1)} %bitcast.89), kind=kOutput, calls=%fused_computation.14 | convolution fusion | flops 14161920 | bytes 1188880 | tf_op jit(solution)/shard_map/kfx,kr->frx/dot_general | solution.py:88
  79.6 2.9 %convolution_convert_fusion = bf16[4,192,384]{2,1,0:T(8,128)(2,1)S(1)} fusion(f32[4,192,384]{2,1,0:T(8,128)} %convolution_bitcast_fusion, f32[4,192,384]{2,1,0:T(8,128)} %fusion.15, bf16[1,1,4,384,384]{4,3,2,1,0:T(8,128)(2,1)S(1)} %copy-done.1, bf16[1,1,4,384,384]{4,3,2,1,0:T(8,128)(2,1)S(1)} %copy-done, f32[4]{0:T(128)} %multiply_bitcast_fusion), kind=kOutput, calls=%fused_computation.18 | convolution fusion | flops 454754304 | bytes 5308432 | tf_op jit(solution)/shard_map/fry,fyx->frx/dot_general | solution.py:48
  82.6 2.5 %collective-permute-start.12 = (bf16[1,192,384]{2,1,0:T(8,128)(2,1)S(1)}, bf16[1,192,384]{2,1,0:T(8,128)(2,1)S(1)}, u32[]{:S(2)}, u32[]{:S(2)}) collective-permute-start(bf16[1,192,384]{2,1,0:T(8,128)(2,1)S(1)} %get-tuple-element.9), channel_id=1, source_target_pairs={{0,2},{2,4},{4,6},{6,8},{8,10},{10,12},{12,14},{14,16},{16,18},{18... | collective-permute-start | bytes 442376 | tf_op jit(solution)/shard_map/ppermute | solution.py:12
  86.3 3.0 %collective-permute-start.14 = (bf16[1,192,384]{2,1,0:T(8,128)(2,1)S(1)}, bf16[1,192,384]{2,1,0:T(8,128)(2,1)S(1)}, u32[]{:S(2)}, u32[]{:S(2)}) collective-permute-start(bf16[1,192,384]{2,1,0:T(8,128)(2,1)S(1)} %get-tuple-element.11), channel_id=1, source_target_pairs={{0,1},{2,3},{4,5},{6,7},{8,9},{10,11},{12,13},{14,15},{16,17},{18,... | collective-permute-start | bytes 442376 | tf_op jit(solution)/shard_map/ppermute | solution.py:12
  89.4 1.4 %collective-permute-start.13 = (bf16[1,192,384]{2,1,0:T(8,128)(2,1)S(1)}, bf16[1,192,384]{2,1,0:T(8,128)(2,1)S(1)}, u32[]{:S(2)}, u32[]{:S(2)}) collective-permute-start(bf16[1,192,384]{2,1,0:T(8,128)(2,1)S(1)} %get-tuple-element.12), channel_id=1, source_target_pairs={{2,0},{4,2},{6,4},{8,6},{10,8},{12,10},{14,12},{16,14},{18,16},{20... | collective-permute-start | bytes 442376 | tf_op jit(solution)/shard_map/ppermute | solution.py:15
  90.9 5.7 %collective-permute-done.13 = bf16[1,192,384]{2,1,0:T(8,128)(2,1)S(1)} collective-permute-done((bf16[1,192,384]{2,1,0:T(8,128)(2,1)S(1)}, bf16[1,192,384]{2,1,0:T(8,128)(2,1)S(1)}, u32[]{:S(2)}, u32[]{:S(2)}) %collective-permute-start.13) | collective-permute-done | bytes 147488 | tf_op jit(solution)/shard_map/ppermute | solution.py:15
  99.0 12.2 %all_to_all.15 = f32[32,1,2,192]{3,2,1,0:T(2,128)S(1)} all-to-all(f32[32,1,2,192]{3,2,1,0:T(2,128)S(1)} %broadcast_in_dim.10), channel_id=1, replica_groups=mesh['gx'=16,'gy'=2] {'gx','gy'}, dimensions={0} | all-to-all | bytes 98304 | tf_op jit(solution)/shard_map/all_to_all | solution.py:23
  111.3 2.3 %fusion.33 = bf16[1,1,4,192,384]{4,3,2,1,0:T(8,128)(2,1)} fusion(bf16[4,192,384]{2,1,0:T(8,128)(2,1)S(1)} %convolution_convert_fusion, bf16[4,192,384]{2,1,0:T(8,128)(2,1)S(1)} %convolution_convert_fusion.2, f32[192]{0:T(256)S(1)} %bitcast.90, bf16[1,192,384]{2,1,0:T(8,128)(2,1)S(1)} %copy-done.14, bf16[1,192,384]{2,1,0:T(8,128)(2,1)S(1)} %copy-done.16, ...), kind=kLoop, calls=%fused_computation.50 | loop fusion | flops 4423680 | bytes 2949888 | tf_op jit(solution)/shard_map/broadcast_in_dim | solution.py:114
  (121 shorter events, 20.8 us)
Async XLA Ops:
  0.0 14.4 %copy-start = (bf16[1,1,4,384,384]{4,3,2,1,0:T(8,128)(2,1)S(1)}, bf16[1,1,4,384,384]{4,3,2,1,0:T(8,128)(2,1)}, u32[]{:S(2)}) copy-start(bf16[1,1,4,384,384]{4,3,2,1,0:T(8,128)(2,1)} %param.9) | copy-start | bytes 3538948
  0.0 14.4 %copy-start.6 = (bf16[1,1,4,192,384]{4,3,2,1,0:T(8,128)(2,1)S(1)}, bf16[1,1,4,192,384]{4,3,2,1,0:T(8,128)(2,1)}, u32[]{:S(2)}) copy-start(bf16[1,1,4,192,384]{4,3,2,1,0:T(8,128)(2,1)} %param.7) | copy-start | bytes 1769476
  1.3 11.1 %collective-permute-start = (bf16[1,192,384]{2,1,0:T(8,128)(2,1)S(1)}, bf16[1,192,384]{2,1,0:T(8,128)(2,1)S(1)}, u32[]{:S(2)}, u32[]{:S(2)}) collective-permute-start(bf16[1,192,384]{2,1,0:T(8,128)(2,1)S(1)} %get-tuple-element.17), channel_id=1, source_target_pairs={{0,2},{2,4},{4,6},{6,8},{8,10},{10,12},{12,14},{14,16},{16,18},{18... | collective-permute-start | bytes 442376 | tf_op jit(solution)/shard_map/ppermute | solution.py:12
  6.2 8.2 %collective-permute-start.1 = (bf16[1,192,384]{2,1,0:T(8,128)(2,1)S(1)}, bf16[1,192,384]{2,1,0:T(8,128)(2,1)S(1)}, u32[]{:S(2)}, u32[]{:S(2)}) collective-permute-start(bf16[1,192,384]{2,1,0:T(8,128)(2,1)S(1)} %get-tuple-element.18), channel_id=1, source_target_pairs={{2,0},{4,2},{6,4},{8,6},{10,8},{12,10},{14,12},{16,14},{18,16},{20... | collective-permute-start | bytes 442376 | tf_op jit(solution)/shard_map/ppermute | solution.py:15
  7.5 6.9 %collective-permute-start.3 = (bf16[1,192,384]{2,1,0:T(8,128)(2,1)S(1)}, bf16[1,192,384]{2,1,0:T(8,128)(2,1)S(1)}, u32[]{:S(2)}, u32[]{:S(2)}) collective-permute-start(bf16[1,192,384]{2,1,0:T(8,128)(2,1)S(1)} %get-tuple-element.19), channel_id=1, source_target_pairs={{1,0},{3,2},{5,4},{7,6},{9,8},{11,10},{13,12},{15,14},{17,16},{19,... | collective-permute-start | bytes 442376 | tf_op jit(solution)/shard_map/ppermute | solution.py:15
  8.8 5.6 %collective-permute-start.2 = (bf16[1,192,384]{2,1,0:T(8,128)(2,1)S(1)}, bf16[1,192,384]{2,1,0:T(8,128)(2,1)S(1)}, u32[]{:S(2)}, u32[]{:S(2)}) collective-permute-start(bf16[1,192,384]{2,1,0:T(8,128)(2,1)S(1)} %get-tuple-element.20), channel_id=1, source_target_pairs={{0,1},{2,3},{4,5},{6,7},{8,9},{10,11},{12,13},{14,15},{16,17},{18,... | collective-permute-start | bytes 442376 | tf_op jit(solution)/shard_map/ppermute | solution.py:12
  16.1 13.2 %all-to-all-start = ((bf16[32,4,192]{2,1,0:T(4,128)(2,1)}), bf16[32,4,192]{2,1,0:T(4,128)(2,1)}, u32[]{:S(2)}, u32[]{:S(2)}) async-start(bf16[32,4,192]{2,1,0:T(4,128)(2,1)} %broadcast_in_dim.8), calls=%async_computation | async-start | bytes 131072 | tf_op jit(solution)/shard_map/all_to_all | solution.py:23
  35.0 12.8 %collective-permute-start.4 = (bf16[1,192,384]{2,1,0:T(8,128)(2,1)S(1)}, bf16[1,192,384]{2,1,0:T(8,128)(2,1)S(1)}, u32[]{:S(2)}, u32[]{:S(2)}) collective-permute-start(bf16[1,192,384]{2,1,0:T(8,128)(2,1)S(1)} %get-tuple-element.13), channel_id=1, source_target_pairs={{0,2},{2,4},{4,6},{6,8},{8,10},{10,12},{12,14},{14,16},{16,18},{18... | collective-permute-start | bytes 442376 | tf_op jit(solution)/shard_map/ppermute | solution.py:12
  37.5 11.7 %collective-permute-start.7 = (bf16[1,192,384]{2,1,0:T(8,128)(2,1)S(1)}, bf16[1,192,384]{2,1,0:T(8,128)(2,1)S(1)}, u32[]{:S(2)}, u32[]{:S(2)}) collective-permute-start(bf16[1,192,384]{2,1,0:T(8,128)(2,1)S(1)} %get-tuple-element.14), channel_id=1, source_target_pairs={{1,0},{3,2},{5,4},{7,6},{9,8},{11,10},{13,12},{15,14},{17,16},{19,... | collective-permute-start | bytes 442376 | tf_op jit(solution)/shard_map/ppermute | solution.py:15
  38.8 11.7 %collective-permute-start.6 = (bf16[1,192,384]{2,1,0:T(8,128)(2,1)S(1)}, bf16[1,192,384]{2,1,0:T(8,128)(2,1)S(1)}, u32[]{:S(2)}, u32[]{:S(2)}) collective-permute-start(bf16[1,192,384]{2,1,0:T(8,128)(2,1)S(1)} %get-tuple-element.15), channel_id=1, source_target_pairs={{0,1},{2,3},{4,5},{6,7},{8,9},{10,11},{12,13},{14,15},{16,17},{18,... | collective-permute-start | bytes 442376 | tf_op jit(solution)/shard_map/ppermute | solution.py:12
  41.9 11.9 %collective-permute-start.5 = (bf16[1,192,384]{2,1,0:T(8,128)(2,1)S(1)}, bf16[1,192,384]{2,1,0:T(8,128)(2,1)S(1)}, u32[]{:S(2)}, u32[]{:S(2)}) collective-permute-start(bf16[1,192,384]{2,1,0:T(8,128)(2,1)S(1)} %get-tuple-element.16), channel_id=1, source_target_pairs={{2,0},{4,2},{6,4},{8,6},{10,8},{12,10},{14,12},{16,14},{18,16},{20... | collective-permute-start | bytes 442376 | tf_op jit(solution)/shard_map/ppermute | solution.py:15
  43.3 19.2 %collective-permute-start.8 = (bf16[384,384]{1,0:T(8,128)(2,1)S(1)}, bf16[384,384]{1,0:T(8,128)(2,1)S(1)}, u32[]{:S(2)}, u32[]{:S(2)}) collective-permute-start(bf16[384,384]{1,0:T(8,128)(2,1)S(1)} %get-tuple-element.5), channel_id=1, source_target_pairs={{0,2},{2,4},{4,6},{6,8},{8,10},{10,12},{12,14},{14,16},{16,18},{18... | collective-permute-start | bytes 884744 | tf_op jit(solution)/shard_map/ppermute | solution.py:40
  47.9 14.8 %copy-start.11 = (bf16[1,192,384]{2,1,0:T(8,128)(2,1)}, bf16[1,192,384]{2,1,0:T(8,128)(2,1)S(1)}, u32[]{:S(2)}) copy-start(bf16[1,192,384]{2,1,0:T(8,128)(2,1)S(1)} %collective-permute-done.4) | copy-start | bytes 442372
  47.9 14.8 %collective-permute-start.9 = (bf16[384,384]{1,0:T(8,128)(2,1)S(1)}, bf16[384,384]{1,0:T(8,128)(2,1)S(1)}, u32[]{:S(2)}, u32[]{:S(2)}) collective-permute-start(bf16[384,384]{1,0:T(8,128)(2,1)S(1)} %get-tuple-element.6), channel_id=1, source_target_pairs={{2,0},{4,2},{6,4},{8,6},{10,8},{12,10},{14,12},{16,14},{18,16},{20... | collective-permute-start | bytes 884744 | tf_op jit(solution)/shard_map/ppermute | solution.py:40
  49.2 13.5 %copy-start.13 = (bf16[1,192,384]{2,1,0:T(8,128)(2,1)}, bf16[1,192,384]{2,1,0:T(8,128)(2,1)S(1)}, u32[]{:S(2)}) copy-start(bf16[1,192,384]{2,1,0:T(8,128)(2,1)S(1)} %collective-permute-done.7) | copy-start | bytes 442372
  49.2 13.5 %collective-permute-start.11 = (bf16[384,384]{1,0:T(8,128)(2,1)S(1)}, bf16[384,384]{1,0:T(8,128)(2,1)S(1)}, u32[]{:S(2)}, u32[]{:S(2)}) collective-permute-start(bf16[384,384]{1,0:T(8,128)(2,1)S(1)} %get-tuple-element.7), channel_id=1, source_target_pairs={{1,0},{3,2},{5,4},{7,6},{9,8},{11,10},{13,12},{15,14},{17,16},{19,... | collective-permute-start | bytes 884744 | tf_op jit(solution)/shard_map/ppermute | solution.py:40
  50.6 12.1 %collective-permute-start.10 = (bf16[384,384]{1,0:T(8,128)(2,1)S(1)}, bf16[384,384]{1,0:T(8,128)(2,1)S(1)}, u32[]{:S(2)}, u32[]{:S(2)}) collective-permute-start(bf16[384,384]{1,0:T(8,128)(2,1)S(1)} %get-tuple-element.8), channel_id=1, source_target_pairs={{0,1},{2,3},{4,5},{6,7},{8,9},{10,11},{12,13},{14,15},{16,17},{18,... | collective-permute-start | bytes 884744 | tf_op jit(solution)/shard_map/ppermute | solution.py:40
  65.6 11.2 %all-to-all-start.1 = ((bf16[32,4,192]{2,1,0:T(4,128)(2,1)}), bf16[32,4,192]{2,1,0:T(4,128)(2,1)}, u32[]{:S(2)}, u32[]{:S(2)}) async-start(bf16[32,4,192]{2,1,0:T(4,128)(2,1)} %broadcast_in_dim.9), calls=%async_computation.1 | async-start | bytes 131072 | tf_op jit(solution)/shard_map/all_to_all | solution.py:23
  82.5 14.1 %copy-start.3 = (f32[4,192,384]{2,1,0:T(8,128)S(1)}, f32[4,192,384]{2,1,0:T(8,128)}, u32[]{:S(2)}) copy-start(f32[4,192,384]{2,1,0:T(8,128)} %copy-done.2) | copy-start | bytes 3538948
  82.6 8.3 %collective-permute-start.12 = (bf16[1,192,384]{2,1,0:T(8,128)(2,1)S(1)}, bf16[1,192,384]{2,1,0:T(8,128)(2,1)S(1)}, u32[]{:S(2)}, u32[]{:S(2)}) collective-permute-start(bf16[1,192,384]{2,1,0:T(8,128)(2,1)S(1)} %get-tuple-element.9), channel_id=1, source_target_pairs={{0,2},{2,4},{4,6},{6,8},{8,10},{10,12},{12,14},{14,16},{16,18},{18... | collective-permute-start | bytes 442376 | tf_op jit(solution)/shard_map/ppermute | solution.py:12
  85.0 5.8 %collective-permute-start.15 = (bf16[1,192,384]{2,1,0:T(8,128)(2,1)S(1)}, bf16[1,192,384]{2,1,0:T(8,128)(2,1)S(1)}, u32[]{:S(2)}, u32[]{:S(2)}) collective-permute-start(bf16[1,192,384]{2,1,0:T(8,128)(2,1)S(1)} %get-tuple-element.10), channel_id=1, source_target_pairs={{1,0},{3,2},{5,4},{7,6},{9,8},{11,10},{13,12},{15,14},{17,16},{19,... | collective-permute-start | bytes 442376 | tf_op jit(solution)/shard_map/ppermute | solution.py:15
  86.3 4.5 %collective-permute-start.14 = (bf16[1,192,384]{2,1,0:T(8,128)(2,1)S(1)}, bf16[1,192,384]{2,1,0:T(8,128)(2,1)S(1)}, u32[]{:S(2)}, u32[]{:S(2)}) collective-permute-start(bf16[1,192,384]{2,1,0:T(8,128)(2,1)S(1)} %get-tuple-element.11), channel_id=1, source_target_pairs={{0,1},{2,3},{4,5},{6,7},{8,9},{10,11},{12,13},{14,15},{16,17},{18,... | collective-permute-start | bytes 442376 | tf_op jit(solution)/shard_map/ppermute | solution.py:12
  89.4 7.2 %collective-permute-start.13 = (bf16[1,192,384]{2,1,0:T(8,128)(2,1)S(1)}, bf16[1,192,384]{2,1,0:T(8,128)(2,1)S(1)}, u32[]{:S(2)}, u32[]{:S(2)}) collective-permute-start(bf16[1,192,384]{2,1,0:T(8,128)(2,1)S(1)} %get-tuple-element.12), channel_id=1, source_target_pairs={{2,0},{4,2},{6,4},{8,6},{10,8},{12,10},{14,12},{16,14},{18,16},{20... | collective-permute-start | bytes 442376 | tf_op jit(solution)/shard_map/ppermute | solution.py:15
  98.1 13.1 %copy-start.18 = (bf16[1,192,384]{2,1,0:T(8,128)(2,1)S(1)}, bf16[1,192,384]{2,1,0:T(8,128)(2,1)}, u32[]{:S(2)}) copy-start(bf16[1,192,384]{2,1,0:T(8,128)(2,1)} %copy-done.17) | copy-start | bytes 442372
  (32 other events, 189.6 us)

commit v4 on v3

--- a/solution.py
+++ b/solution.py
@@ -73,26 +73,63 @@
     picks_full = picks.astype(jnp.float32)
     flags_full = flag_values.astype(jnp.float32)
 
-    def add_coarse(piece):
-        return jnp.dot(coarse_inverse, piece.astype(jnp.float32), precision=lax.Precision.HIGHEST)
+    def add_coarse(rows, piece):
+        return jnp.dot(rows, piece, precision=lax.Precision.HIGHEST)
 
-    def precondition(resid):
+    partner_mats = jnp.stack(
+        [
+            from_partner(jnp.stack([deluxe_panel[face], schur_panel[face]]), axis, from_lower)
+            for axis, from_lower, face in PARTNERS
+        ]
+    )
+    deluxe_partner = partner_mats[:, 0]
+    schur_partner = partner_mats[:, 1]
+
+    own_small = jnp.concatenate(
+        [coarse_inverse.reshape(-1), primal_slots.astype(jnp.float32)]
+    )
+    small_rows = -(-own_small.shape[0] // width)
+    own_small = jnp.pad(own_small, (0, small_rows * width - own_small.shape[0])).reshape(
+        small_rows, width
+    )
+    face_positions = jnp.arange(width, dtype=jnp.int32)
+    partner_offsets = jnp.array([face * width for _, _, face in PARTNERS], jnp.int32)
+
+    def precondition(resid, partner_small):
         scaled = face_mul_turned(resid.astype(jnp.bfloat16), deluxe_panel).astype(jnp.bfloat16)
         local_part = face_mul(scaled, inverse_panel)
         extra = face_mul(local_part.astype(jnp.bfloat16), inverse_panel)
         softened = local_part + 0.5 * flags_full[:, None, None] * extra
+        received = []
+        for axis, from_lower, face in PARTNERS:
+            payload = softened[face]
+            if partner_small is None:
+                payload = jnp.concatenate([payload, own_small])
+            received.append(from_partner(payload, axis, from_lower))
+        received = jnp.stack(received)
+        softened_partner = received[:, : resid.shape[1]]
+        if partner_small is None:
+            partner_small = received[:, resid.shape[1] :].reshape(4, -1)
+        partner_rows = partner_small[:, : coarse_inverse.size].reshape(-1, coarse_inverse.shape[1])
+        partner_slots = partner_small[:, coarse_inverse.size : coarse_inverse.size + primal_count]
+        partner_picks = (
+            partner_slots.astype(jnp.int32)[:, :, None]
+            == (partner_offsets[:, None, None] + face_positions[None, None, :])
+        ).astype(jnp.float32)
+
         primal = jnp.einsum(
             "kfx,frx->kr", picks_half, scaled, preferred_element_type=jnp.float32
         ).astype(jnp.bfloat16)
-        coarse = add_coarse(gather_rows(primal, ("gx", "gy")))
+        primal_all = gather_rows(primal, ("gx", "gy")).astype(jnp.float32)
+        coarse = add_coarse(coarse_inverse, primal_all)
+        coarse_partner = add_coarse(partner_rows, primal_all).reshape(4, primal_count, -1)
         placed = jnp.einsum("kfx,kr->frx", picks_full, coarse, precision=lax.Precision.HIGHEST)
+        placed_partner = jnp.sum(partner_picks[:, :, None, :] * coarse_partner[:, :, :, None], axis=1)
         weighted = (softened + placed).astype(jnp.bfloat16)
-        spread = face_mul(weighted, deluxe_panel).astype(jnp.bfloat16)
-        return spread.astype(jnp.float32) + face_pairs(spread).astype(jnp.float32)
-
-    schur_partner = jnp.stack(
-        [from_partner(schur_panel[face], axis, from_lower) for axis, from_lower, face in PARTNERS]
-    )
+        weighted_partner = (softened_partner + placed_partner).astype(jnp.bfloat16)
+        spread = to_half(face_mul(weighted, deluxe_panel))
+        spread_partner = to_half(face_mul(weighted_partner, deluxe_partner))
+        return spread + spread_partner, partner_small
 
     def apply_operator(field):
         field_half = field.astype(jnp.bfloat16)
@@ -101,9 +138,9 @@
         return bent_own + bent_partner
 
     resid0 = loads_here.astype(jnp.float32) + face_pairs(loads_here).astype(jnp.float32)
-    first = precondition(resid0)
+    first, partner_small = precondition(resid0, None)
     resid1 = resid0 - apply_operator(first)
-    second = precondition(resid1)
+    second, _ = precondition(resid1, partner_small)
     curved = apply_operator(second)
     partial = jnp.stack(
         [jnp.sum(resid1 * second, axis=(0, 2)), jnp.sum(second * curved, axis=(0, 2))]

time: 114 us -> 146 us (1.28)
  other arithmetic: 3.28 us -> 16.1 us
  starting transfers between devices: 46.8 us -> 56.4 us
  local copies, waits for them, and re-layouts: 6.08 us -> 14.4 us
  waiting for transfers between devices: 27.5 us -> 21.4 us
  matrix products: 17 us -> 22.8 us
    ppermute x4 -> x12, starting transfers between devices: 10.3 us -> 30.1 us  [from_partner(): return lax.ppermute(values, axis, pairs)]
    ppermute x4 -> x12, waiting for transfers between devices: 8.32 us -> 21.4 us  [from_partner(): return lax.ppermute(values, axis, pairs)]
    all_to_all x2, waiting for transfers between devices: 11.6 us -> 0.01 us  [gather_rows(): swapped = lax.all_to_all(spread, axes, 0, 0, tiled=False)]
    ppermute x6 -> x2, starting transfers between devices: 18.9 us -> 9.97 us  [with_halo(): lax.ppermute(lax.slice_in_dim(block, block.shape[dim] - width, None, axis...]
    another operation x0 -> x6, other arithmetic: none -> 8.04 us  [the longest x4 3.56 us: per_device(): jnp.stack([deluxe_panel[face], schur_panel[face]])]
    ppermute x6 -> x2, waiting for transfers between devices: 7.6 us -> 0.01 us  [with_halo(): lax.ppermute(lax.slice_in_dim(block, 0, width, axis=dim), axis, backward)]
    ppermute x6 -> x2, starting transfers between devices: 7.88 us -> 2.57 us  [with_halo(): lax.ppermute(lax.slice_in_dim(block, 0, width, axis=dim), axis, backward)]
    all_to_all x2, starting transfers between devices: 9.61 us -> 13.7 us  [gather_rows(): swapped = lax.all_to_all(spread, axes, 0, 0, tiled=False)]
  transfers between devices with their start and end apart: 18 -> 18, of which waited for: 6 -> 5; matrix products, arithmetic and copies ran while one was open for 4% -> 22% of each run, Pallas kernels for 0% -> 0%
where the time goes in v4:
time: 146 us; the launch traced here: 145 us
  starting transfers between devices  56.4 us (39%)
  matrix products  22.8 us (16%)
  waiting for transfers between devices  21.4 us (15%)
  other arithmetic  16.1 us (11%)
  local copies, waits for them, and re-layouts  14.4 us (10%)
  blocking collectives  12.9 us (9%)
    ppermute x12, starting transfers between devices, from_partner(): return lax.ppermute(values, axis, pairs)  30.1 us
    ppermute x12, waiting for transfers between devices, from_partner(): return lax.ppermute(values, axis, pairs)  21.4 us
    all_to_all x2, starting transfers between devices, gather_rows(): swapped = lax.all_to_all(spread, axes, 0, 0, tiled=False)  13.7 us
    dot_general x12, matrix products, face_mul(): jnp.einsum('fry,fyx->frx', vectors, matrices, preferred_element_type=jnp....  13.1 us
    all_to_all x1, blocking collectives, gather_rows(): swapped = lax.all_to_all(spread, axes, 0, 0, tiled=False)  12.9 us
    ppermute x2, starting transfers between devices, with_halo(): lax.ppermute(lax.slice_in_dim(block, block.shape[dim] - width, None, axis...  9.97 us
    unnamed x61, local copies, waits for them, and re-layouts  4.57 us
    dot_general x4, matrix products, add_coarse(): return jnp.dot(rows, piece, precision=lax.Precision.HIGHEST)  3.94 us
  transfers between devices with their start and end apart: 18, of which 5 were waited for; matrix products, arithmetic and copies ran while one was open for 22% of the time, Pallas kernels for 0%

profile of v4, /device:TPU:0, one launch (start us, length us, event | category | flops | bytes accessed | tf_op | source)
XLA Modules:
  0.0 144.5 jit_solution(12137071545278126091)
XLA Ops:
  0.0 2.1 %slice_bitcast_fusion.25 = (bf16[1,192,384]{2,1,0:T(8,128)(2,1)}, bf16[1,192,384]{2,1,0:T(8,128)(2,1)}, bf16[1,192,384]{2,1,0:T(8,128)(2,1)}, bf16[1,192,384]{2,1,0:T(8,128)(2,1)}) fusion(bf16[1,1,4,192,384]{4,3,2,1,0:T(8,128)(2,1)} %param.8), kind=kLoop, calls=%fused_computation.96 | loop fusion | bytes 1179648 | tf_op jit(solution)/shard_map/slice | solution.py:13
  2.1 5.5 %collective-permute-start = (bf16[1,192,384]{2,1,0:T(8,128)(2,1)}, bf16[1,192,384]{2,1,0:T(8,128)(2,1)}, u32[]{:S(2)}, u32[]{:S(2)}) collective-permute-start(bf16[1,192,384]{2,1,0:T(8,128)(2,1)} %get-tuple-element.21), channel_id=1, source_target_pairs={{0,2},{2,4},{4,6},{6,8},{8,10},{10,12},{12,14},{14,16},{16,18},{18... | collective-permute-start | bytes 442376 | tf_op jit(solution)/shard_map/ppermute | solution.py:12
  10.3 4.5 %collective-permute-start.2 = (bf16[1,192,384]{2,1,0:T(8,128)(2,1)}, bf16[1,192,384]{2,1,0:T(8,128)(2,1)}, u32[]{:S(2)}, u32[]{:S(2)}) collective-permute-start(bf16[1,192,384]{2,1,0:T(8,128)(2,1)} %get-tuple-element.24), channel_id=1, source_target_pairs={{0,1},{2,3},{4,5},{6,7},{8,9},{10,11},{12,13},{14,15},{16,17},{18,... | collective-permute-start | bytes 442376 | tf_op jit(solution)/shard_map/ppermute | solution.py:12
  15.9 2.1 %collective-permute-start.10 = (bf16[2,384,384]{2,1,0:T(8,128)(2,1)}, bf16[2,384,384]{2,1,0:T(8,128)(2,1)}, u32[]{:S(2)}, u32[]{:S(2)}) collective-permute-start(bf16[2,384,384]{2,1,0:T(8,128)(2,1)} %pad_maximum_fusion.9), channel_id=1, source_target_pairs={{0,1},{2,3},{4,5},{6,7},{8,9},{10,11},{12,13},{14,15},{16,17},{18,... | collective-permute-start | bytes 1769480 | tf_op jit(solution)/shard_map/ppermute | solution.py:40
  22.6 1.7 %convolution_convert_fusion.1 = bf16[4,192,384]{2,1,0:T(8,128)(2,1)S(1)} fusion(bf16[1,1,4,384,384]{4,3,2,1,0:T(8,128)(2,1)S(1)} %copy-done.2, bf16[1,1,4,192,384]{4,3,2,1,0:T(8,128)(2,1)S(1)} %copy-done.14, bf16[1,192,384]{2,1,0:T(8,128)(2,1)} %collective-permute-done.3, bf16[1,192,384]{2,1,0:T(8,128)(2,1)} %collective-permute-done.2, ...), kind=kOutput, calls=%fused_computation.28 | convolution fusion | flops 228851712 | bytes 2949120 | tf_op jit(solution)/shard_map/fry,fxy->frx/dot_general | solution.py:52
  25.2 7.1 %all-to-all-start = ((bf16[32,4,192]{2,1,0:T(4,128)(2,1)}), bf16[32,4,192]{2,1,0:T(4,128)(2,1)}, u32[]{:S(2)}, u32[]{:S(2)}) async-start(bf16[32,4,192]{2,1,0:T(4,128)(2,1)} %broadcast_in_dim.8), calls=%async_computation | async-start | bytes 131072 | tf_op jit(solution)/shard_map/all_to_all | solution.py:23
  35.3 4.3 %collective-permute-start.4 = (f32[194,384]{1,0:T(8,128)}, f32[194,384]{1,0:T(8,128)}, u32[]{:S(2)}, u32[]{:S(2)}) collective-permute-start(f32[194,384]{1,0:T(8,128)} %get-tuple-element.25), channel_id=1, source_target_pairs={{0,2},{2,4},{4,6},{6,8},{8,10},{10,12},{12,14},{14,16},{16,18},{18... | collective-permute-start | bytes 893960 | tf_op jit(solution)/shard_map/ppermute | solution.py:40
  40.9 2.5 %collective-permute-start.6 = (f32[194,384]{1,0:T(8,128)}, f32[194,384]{1,0:T(8,128)}, u32[]{:S(2)}, u32[]{:S(2)}) collective-permute-start(f32[194,384]{1,0:T(8,128)} %get-tuple-element.27), channel_id=1, source_target_pairs={{0,1},{2,3},{4,5},{6,7},{8,9},{10,11},{12,13},{14,15},{16,17},{18,... | collective-permute-start | bytes 893960 | tf_op jit(solution)/shard_map/ppermute | solution.py:40
  49.5 3.1 %collective-permute-done.4 = f32[194,384]{1,0:T(8,128)} collective-permute-done((f32[194,384]{1,0:T(8,128)}, f32[194,384]{1,0:T(8,128)}, u32[]{:S(2)}, u32[]{:S(2)}) %collective-permute-start.4) | collective-permute-done | bytes 298016 | tf_op jit(solution)/shard_map/ppermute | solution.py:40
  55.9 4.6 %collective-permute-start.8 = (bf16[2,384,384]{2,1,0:T(8,128)(2,1)S(1)}, bf16[2,384,384]{2,1,0:T(8,128)(2,1)S(1)}, u32[]{:S(2)}, u32[]{:S(2)}) collective-permute-start(bf16[2,384,384]{2,1,0:T(8,128)(2,1)S(1)} %copy-done.19), channel_id=1, source_target_pairs={{0,2},{2,4},{4,6},{6,8},{8,10},{10,12},{12,14},{14,16},{16,18},{18... | collective-permute-start | bytes 1769480 | tf_op jit(solution)/shard_map/ppermute | solution.py:40
  61.2 2.4 %pad_maximum_fusion.1 = f32[4,194,384]{2,1,0:T(8,128)} fusion(f32[1,194,384]{2,1,0:T(8,128)} %bitcast.20, f32[1,194,384]{2,1,0:T(8,128)} %bitcast.18, f32[1,194,384]{2,1,0:T(8,128)} %bitcast.16, f32[1,194,384]{2,1,0:T(8,128)} %bitcast.14), kind=kLoop, calls=%fused_computation.30 | loop fusion | flops 893952 | bytes 2383872 | tf_op jit(solution)/shard_map/stack | solution.py:109
  67.8 4.7 %collective-permute-done.9 = bf16[2,384,384]{2,1,0:T(8,128)(2,1)S(1)} collective-permute-done((bf16[2,384,384]{2,1,0:T(8,128)(2,1)}, bf16[2,384,384]{2,1,0:T(8,128)(2,1)S(1)}, u32[]{:S(2)}, u32[]{:S(2)}) %collective-permute-start.9) | collective-permute-done | bytes 589856 | tf_op jit(solution)/shard_map/ppermute | solution.py:40
  72.5 11.3 %collective-permute-done.8 = bf16[2,384,384]{2,1,0:T(8,128)(2,1)S(1)} collective-permute-done((bf16[2,384,384]{2,1,0:T(8,128)(2,1)S(1)}, bf16[2,384,384]{2,1,0:T(8,128)(2,1)S(1)}, u32[]{:S(2)}, u32[]{:S(2)}) %collective-permute-start.8) | collective-permute-done | bytes 589856 | tf_op jit(solution)/shard_map/ppermute | solution.py:40
  84.6 2.1 %pad_maximum_fusion = bf16[4,2,384,384]{3,2,0,1:T(8,128)(2,1)S(1)} fusion(bf16[1,2,384,384]{3,2,0,1:T(8,128)(2,1)} %bitcast.149, bf16[1,2,384,384]{3,2,0,1:T(8,128)(2,1)} %bitcast.30, bf16[1,2,384,384]{3,2,0,1:T(8,128)(2,1)} %bitcast.150, bf16[1,2,384,384]{3,2,0,1:T(8,128)(2,1)} %bitcast.151), kind=kLoop, calls=%fused_computation.2 | loop fusion | flops 3538944 | bytes 4718592 | tf_op jit(solution)/shard_map/stack | solution.py:79
  89.7 1.8 %fusion.5 = f32[4,192,384]{2,1,0:T(8,128)S(1)} fusion(f32[4,192,384]{2,1,0:T(8,128)S(1)} %convolution_reduce-precision_fusion.5, bf16[4,2,384,384]{3,2,0,1:T(8,128)(2,1)S(1)} %pad_maximum_fusion, bf16[1,1,4,192,384]{4,3,2,1,0:T(8,128)(2,1)S(1)} %copy-done.15, f32[4,192,384]{2,1,0:T(8,128)S(1)} %fusion.6, bf16[1,192,384]{2,1,0:T(8,128)(2,1)} %collective-permute-done.3, ...), kind=kOutput, calls=%fused_computation.14 | convolution fusion | flops 230621184 | bytes 5898240 | tf_op jit(solution)/shard_map/fry,fyx->frx/dot_general | solution.py:48
  95.1 6.6 %all-to-all-start.1 = ((bf16[32,4,192]{2,1,0:T(4,128)(2,1)}), bf16[32,4,192]{2,1,0:T(4,128)(2,1)}, u32[]{:S(2)}, u32[]{:S(2)}) async-start(bf16[32,4,192]{2,1,0:T(4,128)(2,1)} %broadcast_in_dim.9), calls=%async_computation.1 | async-start | bytes 131072 | tf_op jit(solution)/shard_map/all_to_all | solution.py:23
  101.7 2.2 %fusion.3 = f32[4,192,384]{2,1,0:T(8,128)S(1)} fusion(f32[4,192,384]{2,1,0:T(8,128)} %fusion.18, bf16[1,1,4,384,384]{4,3,2,1,0:T(8,128)(2,1)S(1)} %copy-done, f32[4]{0:T(128)} %multiply_bitcast_fusion), kind=kOutput, calls=%fused_computation.11 | convolution fusion | flops 227377152 | bytes 3538960 | tf_op jit(solution)/shard_map/fry,fyx->frx/dot_general | solution.py:48
  105.3 4.3 %collective-permute-start.12 = (f32[192,384]{1,0:T(8,128)}, f32[192,384]{1,0:T(8,128)}, u32[]{:S(2)}, u32[]{:S(2)}) collective-permute-start(f32[192,384]{1,0:T(8,128)} %get-tuple-element.5), channel_id=1, source_target_pairs={{0,2},{2,4},{4,6},{6,8},{8,10},{10,12},{12,14},{14,16},{16,18},{18... | collective-permute-start | bytes 884744 | tf_op jit(solution)/shard_map/ppermute | solution.py:40
  110.9 4.5 %collective-permute-start.14 = (f32[192,384]{1,0:T(8,128)}, f32[192,384]{1,0:T(8,128)}, u32[]{:S(2)}, u32[]{:S(2)}) collective-permute-start(f32[192,384]{1,0:T(8,128)} %get-tuple-element.7), channel_id=1, source_target_pairs={{0,1},{2,3},{4,5},{6,7},{8,9},{10,11},{12,13},{14,15},{16,17},{18,... | collective-permute-start | bytes 884744 | tf_op jit(solution)/shard_map/ppermute | solution.py:40
  120.4 2.1 %fusion.11 = bf16[4,192,384]{2,1,0:T(8,128)(2,1)S(1)} fusion(f32[4,192,384]{2,1,0:T(8,128)} %copy-done.9, f32[192,4,1]{0,1,2:T(4,128)S(1)} %convolution_bitcast_fusion.4, s32[4,384]{1,0:T(4,128)S(1)} %multiply_add_fusion, s32[4]{0:T(128)} %bitcast.155), kind=kOutput, calls=%fused_computation.26 | convolution fusion | flops 14751744 | bytes 1778704 | tf_op jit(solution)/shard_map/kfx,kr->frx/dot_general | solution.py:126
  123.6 1.6 %collective-permute-done.13 = f32[192,384]{1,0:T(8,128)} collective-permute-done((f32[192,384]{1,0:T(8,128)}, f32[192,384]{1,0:T(8,128)}, u32[]{:S(2)}, u32[]{:S(2)}) %collective-permute-start.13) | collective-permute-done | bytes 294944 | tf_op jit(solution)/shard_map/ppermute | solution.py:40
  125.2 2.0 %multiply_reduce_fusion.2 = (f32[192]{0:T(256)S(1)}, f32[4,192,384]{2,1,0:T(8,128)S(1)}) fusion(f32[4,192,384]{2,1,0:T(8,128)S(1)} %copy-done.11, f32[4,192,384]{2,1,0:T(8,128)S(1)} %convolution_reduce-precision_fusion.3, bf16[4,2,384,384]{3,2,0,1:T(8,128)(2,1)S(1)} %pad_maximum_fusion, f32[4,192,384]{2,1,0:T(8,128)S(1)} %multiply_reduce_fusion, ...), kind=kOutput, calls=%fused_computation.51 | convolution fusion | flops 229146432 | bytes 7078656 | tf_op jit(solution)/shard_map/fry,fyx->frx/dot_general | solution.py:48
  128.9 12.9 %all_to_all.15 = f32[32,1,2,192]{3,2,1,0:T(2,128)S(1)} all-to-all(f32[32,1,2,192]{3,2,1,0:T(2,128)S(1)} %broadcast_in_dim.10), channel_id=1, replica_groups=mesh['gx'=16,'gy'=2] {'gx','gy'}, dimensions={0} | all-to-all | bytes 98304 | tf_op jit(solution)/shard_map/all_to_all | solution.py:23
  141.9 2.6 %fusion.31 = bf16[1,1,4,192,384]{4,3,2,1,0:T(8,128)(2,1)} fusion(f32[4,192,384]{2,1,0:T(8,128)} %copy-done.1, f32[4,192,384]{2,1,0:T(8,128)} %copy-done.5, f32[192]{0:T(256)S(1)} %bitcast.159), kind=kLoop, calls=%fused_computation.63 | loop fusion | flops 884736 | bytes 2949888 | tf_op jit(solution)/shard_map/broadcast_in_dim | solution.py:151
  (130 shorter events, 45.3 us)
Async XLA Ops:
  0.0 32.4 %copy-start = (bf16[1,1,4,384,384]{4,3,2,1,0:T(8,128)(2,1)S(1)}, bf16[1,1,4,384,384]{4,3,2,1,0:T(8,128)(2,1)}, u32[]{:S(2)}) copy-start(bf16[1,1,4,384,384]{4,3,2,1,0:T(8,128)(2,1)} %param.11) | copy-start | bytes 3538948
  0.0 14.7 %copy-start.6 = (bf16[1,1,4,384,384]{4,3,2,1,0:T(8,128)(2,1)S(1)}, bf16[1,1,4,384,384]{4,3,2,1,0:T(8,128)(2,1)}, u32[]{:S(2)}) copy-start(bf16[1,1,4,384,384]{4,3,2,1,0:T(8,128)(2,1)} %param.9) | copy-start | bytes 3538948
  2.1 20.4 %collective-permute-start = (bf16[1,192,384]{2,1,0:T(8,128)(2,1)}, bf16[1,192,384]{2,1,0:T(8,128)(2,1)}, u32[]{:S(2)}, u32[]{:S(2)}) collective-permute-start(bf16[1,192,384]{2,1,0:T(8,128)(2,1)} %get-tuple-element.21), channel_id=1, source_target_pairs={{0,2},{2,4},{4,6},{6,8},{8,10},{10,12},{12,14},{14,16},{16,18},{18... | collective-permute-start | bytes 442376 | tf_op jit(solution)/shard_map/ppermute | solution.py:12
  7.7 14.9 %collective-permute-start.1 = (bf16[1,192,384]{2,1,0:T(8,128)(2,1)}, bf16[1,192,384]{2,1,0:T(8,128)(2,1)}, u32[]{:S(2)}, u32[]{:S(2)}) collective-permute-start(bf16[1,192,384]{2,1,0:T(8,128)(2,1)} %get-tuple-element.22), channel_id=1, source_target_pairs={{2,0},{4,2},{6,4},{8,6},{10,8},{12,10},{14,12},{16,14},{18,16},{20... | collective-permute-start | bytes 442376 | tf_op jit(solution)/shard_map/ppermute | solution.py:15
  8.9 13.6 %collective-permute-start.3 = (bf16[1,192,384]{2,1,0:T(8,128)(2,1)}, bf16[1,192,384]{2,1,0:T(8,128)(2,1)}, u32[]{:S(2)}, u32[]{:S(2)}) collective-permute-start(bf16[1,192,384]{2,1,0:T(8,128)(2,1)} %get-tuple-element.23), channel_id=1, source_target_pairs={{1,0},{3,2},{5,4},{7,6},{9,8},{11,10},{13,12},{15,14},{17,16},{19,... | collective-permute-start | bytes 442376 | tf_op jit(solution)/shard_map/ppermute | solution.py:15
  10.3 12.3 %collective-permute-start.2 = (bf16[1,192,384]{2,1,0:T(8,128)(2,1)}, bf16[1,192,384]{2,1,0:T(8,128)(2,1)}, u32[]{:S(2)}, u32[]{:S(2)}) collective-permute-start(bf16[1,192,384]{2,1,0:T(8,128)(2,1)} %get-tuple-element.24), channel_id=1, source_target_pairs={{0,1},{2,3},{4,5},{6,7},{8,9},{10,11},{12,13},{14,15},{16,17},{18,... | collective-permute-start | bytes 442376 | tf_op jit(solution)/shard_map/ppermute | solution.py:12
  15.9 51.9 %collective-permute-start.10 = (bf16[2,384,384]{2,1,0:T(8,128)(2,1)}, bf16[2,384,384]{2,1,0:T(8,128)(2,1)}, u32[]{:S(2)}, u32[]{:S(2)}) collective-permute-start(bf16[2,384,384]{2,1,0:T(8,128)(2,1)} %pad_maximum_fusion.9), channel_id=1, source_target_pairs={{0,1},{2,3},{4,5},{6,7},{8,9},{10,11},{12,13},{14,15},{16,17},{18,... | collective-permute-start | bytes 1769480 | tf_op jit(solution)/shard_map/ppermute | solution.py:40
  25.2 19.5 %all-to-all-start = ((bf16[32,4,192]{2,1,0:T(4,128)(2,1)}), bf16[32,4,192]{2,1,0:T(4,128)(2,1)}, u32[]{:S(2)}, u32[]{:S(2)}) async-start(bf16[32,4,192]{2,1,0:T(4,128)(2,1)} %broadcast_in_dim.8), calls=%async_computation | async-start | bytes 131072 | tf_op jit(solution)/shard_map/all_to_all | solution.py:23
  35.3 17.3 %collective-permute-start.4 = (f32[194,384]{1,0:T(8,128)}, f32[194,384]{1,0:T(8,128)}, u32[]{:S(2)}, u32[]{:S(2)}) collective-permute-start(f32[194,384]{1,0:T(8,128)} %get-tuple-element.25), channel_id=1, source_target_pairs={{0,2},{2,4},{4,6},{6,8},{8,10},{10,12},{12,14},{14,16},{16,18},{18... | collective-permute-start | bytes 893960 | tf_op jit(solution)/shard_map/ppermute | solution.py:40
  39.6 14.9 %collective-permute-start.5 = (f32[194,384]{1,0:T(8,128)}, f32[194,384]{1,0:T(8,128)}, u32[]{:S(2)}, u32[]{:S(2)}) collective-permute-start(f32[194,384]{1,0:T(8,128)} %get-tuple-element.26), channel_id=1, source_target_pairs={{2,0},{4,2},{6,4},{8,6},{10,8},{12,10},{14,12},{16,14},{18,16},{20... | collective-permute-start | bytes 893960 | tf_op jit(solution)/shard_map/ppermute | solution.py:40
  40.9 14.9 %collective-permute-start.6 = (f32[194,384]{1,0:T(8,128)}, f32[194,384]{1,0:T(8,128)}, u32[]{:S(2)}, u32[]{:S(2)}) collective-permute-start(f32[194,384]{1,0:T(8,128)} %get-tuple-element.27), channel_id=1, source_target_pairs={{0,1},{2,3},{4,5},{6,7},{8,9},{10,11},{12,13},{14,15},{16,17},{18,... | collective-permute-start | bytes 893960 | tf_op jit(solution)/shard_map/ppermute | solution.py:40
  43.4 17.0 %collective-permute-start.7 = (f32[194,384]{1,0:T(8,128)}, f32[194,384]{1,0:T(8,128)}, u32[]{:S(2)}, u32[]{:S(2)}) collective-permute-start(f32[194,384]{1,0:T(8,128)} %get-tuple-element.28), channel_id=1, source_target_pairs={{1,0},{3,2},{5,4},{7,6},{9,8},{11,10},{13,12},{15,14},{17,16},{19,... | collective-permute-start | bytes 893960 | tf_op jit(solution)/shard_map/ppermute | solution.py:40
  47.9 7.9 %copy-start.19 = (bf16[2,384,384]{2,1,0:T(8,128)(2,1)S(1)}, bf16[2,384,384]{2,1,0:T(8,128)(2,1)}, u32[]{:S(2)}) copy-start(bf16[2,384,384]{2,1,0:T(8,128)(2,1)} %pad_maximum_fusion.7) | copy-start | bytes 1769476
  52.6 15.1 %collective-permute-start.11 = (bf16[2,384,384]{2,1,0:T(8,128)(2,1)}, bf16[2,384,384]{2,1,0:T(8,128)(2,1)S(1)}, u32[]{:S(2)}, u32[]{:S(2)}) collective-permute-start(bf16[2,384,384]{2,1,0:T(8,128)(2,1)} %pad_maximum_fusion.10), channel_id=1, source_target_pairs={{1,0},{3,2},{5,4},{7,6},{9,8},{11,10},{13,12},{15,14},{17,16},{19,... | collective-permute-start | bytes 1769480 | tf_op jit(solution)/shard_map/ppermute | solution.py:40
  54.6 18.0 %collective-permute-start.9 = (bf16[2,384,384]{2,1,0:T(8,128)(2,1)}, bf16[2,384,384]{2,1,0:T(8,128)(2,1)S(1)}, u32[]{:S(2)}, u32[]{:S(2)}) collective-permute-start(bf16[2,384,384]{2,1,0:T(8,128)(2,1)} %pad_maximum_fusion.8), channel_id=1, source_target_pairs={{2,0},{4,2},{6,4},{8,6},{10,8},{12,10},{14,12},{16,14},{18,16},{20... | collective-permute-start | bytes 1769480 | tf_op jit(solution)/shard_map/ppermute | solution.py:40
  55.9 27.9 %collective-permute-start.8 = (bf16[2,384,384]{2,1,0:T(8,128)(2,1)S(1)}, bf16[2,384,384]{2,1,0:T(8,128)(2,1)S(1)}, u32[]{:S(2)}, u32[]{:S(2)}) collective-permute-start(bf16[2,384,384]{2,1,0:T(8,128)(2,1)S(1)} %copy-done.19), channel_id=1, source_target_pairs={{0,2},{2,4},{4,6},{6,8},{8,10},{10,12},{12,14},{14,16},{16,18},{18... | collective-permute-start | bytes 1769480 | tf_op jit(solution)/shard_map/ppermute | solution.py:40
  66.3 17.5 %copy-start.20 = (f32[4,4,384]{2,1,0:T(4,128)}, f32[4,4,384]{2,1,0:T(4,128)S(1)}, u32[]{:S(2)}) copy-start(f32[4,4,384]{2,1,0:T(4,128)S(1)} %compare_convert_fusion) | copy-start | bytes 73732
  67.8 16.0 %copy-start.16 = (bf16[2,384,384]{2,1,0:T(8,128)(2,1)}, bf16[2,384,384]{2,1,0:T(8,128)(2,1)S(1)}, u32[]{:S(2)}) copy-start(bf16[2,384,384]{2,1,0:T(8,128)(2,1)S(1)} %collective-permute-done.11) | copy-start | bytes 1769476
  72.5 11.3 %copy-start.17 = (bf16[2,384,384]{2,1,0:T(8,128)(2,1)}, bf16[2,384,384]{2,1,0:T(8,128)(2,1)S(1)}, u32[]{:S(2)}) copy-start(bf16[2,384,384]{2,1,0:T(8,128)(2,1)S(1)} %collective-permute-done.9) | copy-start | bytes 1769476
  95.1 21.8 %all-to-all-start.1 = ((bf16[32,4,192]{2,1,0:T(4,128)(2,1)}), bf16[32,4,192]{2,1,0:T(4,128)(2,1)}, u32[]{:S(2)}, u32[]{:S(2)}) async-start(bf16[32,4,192]{2,1,0:T(4,128)(2,1)} %broadcast_in_dim.9), calls=%async_computation.1 | async-start | bytes 131072 | tf_op jit(solution)/shard_map/all_to_all | solution.py:23
  105.3 18.2 %collective-permute-start.12 = (f32[192,384]{1,0:T(8,128)}, f32[192,384]{1,0:T(8,128)}, u32[]{:S(2)}, u32[]{:S(2)}) collective-permute-start(f32[192,384]{1,0:T(8,128)} %get-tuple-element.5), channel_id=1, source_target_pairs={{0,2},{2,4},{4,6},{6,8},{8,10},{10,12},{12,14},{14,16},{16,18},{18... | collective-permute-start | bytes 884744 | tf_op jit(solution)/shard_map/ppermute | solution.py:40
  109.6 13.9 %collective-permute-start.15 = (f32[192,384]{1,0:T(8,128)}, f32[192,384]{1,0:T(8,128)}, u32[]{:S(2)}, u32[]{:S(2)}) collective-permute-start(f32[192,384]{1,0:T(8,128)} %get-tuple-element.6), channel_id=1, source_target_pairs={{1,0},{3,2},{5,4},{7,6},{9,8},{11,10},{13,12},{15,14},{17,16},{19,... | collective-permute-start | bytes 884744 | tf_op jit(solution)/shard_map/ppermute | solution.py:40
  110.9 12.6 %collective-permute-start.14 = (f32[192,384]{1,0:T(8,128)}, f32[192,384]{1,0:T(8,128)}, u32[]{:S(2)}, u32[]{:S(2)}) collective-permute-start(f32[192,384]{1,0:T(8,128)} %get-tuple-element.7), channel_id=1, source_target_pairs={{0,1},{2,3},{4,5},{6,7},{8,9},{10,11},{12,13},{14,15},{16,17},{18,... | collective-permute-start | bytes 884744 | tf_op jit(solution)/shard_map/ppermute | solution.py:40
  115.4 9.8 %collective-permute-start.13 = (f32[192,384]{1,0:T(8,128)}, f32[192,384]{1,0:T(8,128)}, u32[]{:S(2)}, u32[]{:S(2)}) collective-permute-start(f32[192,384]{1,0:T(8,128)} %get-tuple-element.8), channel_id=1, source_target_pairs={{2,0},{4,2},{6,4},{8,6},{10,8},{12,10},{14,12},{16,14},{18,16},{20... | collective-permute-start | bytes 884744 | tf_op jit(solution)/shard_map/ppermute | solution.py:40
  (24 other events, 48.3 us)

commit v5 on v3

--- a/solution.py
+++ b/solution.py
@@ -76,7 +76,7 @@
     def add_coarse(piece):
         return jnp.dot(coarse_inverse, piece.astype(jnp.float32), precision=lax.Precision.HIGHEST)
 
-    def precondition(resid):
+    def precondition(resid, schur_partner):
         scaled = face_mul_turned(resid.astype(jnp.bfloat16), deluxe_panel).astype(jnp.bfloat16)
         local_part = face_mul(scaled, inverse_panel)
         extra = face_mul(local_part.astype(jnp.bfloat16), inverse_panel)
@@ -88,23 +88,29 @@
         placed = jnp.einsum("kfx,kr->frx", picks_full, coarse, precision=lax.Precision.HIGHEST)
         weighted = (softened + placed).astype(jnp.bfloat16)
         spread = face_mul(weighted, deluxe_panel).astype(jnp.bfloat16)
-        return spread.astype(jnp.float32) + face_pairs(spread).astype(jnp.float32)
+        if schur_partner is not None:
+            return spread.astype(jnp.float32) + face_pairs(spread).astype(jnp.float32), schur_partner
+        received = jnp.stack(
+            [
+                from_partner(jnp.concatenate([spread[face], schur_panel[face]]), axis, from_lower)
+                for axis, from_lower, face in PARTNERS
+            ]
+        )
+        rows = spread.shape[1]
+        spread_partner = received[:, :rows]
+        return spread.astype(jnp.float32) + spread_partner.astype(jnp.float32), received[:, rows:]
 
-    schur_partner = jnp.stack(
-        [from_partner(schur_panel[face], axis, from_lower) for axis, from_lower, face in PARTNERS]
-    )
-
-    def apply_operator(field):
+    def apply_operator(field, schur_partner):
         field_half = field.astype(jnp.bfloat16)
         bent_own = to_half(face_mul(field_half, schur_panel))
         bent_partner = to_half(face_mul(field_half, schur_partner))
         return bent_own + bent_partner
 
     resid0 = loads_here.astype(jnp.float32) + face_pairs(loads_here).astype(jnp.float32)
-    first = precondition(resid0)
-    resid1 = resid0 - apply_operator(first)
-    second = precondition(resid1)
-    curved = apply_operator(second)
+    first, schur_partner = precondition(resid0, None)
+    resid1 = resid0 - apply_operator(first, schur_partner)
+    second, _ = precondition(resid1, schur_partner)
+    curved = apply_operator(second, schur_partner)
     partial = jnp.stack(
         [jnp.sum(resid1 * second, axis=(0, 2)), jnp.sum(second * curved, axis=(0, 2))]
     )

time: 114 us -> 112 us (0.982)
  starting transfers between devices: 46.8 us -> 38.5 us
  waiting for transfers between devices: 27.5 us -> 32.9 us
    ppermute x4, waiting for transfers between devices: 8.32 us -> 14.7 us  [from_partner(): return lax.ppermute(values, axis, pairs)]
    ppermute x6 -> x4, starting transfers between devices: 18.9 us -> 13.5 us  [with_halo(): lax.ppermute(lax.slice_in_dim(block, block.shape[dim] - width, None, axis...]
    ppermute x6 -> x4, starting transfers between devices: 7.88 us -> 5.3 us  [with_halo(): lax.ppermute(lax.slice_in_dim(block, 0, width, axis=dim), axis, backward)]
    ppermute x6 -> x4, waiting for transfers between devices: 7.6 us -> 6.57 us  [with_halo(): lax.ppermute(lax.slice_in_dim(block, 0, width, axis=dim), axis, backward)]
  transfers between devices with their start and end apart: 18 -> 14, of which waited for: 6 -> 6; matrix products, arithmetic and copies ran while one was open for 4% -> 4% of each run, Pallas kernels for 0% -> 0%
where the time goes in v5:
time: 112 us; the launch traced here: 111 us
  starting transfers between devices  38.5 us (34%)
  waiting for transfers between devices  32.9 us (29%)
  matrix products  16.8 us (15%)
  blocking collectives  12.1 us (11%)
  local copies, waits for them, and re-layouts  6.86 us (6%)
  other arithmetic  3.5 us (3%)
    ppermute x4, waiting for transfers between devices, from_partner(): return lax.ppermute(values, axis, pairs)  14.7 us
    ppermute x4, starting transfers between devices, with_halo(): lax.ppermute(lax.slice_in_dim(block, block.shape[dim] - width, None, axis...  13.5 us
    all_to_all x1, blocking collectives, gather_rows(): swapped = lax.all_to_all(spread, axes, 0, 0, tiled=False)  12.1 us
    all_to_all x2, waiting for transfers between devices, gather_rows(): swapped = lax.all_to_all(spread, axes, 0, 0, tiled=False)  11.7 us
    dot_general x8, matrix products, face_mul(): jnp.einsum('fry,fyx->frx', vectors, matrices, preferred_element_type=jnp....  11.3 us
    ppermute x4, starting transfers between devices, from_partner(): return lax.ppermute(values, axis, pairs)  10.2 us
    all_to_all x2, starting transfers between devices, gather_rows(): swapped = lax.all_to_all(spread, axes, 0, 0, tiled=False)  9.42 us
    ppermute x4, waiting for transfers between devices, with_halo(): lax.ppermute(lax.slice_in_dim(block, 0, width, axis=dim), axis, backward)  6.57 us
  transfers between devices with their start and end apart: 14, of which 6 were waited for; matrix products, arithmetic and copies ran while one was open for 4% of the time, Pallas kernels for 0%

profile of v5, /device:TPU:0, one launch (start us, length us, event | category | flops | bytes accessed | tf_op | source)
XLA Modules:
  0.0 111.4 jit_solution(8409649566027016863)
XLA Ops:
  1.3 4.9 %collective-permute-start = (bf16[1,192,384]{2,1,0:T(8,128)(2,1)S(1)}, bf16[1,192,384]{2,1,0:T(8,128)(2,1)S(1)}, u32[]{:S(2)}, u32[]{:S(2)}) collective-permute-start(bf16[1,192,384]{2,1,0:T(8,128)(2,1)S(1)} %get-tuple-element.17), channel_id=1, source_target_pairs={{0,2},{2,4},{4,6},{6,8},{8,10},{10,12},{12,14},{14,16},{16,18},{18... | collective-permute-start | bytes 442376 | tf_op jit(solution)/shard_map/ppermute | solution.py:12
  8.8 3.2 %collective-permute-start.2 = (bf16[1,192,384]{2,1,0:T(8,128)(2,1)S(1)}, bf16[1,192,384]{2,1,0:T(8,128)(2,1)S(1)}, u32[]{:S(2)}, u32[]{:S(2)}) collective-permute-start(bf16[1,192,384]{2,1,0:T(8,128)(2,1)S(1)} %get-tuple-element.20), channel_id=1, source_target_pairs={{0,1},{2,3},{4,5},{6,7},{8,9},{10,11},{12,13},{14,15},{16,17},{18,... | collective-permute-start | bytes 442376 | tf_op jit(solution)/shard_map/ppermute | solution.py:12
  16.1 6.1 %all-to-all-start = ((bf16[32,4,192]{2,1,0:T(4,128)(2,1)}), bf16[32,4,192]{2,1,0:T(4,128)(2,1)S(1)}, u32[]{:S(2)}, u32[]{:S(2)}) async-start(bf16[32,4,192]{2,1,0:T(4,128)(2,1)} %broadcast_in_dim.8), calls=%async_computation | async-start | bytes 131072 | tf_op jit(solution)/shard_map/all_to_all | solution.py:23
  22.3 1.6 %fusion.19 = f32[4,192,384]{2,1,0:T(8,128)} fusion(bf16[4,192,384]{2,1,0:T(8,128)(2,1)S(1)} %convolution_convert_fusion.3, bf16[1,1,4,384,384]{4,3,2,1,0:T(8,128)(2,1)S(1)} %copy-done.1), kind=kOutput, calls=%fused_computation.33 | convolution fusion | flops 226492416 | bytes 2949120 | tf_op jit(solution)/shard_map/fry,fyx->frx/dot_general | solution.py:48
  23.9 5.8 %all-to-all-done = bf16[32,4,192]{2,1,0:T(4,128)(2,1)S(1)} async-done(((bf16[32,4,192]{2,1,0:T(4,128)(2,1)}), bf16[32,4,192]{2,1,0:T(4,128)(2,1)S(1)}, u32[]{:S(2)}, u32[]{:S(2)}) %all-to-all-start) | async-done | bytes 49184 | tf_op jit(solution)/shard_map/all_to_all | solution.py:23
  29.8 1.8 %convolution_bitcast_fusion.1 = f32[4,192,384]{2,1,0:T(8,128)} fusion(f32[192,4,1]{0,1,2:T(4,128)S(1)} %convolution_bitcast_fusion.5, s32[4,384]{1,0:T(4,128)S(1)} %multiply_add_fusion, s32[4]{0:T(128)S(1)} %bitcast.111), kind=kOutput, calls=%fused_computation.15 | convolution fusion | flops 14161920 | bytes 1188880 | tf_op jit(solution)/shard_map/kfx,kr->frx/dot_general | solution.py:88
  31.6 2.9 %convolution_convert_fusion.2 = bf16[4,192,384]{2,1,0:T(8,128)(2,1)S(1)} fusion(f32[4,192,384]{2,1,0:T(8,128)} %convolution_bitcast_fusion.1, f32[4,192,384]{2,1,0:T(8,128)} %fusion.19, bf16[1,1,4,384,384]{4,3,2,1,0:T(8,128)(2,1)S(1)} %copy-done.1, bf16[1,1,4,384,384]{4,3,2,1,0:T(8,128)(2,1)S(1)} %copy-done, f32[4]{0:T(128)S(1)} %copy-done.26), kind=kOutput, calls=%fused_computation.20 | convolution fusion | flops 454754304 | bytes 5308432 | tf_op jit(solution)/shard_map/fry,fyx->frx/dot_general | solution.py:48
  34.7 1.4 %collective-permute-start.7 = (bf16[576,384]{1,0:T(8,128)(2,1)S(1)}, bf16[576,384]{1,0:T(8,128)(2,1)S(1)}, u32[]{:S(2)}, u32[]{:S(2)}) collective-permute-start(bf16[576,384]{1,0:T(8,128)(2,1)S(1)} %pad_maximum_fusion.9), channel_id=1, source_target_pairs={{1,0},{3,2},{5,4},{7,6},{9,8},{11,10},{13,12},{15,14},{17,16},{19,... | collective-permute-start | bytes 1327112 | tf_op jit(solution)/shard_map/ppermute | solution.py:40
  36.2 1.4 %collective-permute-start.5 = (bf16[576,384]{1,0:T(8,128)(2,1)S(1)}, bf16[576,384]{1,0:T(8,128)(2,1)S(1)}, u32[]{:S(2)}, u32[]{:S(2)}) collective-permute-start(bf16[576,384]{1,0:T(8,128)(2,1)S(1)} %pad_maximum_fusion.7), channel_id=1, source_target_pairs={{2,0},{4,2},{6,4},{8,6},{10,8},{12,10},{14,12},{16,14},{18,16},{20... | collective-permute-start | bytes 1327112 | tf_op jit(solution)/shard_map/ppermute | solution.py:40
  37.7 3.1 %collective-permute-start.6 = (bf16[576,384]{1,0:T(8,128)(2,1)S(1)}, bf16[576,384]{1,0:T(8,128)(2,1)S(1)}, u32[]{:S(2)}, u32[]{:S(2)}) collective-permute-start(bf16[576,384]{1,0:T(8,128)(2,1)S(1)} %pad_maximum_fusion.8), channel_id=1, source_target_pairs={{0,1},{2,3},{4,5},{6,7},{8,9},{10,11},{12,13},{14,15},{16,17},{18,... | collective-permute-start | bytes 1327112 | tf_op jit(solution)/shard_map/ppermute | solution.py:40
  40.8 4.3 %collective-permute-start.4 = (bf16[576,384]{1,0:T(8,128)(2,1)S(1)}, bf16[576,384]{1,0:T(8,128)(2,1)S(1)}, u32[]{:S(2)}, u32[]{:S(2)}) collective-permute-start(bf16[576,384]{1,0:T(8,128)(2,1)S(1)} %pad_maximum_fusion.6), channel_id=1, source_target_pairs={{0,2},{2,4},{4,6},{6,8},{8,10},{10,12},{12,14},{14,16},{16,18},{18... | collective-permute-start | bytes 1327112 | tf_op jit(solution)/shard_map/ppermute | solution.py:40
  45.1 5.9 %collective-permute-done.5 = bf16[576,384]{1,0:T(8,128)(2,1)S(1)} collective-permute-done((bf16[576,384]{1,0:T(8,128)(2,1)S(1)}, bf16[576,384]{1,0:T(8,128)(2,1)S(1)}, u32[]{:S(2)}, u32[]{:S(2)}) %collective-permute-start.5) | collective-permute-done | bytes 442400 | tf_op jit(solution)/shard_map/ppermute | solution.py:40
  51.1 8.8 %collective-permute-done.4 = bf16[576,384]{1,0:T(8,128)(2,1)S(1)} collective-permute-done((bf16[576,384]{1,0:T(8,128)(2,1)S(1)}, bf16[576,384]{1,0:T(8,128)(2,1)S(1)}, u32[]{:S(2)}, u32[]{:S(2)}) %collective-permute-start.4) | collective-permute-done | bytes 442400 | tf_op jit(solution)/shard_map/ppermute | solution.py:40
  63.8 3.3 %all-to-all-start.1 = ((bf16[32,4,192]{2,1,0:T(4,128)(2,1)}), bf16[32,4,192]{2,1,0:T(4,128)(2,1)}, u32[]{:S(2)}, u32[]{:S(2)}) async-start(bf16[32,4,192]{2,1,0:T(4,128)(2,1)} %broadcast_in_dim.9), calls=%async_computation.1 | async-start | bytes 131072 | tf_op jit(solution)/shard_map/all_to_all | solution.py:23
  67.1 1.5 %fusion.15 = f32[4,192,384]{2,1,0:T(8,128)} fusion(bf16[4,192,384]{2,1,0:T(8,128)(2,1)S(1)} %convolution_convert_fusion.1, bf16[1,1,4,384,384]{4,3,2,1,0:T(8,128)(2,1)S(1)} %copy-done.1), kind=kOutput, calls=%fused_computation.30 | convolution fusion | flops 226492416 | bytes 2949120 | tf_op jit(solution)/shard_map/fry,fyx->frx/dot_general | solution.py:48
  68.7 5.8 %all-to-all-done.1 = bf16[32,4,192]{2,1,0:T(4,128)(2,1)} async-done(((bf16[32,4,192]{2,1,0:T(4,128)(2,1)}), bf16[32,4,192]{2,1,0:T(4,128)(2,1)}, u32[]{:S(2)}, u32[]{:S(2)}) %all-to-all-start.1) | async-done | bytes 49184 | tf_op jit(solution)/shard_map/all_to_all | solution.py:23
  75.5 1.8 %convolution_bitcast_fusion = f32[4,192,384]{2,1,0:T(8,128)} fusion(f32[192,4,1]{0,1,2:T(4,128)S(1)} %convolution_bitcast_fusion.4, s32[4,384]{1,0:T(4,128)S(1)} %multiply_add_fusion, s32[4]{0:T(128)S(1)} %bitcast.113), kind=kOutput, calls=%fused_computation.14 | convolution fusion | flops 14161920 | bytes 1188880 | tf_op jit(solution)/shard_map/kfx,kr->frx/dot_general | solution.py:88
  77.3 2.9 %convolution_convert_fusion = bf16[4,192,384]{2,1,0:T(8,128)(2,1)S(1)} fusion(f32[4,192,384]{2,1,0:T(8,128)} %convolution_bitcast_fusion, f32[4,192,384]{2,1,0:T(8,128)} %fusion.15, bf16[1,1,4,384,384]{4,3,2,1,0:T(8,128)(2,1)S(1)} %copy-done.1, bf16[1,1,4,384,384]{4,3,2,1,0:T(8,128)(2,1)S(1)} %copy-done, f32[4]{0:T(128)} %multiply_bitcast_fusion), kind=kOutput, calls=%fused_computation.18 | convolution fusion | flops 454754304 | bytes 5308432 | tf_op jit(solution)/shard_map/fry,fyx->frx/dot_general | solution.py:48
  80.2 2.5 %collective-permute-start.8 = (bf16[1,192,384]{2,1,0:T(8,128)(2,1)S(1)}, bf16[1,192,384]{2,1,0:T(8,128)(2,1)S(1)}, u32[]{:S(2)}, u32[]{:S(2)}) collective-permute-start(bf16[1,192,384]{2,1,0:T(8,128)(2,1)S(1)} %get-tuple-element.9), channel_id=1, source_target_pairs={{0,2},{2,4},{4,6},{6,8},{8,10},{10,12},{12,14},{14,16},{16,18},{18... | collective-permute-start | bytes 442376 | tf_op jit(solution)/shard_map/ppermute | solution.py:12
  84.0 3.0 %collective-permute-start.10 = (bf16[1,192,384]{2,1,0:T(8,128)(2,1)S(1)}, bf16[1,192,384]{2,1,0:T(8,128)(2,1)S(1)}, u32[]{:S(2)}, u32[]{:S(2)}) collective-permute-start(bf16[1,192,384]{2,1,0:T(8,128)(2,1)S(1)} %get-tuple-element.11), channel_id=1, source_target_pairs={{0,1},{2,3},{4,5},{6,7},{8,9},{10,11},{12,13},{14,15},{16,17},{18,... | collective-permute-start | bytes 442376 | tf_op jit(solution)/shard_map/ppermute | solution.py:12
  87.1 1.4 %collective-permute-start.9 = (bf16[1,192,384]{2,1,0:T(8,128)(2,1)S(1)}, bf16[1,192,384]{2,1,0:T(8,128)(2,1)S(1)}, u32[]{:S(2)}, u32[]{:S(2)}) collective-permute-start(bf16[1,192,384]{2,1,0:T(8,128)(2,1)S(1)} %get-tuple-element.12), channel_id=1, source_target_pairs={{2,0},{4,2},{6,4},{8,6},{10,8},{12,10},{14,12},{16,14},{18,16},{20... | collective-permute-start | bytes 442376 | tf_op jit(solution)/shard_map/ppermute | solution.py:15
  88.6 5.7 %collective-permute-done.9 = bf16[1,192,384]{2,1,0:T(8,128)(2,1)S(1)} collective-permute-done((bf16[1,192,384]{2,1,0:T(8,128)(2,1)S(1)}, bf16[1,192,384]{2,1,0:T(8,128)(2,1)S(1)}, u32[]{:S(2)}, u32[]{:S(2)}) %collective-permute-start.9) | collective-permute-done | bytes 147488 | tf_op jit(solution)/shard_map/ppermute | solution.py:15
  96.7 12.1 %all_to_all.15 = f32[32,1,2,192]{3,2,1,0:T(2,128)S(1)} all-to-all(f32[32,1,2,192]{3,2,1,0:T(2,128)S(1)} %broadcast_in_dim.10), channel_id=1, replica_groups=mesh['gx'=16,'gy'=2] {'gx','gy'}, dimensions={0} | all-to-all | bytes 98304 | tf_op jit(solution)/shard_map/all_to_all | solution.py:23
  108.9 2.4 %fusion.33 = bf16[1,1,4,192,384]{4,3,2,1,0:T(8,128)(2,1)} fusion(bf16[4,192,384]{2,1,0:T(8,128)(2,1)S(1)} %convolution_convert_fusion, bf16[4,192,384]{2,1,0:T(8,128)(2,1)S(1)} %convolution_convert_fusion.2, f32[192]{0:T(256)S(1)} %bitcast.114, bf16[1,192,384]{2,1,0:T(8,128)(2,1)} %copy-done.19, bf16[1,192,384]{2,1,0:T(8,128)(2,1)} %copy-done.20, ...), kind=kLoop, calls=%fused_computation.52 | loop fusion | flops 6782976 | bytes 4129536 | tf_op jit(solution)/shard_map/broadcast_in_dim | solution.py:120
  (113 shorter events, 17.1 us)
Async XLA Ops:
  0.0 14.4 %copy-start = (bf16[1,1,4,384,384]{4,3,2,1,0:T(8,128)(2,1)S(1)}, bf16[1,1,4,384,384]{4,3,2,1,0:T(8,128)(2,1)}, u32[]{:S(2)}) copy-start(bf16[1,1,4,384,384]{4,3,2,1,0:T(8,128)(2,1)} %param.9) | copy-start | bytes 3538948
  0.0 12.0 %copy-start.2 = (bf16[1,1,4,384,384]{4,3,2,1,0:T(8,128)(2,1)S(1)}, bf16[1,1,4,384,384]{4,3,2,1,0:T(8,128)(2,1)}, u32[]{:S(2)}) copy-start(bf16[1,1,4,384,384]{4,3,2,1,0:T(8,128)(2,1)} %param.8) | copy-start | bytes 3538948
  1.3 12.1 %collective-permute-start = (bf16[1,192,384]{2,1,0:T(8,128)(2,1)S(1)}, bf16[1,192,384]{2,1,0:T(8,128)(2,1)S(1)}, u32[]{:S(2)}, u32[]{:S(2)}) collective-permute-start(bf16[1,192,384]{2,1,0:T(8,128)(2,1)S(1)} %get-tuple-element.17), channel_id=1, source_target_pairs={{0,2},{2,4},{4,6},{6,8},{8,10},{10,12},{12,14},{14,16},{16,18},{18... | collective-permute-start | bytes 442376 | tf_op jit(solution)/shard_map/ppermute | solution.py:12
  6.2 8.2 %collective-permute-start.1 = (bf16[1,192,384]{2,1,0:T(8,128)(2,1)S(1)}, bf16[1,192,384]{2,1,0:T(8,128)(2,1)S(1)}, u32[]{:S(2)}, u32[]{:S(2)}) collective-permute-start(bf16[1,192,384]{2,1,0:T(8,128)(2,1)S(1)} %get-tuple-element.18), channel_id=1, source_target_pairs={{2,0},{4,2},{6,4},{8,6},{10,8},{12,10},{14,12},{16,14},{18,16},{20... | collective-permute-start | bytes 442376 | tf_op jit(solution)/shard_map/ppermute | solution.py:15
  7.5 6.9 %collective-permute-start.3 = (bf16[1,192,384]{2,1,0:T(8,128)(2,1)S(1)}, bf16[1,192,384]{2,1,0:T(8,128)(2,1)S(1)}, u32[]{:S(2)}, u32[]{:S(2)}) collective-permute-start(bf16[1,192,384]{2,1,0:T(8,128)(2,1)S(1)} %get-tuple-element.19), channel_id=1, source_target_pairs={{1,0},{3,2},{5,4},{7,6},{9,8},{11,10},{13,12},{15,14},{17,16},{19,... | collective-permute-start | bytes 442376 | tf_op jit(solution)/shard_map/ppermute | solution.py:15
  8.8 5.6 %collective-permute-start.2 = (bf16[1,192,384]{2,1,0:T(8,128)(2,1)S(1)}, bf16[1,192,384]{2,1,0:T(8,128)(2,1)S(1)}, u32[]{:S(2)}, u32[]{:S(2)}) collective-permute-start(bf16[1,192,384]{2,1,0:T(8,128)(2,1)S(1)} %get-tuple-element.20), channel_id=1, source_target_pairs={{0,1},{2,3},{4,5},{6,7},{8,9},{10,11},{12,13},{14,15},{16,17},{18,... | collective-permute-start | bytes 442376 | tf_op jit(solution)/shard_map/ppermute | solution.py:12
  14.4 7.8 %copy-start.1 = (bf16[1,1,4,384,384]{4,3,2,1,0:T(8,128)(2,1)S(1)}, bf16[1,1,4,384,384]{4,3,2,1,0:T(8,128)(2,1)}, u32[]{:S(2)}) copy-start(bf16[1,1,4,384,384]{4,3,2,1,0:T(8,128)(2,1)} %param.10) | copy-start | bytes 3538948
  16.1 13.6 %all-to-all-start = ((bf16[32,4,192]{2,1,0:T(4,128)(2,1)}), bf16[32,4,192]{2,1,0:T(4,128)(2,1)S(1)}, u32[]{:S(2)}, u32[]{:S(2)}) async-start(bf16[32,4,192]{2,1,0:T(4,128)(2,1)} %broadcast_in_dim.8), calls=%async_computation | async-start | bytes 131072 | tf_op jit(solution)/shard_map/all_to_all | solution.py:23
  23.9 7.8 %copy-start.26 = (f32[4]{0:T(128)S(1)}, f32[4]{0:T(128)}, u32[]{:S(2)}) copy-start(f32[4]{0:T(128)} %multiply_bitcast_fusion) | copy-start | bytes 52
  34.7 10.5 %collective-permute-start.7 = (bf16[576,384]{1,0:T(8,128)(2,1)S(1)}, bf16[576,384]{1,0:T(8,128)(2,1)S(1)}, u32[]{:S(2)}, u32[]{:S(2)}) collective-permute-start(bf16[576,384]{1,0:T(8,128)(2,1)S(1)} %pad_maximum_fusion.9), channel_id=1, source_target_pairs={{1,0},{3,2},{5,4},{7,6},{9,8},{11,10},{13,12},{15,14},{17,16},{19,... | collective-permute-start | bytes 1327112 | tf_op jit(solution)/shard_map/ppermute | solution.py:40
  36.1 23.8 %copy-start.3 = (bf16[1,1,4,384,384]{4,3,2,1,0:T(8,128)(2,1)S(1)}, bf16[1,1,4,384,384]{4,3,2,1,0:T(8,128)(2,1)}, u32[]{:S(2)}) copy-start(bf16[1,1,4,384,384]{4,3,2,1,0:T(8,128)(2,1)} %param.8) | copy-start | bytes 3538948
  36.2 14.9 %collective-permute-start.5 = (bf16[576,384]{1,0:T(8,128)(2,1)S(1)}, bf16[576,384]{1,0:T(8,128)(2,1)S(1)}, u32[]{:S(2)}, u32[]{:S(2)}) collective-permute-start(bf16[576,384]{1,0:T(8,128)(2,1)S(1)} %pad_maximum_fusion.7), channel_id=1, source_target_pairs={{2,0},{4,2},{6,4},{8,6},{10,8},{12,10},{14,12},{16,14},{18,16},{20... | collective-permute-start | bytes 1327112 | tf_op jit(solution)/shard_map/ppermute | solution.py:40
  37.7 13.4 %collective-permute-start.6 = (bf16[576,384]{1,0:T(8,128)(2,1)S(1)}, bf16[576,384]{1,0:T(8,128)(2,1)S(1)}, u32[]{:S(2)}, u32[]{:S(2)}) collective-permute-start(bf16[576,384]{1,0:T(8,128)(2,1)S(1)} %pad_maximum_fusion.8), channel_id=1, source_target_pairs={{0,1},{2,3},{4,5},{6,7},{8,9},{10,11},{12,13},{14,15},{16,17},{18,... | collective-permute-start | bytes 1327112 | tf_op jit(solution)/shard_map/ppermute | solution.py:40
  40.8 19.0 %collective-permute-start.4 = (bf16[576,384]{1,0:T(8,128)(2,1)S(1)}, bf16[576,384]{1,0:T(8,128)(2,1)S(1)}, u32[]{:S(2)}, u32[]{:S(2)}) collective-permute-start(bf16[576,384]{1,0:T(8,128)(2,1)S(1)} %pad_maximum_fusion.6), channel_id=1, source_target_pairs={{0,2},{2,4},{4,6},{6,8},{8,10},{10,12},{12,14},{14,16},{16,18},{18... | collective-permute-start | bytes 1327112 | tf_op jit(solution)/shard_map/ppermute | solution.py:40
  45.1 15.3 %copy-start.7 = (bf16[576,384]{1,0:T(8,128)(2,1)}, bf16[576,384]{1,0:T(8,128)(2,1)S(1)}, u32[]{:S(2)}) copy-start(bf16[576,384]{1,0:T(8,128)(2,1)S(1)} %collective-permute-done.7) | copy-start | bytes 1327108
  51.0 9.4 %copy-start.9 = (bf16[576,384]{1,0:T(8,128)(2,1)}, bf16[576,384]{1,0:T(8,128)(2,1)S(1)}, u32[]{:S(2)}) copy-start(bf16[576,384]{1,0:T(8,128)(2,1)S(1)} %collective-permute-done.5) | copy-start | bytes 1327108
  51.1 9.4 %copy-start.11 = (bf16[576,384]{1,0:T(8,128)(2,1)}, bf16[576,384]{1,0:T(8,128)(2,1)S(1)}, u32[]{:S(2)}) copy-start(bf16[576,384]{1,0:T(8,128)(2,1)S(1)} %collective-permute-done.6) | copy-start | bytes 1327108
  63.8 10.7 %all-to-all-start.1 = ((bf16[32,4,192]{2,1,0:T(4,128)(2,1)}), bf16[32,4,192]{2,1,0:T(4,128)(2,1)}, u32[]{:S(2)}, u32[]{:S(2)}) async-start(bf16[32,4,192]{2,1,0:T(4,128)(2,1)} %broadcast_in_dim.9), calls=%async_computation.1 | async-start | bytes 131072 | tf_op jit(solution)/shard_map/all_to_all | solution.py:23
  80.1 14.1 %copy-start.6 = (f32[4,192,384]{2,1,0:T(8,128)S(1)}, f32[4,192,384]{2,1,0:T(8,128)}, u32[]{:S(2)}) copy-start(f32[4,192,384]{2,1,0:T(8,128)} %copy-done.5) | copy-start | bytes 3538948
  80.2 8.3 %collective-permute-start.8 = (bf16[1,192,384]{2,1,0:T(8,128)(2,1)S(1)}, bf16[1,192,384]{2,1,0:T(8,128)(2,1)S(1)}, u32[]{:S(2)}, u32[]{:S(2)}) collective-permute-start(bf16[1,192,384]{2,1,0:T(8,128)(2,1)S(1)} %get-tuple-element.9), channel_id=1, source_target_pairs={{0,2},{2,4},{4,6},{6,8},{8,10},{10,12},{12,14},{14,16},{16,18},{18... | collective-permute-start | bytes 442376 | tf_op jit(solution)/shard_map/ppermute | solution.py:12
  82.7 5.8 %collective-permute-start.11 = (bf16[1,192,384]{2,1,0:T(8,128)(2,1)S(1)}, bf16[1,192,384]{2,1,0:T(8,128)(2,1)S(1)}, u32[]{:S(2)}, u32[]{:S(2)}) collective-permute-start(bf16[1,192,384]{2,1,0:T(8,128)(2,1)S(1)} %get-tuple-element.10), channel_id=1, source_target_pairs={{1,0},{3,2},{5,4},{7,6},{9,8},{11,10},{13,12},{15,14},{17,16},{19,... | collective-permute-start | bytes 442376 | tf_op jit(solution)/shard_map/ppermute | solution.py:15
  84.0 4.5 %collective-permute-start.10 = (bf16[1,192,384]{2,1,0:T(8,128)(2,1)S(1)}, bf16[1,192,384]{2,1,0:T(8,128)(2,1)S(1)}, u32[]{:S(2)}, u32[]{:S(2)}) collective-permute-start(bf16[1,192,384]{2,1,0:T(8,128)(2,1)S(1)} %get-tuple-element.11), channel_id=1, source_target_pairs={{0,1},{2,3},{4,5},{6,7},{8,9},{10,11},{12,13},{14,15},{16,17},{18,... | collective-permute-start | bytes 442376 | tf_op jit(solution)/shard_map/ppermute | solution.py:12
  87.1 7.5 %copy-start.4 = (bf16[1,1,4,384,384]{4,3,2,1,0:T(8,128)(2,1)S(1)}, bf16[1,1,4,384,384]{4,3,2,1,0:T(8,128)(2,1)}, u32[]{:S(2)}) copy-start(bf16[1,1,4,384,384]{4,3,2,1,0:T(8,128)(2,1)} %param.8) | copy-start | bytes 3538948
  87.1 7.2 %collective-permute-start.9 = (bf16[1,192,384]{2,1,0:T(8,128)(2,1)S(1)}, bf16[1,192,384]{2,1,0:T(8,128)(2,1)S(1)}, u32[]{:S(2)}, u32[]{:S(2)}) collective-permute-start(bf16[1,192,384]{2,1,0:T(8,128)(2,1)S(1)} %get-tuple-element.12), channel_id=1, source_target_pairs={{2,0},{4,2},{6,4},{8,6},{10,8},{12,10},{14,12},{16,14},{18,16},{20... | collective-permute-start | bytes 442376 | tf_op jit(solution)/shard_map/ppermute | solution.py:15
  (26 other events, 67.3 us)

commit v6 on v5

--- a/solution.py
+++ b/solution.py
@@ -15,6 +15,12 @@
         high = lax.ppermute(lax.slice_in_dim(block, 0, width, axis=dim), axis, backward)
         block = jnp.concatenate([low, block, high], axis=dim)
     return block
+
+
+def gather_blocks(block, axes):
+    count = lax.axis_size(axes)
+    spread = jnp.broadcast_to(block[None], (count,) + block.shape)
+    return lax.all_to_all(spread, axes, 0, 0, tiled=False)
 
 
 def gather_rows(block, axes):
@@ -73,9 +79,6 @@
     picks_full = picks.astype(jnp.float32)
     flags_full = flag_values.astype(jnp.float32)
 
-    def add_coarse(piece):
-        return jnp.dot(coarse_inverse, piece.astype(jnp.float32), precision=lax.Precision.HIGHEST)
-
     def precondition(resid, schur_partner):
         scaled = face_mul_turned(resid.astype(jnp.bfloat16), deluxe_panel).astype(jnp.bfloat16)
         local_part = face_mul(scaled, inverse_panel)
@@ -84,8 +87,14 @@
         primal = jnp.einsum(
             "kfx,frx->kr", picks_half, scaled, preferred_element_type=jnp.float32
         ).astype(jnp.bfloat16)
-        coarse = add_coarse(gather_rows(primal, ("gx", "gy")))
-        placed = jnp.einsum("kfx,kr->frx", picks_full, coarse, precision=lax.Precision.HIGHEST)
+        gathered = gather_blocks(primal, ("gx", "gy")).astype(jnp.float32)
+        coarse = jnp.einsum(
+            "ijk,jkr->ir",
+            coarse_inverse.reshape(primal_count, gathered.shape[0], gathered.shape[1]),
+            gathered,
+            precision=lax.Precision.HIGHEST,
+        )
+        placed = jnp.sum(picks_full[:, :, None, :] * coarse[:, None, :, None], axis=0)
         weighted = (softened + placed).astype(jnp.bfloat16)
         spread = face_mul(weighted, deluxe_panel).astype(jnp.bfloat16)
         if schur_partner is not None:

time: 112 us -> 121 us (1.080)
  other arithmetic: 3.5 us -> 8.96 us
  starting transfers between devices: 38.5 us -> 41.1 us
    reduce_sum x0 -> x2, other arithmetic: none -> 4.6 us  [precondition(): jnp.sum(picks_full[:, :, None, :] * coarse[:, None, :, None], axis=0)]
    ppermute x4, starting transfers between devices: 13.5 us -> 15.3 us  [with_halo(): lax.ppermute(lax.slice_in_dim(block, block.shape[dim] - width, None, axis...]
    dot_general x4 -> x2, matrix products: 3.76 us -> 2.05 us  [precondition(): jnp.einsum('ijk,jkr->ir', coarse_inverse.reshape(primal_count, gathered.s...]
    broadcast_in_dim x3 -> x1, local copies, waits for them, and re-layouts: 1.35 us -> 0.02 us  [gather_rows(): spread = jnp.broadcast_to(block[None], (count,) + block.shape)]
    broadcast_in_dim x0 -> x2, local copies, waits for them, and re-layouts: none -> 1.32 us  [gather_blocks(): spread = jnp.broadcast_to(block[None], (count,) + block.shape)]
    dot_general x2, matrix products: 1.23 us -> 2.46 us  [face_mul_turned(): jnp.einsum('fry,fxy->frx', vectors, matrices, preferred_element_type=jnp....]
    unnamed x72 -> x54, local copies, waits for them, and re-layouts: 2.18 us -> 2.81 us
  transfers between devices with their start and end apart: 14 -> 14, of which waited for: 6 -> 5; matrix products, arithmetic and copies ran while one was open for 4% -> 5% of each run, Pallas kernels for 0% -> 0%
where the time goes in v6:
time: 121 us; the launch traced here: 120 us
  starting transfers between devices  41.1 us (34%)
  waiting for transfers between devices  32.1 us (27%)
  matrix products  17.5 us (14%)
  blocking collectives  12.2 us (10%)
  other arithmetic  8.96 us (7%)
  local copies, waits for them, and re-layouts  8.03 us (7%)
    ppermute x4, starting transfers between devices, with_halo(): lax.ppermute(lax.slice_in_dim(block, block.shape[dim] - width, None, axis...  15.3 us
    ppermute x4, waiting for transfers between devices, from_partner(): return lax.ppermute(values, axis, pairs)  14.7 us
    dot_general x8, matrix products, face_mul(): jnp.einsum('fry,fyx->frx', vectors, matrices, preferred_element_type=jnp....  12.4 us
    all_to_all x1, blocking collectives, gather_rows(): swapped = lax.all_to_all(spread, axes, 0, 0, tiled=False)  12.2 us
    all_to_all x2, waiting for transfers between devices, gather_blocks(): return lax.all_to_all(spread, axes, 0, 0, tiled=False)  11.7 us
    all_to_all x2, starting transfers between devices, gather_blocks(): return lax.all_to_all(spread, axes, 0, 0, tiled=False)  10.4 us
    ppermute x4, starting transfers between devices, from_partner(): return lax.ppermute(values, axis, pairs)  10.1 us
    ppermute x4, waiting for transfers between devices, with_halo(): lax.ppermute(lax.slice_in_dim(block, 0, width, axis=dim), axis, backward)  5.7 us
  transfers between devices with their start and end apart: 14, of which 5 were waited for; matrix products, arithmetic and copies ran while one was open for 5% of the time, Pallas kernels for 0%

profile of v6, /device:TPU:0, one launch (start us, length us, event | category | flops | bytes accessed | tf_op | source)
XLA Modules:
  0.0 120.4 jit_solution(13644736902926494947)
XLA Ops:
  0.0 2.0 %slice_bitcast_fusion.11 = (bf16[1,192,384]{2,1,0:T(8,128)(2,1)}, bf16[1,192,384]{2,1,0:T(8,128)(2,1)S(1)}, bf16[1,192,384]{2,1,0:T(8,128)(2,1)S(1)}, bf16[1,192,384]{2,1,0:T(8,128)(2,1)S(1)}) fusion(bf16[1,1,4,192,384]{4,3,2,1,0:T(8,128)(2,1)} %param.7), kind=kLoop, calls=%fused_computation.77 | loop fusion | bytes 1179648 | tf_op jit(solution)/shard_map/slice | solution.py:13
  2.0 5.5 %collective-permute-start = (bf16[1,192,384]{2,1,0:T(8,128)(2,1)}, bf16[1,192,384]{2,1,0:T(8,128)(2,1)}, u32[]{:S(2)}, u32[]{:S(2)}) collective-permute-start(bf16[1,192,384]{2,1,0:T(8,128)(2,1)} %get-tuple-element.17), channel_id=1, source_target_pairs={{0,2},{2,4},{4,6},{6,8},{8,10},{10,12},{12,14},{14,16},{16,18},{18... | collective-permute-start | bytes 442376 | tf_op jit(solution)/shard_map/ppermute | solution.py:12
  10.1 4.3 %collective-permute-start.2 = (bf16[1,192,384]{2,1,0:T(8,128)(2,1)S(1)}, bf16[1,192,384]{2,1,0:T(8,128)(2,1)}, u32[]{:S(2)}, u32[]{:S(2)}) collective-permute-start(bf16[1,192,384]{2,1,0:T(8,128)(2,1)S(1)} %get-tuple-element.20), channel_id=1, source_target_pairs={{0,1},{2,3},{4,5},{6,7},{8,9},{10,11},{12,13},{14,15},{16,17},{18,... | collective-permute-start | bytes 442376 | tf_op jit(solution)/shard_map/ppermute | solution.py:12
  16.9 1.8 %convolution_convert_fusion.3 = bf16[4,192,384]{2,1,0:T(8,128)(2,1)S(1)} fusion(bf16[1,1,4,384,384]{4,3,2,1,0:T(8,128)(2,1)S(1)} %copy-done, bf16[1,1,4,192,384]{4,3,2,1,0:T(8,128)(2,1)S(1)} %copy-done.19, bf16[1,192,384]{2,1,0:T(8,128)(2,1)} %collective-permute-done.3, bf16[1,192,384]{2,1,0:T(8,128)(2,1)} %collective-permute-done.2, ...), kind=kOutput, calls=%fused_computation.21 | convolution fusion | flops 228851712 | bytes 2949120 | tf_op jit(solution)/shard_map/fry,fxy->frx/dot_general | solution.py:58
  19.7 7.1 %all-to-all-start = ((bf16[32,4,192]{2,1,0:T(4,128)(2,1)}), bf16[32,4,192]{2,1,0:T(4,128)(2,1)}, u32[]{:S(2)}, u32[]{:S(2)}) async-start(bf16[32,4,192]{2,1,0:T(4,128)(2,1)} %broadcast_in_dim.8), calls=%async_computation | async-start | bytes 131072 | tf_op jit(solution)/shard_map/all_to_all | solution.py:23
  26.9 1.5 %fusion.19 = f32[4,192,384]{2,1,0:T(8,128)} fusion(bf16[4,192,384]{2,1,0:T(8,128)(2,1)S(1)} %convolution_convert_fusion.3, bf16[1,1,4,384,384]{4,3,2,1,0:T(8,128)(2,1)S(1)} %copy-done.1), kind=kOutput, calls=%fused_computation.33 | convolution fusion | flops 226492416 | bytes 2949120 | tf_op jit(solution)/shard_map/fry,fyx->frx/dot_general | solution.py:54
  28.4 5.8 %all-to-all-done = bf16[32,4,192]{2,1,0:T(4,128)(2,1)} async-done(((bf16[32,4,192]{2,1,0:T(4,128)(2,1)}), bf16[32,4,192]{2,1,0:T(4,128)(2,1)}, u32[]{:S(2)}, u32[]{:S(2)}) %all-to-all-start) | async-done | bytes 49184 | tf_op jit(solution)/shard_map/all_to_all | solution.py:23
  35.3 2.3 %multiply_reduce_fusion.1 = f32[4,192,384]{2,1,0:T(8,128)} fusion(f32[4,192]{1,0:T(4,128)S(1)} %convolution_bitcast_fusion.3, f32[4,4,384]{2,1,0:T(4,128)} %copy.11), kind=kLoop, calls=%fused_computation.1 | loop fusion | flops 2064384 | bytes 1207296 | tf_op jit(solution)/shard_map/reduce_sum | solution.py:97
  37.6 2.9 %convolution_convert_fusion.2 = bf16[4,192,384]{2,1,0:T(8,128)(2,1)S(1)} fusion(f32[4,192,384]{2,1,0:T(8,128)} %multiply_reduce_fusion.1, f32[4,192,384]{2,1,0:T(8,128)} %fusion.19, bf16[1,1,4,384,384]{4,3,2,1,0:T(8,128)(2,1)S(1)} %copy-done.1, bf16[1,1,4,384,384]{4,3,2,1,0:T(8,128)(2,1)S(1)} %copy-done, f32[4]{0:T(128)} %multiply_bitcast_fusion), kind=kOutput, calls=%fused_computation.20 | convolution fusion | flops 454754304 | bytes 5308432 | tf_op jit(solution)/shard_map/fry,fyx->frx/dot_general | solution.py:54
  44.4 3.1 %collective-permute-start.6 = (bf16[576,384]{1,0:T(8,128)(2,1)S(1)}, bf16[576,384]{1,0:T(8,128)(2,1)S(1)}, u32[]{:S(2)}, u32[]{:S(2)}) collective-permute-start(bf16[576,384]{1,0:T(8,128)(2,1)S(1)} %pad_maximum_fusion.8), channel_id=1, source_target_pairs={{0,1},{2,3},{4,5},{6,7},{8,9},{10,11},{12,13},{14,15},{16,17},{18,... | collective-permute-start | bytes 1327112 | tf_op jit(solution)/shard_map/ppermute | solution.py:46
  47.5 4.3 %collective-permute-start.4 = (bf16[576,384]{1,0:T(8,128)(2,1)S(1)}, bf16[576,384]{1,0:T(8,128)(2,1)S(1)}, u32[]{:S(2)}, u32[]{:S(2)}) collective-permute-start(bf16[576,384]{1,0:T(8,128)(2,1)S(1)} %pad_maximum_fusion.6), channel_id=1, source_target_pairs={{0,2},{2,4},{4,6},{6,8},{8,10},{10,12},{12,14},{14,16},{16,18},{18... | collective-permute-start | bytes 1327112 | tf_op jit(solution)/shard_map/ppermute | solution.py:46
  51.8 5.9 %collective-permute-done.5 = bf16[576,384]{1,0:T(8,128)(2,1)S(1)} collective-permute-done((bf16[576,384]{1,0:T(8,128)(2,1)S(1)}, bf16[576,384]{1,0:T(8,128)(2,1)S(1)}, u32[]{:S(2)}, u32[]{:S(2)}) %collective-permute-start.5) | collective-permute-done | bytes 442400 | tf_op jit(solution)/shard_map/ppermute | solution.py:46
  57.8 8.8 %collective-permute-done.4 = bf16[576,384]{1,0:T(8,128)(2,1)S(1)} collective-permute-done((bf16[576,384]{1,0:T(8,128)(2,1)S(1)}, bf16[576,384]{1,0:T(8,128)(2,1)S(1)}, u32[]{:S(2)}, u32[]{:S(2)}) %collective-permute-start.4) | collective-permute-done | bytes 442400 | tf_op jit(solution)/shard_map/ppermute | solution.py:46
  67.8 1.7 %fusion.5 = f32[4,192,384]{2,1,0:T(8,128)S(1)} fusion(f32[4,192,384]{2,1,0:T(8,128)S(1)} %convolution_reduce-precision_fusion.3, bf16[1,1,4,192,384]{4,3,2,1,0:T(8,128)(2,1)S(1)} %copy-done.20, bf16[4,192,384]{2,1,0:T(8,128)(2,1)S(1)} %convolution_convert_fusion.2, bf16[1,192,384]{2,1,0:T(8,128)(2,1)} %collective-permute-done.3, ...), kind=kOutput, calls=%fused_computation.11 | convolution fusion | flops 238288896 | bytes 5898240 | tf_op jit(solution)/shard_map/fry,fyx->frx/dot_general | solution.py:54
  71.5 3.3 %all-to-all-start.1 = ((bf16[32,4,192]{2,1,0:T(4,128)(2,1)}), bf16[32,4,192]{2,1,0:T(4,128)(2,1)}, u32[]{:S(2)}, u32[]{:S(2)}) async-start(bf16[32,4,192]{2,1,0:T(4,128)(2,1)} %broadcast_in_dim.9), calls=%async_computation.1 | async-start | bytes 131072 | tf_op jit(solution)/shard_map/all_to_all | solution.py:23
  74.8 1.6 %fusion.15 = f32[4,192,384]{2,1,0:T(8,128)} fusion(bf16[4,192,384]{2,1,0:T(8,128)(2,1)S(1)} %convolution_convert_fusion.1, bf16[1,1,4,384,384]{4,3,2,1,0:T(8,128)(2,1)S(1)} %copy-done.1), kind=kOutput, calls=%fused_computation.30 | convolution fusion | flops 226492416 | bytes 2949120 | tf_op jit(solution)/shard_map/fry,fyx->frx/dot_general | solution.py:54
  76.3 5.8 %all-to-all-done.1 = bf16[32,4,192]{2,1,0:T(4,128)(2,1)} async-done(((bf16[32,4,192]{2,1,0:T(4,128)(2,1)}), bf16[32,4,192]{2,1,0:T(4,128)(2,1)}, u32[]{:S(2)}, u32[]{:S(2)}) %all-to-all-start.1) | async-done | bytes 49184 | tf_op jit(solution)/shard_map/all_to_all | solution.py:23
  83.2 2.3 %multiply_reduce_fusion = f32[4,192,384]{2,1,0:T(8,128)} fusion(f32[4,192]{1,0:T(4,128)S(1)} %convolution_bitcast_fusion.2, f32[4,4,384]{2,1,0:T(4,128)} %copy.11), kind=kLoop, calls=%fused_computation | loop fusion | flops 2064384 | bytes 1207296 | tf_op jit(solution)/shard_map/reduce_sum | solution.py:97
  85.5 2.9 %convolution_convert_fusion = bf16[4,192,384]{2,1,0:T(8,128)(2,1)S(1)} fusion(f32[4,192,384]{2,1,0:T(8,128)} %multiply_reduce_fusion, f32[4,192,384]{2,1,0:T(8,128)} %fusion.15, bf16[1,1,4,384,384]{4,3,2,1,0:T(8,128)(2,1)S(1)} %copy-done.1, bf16[1,1,4,384,384]{4,3,2,1,0:T(8,128)(2,1)S(1)} %copy-done, f32[4]{0:T(128)S(1)} %copy-done.24), kind=kOutput, calls=%fused_computation.18 | convolution fusion | flops 454754304 | bytes 5308432 | tf_op jit(solution)/shard_map/fry,fyx->frx/dot_general | solution.py:54
  88.4 2.5 %collective-permute-start.8 = (bf16[1,192,384]{2,1,0:T(8,128)(2,1)S(1)}, bf16[1,192,384]{2,1,0:T(8,128)(2,1)S(1)}, u32[]{:S(2)}, u32[]{:S(2)}) collective-permute-start(bf16[1,192,384]{2,1,0:T(8,128)(2,1)S(1)} %get-tuple-element.9), channel_id=1, source_target_pairs={{0,2},{2,4},{4,6},{6,8},{8,10},{10,12},{12,14},{14,16},{16,18},{18... | collective-permute-start | bytes 442376 | tf_op jit(solution)/shard_map/ppermute | solution.py:12
  92.2 3.0 %collective-permute-start.10 = (bf16[1,192,384]{2,1,0:T(8,128)(2,1)S(1)}, bf16[1,192,384]{2,1,0:T(8,128)(2,1)S(1)}, u32[]{:S(2)}, u32[]{:S(2)}) collective-permute-start(bf16[1,192,384]{2,1,0:T(8,128)(2,1)S(1)} %get-tuple-element.11), channel_id=1, source_target_pairs={{0,1},{2,3},{4,5},{6,7},{8,9},{10,11},{12,13},{14,15},{16,17},{18,... | collective-permute-start | bytes 442376 | tf_op jit(solution)/shard_map/ppermute | solution.py:12
  96.8 5.7 %collective-permute-done.9 = bf16[1,192,384]{2,1,0:T(8,128)(2,1)S(1)} collective-permute-done((bf16[1,192,384]{2,1,0:T(8,128)(2,1)S(1)}, bf16[1,192,384]{2,1,0:T(8,128)(2,1)S(1)}, u32[]{:S(2)}, u32[]{:S(2)}) %collective-permute-start.9) | collective-permute-done | bytes 147488 | tf_op jit(solution)/shard_map/ppermute | solution.py:15
  104.9 12.2 %all_to_all.15 = f32[32,1,2,192]{3,2,1,0:T(2,128)} all-to-all(f32[32,1,2,192]{3,2,1,0:T(2,128)S(1)} %broadcast_in_dim.10), channel_id=1, replica_groups=mesh['gx'=16,'gy'=2] {'gx','gy'}, dimensions={0} | all-to-all | bytes 98304 | tf_op jit(solution)/shard_map/all_to_all | solution.py:29
  118.1 2.3 %fusion.33 = bf16[1,1,4,192,384]{4,3,2,1,0:T(8,128)(2,1)} fusion(bf16[4,192,384]{2,1,0:T(8,128)(2,1)S(1)} %convolution_convert_fusion, bf16[4,192,384]{2,1,0:T(8,128)(2,1)S(1)} %convolution_convert_fusion.2, f32[192]{0:T(256)S(1)} %bitcast.109, bf16[1,192,384]{2,1,0:T(8,128)(2,1)S(1)} %collective-permute-done.11, bf16[1,192,384]{2,1,0:T(8,128)(2,1)} %copy-done.17, ...), kind=kLoop, calls=%fused_computation.52 | loop fusion | flops 6782976 | bytes 4129536 | tf_op jit(solution)/shard_map/broadcast_in_dim | solution.py:129
  (97 shorter events, 21.1 us)
Async XLA Ops:
  0.0 16.9 %copy-start = (bf16[1,1,4,384,384]{4,3,2,1,0:T(8,128)(2,1)S(1)}, bf16[1,1,4,384,384]{4,3,2,1,0:T(8,128)(2,1)}, u32[]{:S(2)}) copy-start(bf16[1,1,4,384,384]{4,3,2,1,0:T(8,128)(2,1)} %param.9) | copy-start | bytes 3538948
  0.0 14.4 %copy-start.21 = (s32[1,1,4]{2,1,0:T(1,128)S(1)}, s32[1,1,4]{2,1,0:T(1,128)}, u32[]{:S(2)}) copy-start(s32[1,1,4]{2,1,0:T(1,128)} %param.12) | copy-start | bytes 52
  0.0 15.1 %copy-start.25 = (f32[4,128]{1,0:T(4,128)S(1)}, f32[4,128]{1,0:T(4,128)}, u32[]{:S(2)}) copy-start(f32[4,128]{1,0:T(4,128)} %param.11) | copy-start | bytes 6148
  0.0 15.3 %copy-start.2 = (bf16[1,1,4,384,384]{4,3,2,1,0:T(8,128)(2,1)S(1)}, bf16[1,1,4,384,384]{4,3,2,1,0:T(8,128)(2,1)}, u32[]{:S(2)}) copy-start(bf16[1,1,4,384,384]{4,3,2,1,0:T(8,128)(2,1)} %param.8) | copy-start | bytes 3538948
  2.0 14.9 %collective-permute-start = (bf16[1,192,384]{2,1,0:T(8,128)(2,1)}, bf16[1,192,384]{2,1,0:T(8,128)(2,1)}, u32[]{:S(2)}, u32[]{:S(2)}) collective-permute-start(bf16[1,192,384]{2,1,0:T(8,128)(2,1)} %get-tuple-element.17), channel_id=1, source_target_pairs={{0,2},{2,4},{4,6},{6,8},{8,10},{10,12},{12,14},{14,16},{16,18},{18... | collective-permute-start | bytes 442376 | tf_op jit(solution)/shard_map/ppermute | solution.py:12
  7.5 9.4 %collective-permute-start.1 = (bf16[1,192,384]{2,1,0:T(8,128)(2,1)S(1)}, bf16[1,192,384]{2,1,0:T(8,128)(2,1)}, u32[]{:S(2)}, u32[]{:S(2)}) collective-permute-start(bf16[1,192,384]{2,1,0:T(8,128)(2,1)S(1)} %get-tuple-element.18), channel_id=1, source_target_pairs={{2,0},{4,2},{6,4},{8,6},{10,8},{12,10},{14,12},{16,14},{18,16},{20... | collective-permute-start | bytes 442376 | tf_op jit(solution)/shard_map/ppermute | solution.py:15
  8.8 8.1 %collective-permute-start.3 = (bf16[1,192,384]{2,1,0:T(8,128)(2,1)S(1)}, bf16[1,192,384]{2,1,0:T(8,128)(2,1)}, u32[]{:S(2)}, u32[]{:S(2)}) collective-permute-start(bf16[1,192,384]{2,1,0:T(8,128)(2,1)S(1)} %get-tuple-element.19), channel_id=1, source_target_pairs={{1,0},{3,2},{5,4},{7,6},{9,8},{11,10},{13,12},{15,14},{17,16},{19,... | collective-permute-start | bytes 442376 | tf_op jit(solution)/shard_map/ppermute | solution.py:15
  10.1 6.8 %collective-permute-start.2 = (bf16[1,192,384]{2,1,0:T(8,128)(2,1)S(1)}, bf16[1,192,384]{2,1,0:T(8,128)(2,1)}, u32[]{:S(2)}, u32[]{:S(2)}) collective-permute-start(bf16[1,192,384]{2,1,0:T(8,128)(2,1)S(1)} %get-tuple-element.20), channel_id=1, source_target_pairs={{0,1},{2,3},{4,5},{6,7},{8,9},{10,11},{12,13},{14,15},{16,17},{18,... | collective-permute-start | bytes 442376 | tf_op jit(solution)/shard_map/ppermute | solution.py:12
  16.9 10.0 %copy-start.1 = (bf16[1,1,4,384,384]{4,3,2,1,0:T(8,128)(2,1)S(1)}, bf16[1,1,4,384,384]{4,3,2,1,0:T(8,128)(2,1)}, u32[]{:S(2)}) copy-start(bf16[1,1,4,384,384]{4,3,2,1,0:T(8,128)(2,1)} %param.10) | copy-start | bytes 3538948
  19.7 14.5 %all-to-all-start = ((bf16[32,4,192]{2,1,0:T(4,128)(2,1)}), bf16[32,4,192]{2,1,0:T(4,128)(2,1)}, u32[]{:S(2)}, u32[]{:S(2)}) async-start(bf16[32,4,192]{2,1,0:T(4,128)(2,1)} %broadcast_in_dim.8), calls=%async_computation | async-start | bytes 131072 | tf_op jit(solution)/shard_map/all_to_all | solution.py:23
  41.5 10.3 %collective-permute-start.7 = (bf16[576,384]{1,0:T(8,128)(2,1)S(1)}, bf16[576,384]{1,0:T(8,128)(2,1)S(1)}, u32[]{:S(2)}, u32[]{:S(2)}) collective-permute-start(bf16[576,384]{1,0:T(8,128)(2,1)S(1)} %pad_maximum_fusion.9), channel_id=1, source_target_pairs={{1,0},{3,2},{5,4},{7,6},{9,8},{11,10},{13,12},{15,14},{17,16},{19,... | collective-permute-start | bytes 1327112 | tf_op jit(solution)/shard_map/ppermute | solution.py:46
  42.8 23.8 %copy-start.3 = (bf16[1,1,4,384,384]{4,3,2,1,0:T(8,128)(2,1)S(1)}, bf16[1,1,4,384,384]{4,3,2,1,0:T(8,128)(2,1)}, u32[]{:S(2)}) copy-start(bf16[1,1,4,384,384]{4,3,2,1,0:T(8,128)(2,1)} %param.8) | copy-start | bytes 3538948
  42.9 14.9 %collective-permute-start.5 = (bf16[576,384]{1,0:T(8,128)(2,1)S(1)}, bf16[576,384]{1,0:T(8,128)(2,1)S(1)}, u32[]{:S(2)}, u32[]{:S(2)}) collective-permute-start(bf16[576,384]{1,0:T(8,128)(2,1)S(1)} %pad_maximum_fusion.7), channel_id=1, source_target_pairs={{2,0},{4,2},{6,4},{8,6},{10,8},{12,10},{14,12},{16,14},{18,16},{20... | collective-permute-start | bytes 1327112 | tf_op jit(solution)/shard_map/ppermute | solution.py:46
  44.4 13.4 %collective-permute-start.6 = (bf16[576,384]{1,0:T(8,128)(2,1)S(1)}, bf16[576,384]{1,0:T(8,128)(2,1)S(1)}, u32[]{:S(2)}, u32[]{:S(2)}) collective-permute-start(bf16[576,384]{1,0:T(8,128)(2,1)S(1)} %pad_maximum_fusion.8), channel_id=1, source_target_pairs={{0,1},{2,3},{4,5},{6,7},{8,9},{10,11},{12,13},{14,15},{16,17},{18,... | collective-permute-start | bytes 1327112 | tf_op jit(solution)/shard_map/ppermute | solution.py:46
  47.5 19.1 %collective-permute-start.4 = (bf16[576,384]{1,0:T(8,128)(2,1)S(1)}, bf16[576,384]{1,0:T(8,128)(2,1)S(1)}, u32[]{:S(2)}, u32[]{:S(2)}) collective-permute-start(bf16[576,384]{1,0:T(8,128)(2,1)S(1)} %pad_maximum_fusion.6), channel_id=1, source_target_pairs={{0,2},{2,4},{4,6},{6,8},{8,10},{10,12},{12,14},{14,16},{16,18},{18... | collective-permute-start | bytes 1327112 | tf_op jit(solution)/shard_map/ppermute | solution.py:46
  51.8 15.3 %copy-start.7 = (bf16[576,384]{1,0:T(8,128)(2,1)}, bf16[576,384]{1,0:T(8,128)(2,1)S(1)}, u32[]{:S(2)}) copy-start(bf16[576,384]{1,0:T(8,128)(2,1)S(1)} %collective-permute-done.7) | copy-start | bytes 1327108
  57.8 9.4 %copy-start.9 = (bf16[576,384]{1,0:T(8,128)(2,1)}, bf16[576,384]{1,0:T(8,128)(2,1)S(1)}, u32[]{:S(2)}) copy-start(bf16[576,384]{1,0:T(8,128)(2,1)S(1)} %collective-permute-done.5) | copy-start | bytes 1327108
  57.8 9.4 %copy-start.11 = (bf16[576,384]{1,0:T(8,128)(2,1)}, bf16[576,384]{1,0:T(8,128)(2,1)S(1)}, u32[]{:S(2)}) copy-start(bf16[576,384]{1,0:T(8,128)(2,1)S(1)} %collective-permute-done.6) | copy-start | bytes 1327108
  71.5 10.7 %all-to-all-start.1 = ((bf16[32,4,192]{2,1,0:T(4,128)(2,1)}), bf16[32,4,192]{2,1,0:T(4,128)(2,1)}, u32[]{:S(2)}, u32[]{:S(2)}) async-start(bf16[32,4,192]{2,1,0:T(4,128)(2,1)} %broadcast_in_dim.9), calls=%async_computation.1 | async-start | bytes 131072 | tf_op jit(solution)/shard_map/all_to_all | solution.py:23
  88.4 14.1 %copy-start.6 = (f32[4,192,384]{2,1,0:T(8,128)S(1)}, f32[4,192,384]{2,1,0:T(8,128)}, u32[]{:S(2)}) copy-start(f32[4,192,384]{2,1,0:T(8,128)} %copy-done.5) | copy-start | bytes 3538948
  88.4 8.3 %collective-permute-start.8 = (bf16[1,192,384]{2,1,0:T(8,128)(2,1)S(1)}, bf16[1,192,384]{2,1,0:T(8,128)(2,1)S(1)}, u32[]{:S(2)}, u32[]{:S(2)}) collective-permute-start(bf16[1,192,384]{2,1,0:T(8,128)(2,1)S(1)} %get-tuple-element.9), channel_id=1, source_target_pairs={{0,2},{2,4},{4,6},{6,8},{8,10},{10,12},{12,14},{14,16},{16,18},{18... | collective-permute-start | bytes 442376 | tf_op jit(solution)/shard_map/ppermute | solution.py:12
  90.9 5.8 %collective-permute-start.11 = (bf16[1,192,384]{2,1,0:T(8,128)(2,1)S(1)}, bf16[1,192,384]{2,1,0:T(8,128)(2,1)S(1)}, u32[]{:S(2)}, u32[]{:S(2)}) collective-permute-start(bf16[1,192,384]{2,1,0:T(8,128)(2,1)S(1)} %get-tuple-element.10), channel_id=1, source_target_pairs={{1,0},{3,2},{5,4},{7,6},{9,8},{11,10},{13,12},{15,14},{17,16},{19,... | collective-permute-start | bytes 442376 | tf_op jit(solution)/shard_map/ppermute | solution.py:15
  92.2 4.5 %collective-permute-start.10 = (bf16[1,192,384]{2,1,0:T(8,128)(2,1)S(1)}, bf16[1,192,384]{2,1,0:T(8,128)(2,1)S(1)}, u32[]{:S(2)}, u32[]{:S(2)}) collective-permute-start(bf16[1,192,384]{2,1,0:T(8,128)(2,1)S(1)} %get-tuple-element.11), channel_id=1, source_target_pairs={{0,1},{2,3},{4,5},{6,7},{8,9},{10,11},{12,13},{14,15},{16,17},{18,... | collective-permute-start | bytes 442376 | tf_op jit(solution)/shard_map/ppermute | solution.py:12
  95.3 7.2 %collective-permute-start.9 = (bf16[1,192,384]{2,1,0:T(8,128)(2,1)S(1)}, bf16[1,192,384]{2,1,0:T(8,128)(2,1)S(1)}, u32[]{:S(2)}, u32[]{:S(2)}) collective-permute-start(bf16[1,192,384]{2,1,0:T(8,128)(2,1)S(1)} %get-tuple-element.12), channel_id=1, source_target_pairs={{2,0},{4,2},{6,4},{8,6},{10,8},{12,10},{14,12},{16,14},{18,16},{20... | collective-permute-start | bytes 442376 | tf_op jit(solution)/shard_map/ppermute | solution.py:15
  (17 other events, 40.6 us)

commit v7 on v3

--- a/solution.py
+++ b/solution.py
@@ -76,7 +76,7 @@
     def add_coarse(piece):
         return jnp.dot(coarse_inverse, piece.astype(jnp.float32), precision=lax.Precision.HIGHEST)
 
-    def precondition(resid):
+    def precondition(resid, carried):
         scaled = face_mul_turned(resid.astype(jnp.bfloat16), deluxe_panel).astype(jnp.bfloat16)
         local_part = face_mul(scaled, inverse_panel)
         extra = face_mul(local_part.astype(jnp.bfloat16), inverse_panel)
@@ -84,15 +84,13 @@
         primal = jnp.einsum(
             "kfx,frx->kr", picks_half, scaled, preferred_element_type=jnp.float32
         ).astype(jnp.bfloat16)
+        if carried is not None:
+            carried, primal = lax.optimization_barrier((carried, primal))
         coarse = add_coarse(gather_rows(primal, ("gx", "gy")))
         placed = jnp.einsum("kfx,kr->frx", picks_full, coarse, precision=lax.Precision.HIGHEST)
         weighted = (softened + placed).astype(jnp.bfloat16)
         spread = face_mul(weighted, deluxe_panel).astype(jnp.bfloat16)
-        return spread.astype(jnp.float32) + face_pairs(spread).astype(jnp.float32)
-
-    schur_partner = jnp.stack(
-        [from_partner(schur_panel[face], axis, from_lower) for axis, from_lower, face in PARTNERS]
-    )
+        return spread.astype(jnp.float32) + face_pairs(spread).astype(jnp.float32), carried
 
     def apply_operator(field):
         field_half = field.astype(jnp.bfloat16)
@@ -100,10 +98,22 @@
         bent_partner = to_half(face_mul(field_half, schur_partner))
         return bent_own + bent_partner
 
-    resid0 = loads_here.astype(jnp.float32) + face_pairs(loads_here).astype(jnp.float32)
-    first = precondition(resid0)
+    rows = loads_here.shape[1]
+    halo = []
+    for axis, from_lower, face in PARTNERS:
+        payload = loads_here[face]
+        if axis == "gy":
+            payload = jnp.concatenate([payload, schur_panel[face]])
+        halo.append(from_partner(payload, axis, from_lower))
+    load_partner = jnp.stack([received[:rows] for received in halo])
+    resid0 = loads_here.astype(jnp.float32) + load_partner.astype(jnp.float32)
+    first, schur_along_x = precondition(resid0, schur_panel[0:2])
+    schur_partner = jnp.stack(
+        [from_partner(schur_along_x[face], axis, from_lower) for axis, from_lower, face in PARTNERS[:2]]
+        + [received[rows:] for received in halo[2:]]
+    )
     resid1 = resid0 - apply_operator(first)
-    second = precondition(resid1)
+    second, _ = precondition(resid1, None)
     curved = apply_operator(second)
     partial = jnp.stack(
         [jnp.sum(resid1 * second, axis=(0, 2)), jnp.sum(second * curved, axis=(0, 2))]

time: 114 us -> 113 us (level)
  waiting for transfers between devices: 27.5 us -> 22.9 us
  matrix products: 17 us -> 19 us
  local copies, waits for them, and re-layouts: 6.08 us -> 7.57 us
    ppermute x6 -> x4, starting transfers between devices: 18.9 us -> 11.4 us  [with_halo(): lax.ppermute(lax.slice_in_dim(block, block.shape[dim] - width, None, axis...]
    ppermute x4 -> x6, starting transfers between devices: 10.3 us -> 16.5 us  [from_partner(): return lax.ppermute(values, axis, pairs)]
    all_to_all x2, waiting for transfers between devices: 11.6 us -> 5.82 us  [gather_rows(): swapped = lax.all_to_all(spread, axes, 0, 0, tiled=False)]
    all_to_all x2, starting transfers between devices: 9.61 us -> 13.6 us  [gather_rows(): swapped = lax.all_to_all(spread, axes, 0, 0, tiled=False)]
    ppermute x6 -> x4, waiting for transfers between devices: 7.6 us -> 10.8 us  [with_halo(): lax.ppermute(lax.slice_in_dim(block, 0, width, axis=dim), axis, backward)]
    ppermute x6 -> x4, starting transfers between devices: 7.88 us -> 5.3 us  [with_halo(): lax.ppermute(lax.slice_in_dim(block, 0, width, axis=dim), axis, backward)]
    squeeze x1 -> x3, local copies, waits for them, and re-layouts: 0.12 us -> 2.28 us  [the longest x1 1.33 us: per_device(): payload = loads_here[face]]
    ppermute x4 -> x6, waiting for transfers between devices: 8.32 us -> 6.21 us  [from_partner(): return lax.ppermute(values, axis, pairs)]
  transfers between devices with their start and end apart: 18 -> 16, of which waited for: 6 -> 6; matrix products, arithmetic and copies ran while one was open for 4% -> 11% of each run, Pallas kernels for 0% -> 0%
where the time goes in v7:
time: 113 us; the launch traced here: 112 us
  starting transfers between devices  46.8 us (41%)
  waiting for transfers between devices  22.9 us (20%)
  matrix products  19 us (17%)
  blocking collectives  12.2 us (11%)
  local copies, waits for them, and re-layouts  7.57 us (7%)
  other arithmetic  3.28 us (3%)
    ppermute x6, starting transfers between devices, from_partner(): return lax.ppermute(values, axis, pairs)  16.5 us
    all_to_all x2, starting transfers between devices, gather_rows(): swapped = lax.all_to_all(spread, axes, 0, 0, tiled=False)  13.6 us
    dot_general x8, matrix products, face_mul(): jnp.einsum('fry,fyx->frx', vectors, matrices, preferred_element_type=jnp....  13.4 us
    all_to_all x1, blocking collectives, gather_rows(): swapped = lax.all_to_all(spread, axes, 0, 0, tiled=False)  12.2 us
    ppermute x4, starting transfers between devices, with_halo(): lax.ppermute(lax.slice_in_dim(block, block.shape[dim] - width, None, axis...  11.4 us
    ppermute x4, waiting for transfers between devices, with_halo(): lax.ppermute(lax.slice_in_dim(block, 0, width, axis=dim), axis, backward)  10.8 us
    ppermute x6, waiting for transfers between devices, from_partner(): return lax.ppermute(values, axis, pairs)  6.21 us
    all_to_all x2, waiting for transfers between devices, gather_rows(): swapped = lax.all_to_all(spread, axes, 0, 0, tiled=False)  5.82 us
  transfers between devices with their start and end apart: 16, of which 6 were waited for; matrix products, arithmetic and copies ran while one was open for 11% of the time, Pallas kernels for 0%

profile of v7, /device:TPU:0, one launch (start us, length us, event | category | flops | bytes accessed | tf_op | source)
XLA Modules:
  0.0 112.4 jit_solution(8324360682996951836)
XLA Ops:
  1.3 4.9 %collective-permute-start = (bf16[192,384]{1,0:T(8,128)(2,1)S(1)}, bf16[192,384]{1,0:T(8,128)(2,1)S(1)}, u32[]{:S(2)}, u32[]{:S(2)}) collective-permute-start(bf16[192,384]{1,0:T(8,128)(2,1)S(1)} %get-tuple-element.21), channel_id=1, source_target_pairs={{0,2},{2,4},{4,6},{6,8},{8,10},{10,12},{12,14},{14,16},{16,18},{18... | collective-permute-start | bytes 442376 | tf_op jit(solution)/shard_map/ppermute | solution.py:40
  9.0 3.2 %collective-permute-start.2 = (bf16[576,384]{1,0:T(8,128)(2,1)S(1)}, bf16[576,384]{1,0:T(8,128)(2,1)S(1)}, u32[]{:S(2)}, u32[]{:S(2)}) collective-permute-start(bf16[576,384]{1,0:T(8,128)(2,1)S(1)} %pad_maximum_fusion.4), channel_id=1, source_target_pairs={{0,1},{2,3},{4,5},{6,7},{8,9},{10,11},{12,13},{14,15},{16,17},{18,... | collective-permute-start | bytes 1327112 | tf_op jit(solution)/shard_map/ppermute | solution.py:40
  16.1 7.1 %all-to-all-start = ((bf16[32,4,192]{2,1,0:T(4,128)(2,1)}), bf16[32,4,192]{2,1,0:T(4,128)(2,1)}, u32[]{:S(2)}, u32[]{:S(2)}) async-start(bf16[32,4,192]{2,1,0:T(4,128)(2,1)} %broadcast_in_dim.8), calls=%async_computation | async-start | bytes 131072 | tf_op jit(solution)/shard_map/all_to_all | solution.py:23
  23.2 1.6 %fusion.19 = f32[4,192,384]{2,1,0:T(8,128)} fusion(bf16[4,192,384]{2,1,0:T(8,128)(2,1)S(1)} %convolution_convert_fusion.3, bf16[1,1,4,384,384]{4,3,2,1,0:T(8,128)(2,1)S(1)} %copy-done.1), kind=kOutput, calls=%fused_computation.31 | convolution fusion | flops 226492416 | bytes 2949120 | tf_op jit(solution)/shard_map/fry,fyx->frx/dot_general | solution.py:48
  25.7 4.4 %collective-permute-start.8 = (bf16[384,384]{1,0:T(8,128)(2,1)}, bf16[384,384]{1,0:T(8,128)(2,1)}, u32[]{:S(2)}, u32[]{:S(2)}) collective-permute-start(bf16[384,384]{1,0:T(8,128)(2,1)} %get-tuple-element.15), channel_id=1, source_target_pairs={{0,2},{2,4},{4,6},{6,8},{8,10},{10,12},{12,14},{14,16},{16,18},{18... | collective-permute-start | bytes 884744 | tf_op jit(solution)/shard_map/ppermute | solution.py:40
  31.9 1.8 %convolution_bitcast_fusion.1 = f32[4,192,384]{2,1,0:T(8,128)} fusion(f32[192,4,1]{0,1,2:T(4,128)S(1)} %convolution_bitcast_fusion.5, s32[4,384]{1,0:T(4,128)S(1)} %multiply_add_fusion, s32[4]{0:T(128)S(1)} %bitcast.97), kind=kOutput, calls=%fused_computation.15 | convolution fusion | flops 14161920 | bytes 1188880 | tf_op jit(solution)/shard_map/kfx,kr->frx/dot_general | solution.py:90
  33.6 2.9 %convolution_convert_fusion.2 = bf16[4,192,384]{2,1,0:T(8,128)(2,1)S(1)} fusion(f32[4,192,384]{2,1,0:T(8,128)} %convolution_bitcast_fusion.1, f32[4,192,384]{2,1,0:T(8,128)} %fusion.19, bf16[1,1,4,384,384]{4,3,2,1,0:T(8,128)(2,1)S(1)} %copy-done.1, bf16[1,1,4,384,384]{4,3,2,1,0:T(8,128)(2,1)S(1)} %copy-done, f32[4]{0:T(128)S(1)} %copy-done.28), kind=kOutput, calls=%fused_computation.20 | convolution fusion | flops 454754304 | bytes 5308432 | tf_op jit(solution)/shard_map/fry,fyx->frx/dot_general | solution.py:48
  36.7 2.8 %collective-permute-start.4 = (bf16[1,192,384]{2,1,0:T(8,128)(2,1)S(1)}, bf16[1,192,384]{2,1,0:T(8,128)(2,1)S(1)}, u32[]{:S(2)}, u32[]{:S(2)}) collective-permute-start(bf16[1,192,384]{2,1,0:T(8,128)(2,1)S(1)} %get-tuple-element.17), channel_id=1, source_target_pairs={{0,2},{2,4},{4,6},{6,8},{8,10},{10,12},{12,14},{14,16},{16,18},{18... | collective-permute-start | bytes 442376 | tf_op jit(solution)/shard_map/ppermute | solution.py:12
  40.8 3.0 %collective-permute-start.6 = (bf16[1,192,384]{2,1,0:T(8,128)(2,1)S(1)}, bf16[1,192,384]{2,1,0:T(8,128)(2,1)S(1)}, u32[]{:S(2)}, u32[]{:S(2)}) collective-permute-start(bf16[1,192,384]{2,1,0:T(8,128)(2,1)S(1)} %get-tuple-element.19), channel_id=1, source_target_pairs={{0,1},{2,3},{4,5},{6,7},{8,9},{10,11},{12,13},{14,15},{16,17},{18,... | collective-permute-start | bytes 442376 | tf_op jit(solution)/shard_map/ppermute | solution.py:12
  46.8 5.1 %collective-permute-done.5 = bf16[1,192,384]{2,1,0:T(8,128)(2,1)S(1)} collective-permute-done((bf16[1,192,384]{2,1,0:T(8,128)(2,1)S(1)}, bf16[1,192,384]{2,1,0:T(8,128)(2,1)S(1)}, u32[]{:S(2)}, u32[]{:S(2)}) %collective-permute-start.5) | collective-permute-done | bytes 147488 | tf_op jit(solution)/shard_map/ppermute | solution.py:15
  52.5 4.7 %collective-permute-done.9 = bf16[384,384]{1,0:T(8,128)(2,1)S(1)} collective-permute-done((bf16[384,384]{1,0:T(8,128)(2,1)S(1)}, bf16[384,384]{1,0:T(8,128)(2,1)S(1)}, u32[]{:S(2)}, u32[]{:S(2)}) %collective-permute-start.9) | collective-permute-done | bytes 294944 | tf_op jit(solution)/shard_map/ppermute | solution.py:40
  57.3 1.6 %fusion.5 = f32[4,192,384]{2,1,0:T(8,128)S(1)} fusion(f32[4,192,384]{2,1,0:T(8,128)S(1)} %convolution_reduce-precision_fusion.3, bf16[1,1,4,192,384]{4,3,2,1,0:T(8,128)(2,1)S(1)} %copy-done.8, bf16[4,192,384]{2,1,0:T(8,128)(2,1)S(1)} %convolution_convert_fusion.2, bf16[1,384,384]{2,1,0:T(8,128)(2,1)S(1)} %copy-done.13, ...), kind=kOutput, calls=%fused_computation.9 | convolution fusion | flops 234160128 | bytes 5898240 | tf_op jit(solution)/shard_map/fry,fyx->frx/dot_general | solution.py:48
  61.0 6.5 %all-to-all-start.1 = ((bf16[32,4,192]{2,1,0:T(4,128)(2,1)}), bf16[32,4,192]{2,1,0:T(4,128)(2,1)}, u32[]{:S(2)}, u32[]{:S(2)}) async-start(bf16[32,4,192]{2,1,0:T(4,128)(2,1)} %broadcast_in_dim.9), calls=%async_computation.1 | async-start | bytes 131072 | tf_op jit(solution)/shard_map/all_to_all | solution.py:23
  67.5 1.6 %fusion.15 = f32[4,192,384]{2,1,0:T(8,128)} fusion(bf16[4,192,384]{2,1,0:T(8,128)(2,1)S(1)} %convolution_convert_fusion.1, bf16[1,1,4,384,384]{4,3,2,1,0:T(8,128)(2,1)S(1)} %copy-done.1), kind=kOutput, calls=%fused_computation.28 | convolution fusion | flops 226492416 | bytes 2949120 | tf_op jit(solution)/shard_map/fry,fyx->frx/dot_general | solution.py:48
  69.1 5.8 %all-to-all-done.1 = bf16[32,4,192]{2,1,0:T(4,128)(2,1)} async-done(((bf16[32,4,192]{2,1,0:T(4,128)(2,1)}), bf16[32,4,192]{2,1,0:T(4,128)(2,1)}, u32[]{:S(2)}, u32[]{:S(2)}) %all-to-all-start.1) | async-done | bytes 49184 | tf_op jit(solution)/shard_map/all_to_all | solution.py:23
  75.9 1.8 %convolution_bitcast_fusion = f32[4,192,384]{2,1,0:T(8,128)} fusion(f32[192,4,1]{0,1,2:T(4,128)S(1)} %convolution_bitcast_fusion.4, s32[4,384]{1,0:T(4,128)S(1)} %multiply_add_fusion, s32[4]{0:T(128)S(1)} %bitcast.99), kind=kOutput, calls=%fused_computation.14 | convolution fusion | flops 14161920 | bytes 1188880 | tf_op jit(solution)/shard_map/kfx,kr->frx/dot_general | solution.py:90
  77.6 2.9 %convolution_convert_fusion = bf16[4,192,384]{2,1,0:T(8,128)(2,1)S(1)} fusion(f32[4,192,384]{2,1,0:T(8,128)} %convolution_bitcast_fusion, f32[4,192,384]{2,1,0:T(8,128)} %fusion.15, bf16[1,1,4,384,384]{4,3,2,1,0:T(8,128)(2,1)S(1)} %copy-done.1, bf16[1,1,4,384,384]{4,3,2,1,0:T(8,128)(2,1)S(1)} %copy-done, f32[4]{0:T(128)} %multiply_bitcast_fusion), kind=kOutput, calls=%fused_computation.18 | convolution fusion | flops 454754304 | bytes 5308432 | tf_op jit(solution)/shard_map/fry,fyx->frx/dot_general | solution.py:48
  80.6 2.5 %collective-permute-start.10 = (bf16[1,192,384]{2,1,0:T(8,128)(2,1)S(1)}, bf16[1,192,384]{2,1,0:T(8,128)(2,1)S(1)}, u32[]{:S(2)}, u32[]{:S(2)}) collective-permute-start(bf16[1,192,384]{2,1,0:T(8,128)(2,1)S(1)} %get-tuple-element.11), channel_id=1, source_target_pairs={{0,2},{2,4},{4,6},{6,8},{8,10},{10,12},{12,14},{14,16},{16,18},{18... | collective-permute-start | bytes 442376 | tf_op jit(solution)/shard_map/ppermute | solution.py:12
  84.4 3.0 %collective-permute-start.12 = (bf16[1,192,384]{2,1,0:T(8,128)(2,1)S(1)}, bf16[1,192,384]{2,1,0:T(8,128)(2,1)S(1)}, u32[]{:S(2)}, u32[]{:S(2)}) collective-permute-start(bf16[1,192,384]{2,1,0:T(8,128)(2,1)S(1)} %get-tuple-element.13), channel_id=1, source_target_pairs={{0,1},{2,3},{4,5},{6,7},{8,9},{10,11},{12,13},{14,15},{16,17},{18,... | collective-permute-start | bytes 442376 | tf_op jit(solution)/shard_map/ppermute | solution.py:12
  87.5 1.4 %collective-permute-start.11 = (bf16[1,192,384]{2,1,0:T(8,128)(2,1)S(1)}, bf16[1,192,384]{2,1,0:T(8,128)(2,1)S(1)}, u32[]{:S(2)}, u32[]{:S(2)}) collective-permute-start(bf16[1,192,384]{2,1,0:T(8,128)(2,1)S(1)} %get-tuple-element.14), channel_id=1, source_target_pairs={{2,0},{4,2},{6,4},{8,6},{10,8},{12,10},{14,12},{16,14},{18,16},{20... | collective-permute-start | bytes 442376 | tf_op jit(solution)/shard_map/ppermute | solution.py:15
  88.9 5.7 %collective-permute-done.11 = bf16[1,192,384]{2,1,0:T(8,128)(2,1)S(1)} collective-permute-done((bf16[1,192,384]{2,1,0:T(8,128)(2,1)S(1)}, bf16[1,192,384]{2,1,0:T(8,128)(2,1)S(1)}, u32[]{:S(2)}, u32[]{:S(2)}) %collective-permute-start.11) | collective-permute-done | bytes 147488 | tf_op jit(solution)/shard_map/ppermute | solution.py:15
  96.1 1.7 %fusion.10 = f32[192]{0:T(256)S(1)} fusion(f32[4,192,384]{2,1,0:T(8,128)S(1)} %convolution_reduce-precision_fusion.1, bf16[4,192,384]{2,1,0:T(8,128)(2,1)S(1)} %convolution_convert_fusion, bf16[1,384,384]{2,1,0:T(8,128)(2,1)S(1)} %copy-done.14, bf16[1,384,384]{2,1,0:T(8,128)(2,1)S(1)} %copy-done.16, bf16[1,384,384]{2,1,0:T(8,128)(2,1)S(1)} %bitcast.104, ...), kind=kOutput, calls=%fused_computation.22 | convolution fusion | flops 234454848 | bytes 3539712 | tf_op jit(solution)/shard_map/fry,fyx->frx/dot_general | solution.py:48
  97.8 12.2 %all_to_all.15 = f32[32,1,2,192]{3,2,1,0:T(2,128)S(1)} all-to-all(f32[32,1,2,192]{3,2,1,0:T(2,128)S(1)} %broadcast_in_dim.10), channel_id=1, replica_groups=mesh['gx'=16,'gy'=2] {'gx','gy'}, dimensions={0} | all-to-all | bytes 98304 | tf_op jit(solution)/shard_map/all_to_all | solution.py:23
  110.1 2.3 %fusion.33 = bf16[1,1,4,192,384]{4,3,2,1,0:T(8,128)(2,1)} fusion(bf16[4,192,384]{2,1,0:T(8,128)(2,1)S(1)} %convolution_convert_fusion, bf16[4,192,384]{2,1,0:T(8,128)(2,1)S(1)} %convolution_convert_fusion.2, f32[192]{0:T(256)S(1)} %bitcast.100, bf16[1,192,384]{2,1,0:T(8,128)(2,1)} %copy-done.23, bf16[1,192,384]{2,1,0:T(8,128)(2,1)} %copy-done.24, ...), kind=kLoop, calls=%fused_computation.50 | loop fusion | flops 4423680 | bytes 2949888 | tf_op jit(solution)/shard_map/broadcast_in_dim | solution.py:124
  (121 shorter events, 21.0 us)
Async XLA Ops:
  0.0 14.4 %copy-start = (bf16[1,1,4,384,384]{4,3,2,1,0:T(8,128)(2,1)S(1)}, bf16[1,1,4,384,384]{4,3,2,1,0:T(8,128)(2,1)}, u32[]{:S(2)}) copy-start(bf16[1,1,4,384,384]{4,3,2,1,0:T(8,128)(2,1)} %param.9) | copy-start | bytes 3538948
  1.3 12.3 %collective-permute-start = (bf16[192,384]{1,0:T(8,128)(2,1)S(1)}, bf16[192,384]{1,0:T(8,128)(2,1)S(1)}, u32[]{:S(2)}, u32[]{:S(2)}) collective-permute-start(bf16[192,384]{1,0:T(8,128)(2,1)S(1)} %get-tuple-element.21), channel_id=1, source_target_pairs={{0,2},{2,4},{4,6},{6,8},{8,10},{10,12},{12,14},{14,16},{16,18},{18... | collective-permute-start | bytes 442376 | tf_op jit(solution)/shard_map/ppermute | solution.py:40
  6.2 8.2 %collective-permute-start.1 = (bf16[192,384]{1,0:T(8,128)(2,1)S(1)}, bf16[192,384]{1,0:T(8,128)(2,1)S(1)}, u32[]{:S(2)}, u32[]{:S(2)}) collective-permute-start(bf16[192,384]{1,0:T(8,128)(2,1)S(1)} %get-tuple-element.22), channel_id=1, source_target_pairs={{2,0},{4,2},{6,4},{8,6},{10,8},{12,10},{14,12},{16,14},{18,16},{20... | collective-permute-start | bytes 442376 | tf_op jit(solution)/shard_map/ppermute | solution.py:40
  7.6 5.2 %collective-permute-start.3 = (bf16[576,384]{1,0:T(8,128)(2,1)S(1)}, bf16[576,384]{1,0:T(8,128)(2,1)S(1)}, u32[]{:S(2)}, u32[]{:S(2)}) collective-permute-start(bf16[576,384]{1,0:T(8,128)(2,1)S(1)} %pad_maximum_fusion.5), channel_id=1, source_target_pairs={{1,0},{3,2},{5,4},{7,6},{9,8},{11,10},{13,12},{15,14},{17,16},{19,... | collective-permute-start | bytes 1327112 | tf_op jit(solution)/shard_map/ppermute | solution.py:40
  9.0 4.6 %collective-permute-start.2 = (bf16[576,384]{1,0:T(8,128)(2,1)S(1)}, bf16[576,384]{1,0:T(8,128)(2,1)S(1)}, u32[]{:S(2)}, u32[]{:S(2)}) collective-permute-start(bf16[576,384]{1,0:T(8,128)(2,1)S(1)} %pad_maximum_fusion.4), channel_id=1, source_target_pairs={{0,1},{2,3},{4,5},{6,7},{8,9},{10,11},{12,13},{14,15},{16,17},{18,... | collective-permute-start | bytes 1327112 | tf_op jit(solution)/shard_map/ppermute | solution.py:40
  16.1 14.8 %all-to-all-start = ((bf16[32,4,192]{2,1,0:T(4,128)(2,1)}), bf16[32,4,192]{2,1,0:T(4,128)(2,1)}, u32[]{:S(2)}, u32[]{:S(2)}) async-start(bf16[32,4,192]{2,1,0:T(4,128)(2,1)} %broadcast_in_dim.8), calls=%async_computation | async-start | bytes 131072 | tf_op jit(solution)/shard_map/all_to_all | solution.py:23
  25.7 26.8 %collective-permute-start.8 = (bf16[384,384]{1,0:T(8,128)(2,1)}, bf16[384,384]{1,0:T(8,128)(2,1)}, u32[]{:S(2)}, u32[]{:S(2)}) collective-permute-start(bf16[384,384]{1,0:T(8,128)(2,1)} %get-tuple-element.15), channel_id=1, source_target_pairs={{0,2},{2,4},{4,6},{6,8},{8,10},{10,12},{12,14},{14,16},{16,18},{18... | collective-permute-start | bytes 884744 | tf_op jit(solution)/shard_map/ppermute | solution.py:40
  36.6 15.3 %copy-start.5 = (bf16[1,1,4,384,384]{4,3,2,1,0:T(8,128)(2,1)S(1)}, bf16[1,1,4,384,384]{4,3,2,1,0:T(8,128)(2,1)}, u32[]{:S(2)}) copy-start(bf16[1,1,4,384,384]{4,3,2,1,0:T(8,128)(2,1)} %param.8) | copy-start | bytes 3538948
  36.7 8.5 %collective-permute-start.4 = (bf16[1,192,384]{2,1,0:T(8,128)(2,1)S(1)}, bf16[1,192,384]{2,1,0:T(8,128)(2,1)S(1)}, u32[]{:S(2)}, u32[]{:S(2)}) collective-permute-start(bf16[1,192,384]{2,1,0:T(8,128)(2,1)S(1)} %get-tuple-element.17), channel_id=1, source_target_pairs={{0,2},{2,4},{4,6},{6,8},{8,10},{10,12},{12,14},{14,16},{16,18},{18... | collective-permute-start | bytes 442376 | tf_op jit(solution)/shard_map/ppermute | solution.py:12
  39.5 7.2 %collective-permute-start.7 = (bf16[1,192,384]{2,1,0:T(8,128)(2,1)S(1)}, bf16[1,192,384]{2,1,0:T(8,128)(2,1)S(1)}, u32[]{:S(2)}, u32[]{:S(2)}) collective-permute-start(bf16[1,192,384]{2,1,0:T(8,128)(2,1)S(1)} %get-tuple-element.18), channel_id=1, source_target_pairs={{1,0},{3,2},{5,4},{7,6},{9,8},{11,10},{13,12},{15,14},{17,16},{19,... | collective-permute-start | bytes 442376 | tf_op jit(solution)/shard_map/ppermute | solution.py:15
  40.8 6.0 %collective-permute-start.6 = (bf16[1,192,384]{2,1,0:T(8,128)(2,1)S(1)}, bf16[1,192,384]{2,1,0:T(8,128)(2,1)S(1)}, u32[]{:S(2)}, u32[]{:S(2)}) collective-permute-start(bf16[1,192,384]{2,1,0:T(8,128)(2,1)S(1)} %get-tuple-element.19), channel_id=1, source_target_pairs={{0,1},{2,3},{4,5},{6,7},{8,9},{10,11},{12,13},{14,15},{16,17},{18,... | collective-permute-start | bytes 442376 | tf_op jit(solution)/shard_map/ppermute | solution.py:12
  43.8 8.0 %collective-permute-start.5 = (bf16[1,192,384]{2,1,0:T(8,128)(2,1)S(1)}, bf16[1,192,384]{2,1,0:T(8,128)(2,1)S(1)}, u32[]{:S(2)}, u32[]{:S(2)}) collective-permute-start(bf16[1,192,384]{2,1,0:T(8,128)(2,1)S(1)} %get-tuple-element.20), channel_id=1, source_target_pairs={{2,0},{4,2},{6,4},{8,6},{10,8},{12,10},{14,12},{16,14},{18,16},{20... | collective-permute-start | bytes 442376 | tf_op jit(solution)/shard_map/ppermute | solution.py:15
  45.2 12.0 %copy-start.15 = (bf16[1,384,384]{2,1,0:T(8,128)(2,1)}, bf16[1,384,384]{2,1,0:T(8,128)(2,1)S(1)}, u32[]{:S(2)}) copy-start(bf16[1,384,384]{2,1,0:T(8,128)(2,1)S(1)} %slice_bitcast_fusion.2) | copy-start | bytes 884740
  45.2 12.0 %copy-start.8 = (bf16[1,1,4,192,384]{4,3,2,1,0:T(8,128)(2,1)S(1)}, bf16[1,1,4,192,384]{4,3,2,1,0:T(8,128)(2,1)}, u32[]{:S(2)}) copy-start(bf16[1,1,4,192,384]{4,3,2,1,0:T(8,128)(2,1)} %param.7) | copy-start | bytes 1769476
  45.2 12.0 %copy-start.13 = (bf16[1,384,384]{2,1,0:T(8,128)(2,1)S(1)}, bf16[1,384,384]{2,1,0:T(8,128)(2,1)}, u32[]{:S(2)}) copy-start(bf16[1,384,384]{2,1,0:T(8,128)(2,1)} %slice_bitcast_fusion.1) | copy-start | bytes 884740
  45.3 12.0 %copy-start.19 = (bf16[1,192,384]{2,1,0:T(8,128)(2,1)S(1)}, bf16[1,192,384]{2,1,0:T(8,128)(2,1)}, u32[]{:S(2)}) copy-start(bf16[1,192,384]{2,1,0:T(8,128)(2,1)} %copy-done.18) | copy-start | bytes 442372
  45.3 12.0 %copy-start.21 = (bf16[1,192,384]{2,1,0:T(8,128)(2,1)S(1)}, bf16[1,192,384]{2,1,0:T(8,128)(2,1)}, u32[]{:S(2)}) copy-start(bf16[1,192,384]{2,1,0:T(8,128)(2,1)} %copy-done.20) | copy-start | bytes 442372
  45.3 11.9 %collective-permute-start.9 = (bf16[384,384]{1,0:T(8,128)(2,1)S(1)}, bf16[384,384]{1,0:T(8,128)(2,1)S(1)}, u32[]{:S(2)}, u32[]{:S(2)}) collective-permute-start(bf16[384,384]{1,0:T(8,128)(2,1)S(1)} %copy-done.17), channel_id=1, source_target_pairs={{2,0},{4,2},{6,4},{8,6},{10,8},{12,10},{14,12},{16,14},{18,16},{20... | collective-permute-start | bytes 884744 | tf_op jit(solution)/shard_map/ppermute | solution.py:40
  61.0 13.9 %all-to-all-start.1 = ((bf16[32,4,192]{2,1,0:T(4,128)(2,1)}), bf16[32,4,192]{2,1,0:T(4,128)(2,1)}, u32[]{:S(2)}, u32[]{:S(2)}) async-start(bf16[32,4,192]{2,1,0:T(4,128)(2,1)} %broadcast_in_dim.9), calls=%async_computation.1 | async-start | bytes 131072 | tf_op jit(solution)/shard_map/all_to_all | solution.py:23
  80.5 14.1 %copy-start.3 = (f32[4,192,384]{2,1,0:T(8,128)S(1)}, f32[4,192,384]{2,1,0:T(8,128)}, u32[]{:S(2)}) copy-start(f32[4,192,384]{2,1,0:T(8,128)} %copy-done.2) | copy-start | bytes 3538948
  80.6 8.3 %collective-permute-start.10 = (bf16[1,192,384]{2,1,0:T(8,128)(2,1)S(1)}, bf16[1,192,384]{2,1,0:T(8,128)(2,1)S(1)}, u32[]{:S(2)}, u32[]{:S(2)}) collective-permute-start(bf16[1,192,384]{2,1,0:T(8,128)(2,1)S(1)} %get-tuple-element.11), channel_id=1, source_target_pairs={{0,2},{2,4},{4,6},{6,8},{8,10},{10,12},{12,14},{14,16},{16,18},{18... | collective-permute-start | bytes 442376 | tf_op jit(solution)/shard_map/ppermute | solution.py:12
  83.1 5.8 %collective-permute-start.13 = (bf16[1,192,384]{2,1,0:T(8,128)(2,1)S(1)}, bf16[1,192,384]{2,1,0:T(8,128)(2,1)S(1)}, u32[]{:S(2)}, u32[]{:S(2)}) collective-permute-start(bf16[1,192,384]{2,1,0:T(8,128)(2,1)S(1)} %get-tuple-element.12), channel_id=1, source_target_pairs={{1,0},{3,2},{5,4},{7,6},{9,8},{11,10},{13,12},{15,14},{17,16},{19,... | collective-permute-start | bytes 442376 | tf_op jit(solution)/shard_map/ppermute | solution.py:15
  84.4 4.5 %collective-permute-start.12 = (bf16[1,192,384]{2,1,0:T(8,128)(2,1)S(1)}, bf16[1,192,384]{2,1,0:T(8,128)(2,1)S(1)}, u32[]{:S(2)}, u32[]{:S(2)}) collective-permute-start(bf16[1,192,384]{2,1,0:T(8,128)(2,1)S(1)} %get-tuple-element.13), channel_id=1, source_target_pairs={{0,1},{2,3},{4,5},{6,7},{8,9},{10,11},{12,13},{14,15},{16,17},{18,... | collective-permute-start | bytes 442376 | tf_op jit(solution)/shard_map/ppermute | solution.py:12
  87.5 7.2 %collective-permute-start.11 = (bf16[1,192,384]{2,1,0:T(8,128)(2,1)S(1)}, bf16[1,192,384]{2,1,0:T(8,128)(2,1)S(1)}, u32[]{:S(2)}, u32[]{:S(2)}) collective-permute-start(bf16[1,192,384]{2,1,0:T(8,128)(2,1)S(1)} %get-tuple-element.14), channel_id=1, source_target_pairs={{2,0},{4,2},{6,4},{8,6},{10,8},{12,10},{14,12},{16,14},{18,16},{20... | collective-permute-start | bytes 442376 | tf_op jit(solution)/shard_map/ppermute | solution.py:15
  (28 other events, 151.2 us)

commit v8 on v5

--- a/solution.py
+++ b/solution.py
@@ -80,7 +80,7 @@
         scaled = face_mul_turned(resid.astype(jnp.bfloat16), deluxe_panel).astype(jnp.bfloat16)
         local_part = face_mul(scaled, inverse_panel)
         extra = face_mul(local_part.astype(jnp.bfloat16), inverse_panel)
-        softened = local_part + 0.5 * flags_full[:, None, None] * extra
+        softened = lax.optimization_barrier(local_part + 0.5 * flags_full[:, None, None] * extra)
         primal = jnp.einsum(
             "kfx,frx->kr", picks_half, scaled, preferred_element_type=jnp.float32
         ).astype(jnp.bfloat16)

time: 112 us -> 110 us (0.982)
  waiting for transfers between devices: 32.9 us -> 30.7 us
    all_to_all x2, waiting for transfers between devices: 11.7 us -> 9.4 us  [gather_rows(): swapped = lax.all_to_all(spread, axes, 0, 0, tiled=False)]
    dot_general x8 -> x10, matrix products: 11.3 us -> 10.3 us  [face_mul(): jnp.einsum('fry,fyx->frx', vectors, matrices, preferred_element_type=jnp....]
  transfers between devices with their start and end apart: 14 -> 14, of which waited for: 6 -> 6; matrix products, arithmetic and copies ran while one was open for 4% -> 6% of each run, Pallas kernels for 0% -> 0%
where the time goes in v8:
time: 110 us; the launch traced here: 109 us
  starting transfers between devices  38.1 us (35%)
  waiting for transfers between devices  30.7 us (28%)
  matrix products  16.4 us (15%)
  blocking collectives  12.2 us (11%)
  local copies, waits for them, and re-layouts  7.7 us (7%)
  other arithmetic  3.48 us (3%)
    ppermute x4, waiting for transfers between devices, from_partner(): return lax.ppermute(values, axis, pairs)  14.7 us
    ppermute x4, starting transfers between devices, with_halo(): lax.ppermute(lax.slice_in_dim(block, block.shape[dim] - width, None, axis...  13.5 us
    all_to_all x1, blocking collectives, gather_rows(): swapped = lax.all_to_all(spread, axes, 0, 0, tiled=False)  12.2 us
    dot_general x10, matrix products, face_mul(): jnp.einsum('fry,fyx->frx', vectors, matrices, preferred_element_type=jnp....  10.3 us
    ppermute x4, starting transfers between devices, from_partner(): return lax.ppermute(values, axis, pairs)  10.1 us
    all_to_all x2, waiting for transfers between devices, gather_rows(): swapped = lax.all_to_all(spread, axes, 0, 0, tiled=False)  9.4 us
    all_to_all x2, starting transfers between devices, gather_rows(): swapped = lax.all_to_all(spread, axes, 0, 0, tiled=False)  9.17 us
    ppermute x4, waiting for transfers between devices, with_halo(): lax.ppermute(lax.slice_in_dim(block, 0, width, axis=dim), axis, backward)  6.6 us
  transfers between devices with their start and end apart: 14, of which 6 were waited for; matrix products, arithmetic and copies ran while one was open for 6% of the time, Pallas kernels for 0%

profile of v8, /device:TPU:0, one launch (start us, length us, event | category | flops | bytes accessed | tf_op | source)
XLA Modules:
  0.0 109.2 jit_solution(9500973982464799597)
XLA Ops:
  0.0 1.3 %slice_bitcast_fusion.11 = (bf16[1,192,384]{2,1,0:T(8,128)(2,1)S(1)}, bf16[1,192,384]{2,1,0:T(8,128)(2,1)S(1)}, bf16[1,192,384]{2,1,0:T(8,128)(2,1)S(1)}, bf16[1,192,384]{2,1,0:T(8,128)(2,1)S(1)}) fusion(bf16[1,1,4,192,384]{4,3,2,1,0:T(8,128)(2,1)} %param.7), kind=kLoop, calls=%fused_computation.75 | loop fusion | bytes 1179648 | tf_op jit(solution)/shard_map/slice | solution.py:13
  1.3 4.9 %collective-permute-start = (bf16[1,192,384]{2,1,0:T(8,128)(2,1)S(1)}, bf16[1,192,384]{2,1,0:T(8,128)(2,1)S(1)}, u32[]{:S(2)}, u32[]{:S(2)}) collective-permute-start(bf16[1,192,384]{2,1,0:T(8,128)(2,1)S(1)} %get-tuple-element.17), channel_id=1, source_target_pairs={{0,2},{2,4},{4,6},{6,8},{8,10},{10,12},{12,14},{14,16},{16,18},{18... | collective-permute-start | bytes 442376 | tf_op jit(solution)/shard_map/ppermute | solution.py:12
  8.8 3.2 %collective-permute-start.2 = (bf16[1,192,384]{2,1,0:T(8,128)(2,1)S(1)}, bf16[1,192,384]{2,1,0:T(8,128)(2,1)S(1)}, u32[]{:S(2)}, u32[]{:S(2)}) collective-permute-start(bf16[1,192,384]{2,1,0:T(8,128)(2,1)S(1)} %get-tuple-element.20), channel_id=1, source_target_pairs={{0,1},{2,3},{4,5},{6,7},{8,9},{10,11},{12,13},{14,15},{16,17},{18,... | collective-permute-start | bytes 442376 | tf_op jit(solution)/shard_map/ppermute | solution.py:12
  16.1 6.3 %all-to-all-start = ((bf16[32,4,192]{2,1,0:T(4,128)(2,1)}), bf16[32,4,192]{2,1,0:T(4,128)(2,1)}, u32[]{:S(2)}, u32[]{:S(2)}) async-start(bf16[32,4,192]{2,1,0:T(4,128)(2,1)} %broadcast_in_dim.8), calls=%async_computation | async-start | bytes 131072 | tf_op jit(solution)/shard_map/all_to_all | solution.py:23
  22.9 1.6 %fusion.5 = f32[4,192,384]{2,1,0:T(8,128)} fusion(f32[4,192,384]{2,1,0:T(8,128)S(1)} %fusion.17, bf16[1,1,4,384,384]{4,3,2,1,0:T(8,128)(2,1)S(1)} %copy-done, f32[4]{0:T(128)S(1)} %copy-done.25), kind=kOutput, calls=%fused_computation.11 | convolution fusion | flops 227377152 | bytes 3538960 | tf_op jit(solution)/shard_map/fry,fyx->frx/dot_general | solution.py:48
  24.5 5.2 %all-to-all-done = bf16[32,4,192]{2,1,0:T(4,128)(2,1)} async-done(((bf16[32,4,192]{2,1,0:T(4,128)(2,1)}), bf16[32,4,192]{2,1,0:T(4,128)(2,1)}, u32[]{:S(2)}, u32[]{:S(2)}) %all-to-all-start) | async-done | bytes 49184 | tf_op jit(solution)/shard_map/all_to_all | solution.py:23
  30.8 2.0 %fusion.8 = bf16[4,192,384]{2,1,0:T(8,128)(2,1)S(1)} fusion(f32[4,192,384]{2,1,0:T(8,128)} %fusion.5, f32[192,4,1]{0,1,2:T(4,128)S(1)} %convolution_bitcast_fusion.5, s32[4,384]{1,0:T(4,128)S(1)} %multiply_add_fusion, s32[4]{0:T(128)S(1)} %bitcast.119), kind=kOutput, calls=%fused_computation.16 | convolution fusion | flops 14751744 | bytes 1778704 | tf_op jit(solution)/shard_map/kfx,kr->frx/dot_general | solution.py:88
  35.7 1.4 %collective-permute-start.5 = (bf16[576,384]{1,0:T(8,128)(2,1)S(1)}, bf16[576,384]{1,0:T(8,128)(2,1)S(1)}, u32[]{:S(2)}, u32[]{:S(2)}) collective-permute-start(bf16[576,384]{1,0:T(8,128)(2,1)S(1)} %pad_maximum_fusion.7), channel_id=1, source_target_pairs={{2,0},{4,2},{6,4},{8,6},{10,8},{12,10},{14,12},{16,14},{18,16},{20... | collective-permute-start | bytes 1327112 | tf_op jit(solution)/shard_map/ppermute | solution.py:40
  37.2 3.1 %collective-permute-start.6 = (bf16[576,384]{1,0:T(8,128)(2,1)S(1)}, bf16[576,384]{1,0:T(8,128)(2,1)S(1)}, u32[]{:S(2)}, u32[]{:S(2)}) collective-permute-start(bf16[576,384]{1,0:T(8,128)(2,1)S(1)} %pad_maximum_fusion.8), channel_id=1, source_target_pairs={{0,1},{2,3},{4,5},{6,7},{8,9},{10,11},{12,13},{14,15},{16,17},{18,... | collective-permute-start | bytes 1327112 | tf_op jit(solution)/shard_map/ppermute | solution.py:40
  40.3 4.3 %collective-permute-start.4 = (bf16[576,384]{1,0:T(8,128)(2,1)S(1)}, bf16[576,384]{1,0:T(8,128)(2,1)S(1)}, u32[]{:S(2)}, u32[]{:S(2)}) collective-permute-start(bf16[576,384]{1,0:T(8,128)(2,1)S(1)} %pad_maximum_fusion.6), channel_id=1, source_target_pairs={{0,2},{2,4},{4,6},{6,8},{8,10},{10,12},{12,14},{14,16},{16,18},{18... | collective-permute-start | bytes 1327112 | tf_op jit(solution)/shard_map/ppermute | solution.py:40
  44.6 5.9 %collective-permute-done.5 = bf16[576,384]{1,0:T(8,128)(2,1)S(1)} collective-permute-done((bf16[576,384]{1,0:T(8,128)(2,1)S(1)}, bf16[576,384]{1,0:T(8,128)(2,1)S(1)}, u32[]{:S(2)}, u32[]{:S(2)}) %collective-permute-start.5) | collective-permute-done | bytes 442400 | tf_op jit(solution)/shard_map/ppermute | solution.py:40
  50.6 8.8 %collective-permute-done.4 = bf16[576,384]{1,0:T(8,128)(2,1)S(1)} collective-permute-done((bf16[576,384]{1,0:T(8,128)(2,1)S(1)}, bf16[576,384]{1,0:T(8,128)(2,1)S(1)}, u32[]{:S(2)}, u32[]{:S(2)}) %collective-permute-start.4) | collective-permute-done | bytes 442400 | tf_op jit(solution)/shard_map/ppermute | solution.py:40
  62.7 1.6 %fusion.14 = f32[4,192,384]{2,1,0:T(8,128)} fusion(bf16[4,192,384]{2,1,0:T(8,128)(2,1)S(1)} %convolution_convert_fusion.1, bf16[1,1,4,384,384]{4,3,2,1,0:T(8,128)(2,1)S(1)} %copy-done), kind=kOutput, calls=%fused_computation.30 | convolution fusion | flops 226492416 | bytes 2949120 | tf_op jit(solution)/shard_map/fry,fyx->frx/dot_general | solution.py:48
  64.9 2.9 %all-to-all-start.1 = ((bf16[32,4,192]{2,1,0:T(4,128)(2,1)}), bf16[32,4,192]{2,1,0:T(4,128)(2,1)S(1)}, u32[]{:S(2)}, u32[]{:S(2)}) async-start(bf16[32,4,192]{2,1,0:T(4,128)(2,1)} %broadcast_in_dim.9), calls=%async_computation.1 | async-start | bytes 131072 | tf_op jit(solution)/shard_map/all_to_all | solution.py:23
  67.8 3.2 %fusion.2 = f32[4,192,384]{2,1,0:T(8,128)} fusion(f32[4,192,384]{2,1,0:T(8,128)} %fusion.14, bf16[1,1,4,384,384]{4,3,2,1,0:T(8,128)(2,1)S(1)} %copy-done, f32[4]{0:T(128)S(1)} %copy-done.26), kind=kOutput, calls=%fused_computation.5 | convolution fusion | flops 227377152 | bytes 3538960 | tf_op jit(solution)/shard_map/fry,fyx->frx/dot_general | solution.py:48
  71.0 4.2 %all-to-all-done.1 = bf16[32,4,192]{2,1,0:T(4,128)(2,1)S(1)} async-done(((bf16[32,4,192]{2,1,0:T(4,128)(2,1)}), bf16[32,4,192]{2,1,0:T(4,128)(2,1)S(1)}, u32[]{:S(2)}, u32[]{:S(2)}) %all-to-all-start.1) | async-done | bytes 49184 | tf_op jit(solution)/shard_map/all_to_all | solution.py:23
  75.4 2.0 %fusion.9 = bf16[4,192,384]{2,1,0:T(8,128)(2,1)S(1)} fusion(f32[4,192,384]{2,1,0:T(8,128)} %fusion.2, f32[192,4,1]{0,1,2:T(4,128)S(1)} %convolution_bitcast_fusion.4, s32[4,384]{1,0:T(4,128)S(1)} %multiply_add_fusion, s32[4]{0:T(128)S(1)} %bitcast.121), kind=kOutput, calls=%fused_computation.17 | convolution fusion | flops 14751744 | bytes 1778704 | tf_op jit(solution)/shard_map/kfx,kr->frx/dot_general | solution.py:88
  78.0 2.5 %collective-permute-start.8 = (bf16[1,192,384]{2,1,0:T(8,128)(2,1)S(1)}, bf16[1,192,384]{2,1,0:T(8,128)(2,1)S(1)}, u32[]{:S(2)}, u32[]{:S(2)}) collective-permute-start(bf16[1,192,384]{2,1,0:T(8,128)(2,1)S(1)} %get-tuple-element.9), channel_id=1, source_target_pairs={{0,2},{2,4},{4,6},{6,8},{8,10},{10,12},{12,14},{14,16},{16,18},{18... | collective-permute-start | bytes 442376 | tf_op jit(solution)/shard_map/ppermute | solution.py:12
  80.5 1.3 %collective-permute-start.11 = (bf16[1,192,384]{2,1,0:T(8,128)(2,1)S(1)}, bf16[1,192,384]{2,1,0:T(8,128)(2,1)S(1)}, u32[]{:S(2)}, u32[]{:S(2)}) collective-permute-start(bf16[1,192,384]{2,1,0:T(8,128)(2,1)S(1)} %get-tuple-element.10), channel_id=1, source_target_pairs={{1,0},{3,2},{5,4},{7,6},{9,8},{11,10},{13,12},{15,14},{17,16},{19,... | collective-permute-start | bytes 442376 | tf_op jit(solution)/shard_map/ppermute | solution.py:15
  81.8 3.0 %collective-permute-start.10 = (bf16[1,192,384]{2,1,0:T(8,128)(2,1)S(1)}, bf16[1,192,384]{2,1,0:T(8,128)(2,1)S(1)}, u32[]{:S(2)}, u32[]{:S(2)}) collective-permute-start(bf16[1,192,384]{2,1,0:T(8,128)(2,1)S(1)} %get-tuple-element.11), channel_id=1, source_target_pairs={{0,1},{2,3},{4,5},{6,7},{8,9},{10,11},{12,13},{14,15},{16,17},{18,... | collective-permute-start | bytes 442376 | tf_op jit(solution)/shard_map/ppermute | solution.py:12
  84.9 1.4 %collective-permute-start.9 = (bf16[1,192,384]{2,1,0:T(8,128)(2,1)S(1)}, bf16[1,192,384]{2,1,0:T(8,128)(2,1)S(1)}, u32[]{:S(2)}, u32[]{:S(2)}) collective-permute-start(bf16[1,192,384]{2,1,0:T(8,128)(2,1)S(1)} %get-tuple-element.12), channel_id=1, source_target_pairs={{2,0},{4,2},{6,4},{8,6},{10,8},{12,10},{14,12},{16,14},{18,16},{20... | collective-permute-start | bytes 442376 | tf_op jit(solution)/shard_map/ppermute | solution.py:15
  86.4 5.7 %collective-permute-done.9 = bf16[1,192,384]{2,1,0:T(8,128)(2,1)S(1)} collective-permute-done((bf16[1,192,384]{2,1,0:T(8,128)(2,1)S(1)}, bf16[1,192,384]{2,1,0:T(8,128)(2,1)S(1)}, u32[]{:S(2)}, u32[]{:S(2)}) %collective-permute-start.9) | collective-permute-done | bytes 147488 | tf_op jit(solution)/shard_map/ppermute | solution.py:15
  94.5 12.2 %all_to_all.15 = f32[32,1,2,192]{3,2,1,0:T(2,128)S(1)} all-to-all(f32[32,1,2,192]{3,2,1,0:T(2,128)S(1)} %broadcast_in_dim.10), channel_id=1, replica_groups=mesh['gx'=16,'gy'=2] {'gx','gy'}, dimensions={0} | all-to-all | bytes 98304 | tf_op jit(solution)/shard_map/all_to_all | solution.py:23
  106.8 2.4 %fusion.31 = bf16[1,1,4,192,384]{4,3,2,1,0:T(8,128)(2,1)} fusion(bf16[4,192,384]{2,1,0:T(8,128)(2,1)S(1)} %convolution_convert_fusion, bf16[4,192,384]{2,1,0:T(8,128)(2,1)S(1)} %convolution_convert_fusion.2, f32[192]{0:T(256)S(1)} %bitcast.122, bf16[1,192,384]{2,1,0:T(8,128)(2,1)} %copy-done.18, bf16[1,192,384]{2,1,0:T(8,128)(2,1)} %copy-done.19, ...), kind=kLoop, calls=%fused_computation.52 | loop fusion | flops 6782976 | bytes 4129536 | tf_op jit(solution)/shard_map/broadcast_in_dim | solution.py:120
  (115 shorter events, 18.2 us)
Async XLA Ops:
  0.0 22.4 %copy-start = (bf16[1,1,4,384,384]{4,3,2,1,0:T(8,128)(2,1)S(1)}, bf16[1,1,4,384,384]{4,3,2,1,0:T(8,128)(2,1)}, u32[]{:S(2)}) copy-start(bf16[1,1,4,384,384]{4,3,2,1,0:T(8,128)(2,1)} %param.10) | copy-start | bytes 3538948
  0.0 12.0 %copy-start.2 = (bf16[1,1,4,384,384]{4,3,2,1,0:T(8,128)(2,1)S(1)}, bf16[1,1,4,384,384]{4,3,2,1,0:T(8,128)(2,1)}, u32[]{:S(2)}) copy-start(bf16[1,1,4,384,384]{4,3,2,1,0:T(8,128)(2,1)} %param.8) | copy-start | bytes 3538948
  1.3 12.1 %collective-permute-start = (bf16[1,192,384]{2,1,0:T(8,128)(2,1)S(1)}, bf16[1,192,384]{2,1,0:T(8,128)(2,1)S(1)}, u32[]{:S(2)}, u32[]{:S(2)}) collective-permute-start(bf16[1,192,384]{2,1,0:T(8,128)(2,1)S(1)} %get-tuple-element.17), channel_id=1, source_target_pairs={{0,2},{2,4},{4,6},{6,8},{8,10},{10,12},{12,14},{14,16},{16,18},{18... | collective-permute-start | bytes 442376 | tf_op jit(solution)/shard_map/ppermute | solution.py:12
  6.2 8.2 %collective-permute-start.1 = (bf16[1,192,384]{2,1,0:T(8,128)(2,1)S(1)}, bf16[1,192,384]{2,1,0:T(8,128)(2,1)S(1)}, u32[]{:S(2)}, u32[]{:S(2)}) collective-permute-start(bf16[1,192,384]{2,1,0:T(8,128)(2,1)S(1)} %get-tuple-element.18), channel_id=1, source_target_pairs={{2,0},{4,2},{6,4},{8,6},{10,8},{12,10},{14,12},{16,14},{18,16},{20... | collective-permute-start | bytes 442376 | tf_op jit(solution)/shard_map/ppermute | solution.py:15
  7.5 6.9 %collective-permute-start.3 = (bf16[1,192,384]{2,1,0:T(8,128)(2,1)S(1)}, bf16[1,192,384]{2,1,0:T(8,128)(2,1)S(1)}, u32[]{:S(2)}, u32[]{:S(2)}) collective-permute-start(bf16[1,192,384]{2,1,0:T(8,128)(2,1)S(1)} %get-tuple-element.19), channel_id=1, source_target_pairs={{1,0},{3,2},{5,4},{7,6},{9,8},{11,10},{13,12},{15,14},{17,16},{19,... | collective-permute-start | bytes 442376 | tf_op jit(solution)/shard_map/ppermute | solution.py:15
  8.8 5.6 %collective-permute-start.2 = (bf16[1,192,384]{2,1,0:T(8,128)(2,1)S(1)}, bf16[1,192,384]{2,1,0:T(8,128)(2,1)S(1)}, u32[]{:S(2)}, u32[]{:S(2)}) collective-permute-start(bf16[1,192,384]{2,1,0:T(8,128)(2,1)S(1)} %get-tuple-element.20), channel_id=1, source_target_pairs={{0,1},{2,3},{4,5},{6,7},{8,9},{10,11},{12,13},{14,15},{16,17},{18,... | collective-permute-start | bytes 442376 | tf_op jit(solution)/shard_map/ppermute | solution.py:12
  16.1 13.7 %all-to-all-start = ((bf16[32,4,192]{2,1,0:T(4,128)(2,1)}), bf16[32,4,192]{2,1,0:T(4,128)(2,1)}, u32[]{:S(2)}, u32[]{:S(2)}) async-start(bf16[32,4,192]{2,1,0:T(4,128)(2,1)} %broadcast_in_dim.8), calls=%async_computation | async-start | bytes 131072 | tf_op jit(solution)/shard_map/all_to_all | solution.py:23
  22.9 7.7 %copy-start.23 = (f32[4,128]{1,0:T(4,128)S(1)}, f32[4,128]{1,0:T(4,128)}, u32[]{:S(2)}) copy-start(f32[4,128]{1,0:T(4,128)} %param.11) | copy-start | bytes 6148
  34.3 10.3 %collective-permute-start.7 = (bf16[576,384]{1,0:T(8,128)(2,1)S(1)}, bf16[576,384]{1,0:T(8,128)(2,1)S(1)}, u32[]{:S(2)}, u32[]{:S(2)}) collective-permute-start(bf16[576,384]{1,0:T(8,128)(2,1)S(1)} %pad_maximum_fusion.9), channel_id=1, source_target_pairs={{1,0},{3,2},{5,4},{7,6},{9,8},{11,10},{13,12},{15,14},{17,16},{19,... | collective-permute-start | bytes 1327112 | tf_op jit(solution)/shard_map/ppermute | solution.py:40
  35.6 23.8 %copy-start.3 = (bf16[1,1,4,384,384]{4,3,2,1,0:T(8,128)(2,1)S(1)}, bf16[1,1,4,384,384]{4,3,2,1,0:T(8,128)(2,1)}, u32[]{:S(2)}) copy-start(bf16[1,1,4,384,384]{4,3,2,1,0:T(8,128)(2,1)} %param.8) | copy-start | bytes 3538948
  35.7 14.9 %collective-permute-start.5 = (bf16[576,384]{1,0:T(8,128)(2,1)S(1)}, bf16[576,384]{1,0:T(8,128)(2,1)S(1)}, u32[]{:S(2)}, u32[]{:S(2)}) collective-permute-start(bf16[576,384]{1,0:T(8,128)(2,1)S(1)} %pad_maximum_fusion.7), channel_id=1, source_target_pairs={{2,0},{4,2},{6,4},{8,6},{10,8},{12,10},{14,12},{16,14},{18,16},{20... | collective-permute-start | bytes 1327112 | tf_op jit(solution)/shard_map/ppermute | solution.py:40
  37.2 13.4 %collective-permute-start.6 = (bf16[576,384]{1,0:T(8,128)(2,1)S(1)}, bf16[576,384]{1,0:T(8,128)(2,1)S(1)}, u32[]{:S(2)}, u32[]{:S(2)}) collective-permute-start(bf16[576,384]{1,0:T(8,128)(2,1)S(1)} %pad_maximum_fusion.8), channel_id=1, source_target_pairs={{0,1},{2,3},{4,5},{6,7},{8,9},{10,11},{12,13},{14,15},{16,17},{18,... | collective-permute-start | bytes 1327112 | tf_op jit(solution)/shard_map/ppermute | solution.py:40
  40.3 19.1 %collective-permute-start.4 = (bf16[576,384]{1,0:T(8,128)(2,1)S(1)}, bf16[576,384]{1,0:T(8,128)(2,1)S(1)}, u32[]{:S(2)}, u32[]{:S(2)}) collective-permute-start(bf16[576,384]{1,0:T(8,128)(2,1)S(1)} %pad_maximum_fusion.6), channel_id=1, source_target_pairs={{0,2},{2,4},{4,6},{6,8},{8,10},{10,12},{12,14},{14,16},{16,18},{18... | collective-permute-start | bytes 1327112 | tf_op jit(solution)/shard_map/ppermute | solution.py:40
  44.6 15.3 %copy-start.7 = (bf16[576,384]{1,0:T(8,128)(2,1)}, bf16[576,384]{1,0:T(8,128)(2,1)S(1)}, u32[]{:S(2)}) copy-start(bf16[576,384]{1,0:T(8,128)(2,1)S(1)} %collective-permute-done.7) | copy-start | bytes 1327108
  50.6 9.4 %copy-start.9 = (bf16[576,384]{1,0:T(8,128)(2,1)}, bf16[576,384]{1,0:T(8,128)(2,1)S(1)}, u32[]{:S(2)}) copy-start(bf16[576,384]{1,0:T(8,128)(2,1)S(1)} %collective-permute-done.5) | copy-start | bytes 1327108
  50.6 9.4 %copy-start.11 = (bf16[576,384]{1,0:T(8,128)(2,1)}, bf16[576,384]{1,0:T(8,128)(2,1)S(1)}, u32[]{:S(2)}) copy-start(bf16[576,384]{1,0:T(8,128)(2,1)S(1)} %collective-permute-done.6) | copy-start | bytes 1327108
  64.9 10.3 %all-to-all-start.1 = ((bf16[32,4,192]{2,1,0:T(4,128)(2,1)}), bf16[32,4,192]{2,1,0:T(4,128)(2,1)S(1)}, u32[]{:S(2)}, u32[]{:S(2)}) async-start(bf16[32,4,192]{2,1,0:T(4,128)(2,1)} %broadcast_in_dim.9), calls=%async_computation.1 | async-start | bytes 131072 | tf_op jit(solution)/shard_map/all_to_all | solution.py:23
  77.9 14.1 %copy-start.6 = (f32[4,192,384]{2,1,0:T(8,128)S(1)}, f32[4,192,384]{2,1,0:T(8,128)}, u32[]{:S(2)}) copy-start(f32[4,192,384]{2,1,0:T(8,128)} %copy-done.5) | copy-start | bytes 3538948
  78.0 8.3 %collective-permute-start.8 = (bf16[1,192,384]{2,1,0:T(8,128)(2,1)S(1)}, bf16[1,192,384]{2,1,0:T(8,128)(2,1)S(1)}, u32[]{:S(2)}, u32[]{:S(2)}) collective-permute-start(bf16[1,192,384]{2,1,0:T(8,128)(2,1)S(1)} %get-tuple-element.9), channel_id=1, source_target_pairs={{0,2},{2,4},{4,6},{6,8},{8,10},{10,12},{12,14},{14,16},{16,18},{18... | collective-permute-start | bytes 442376 | tf_op jit(solution)/shard_map/ppermute | solution.py:12
  80.5 5.8 %collective-permute-start.11 = (bf16[1,192,384]{2,1,0:T(8,128)(2,1)S(1)}, bf16[1,192,384]{2,1,0:T(8,128)(2,1)S(1)}, u32[]{:S(2)}, u32[]{:S(2)}) collective-permute-start(bf16[1,192,384]{2,1,0:T(8,128)(2,1)S(1)} %get-tuple-element.10), channel_id=1, source_target_pairs={{1,0},{3,2},{5,4},{7,6},{9,8},{11,10},{13,12},{15,14},{17,16},{19,... | collective-permute-start | bytes 442376 | tf_op jit(solution)/shard_map/ppermute | solution.py:15
  81.8 4.5 %collective-permute-start.10 = (bf16[1,192,384]{2,1,0:T(8,128)(2,1)S(1)}, bf16[1,192,384]{2,1,0:T(8,128)(2,1)S(1)}, u32[]{:S(2)}, u32[]{:S(2)}) collective-permute-start(bf16[1,192,384]{2,1,0:T(8,128)(2,1)S(1)} %get-tuple-element.11), channel_id=1, source_target_pairs={{0,1},{2,3},{4,5},{6,7},{8,9},{10,11},{12,13},{14,15},{16,17},{18,... | collective-permute-start | bytes 442376 | tf_op jit(solution)/shard_map/ppermute | solution.py:12
  84.8 7.5 %copy-start.4 = (bf16[1,1,4,384,384]{4,3,2,1,0:T(8,128)(2,1)S(1)}, bf16[1,1,4,384,384]{4,3,2,1,0:T(8,128)(2,1)}, u32[]{:S(2)}) copy-start(bf16[1,1,4,384,384]{4,3,2,1,0:T(8,128)(2,1)} %param.8) | copy-start | bytes 3538948
  84.9 7.2 %collective-permute-start.9 = (bf16[1,192,384]{2,1,0:T(8,128)(2,1)S(1)}, bf16[1,192,384]{2,1,0:T(8,128)(2,1)S(1)}, u32[]{:S(2)}, u32[]{:S(2)}) collective-permute-start(bf16[1,192,384]{2,1,0:T(8,128)(2,1)S(1)} %get-tuple-element.12), channel_id=1, source_target_pairs={{2,0},{4,2},{6,4},{8,6},{10,8},{12,10},{14,12},{16,14},{18,16},{20... | collective-permute-start | bytes 442376 | tf_op jit(solution)/shard_map/ppermute | solution.py:15
  86.3 6.6 %copy-start.17 = (bf16[1,192,384]{2,1,0:T(8,128)(2,1)}, bf16[1,192,384]{2,1,0:T(8,128)(2,1)S(1)}, u32[]{:S(2)}) copy-start(bf16[1,192,384]{2,1,0:T(8,128)(2,1)S(1)} %collective-permute-done.8) | copy-start | bytes 442372
  (26 other events, 57.0 us)

commit v9 on v8

--- a/solution.py
+++ b/solution.py
@@ -70,7 +70,7 @@
     positions = jnp.arange(4 * width, dtype=jnp.int32)
     picks = (primal_slots[:, None] == positions[None, :]).reshape(primal_count, 4, width)
     picks_half = picks.astype(jnp.bfloat16)
-    picks_full = picks.astype(jnp.float32)
+    picks_triple = jnp.concatenate([picks_half] * 3)
     flags_full = flag_values.astype(jnp.float32)
 
     def add_coarse(piece):
@@ -85,7 +85,13 @@
             "kfx,frx->kr", picks_half, scaled, preferred_element_type=jnp.float32
         ).astype(jnp.bfloat16)
         coarse = add_coarse(gather_rows(primal, ("gx", "gy")))
-        placed = jnp.einsum("kfx,kr->frx", picks_full, coarse, precision=lax.Precision.HIGHEST)
+        high = to_half(coarse)
+        rest = coarse - high
+        middle = to_half(rest)
+        pieces = jnp.concatenate([high, middle, rest - middle]).astype(jnp.bfloat16)
+        placed = jnp.einsum(
+            "kfx,kr->frx", picks_triple, pieces, preferred_element_type=jnp.float32
+        )
         weighted = (softened + placed).astype(jnp.bfloat16)
         spread = face_mul(weighted, deluxe_panel).astype(jnp.bfloat16)
         if schur_partner is not None:

time: 110 us -> 110 us (level)
    dot_general x2 -> x0, matrix products: 4.01 us -> none  [precondition(): jnp.einsum('kfx,kr->frx', picks_full, coarse, precision=lax.Precision.HIG...]
    dot_general x10, matrix products: 10.3 us -> 13.3 us  [face_mul(): jnp.einsum('fry,fyx->frx', vectors, matrices, preferred_element_type=jnp....]
    dot_general x2, matrix products: 0.24 us -> 1.5 us  [add_coarse(): jnp.dot(coarse_inverse, piece.astype(jnp.float32), precision=lax.Precisio...]
where the time goes in v9:
time: 110 us; the launch traced here: 109 us
  starting transfers between devices  37.9 us (34%)
  waiting for transfers between devices  31.2 us (28%)
  matrix products  16.5 us (15%)
  blocking collectives  12.2 us (11%)
  local copies, waits for them, and re-layouts  7.7 us (7%)
  other arithmetic  3.08 us (3%)
    ppermute x4, waiting for transfers between devices, from_partner(): return lax.ppermute(values, axis, pairs)  14.7 us
    ppermute x4, starting transfers between devices, with_halo(): lax.ppermute(lax.slice_in_dim(block, block.shape[dim] - width, None, axis...  13.4 us
    dot_general x10, matrix products, face_mul(): jnp.einsum('fry,fyx->frx', vectors, matrices, preferred_element_type=jnp....  13.3 us
    all_to_all x1, blocking collectives, gather_rows(): swapped = lax.all_to_all(spread, axes, 0, 0, tiled=False)  12.2 us
    ppermute x4, starting transfers between devices, from_partner(): return lax.ppermute(values, axis, pairs)  10.1 us
    all_to_all x2, waiting for transfers between devices, gather_rows(): swapped = lax.all_to_all(spread, axes, 0, 0, tiled=False)  9.43 us
    all_to_all x2, starting transfers between devices, gather_rows(): swapped = lax.all_to_all(spread, axes, 0, 0, tiled=False)  9.11 us
    ppermute x4, waiting for transfers between devices, with_halo(): lax.ppermute(lax.slice_in_dim(block, 0, width, axis=dim), axis, backward)  7.07 us
  transfers between devices with their start and end apart: 14, of which 6 were waited for; matrix products, arithmetic and copies ran while one was open for 6% of the time, Pallas kernels for 0%

profile of v9, /device:TPU:0, one launch (start us, length us, event | category | flops | bytes accessed | tf_op | source)
XLA Modules:
  0.0 109.3 jit_solution(17123157625256438061)
XLA Ops:
  0.0 1.3 %slice_bitcast_fusion.11 = (bf16[1,192,384]{2,1,0:T(8,128)(2,1)S(1)}, bf16[1,192,384]{2,1,0:T(8,128)(2,1)S(1)}, bf16[1,192,384]{2,1,0:T(8,128)(2,1)S(1)}, bf16[1,192,384]{2,1,0:T(8,128)(2,1)S(1)}) fusion(bf16[1,1,4,192,384]{4,3,2,1,0:T(8,128)(2,1)} %param.7), kind=kLoop, calls=%fused_computation.75 | loop fusion | bytes 1179648 | tf_op jit(solution)/shard_map/slice | solution.py:13
  1.3 4.9 %collective-permute-start = (bf16[1,192,384]{2,1,0:T(8,128)(2,1)S(1)}, bf16[1,192,384]{2,1,0:T(8,128)(2,1)S(1)}, u32[]{:S(2)}, u32[]{:S(2)}) collective-permute-start(bf16[1,192,384]{2,1,0:T(8,128)(2,1)S(1)} %get-tuple-element.17), channel_id=1, source_target_pairs={{0,2},{2,4},{4,6},{6,8},{8,10},{10,12},{12,14},{14,16},{16,18},{18... | collective-permute-start | bytes 442376 | tf_op jit(solution)/shard_map/ppermute | solution.py:12
  8.8 3.0 %collective-permute-start.2 = (bf16[1,192,384]{2,1,0:T(8,128)(2,1)S(1)}, bf16[1,192,384]{2,1,0:T(8,128)(2,1)S(1)}, u32[]{:S(2)}, u32[]{:S(2)}) collective-permute-start(bf16[1,192,384]{2,1,0:T(8,128)(2,1)S(1)} %get-tuple-element.20), channel_id=1, source_target_pairs={{0,1},{2,3},{4,5},{6,7},{8,9},{10,11},{12,13},{14,15},{16,17},{18,... | collective-permute-start | bytes 442376 | tf_op jit(solution)/shard_map/ppermute | solution.py:12
  13.0 1.4 %collective-permute-done.1 = bf16[1,192,384]{2,1,0:T(8,128)(2,1)S(1)} collective-permute-done((bf16[1,192,384]{2,1,0:T(8,128)(2,1)S(1)}, bf16[1,192,384]{2,1,0:T(8,128)(2,1)S(1)}, u32[]{:S(2)}, u32[]{:S(2)}) %collective-permute-start.1) | collective-permute-done | bytes 147488 | tf_op jit(solution)/shard_map/ppermute | solution.py:15
  16.1 6.2 %all-to-all-start = ((bf16[32,4,192]{2,1,0:T(4,128)(2,1)}), bf16[32,4,192]{2,1,0:T(4,128)(2,1)}, u32[]{:S(2)}, u32[]{:S(2)}) async-start(bf16[32,4,192]{2,1,0:T(4,128)(2,1)} %broadcast_in_dim.8), calls=%async_computation | async-start | bytes 131072 | tf_op jit(solution)/shard_map/all_to_all | solution.py:23
  22.8 1.6 %fusion.5 = f32[4,192,384]{2,1,0:T(8,128)} fusion(f32[4,192,384]{2,1,0:T(8,128)S(1)} %fusion.17, bf16[1,1,4,384,384]{4,3,2,1,0:T(8,128)(2,1)S(1)} %copy-done, f32[4]{0:T(128)S(1)} %multiply_bitcast_fusion), kind=kOutput, calls=%fused_computation.13 | convolution fusion | flops 227377152 | bytes 3538960 | tf_op jit(solution)/shard_map/fry,fyx->frx/dot_general | solution.py:48
  24.4 5.2 %all-to-all-done = bf16[32,4,192]{2,1,0:T(4,128)(2,1)} async-done(((bf16[32,4,192]{2,1,0:T(4,128)(2,1)}), bf16[32,4,192]{2,1,0:T(4,128)(2,1)}, u32[]{:S(2)}, u32[]{:S(2)}) %all-to-all-start) | async-done | bytes 49184 | tf_op jit(solution)/shard_map/all_to_all | solution.py:23
  31.3 2.0 %convolution_convert_fusion.2 = bf16[4,192,384]{2,1,0:T(8,128)(2,1)S(1)} fusion(f32[4,192,384]{2,1,0:T(8,128)} %fusion.5, bf16[1,1,4,384,384]{4,3,2,1,0:T(8,128)(2,1)S(1)} %copy-done.1, pred[4,4,384]{2,0,1:T(4,128)(4,1)S(1)} %broadcast_compare_fusion, bf16[4,192]{1,0:T(4,128)(2,1)} %get-tuple-element.25, bf16[4,192]{1,0:T(4,128)(2,1)} %get-tuple-element.26, ...), kind=kOutput, calls=%fused_computation.18 | convolution fusion | flops 234505728 | bytes 2959872 | tf_op jit(solution)/shard_map/fry,fyx->frx/dot_general | solution.py:48
  35.7 1.4 %collective-permute-start.5 = (bf16[576,384]{1,0:T(8,128)(2,1)S(1)}, bf16[576,384]{1,0:T(8,128)(2,1)S(1)}, u32[]{:S(2)}, u32[]{:S(2)}) collective-permute-start(bf16[576,384]{1,0:T(8,128)(2,1)S(1)} %pad_maximum_fusion.7), channel_id=1, source_target_pairs={{2,0},{4,2},{6,4},{8,6},{10,8},{12,10},{14,12},{16,14},{18,16},{20... | collective-permute-start | bytes 1327112 | tf_op jit(solution)/shard_map/ppermute | solution.py:40
  37.2 3.1 %collective-permute-start.6 = (bf16[576,384]{1,0:T(8,128)(2,1)S(1)}, bf16[576,384]{1,0:T(8,128)(2,1)S(1)}, u32[]{:S(2)}, u32[]{:S(2)}) collective-permute-start(bf16[576,384]{1,0:T(8,128)(2,1)S(1)} %pad_maximum_fusion.8), channel_id=1, source_target_pairs={{0,1},{2,3},{4,5},{6,7},{8,9},{10,11},{12,13},{14,15},{16,17},{18,... | collective-permute-start | bytes 1327112 | tf_op jit(solution)/shard_map/ppermute | solution.py:40
  40.3 4.3 %collective-permute-start.4 = (bf16[576,384]{1,0:T(8,128)(2,1)S(1)}, bf16[576,384]{1,0:T(8,128)(2,1)S(1)}, u32[]{:S(2)}, u32[]{:S(2)}) collective-permute-start(bf16[576,384]{1,0:T(8,128)(2,1)S(1)} %pad_maximum_fusion.6), channel_id=1, source_target_pairs={{0,2},{2,4},{4,6},{6,8},{8,10},{10,12},{12,14},{14,16},{16,18},{18... | collective-permute-start | bytes 1327112 | tf_op jit(solution)/shard_map/ppermute | solution.py:40
  44.6 5.9 %collective-permute-done.5 = bf16[576,384]{1,0:T(8,128)(2,1)S(1)} collective-permute-done((bf16[576,384]{1,0:T(8,128)(2,1)S(1)}, bf16[576,384]{1,0:T(8,128)(2,1)S(1)}, u32[]{:S(2)}, u32[]{:S(2)}) %collective-permute-start.5) | collective-permute-done | bytes 442400 | tf_op jit(solution)/shard_map/ppermute | solution.py:40
  50.6 8.8 %collective-permute-done.4 = bf16[576,384]{1,0:T(8,128)(2,1)S(1)} collective-permute-done((bf16[576,384]{1,0:T(8,128)(2,1)S(1)}, bf16[576,384]{1,0:T(8,128)(2,1)S(1)}, u32[]{:S(2)}, u32[]{:S(2)}) %collective-permute-start.4) | collective-permute-done | bytes 442400 | tf_op jit(solution)/shard_map/ppermute | solution.py:40
  62.7 1.6 %fusion.14 = f32[4,192,384]{2,1,0:T(8,128)} fusion(bf16[4,192,384]{2,1,0:T(8,128)(2,1)S(1)} %convolution_convert_fusion.1, bf16[1,1,4,384,384]{4,3,2,1,0:T(8,128)(2,1)S(1)} %copy-done), kind=kOutput, calls=%fused_computation.30 | convolution fusion | flops 226492416 | bytes 2949120 | tf_op jit(solution)/shard_map/fry,fyx->frx/dot_general | solution.py:48
  64.9 2.9 %all-to-all-start.1 = ((bf16[32,4,192]{2,1,0:T(4,128)(2,1)}), bf16[32,4,192]{2,1,0:T(4,128)(2,1)S(1)}, u32[]{:S(2)}, u32[]{:S(2)}) async-start(bf16[32,4,192]{2,1,0:T(4,128)(2,1)} %broadcast_in_dim.9), calls=%async_computation.1 | async-start | bytes 131072 | tf_op jit(solution)/shard_map/all_to_all | solution.py:23
  67.8 3.2 %fusion.2 = f32[4,192,384]{2,1,0:T(8,128)} fusion(f32[4,192,384]{2,1,0:T(8,128)} %fusion.14, bf16[1,1,4,384,384]{4,3,2,1,0:T(8,128)(2,1)S(1)} %copy-done, f32[4]{0:T(128)S(1)} %copy-done.25), kind=kOutput, calls=%fused_computation.6 | convolution fusion | flops 227377152 | bytes 3538960 | tf_op jit(solution)/shard_map/fry,fyx->frx/dot_general | solution.py:48
  71.0 4.2 %all-to-all-done.1 = bf16[32,4,192]{2,1,0:T(4,128)(2,1)S(1)} async-done(((bf16[32,4,192]{2,1,0:T(4,128)(2,1)}), bf16[32,4,192]{2,1,0:T(4,128)(2,1)S(1)}, u32[]{:S(2)}, u32[]{:S(2)}) %all-to-all-start.1) | async-done | bytes 49184 | tf_op jit(solution)/shard_map/all_to_all | solution.py:23
  76.0 2.0 %convolution_convert_fusion = bf16[4,192,384]{2,1,0:T(8,128)(2,1)S(1)} fusion(f32[4,192,384]{2,1,0:T(8,128)} %fusion.2, bf16[1,1,4,384,384]{4,3,2,1,0:T(8,128)(2,1)S(1)} %copy-done.1, pred[4,4,384]{2,0,1:T(4,128)(4,1)S(1)} %broadcast_compare_fusion, bf16[4,192]{1,0:T(4,128)(2,1)} %get-tuple-element.22, bf16[4,192]{1,0:T(4,128)(2,1)} %get-tuple-element.23, ...), kind=kOutput, calls=%fused_computation.16 | convolution fusion | flops 234505728 | bytes 2959872 | tf_op jit(solution)/shard_map/fry,fyx->frx/dot_general | solution.py:48
  78.1 2.5 %collective-permute-start.8 = (bf16[1,192,384]{2,1,0:T(8,128)(2,1)S(1)}, bf16[1,192,384]{2,1,0:T(8,128)(2,1)S(1)}, u32[]{:S(2)}, u32[]{:S(2)}) collective-permute-start(bf16[1,192,384]{2,1,0:T(8,128)(2,1)S(1)} %get-tuple-element.9), channel_id=1, source_target_pairs={{0,2},{2,4},{4,6},{6,8},{8,10},{10,12},{12,14},{14,16},{16,18},{18... | collective-permute-start | bytes 442376 | tf_op jit(solution)/shard_map/ppermute | solution.py:12
  81.9 3.0 %collective-permute-start.10 = (bf16[1,192,384]{2,1,0:T(8,128)(2,1)S(1)}, bf16[1,192,384]{2,1,0:T(8,128)(2,1)S(1)}, u32[]{:S(2)}, u32[]{:S(2)}) collective-permute-start(bf16[1,192,384]{2,1,0:T(8,128)(2,1)S(1)} %get-tuple-element.11), channel_id=1, source_target_pairs={{0,1},{2,3},{4,5},{6,7},{8,9},{10,11},{12,13},{14,15},{16,17},{18,... | collective-permute-start | bytes 442376 | tf_op jit(solution)/shard_map/ppermute | solution.py:12
  85.0 1.4 %collective-permute-start.9 = (bf16[1,192,384]{2,1,0:T(8,128)(2,1)S(1)}, bf16[1,192,384]{2,1,0:T(8,128)(2,1)S(1)}, u32[]{:S(2)}, u32[]{:S(2)}) collective-permute-start(bf16[1,192,384]{2,1,0:T(8,128)(2,1)S(1)} %get-tuple-element.12), channel_id=1, source_target_pairs={{2,0},{4,2},{6,4},{8,6},{10,8},{12,10},{14,12},{16,14},{18,16},{20... | collective-permute-start | bytes 442376 | tf_op jit(solution)/shard_map/ppermute | solution.py:15
  86.4 5.7 %collective-permute-done.9 = bf16[1,192,384]{2,1,0:T(8,128)(2,1)S(1)} collective-permute-done((bf16[1,192,384]{2,1,0:T(8,128)(2,1)S(1)}, bf16[1,192,384]{2,1,0:T(8,128)(2,1)S(1)}, u32[]{:S(2)}, u32[]{:S(2)}) %collective-permute-start.9) | collective-permute-done | bytes 147488 | tf_op jit(solution)/shard_map/ppermute | solution.py:15
  94.6 12.2 %all_to_all.15 = f32[32,1,2,192]{3,2,1,0:T(2,128)S(1)} all-to-all(f32[32,1,2,192]{3,2,1,0:T(2,128)S(1)} %broadcast_in_dim.10), channel_id=1, replica_groups=mesh['gx'=16,'gy'=2] {'gx','gy'}, dimensions={0} | all-to-all | bytes 98304 | tf_op jit(solution)/shard_map/all_to_all | solution.py:23
  106.9 2.4 %fusion.31 = bf16[1,1,4,192,384]{4,3,2,1,0:T(8,128)(2,1)} fusion(bf16[4,192,384]{2,1,0:T(8,128)(2,1)S(1)} %convolution_convert_fusion, bf16[4,192,384]{2,1,0:T(8,128)(2,1)S(1)} %convolution_convert_fusion.2, f32[192]{0:T(256)S(1)} %bitcast.128, bf16[1,192,384]{2,1,0:T(8,128)(2,1)} %copy-done.18, bf16[1,192,384]{2,1,0:T(8,128)(2,1)} %copy-done.19, ...), kind=kLoop, calls=%fused_computation.52 | loop fusion | flops 6782976 | bytes 4129536 | tf_op jit(solution)/shard_map/broadcast_in_dim | solution.py:126
  (114 shorter events, 18.4 us)
Async XLA Ops:
  0.0 22.3 %copy-start = (bf16[1,1,4,384,384]{4,3,2,1,0:T(8,128)(2,1)S(1)}, bf16[1,1,4,384,384]{4,3,2,1,0:T(8,128)(2,1)}, u32[]{:S(2)}) copy-start(bf16[1,1,4,384,384]{4,3,2,1,0:T(8,128)(2,1)} %param.10) | copy-start | bytes 3538948
  0.0 11.9 %copy-start.2 = (bf16[1,1,4,384,384]{4,3,2,1,0:T(8,128)(2,1)S(1)}, bf16[1,1,4,384,384]{4,3,2,1,0:T(8,128)(2,1)}, u32[]{:S(2)}) copy-start(bf16[1,1,4,384,384]{4,3,2,1,0:T(8,128)(2,1)} %param.8) | copy-start | bytes 3538948
  1.3 11.6 %collective-permute-start = (bf16[1,192,384]{2,1,0:T(8,128)(2,1)S(1)}, bf16[1,192,384]{2,1,0:T(8,128)(2,1)S(1)}, u32[]{:S(2)}, u32[]{:S(2)}) collective-permute-start(bf16[1,192,384]{2,1,0:T(8,128)(2,1)S(1)} %get-tuple-element.17), channel_id=1, source_target_pairs={{0,2},{2,4},{4,6},{6,8},{8,10},{10,12},{12,14},{14,16},{16,18},{18... | collective-permute-start | bytes 442376 | tf_op jit(solution)/shard_map/ppermute | solution.py:12
  6.2 8.2 %collective-permute-start.1 = (bf16[1,192,384]{2,1,0:T(8,128)(2,1)S(1)}, bf16[1,192,384]{2,1,0:T(8,128)(2,1)S(1)}, u32[]{:S(2)}, u32[]{:S(2)}) collective-permute-start(bf16[1,192,384]{2,1,0:T(8,128)(2,1)S(1)} %get-tuple-element.18), channel_id=1, source_target_pairs={{2,0},{4,2},{6,4},{8,6},{10,8},{12,10},{14,12},{16,14},{18,16},{20... | collective-permute-start | bytes 442376 | tf_op jit(solution)/shard_map/ppermute | solution.py:15
  7.5 6.9 %collective-permute-start.3 = (bf16[1,192,384]{2,1,0:T(8,128)(2,1)S(1)}, bf16[1,192,384]{2,1,0:T(8,128)(2,1)S(1)}, u32[]{:S(2)}, u32[]{:S(2)}) collective-permute-start(bf16[1,192,384]{2,1,0:T(8,128)(2,1)S(1)} %get-tuple-element.19), channel_id=1, source_target_pairs={{1,0},{3,2},{5,4},{7,6},{9,8},{11,10},{13,12},{15,14},{17,16},{19,... | collective-permute-start | bytes 442376 | tf_op jit(solution)/shard_map/ppermute | solution.py:15
  8.8 5.6 %collective-permute-start.2 = (bf16[1,192,384]{2,1,0:T(8,128)(2,1)S(1)}, bf16[1,192,384]{2,1,0:T(8,128)(2,1)S(1)}, u32[]{:S(2)}, u32[]{:S(2)}) collective-permute-start(bf16[1,192,384]{2,1,0:T(8,128)(2,1)S(1)} %get-tuple-element.20), channel_id=1, source_target_pairs={{0,1},{2,3},{4,5},{6,7},{8,9},{10,11},{12,13},{14,15},{16,17},{18,... | collective-permute-start | bytes 442376 | tf_op jit(solution)/shard_map/ppermute | solution.py:12
  13.0 9.8 %copy-start.24 = (f32[4]{0:T(128)}, f32[4]{0:T(128)S(1)}, u32[]{:S(2)}) copy-start(f32[4]{0:T(128)S(1)} %multiply_bitcast_fusion) | copy-start | bytes 52
  16.1 13.6 %all-to-all-start = ((bf16[32,4,192]{2,1,0:T(4,128)(2,1)}), bf16[32,4,192]{2,1,0:T(4,128)(2,1)}, u32[]{:S(2)}, u32[]{:S(2)}) async-start(bf16[32,4,192]{2,1,0:T(4,128)(2,1)} %broadcast_in_dim.8), calls=%async_computation | async-start | bytes 131072 | tf_op jit(solution)/shard_map/all_to_all | solution.py:23
  22.8 7.7 %copy-start.23 = (f32[4,128]{1,0:T(4,128)S(1)}, f32[4,128]{1,0:T(4,128)}, u32[]{:S(2)}) copy-start(f32[4,128]{1,0:T(4,128)} %param.11) | copy-start | bytes 6148
  34.3 10.3 %collective-permute-start.7 = (bf16[576,384]{1,0:T(8,128)(2,1)S(1)}, bf16[576,384]{1,0:T(8,128)(2,1)S(1)}, u32[]{:S(2)}, u32[]{:S(2)}) collective-permute-start(bf16[576,384]{1,0:T(8,128)(2,1)S(1)} %pad_maximum_fusion.9), channel_id=1, source_target_pairs={{1,0},{3,2},{5,4},{7,6},{9,8},{11,10},{13,12},{15,14},{17,16},{19,... | collective-permute-start | bytes 1327112 | tf_op jit(solution)/shard_map/ppermute | solution.py:40
  35.6 23.8 %copy-start.3 = (bf16[1,1,4,384,384]{4,3,2,1,0:T(8,128)(2,1)S(1)}, bf16[1,1,4,384,384]{4,3,2,1,0:T(8,128)(2,1)}, u32[]{:S(2)}) copy-start(bf16[1,1,4,384,384]{4,3,2,1,0:T(8,128)(2,1)} %param.8) | copy-start | bytes 3538948
  35.7 14.9 %collective-permute-start.5 = (bf16[576,384]{1,0:T(8,128)(2,1)S(1)}, bf16[576,384]{1,0:T(8,128)(2,1)S(1)}, u32[]{:S(2)}, u32[]{:S(2)}) collective-permute-start(bf16[576,384]{1,0:T(8,128)(2,1)S(1)} %pad_maximum_fusion.7), channel_id=1, source_target_pairs={{2,0},{4,2},{6,4},{8,6},{10,8},{12,10},{14,12},{16,14},{18,16},{20... | collective-permute-start | bytes 1327112 | tf_op jit(solution)/shard_map/ppermute | solution.py:40
  37.2 13.4 %collective-permute-start.6 = (bf16[576,384]{1,0:T(8,128)(2,1)S(1)}, bf16[576,384]{1,0:T(8,128)(2,1)S(1)}, u32[]{:S(2)}, u32[]{:S(2)}) collective-permute-start(bf16[576,384]{1,0:T(8,128)(2,1)S(1)} %pad_maximum_fusion.8), channel_id=1, source_target_pairs={{0,1},{2,3},{4,5},{6,7},{8,9},{10,11},{12,13},{14,15},{16,17},{18,... | collective-permute-start | bytes 1327112 | tf_op jit(solution)/shard_map/ppermute | solution.py:40
  40.3 19.1 %collective-permute-start.4 = (bf16[576,384]{1,0:T(8,128)(2,1)S(1)}, bf16[576,384]{1,0:T(8,128)(2,1)S(1)}, u32[]{:S(2)}, u32[]{:S(2)}) collective-permute-start(bf16[576,384]{1,0:T(8,128)(2,1)S(1)} %pad_maximum_fusion.6), channel_id=1, source_target_pairs={{0,2},{2,4},{4,6},{6,8},{8,10},{10,12},{12,14},{14,16},{16,18},{18... | collective-permute-start | bytes 1327112 | tf_op jit(solution)/shard_map/ppermute | solution.py:40
  44.6 15.3 %copy-start.7 = (bf16[576,384]{1,0:T(8,128)(2,1)}, bf16[576,384]{1,0:T(8,128)(2,1)S(1)}, u32[]{:S(2)}) copy-start(bf16[576,384]{1,0:T(8,128)(2,1)S(1)} %collective-permute-done.7) | copy-start | bytes 1327108
  50.6 9.4 %copy-start.9 = (bf16[576,384]{1,0:T(8,128)(2,1)}, bf16[576,384]{1,0:T(8,128)(2,1)S(1)}, u32[]{:S(2)}) copy-start(bf16[576,384]{1,0:T(8,128)(2,1)S(1)} %collective-permute-done.5) | copy-start | bytes 1327108
  50.6 9.4 %copy-start.11 = (bf16[576,384]{1,0:T(8,128)(2,1)}, bf16[576,384]{1,0:T(8,128)(2,1)S(1)}, u32[]{:S(2)}) copy-start(bf16[576,384]{1,0:T(8,128)(2,1)S(1)} %collective-permute-done.6) | copy-start | bytes 1327108
  64.9 10.3 %all-to-all-start.1 = ((bf16[32,4,192]{2,1,0:T(4,128)(2,1)}), bf16[32,4,192]{2,1,0:T(4,128)(2,1)S(1)}, u32[]{:S(2)}, u32[]{:S(2)}) async-start(bf16[32,4,192]{2,1,0:T(4,128)(2,1)} %broadcast_in_dim.9), calls=%async_computation.1 | async-start | bytes 131072 | tf_op jit(solution)/shard_map/all_to_all | solution.py:23
  78.0 14.1 %copy-start.6 = (f32[4,192,384]{2,1,0:T(8,128)S(1)}, f32[4,192,384]{2,1,0:T(8,128)}, u32[]{:S(2)}) copy-start(f32[4,192,384]{2,1,0:T(8,128)} %copy-done.5) | copy-start | bytes 3538948
  78.1 8.3 %collective-permute-start.8 = (bf16[1,192,384]{2,1,0:T(8,128)(2,1)S(1)}, bf16[1,192,384]{2,1,0:T(8,128)(2,1)S(1)}, u32[]{:S(2)}, u32[]{:S(2)}) collective-permute-start(bf16[1,192,384]{2,1,0:T(8,128)(2,1)S(1)} %get-tuple-element.9), channel_id=1, source_target_pairs={{0,2},{2,4},{4,6},{6,8},{8,10},{10,12},{12,14},{14,16},{16,18},{18... | collective-permute-start | bytes 442376 | tf_op jit(solution)/shard_map/ppermute | solution.py:12
  80.6 5.8 %collective-permute-start.11 = (bf16[1,192,384]{2,1,0:T(8,128)(2,1)S(1)}, bf16[1,192,384]{2,1,0:T(8,128)(2,1)S(1)}, u32[]{:S(2)}, u32[]{:S(2)}) collective-permute-start(bf16[1,192,384]{2,1,0:T(8,128)(2,1)S(1)} %get-tuple-element.10), channel_id=1, source_target_pairs={{1,0},{3,2},{5,4},{7,6},{9,8},{11,10},{13,12},{15,14},{17,16},{19,... | collective-permute-start | bytes 442376 | tf_op jit(solution)/shard_map/ppermute | solution.py:15
  81.9 4.5 %collective-permute-start.10 = (bf16[1,192,384]{2,1,0:T(8,128)(2,1)S(1)}, bf16[1,192,384]{2,1,0:T(8,128)(2,1)S(1)}, u32[]{:S(2)}, u32[]{:S(2)}) collective-permute-start(bf16[1,192,384]{2,1,0:T(8,128)(2,1)S(1)} %get-tuple-element.11), channel_id=1, source_target_pairs={{0,1},{2,3},{4,5},{6,7},{8,9},{10,11},{12,13},{14,15},{16,17},{18,... | collective-permute-start | bytes 442376 | tf_op jit(solution)/shard_map/ppermute | solution.py:12
  84.9 7.5 %copy-start.4 = (bf16[1,1,4,384,384]{4,3,2,1,0:T(8,128)(2,1)S(1)}, bf16[1,1,4,384,384]{4,3,2,1,0:T(8,128)(2,1)}, u32[]{:S(2)}) copy-start(bf16[1,1,4,384,384]{4,3,2,1,0:T(8,128)(2,1)} %param.8) | copy-start | bytes 3538948
  85.0 7.2 %collective-permute-start.9 = (bf16[1,192,384]{2,1,0:T(8,128)(2,1)S(1)}, bf16[1,192,384]{2,1,0:T(8,128)(2,1)S(1)}, u32[]{:S(2)}, u32[]{:S(2)}) collective-permute-start(bf16[1,192,384]{2,1,0:T(8,128)(2,1)S(1)} %get-tuple-element.12), channel_id=1, source_target_pairs={{2,0},{4,2},{6,4},{8,6},{10,8},{12,10},{14,12},{16,14},{18,16},{20... | collective-permute-start | bytes 442376 | tf_op jit(solution)/shard_map/ppermute | solution.py:15
  (26 other events, 53.5 us)

commit v10 on v8

--- a/solution.py
+++ b/solution.py
@@ -106,7 +106,10 @@
         bent_partner = to_half(face_mul(field_half, schur_partner))
         return bent_own + bent_partner
 
-    resid0 = loads_here.astype(jnp.float32) + face_pairs(loads_here).astype(jnp.float32)
+    load_partner = jnp.stack(
+        [from_partner(loads_here[face], axis, from_lower) for axis, from_lower, face in PARTNERS]
+    )
+    resid0 = loads_here.astype(jnp.float32) + load_partner.astype(jnp.float32)
     first, schur_partner = precondition(resid0, None)
     resid1 = resid0 - apply_operator(first, schur_partner)
     second, _ = precondition(resid1, schur_partner)

time: 110 us -> 110 us (level)
    ppermute x4 -> x8, starting transfers between devices: 10.1 us -> 20.7 us  [from_partner(): return lax.ppermute(values, axis, pairs)]
    ppermute x4 -> x2, starting transfers between devices: 13.5 us -> 5.52 us  [with_halo(): lax.ppermute(lax.slice_in_dim(block, block.shape[dim] - width, None, axis...]
    ppermute x4 -> x2, starting transfers between devices: 5.3 us -> 2.72 us  [with_halo(): lax.ppermute(lax.slice_in_dim(block, 0, width, axis=dim), axis, backward)]
    squeeze x0 -> x1, local copies, waits for them, and re-layouts: none -> 1.33 us  [per_device(): loads_here[face]]
    slice x2 -> x1, local copies, waits for them, and re-layouts: 1.39 us -> 0.06 us  [with_halo(): lax.slice_in_dim(block, block.shape[dim] - width, None, axis=dim)]
    ppermute x4 -> x8, waiting for transfers between devices: 14.7 us -> 15.7 us  [from_partner(): return lax.ppermute(values, axis, pairs)]
    ppermute x4 -> x2, waiting for transfers between devices: 6.6 us -> 5.68 us  [with_halo(): lax.ppermute(lax.slice_in_dim(block, 0, width, axis=dim), axis, backward)]
where the time goes in v10:
time: 110 us; the launch traced here: 109 us
  starting transfers between devices  38.1 us (35%)
  waiting for transfers between devices  30.7 us (28%)
  matrix products  16.4 us (15%)
  blocking collectives  12.2 us (11%)
  local copies, waits for them, and re-layouts  7.71 us (7%)
  other arithmetic  3.48 us (3%)
    ppermute x8, starting transfers between devices, from_partner(): return lax.ppermute(values, axis, pairs)  20.7 us
    ppermute x8, waiting for transfers between devices, from_partner(): return lax.ppermute(values, axis, pairs)  15.7 us
    all_to_all x1, blocking collectives, gather_rows(): swapped = lax.all_to_all(spread, axes, 0, 0, tiled=False)  12.2 us
    dot_general x10, matrix products, face_mul(): jnp.einsum('fry,fyx->frx', vectors, matrices, preferred_element_type=jnp....  10.3 us
    all_to_all x2, waiting for transfers between devices, gather_rows(): swapped = lax.all_to_all(spread, axes, 0, 0, tiled=False)  9.4 us
    all_to_all x2, starting transfers between devices, gather_rows(): swapped = lax.all_to_all(spread, axes, 0, 0, tiled=False)  9.17 us
    ppermute x2, waiting for transfers between devices, with_halo(): lax.ppermute(lax.slice_in_dim(block, 0, width, axis=dim), axis, backward)  5.68 us
    ppermute x2, starting transfers between devices, with_halo(): lax.ppermute(lax.slice_in_dim(block, block.shape[dim] - width, None, axis...  5.52 us
  transfers between devices with their start and end apart: 14, of which 6 were waited for; matrix products, arithmetic and copies ran while one was open for 6% of the time, Pallas kernels for 0%

profile of v10, /device:TPU:0, one launch (start us, length us, event | category | flops | bytes accessed | tf_op | source)
XLA Modules:
  0.0 109.2 jit_solution(16863599994584414499)
XLA Ops:
  0.0 1.3 %slice_bitcast_fusion.11 = (bf16[192,384]{1,0:T(8,128)(2,1)S(1)}, bf16[192,384]{1,0:T(8,128)(2,1)S(1)}, bf16[192,384]{1,0:T(8,128)(2,1)S(1)}, bf16[192,384]{1,0:T(8,128)(2,1)S(1)}) fusion(bf16[1,1,4,192,384]{4,3,2,1,0:T(8,128)(2,1)} %param.7), kind=kLoop, calls=%fused_computation.75 | loop fusion | bytes 1179648 | tf_op jit(solution)/shard_map/squeeze | solution.py:110
  1.3 4.9 %collective-permute-start = (bf16[192,384]{1,0:T(8,128)(2,1)S(1)}, bf16[192,384]{1,0:T(8,128)(2,1)S(1)}, u32[]{:S(2)}, u32[]{:S(2)}) collective-permute-start(bf16[192,384]{1,0:T(8,128)(2,1)S(1)} %get-tuple-element.17), channel_id=1, source_target_pairs={{0,2},{2,4},{4,6},{6,8},{8,10},{10,12},{12,14},{14,16},{16,18},{18... | collective-permute-start | bytes 442376 | tf_op jit(solution)/shard_map/ppermute | solution.py:40
  6.2 1.3 %collective-permute-start.1 = (bf16[192,384]{1,0:T(8,128)(2,1)S(1)}, bf16[192,384]{1,0:T(8,128)(2,1)S(1)}, u32[]{:S(2)}, u32[]{:S(2)}) collective-permute-start(bf16[192,384]{1,0:T(8,128)(2,1)S(1)} %get-tuple-element.18), channel_id=1, source_target_pairs={{2,0},{4,2},{6,4},{8,6},{10,8},{12,10},{14,12},{16,14},{18,16},{20... | collective-permute-start | bytes 442376 | tf_op jit(solution)/shard_map/ppermute | solution.py:40
  8.8 3.2 %collective-permute-start.2 = (bf16[192,384]{1,0:T(8,128)(2,1)S(1)}, bf16[192,384]{1,0:T(8,128)(2,1)S(1)}, u32[]{:S(2)}, u32[]{:S(2)}) collective-permute-start(bf16[192,384]{1,0:T(8,128)(2,1)S(1)} %get-tuple-element.20), channel_id=1, source_target_pairs={{0,1},{2,3},{4,5},{6,7},{8,9},{10,11},{12,13},{14,15},{16,17},{18,... | collective-permute-start | bytes 442376 | tf_op jit(solution)/shard_map/ppermute | solution.py:40
  16.1 6.3 %all-to-all-start = ((bf16[32,4,192]{2,1,0:T(4,128)(2,1)}), bf16[32,4,192]{2,1,0:T(4,128)(2,1)}, u32[]{:S(2)}, u32[]{:S(2)}) async-start(bf16[32,4,192]{2,1,0:T(4,128)(2,1)} %broadcast_in_dim.8), calls=%async_computation | async-start | bytes 131072 | tf_op jit(solution)/shard_map/all_to_all | solution.py:23
  22.9 1.6 %fusion.5 = f32[4,192,384]{2,1,0:T(8,128)} fusion(f32[4,192,384]{2,1,0:T(8,128)S(1)} %fusion.17, bf16[1,1,4,384,384]{4,3,2,1,0:T(8,128)(2,1)S(1)} %copy-done, f32[4]{0:T(128)S(1)} %copy-done.25), kind=kOutput, calls=%fused_computation.11 | convolution fusion | flops 227377152 | bytes 3538960 | tf_op jit(solution)/shard_map/fry,fyx->frx/dot_general | solution.py:48
  24.5 5.2 %all-to-all-done = bf16[32,4,192]{2,1,0:T(4,128)(2,1)} async-done(((bf16[32,4,192]{2,1,0:T(4,128)(2,1)}), bf16[32,4,192]{2,1,0:T(4,128)(2,1)}, u32[]{:S(2)}, u32[]{:S(2)}) %all-to-all-start) | async-done | bytes 49184 | tf_op jit(solution)/shard_map/all_to_all | solution.py:23
  30.8 2.0 %fusion.8 = bf16[4,192,384]{2,1,0:T(8,128)(2,1)S(1)} fusion(f32[4,192,384]{2,1,0:T(8,128)} %fusion.5, f32[192,4,1]{0,1,2:T(4,128)S(1)} %convolution_bitcast_fusion.5, s32[4,384]{1,0:T(4,128)S(1)} %multiply_add_fusion, s32[4]{0:T(128)S(1)} %bitcast.123), kind=kOutput, calls=%fused_computation.16 | convolution fusion | flops 14751744 | bytes 1778704 | tf_op jit(solution)/shard_map/kfx,kr->frx/dot_general | solution.py:88
  35.7 1.4 %collective-permute-start.5 = (bf16[576,384]{1,0:T(8,128)(2,1)S(1)}, bf16[576,384]{1,0:T(8,128)(2,1)S(1)}, u32[]{:S(2)}, u32[]{:S(2)}) collective-permute-start(bf16[576,384]{1,0:T(8,128)(2,1)S(1)} %pad_maximum_fusion.7), channel_id=1, source_target_pairs={{2,0},{4,2},{6,4},{8,6},{10,8},{12,10},{14,12},{16,14},{18,16},{20... | collective-permute-start | bytes 1327112 | tf_op jit(solution)/shard_map/ppermute | solution.py:40
  37.2 3.1 %collective-permute-start.6 = (bf16[576,384]{1,0:T(8,128)(2,1)S(1)}, bf16[576,384]{1,0:T(8,128)(2,1)S(1)}, u32[]{:S(2)}, u32[]{:S(2)}) collective-permute-start(bf16[576,384]{1,0:T(8,128)(2,1)S(1)} %pad_maximum_fusion.8), channel_id=1, source_target_pairs={{0,1},{2,3},{4,5},{6,7},{8,9},{10,11},{12,13},{14,15},{16,17},{18,... | collective-permute-start | bytes 1327112 | tf_op jit(solution)/shard_map/ppermute | solution.py:40
  40.3 4.3 %collective-permute-start.4 = (bf16[576,384]{1,0:T(8,128)(2,1)S(1)}, bf16[576,384]{1,0:T(8,128)(2,1)S(1)}, u32[]{:S(2)}, u32[]{:S(2)}) collective-permute-start(bf16[576,384]{1,0:T(8,128)(2,1)S(1)} %pad_maximum_fusion.6), channel_id=1, source_target_pairs={{0,2},{2,4},{4,6},{6,8},{8,10},{10,12},{12,14},{14,16},{16,18},{18... | collective-permute-start | bytes 1327112 | tf_op jit(solution)/shard_map/ppermute | solution.py:40
  44.6 5.9 %collective-permute-done.5 = bf16[576,384]{1,0:T(8,128)(2,1)S(1)} collective-permute-done((bf16[576,384]{1,0:T(8,128)(2,1)S(1)}, bf16[576,384]{1,0:T(8,128)(2,1)S(1)}, u32[]{:S(2)}, u32[]{:S(2)}) %collective-permute-start.5) | collective-permute-done | bytes 442400 | tf_op jit(solution)/shard_map/ppermute | solution.py:40
  50.6 8.8 %collective-permute-done.4 = bf16[576,384]{1,0:T(8,128)(2,1)S(1)} collective-permute-done((bf16[576,384]{1,0:T(8,128)(2,1)S(1)}, bf16[576,384]{1,0:T(8,128)(2,1)S(1)}, u32[]{:S(2)}, u32[]{:S(2)}) %collective-permute-start.4) | collective-permute-done | bytes 442400 | tf_op jit(solution)/shard_map/ppermute | solution.py:40
  62.7 1.6 %fusion.14 = f32[4,192,384]{2,1,0:T(8,128)} fusion(bf16[4,192,384]{2,1,0:T(8,128)(2,1)S(1)} %convolution_convert_fusion.1, bf16[1,1,4,384,384]{4,3,2,1,0:T(8,128)(2,1)S(1)} %copy-done), kind=kOutput, calls=%fused_computation.30 | convolution fusion | flops 226492416 | bytes 2949120 | tf_op jit(solution)/shard_map/fry,fyx->frx/dot_general | solution.py:48
  64.9 2.9 %all-to-all-start.1 = ((bf16[32,4,192]{2,1,0:T(4,128)(2,1)}), bf16[32,4,192]{2,1,0:T(4,128)(2,1)S(1)}, u32[]{:S(2)}, u32[]{:S(2)}) async-start(bf16[32,4,192]{2,1,0:T(4,128)(2,1)} %broadcast_in_dim.9), calls=%async_computation.1 | async-start | bytes 131072 | tf_op jit(solution)/shard_map/all_to_all | solution.py:23
  67.8 3.2 %fusion.2 = f32[4,192,384]{2,1,0:T(8,128)} fusion(f32[4,192,384]{2,1,0:T(8,128)} %fusion.14, bf16[1,1,4,384,384]{4,3,2,1,0:T(8,128)(2,1)S(1)} %copy-done, f32[4]{0:T(128)S(1)} %copy-done.26), kind=kOutput, calls=%fused_computation.5 | convolution fusion | flops 227377152 | bytes 3538960 | tf_op jit(solution)/shard_map/fry,fyx->frx/dot_general | solution.py:48
  71.0 4.2 %all-to-all-done.1 = bf16[32,4,192]{2,1,0:T(4,128)(2,1)S(1)} async-done(((bf16[32,4,192]{2,1,0:T(4,128)(2,1)}), bf16[32,4,192]{2,1,0:T(4,128)(2,1)S(1)}, u32[]{:S(2)}, u32[]{:S(2)}) %all-to-all-start.1) | async-done | bytes 49184 | tf_op jit(solution)/shard_map/all_to_all | solution.py:23
  75.4 2.0 %fusion.9 = bf16[4,192,384]{2,1,0:T(8,128)(2,1)S(1)} fusion(f32[4,192,384]{2,1,0:T(8,128)} %fusion.2, f32[192,4,1]{0,1,2:T(4,128)S(1)} %convolution_bitcast_fusion.4, s32[4,384]{1,0:T(4,128)S(1)} %multiply_add_fusion, s32[4]{0:T(128)S(1)} %bitcast.125), kind=kOutput, calls=%fused_computation.17 | convolution fusion | flops 14751744 | bytes 1778704 | tf_op jit(solution)/shard_map/kfx,kr->frx/dot_general | solution.py:88
  78.0 2.5 %collective-permute-start.8 = (bf16[1,192,384]{2,1,0:T(8,128)(2,1)S(1)}, bf16[1,192,384]{2,1,0:T(8,128)(2,1)S(1)}, u32[]{:S(2)}, u32[]{:S(2)}) collective-permute-start(bf16[1,192,384]{2,1,0:T(8,128)(2,1)S(1)} %get-tuple-element.9), channel_id=1, source_target_pairs={{0,2},{2,4},{4,6},{6,8},{8,10},{10,12},{12,14},{14,16},{16,18},{18... | collective-permute-start | bytes 442376 | tf_op jit(solution)/shard_map/ppermute | solution.py:12
  81.8 3.0 %collective-permute-start.10 = (bf16[1,192,384]{2,1,0:T(8,128)(2,1)S(1)}, bf16[1,192,384]{2,1,0:T(8,128)(2,1)S(1)}, u32[]{:S(2)}, u32[]{:S(2)}) collective-permute-start(bf16[1,192,384]{2,1,0:T(8,128)(2,1)S(1)} %get-tuple-element.11), channel_id=1, source_target_pairs={{0,1},{2,3},{4,5},{6,7},{8,9},{10,11},{12,13},{14,15},{16,17},{18,... | collective-permute-start | bytes 442376 | tf_op jit(solution)/shard_map/ppermute | solution.py:12
  84.9 1.4 %collective-permute-start.9 = (bf16[1,192,384]{2,1,0:T(8,128)(2,1)S(1)}, bf16[1,192,384]{2,1,0:T(8,128)(2,1)S(1)}, u32[]{:S(2)}, u32[]{:S(2)}) collective-permute-start(bf16[1,192,384]{2,1,0:T(8,128)(2,1)S(1)} %get-tuple-element.12), channel_id=1, source_target_pairs={{2,0},{4,2},{6,4},{8,6},{10,8},{12,10},{14,12},{16,14},{18,16},{20... | collective-permute-start | bytes 442376 | tf_op jit(solution)/shard_map/ppermute | solution.py:15
  86.4 5.7 %collective-permute-done.9 = bf16[1,192,384]{2,1,0:T(8,128)(2,1)S(1)} collective-permute-done((bf16[1,192,384]{2,1,0:T(8,128)(2,1)S(1)}, bf16[1,192,384]{2,1,0:T(8,128)(2,1)S(1)}, u32[]{:S(2)}, u32[]{:S(2)}) %collective-permute-start.9) | collective-permute-done | bytes 147488 | tf_op jit(solution)/shard_map/ppermute | solution.py:15
  94.5 12.2 %all_to_all.15 = f32[32,1,2,192]{3,2,1,0:T(2,128)S(1)} all-to-all(f32[32,1,2,192]{3,2,1,0:T(2,128)S(1)} %broadcast_in_dim.10), channel_id=1, replica_groups=mesh['gx'=16,'gy'=2] {'gx','gy'}, dimensions={0} | all-to-all | bytes 98304 | tf_op jit(solution)/shard_map/all_to_all | solution.py:23
  106.8 2.4 %fusion.31 = bf16[1,1,4,192,384]{4,3,2,1,0:T(8,128)(2,1)} fusion(bf16[4,192,384]{2,1,0:T(8,128)(2,1)S(1)} %convolution_convert_fusion, bf16[4,192,384]{2,1,0:T(8,128)(2,1)S(1)} %convolution_convert_fusion.2, f32[192]{0:T(256)S(1)} %bitcast.126, bf16[1,192,384]{2,1,0:T(8,128)(2,1)} %copy-done.18, bf16[1,192,384]{2,1,0:T(8,128)(2,1)} %copy-done.19, ...), kind=kLoop, calls=%fused_computation.52 | loop fusion | flops 6782976 | bytes 4129536 | tf_op jit(solution)/shard_map/broadcast_in_dim | solution.py:123
  (115 shorter events, 18.2 us)
Async XLA Ops:
  0.0 22.4 %copy-start = (bf16[1,1,4,384,384]{4,3,2,1,0:T(8,128)(2,1)S(1)}, bf16[1,1,4,384,384]{4,3,2,1,0:T(8,128)(2,1)}, u32[]{:S(2)}) copy-start(bf16[1,1,4,384,384]{4,3,2,1,0:T(8,128)(2,1)} %param.10) | copy-start | bytes 3538948
  0.0 12.0 %copy-start.2 = (bf16[1,1,4,384,384]{4,3,2,1,0:T(8,128)(2,1)S(1)}, bf16[1,1,4,384,384]{4,3,2,1,0:T(8,128)(2,1)}, u32[]{:S(2)}) copy-start(bf16[1,1,4,384,384]{4,3,2,1,0:T(8,128)(2,1)} %param.8) | copy-start | bytes 3538948
  1.3 12.1 %collective-permute-start = (bf16[192,384]{1,0:T(8,128)(2,1)S(1)}, bf16[192,384]{1,0:T(8,128)(2,1)S(1)}, u32[]{:S(2)}, u32[]{:S(2)}) collective-permute-start(bf16[192,384]{1,0:T(8,128)(2,1)S(1)} %get-tuple-element.17), channel_id=1, source_target_pairs={{0,2},{2,4},{4,6},{6,8},{8,10},{10,12},{12,14},{14,16},{16,18},{18... | collective-permute-start | bytes 442376 | tf_op jit(solution)/shard_map/ppermute | solution.py:40
  6.2 8.2 %collective-permute-start.1 = (bf16[192,384]{1,0:T(8,128)(2,1)S(1)}, bf16[192,384]{1,0:T(8,128)(2,1)S(1)}, u32[]{:S(2)}, u32[]{:S(2)}) collective-permute-start(bf16[192,384]{1,0:T(8,128)(2,1)S(1)} %get-tuple-element.18), channel_id=1, source_target_pairs={{2,0},{4,2},{6,4},{8,6},{10,8},{12,10},{14,12},{16,14},{18,16},{20... | collective-permute-start | bytes 442376 | tf_op jit(solution)/shard_map/ppermute | solution.py:40
  7.5 6.9 %collective-permute-start.3 = (bf16[192,384]{1,0:T(8,128)(2,1)S(1)}, bf16[192,384]{1,0:T(8,128)(2,1)S(1)}, u32[]{:S(2)}, u32[]{:S(2)}) collective-permute-start(bf16[192,384]{1,0:T(8,128)(2,1)S(1)} %get-tuple-element.19), channel_id=1, source_target_pairs={{1,0},{3,2},{5,4},{7,6},{9,8},{11,10},{13,12},{15,14},{17,16},{19,... | collective-permute-start | bytes 442376 | tf_op jit(solution)/shard_map/ppermute | solution.py:40
  8.8 5.6 %collective-permute-start.2 = (bf16[192,384]{1,0:T(8,128)(2,1)S(1)}, bf16[192,384]{1,0:T(8,128)(2,1)S(1)}, u32[]{:S(2)}, u32[]{:S(2)}) collective-permute-start(bf16[192,384]{1,0:T(8,128)(2,1)S(1)} %get-tuple-element.20), channel_id=1, source_target_pairs={{0,1},{2,3},{4,5},{6,7},{8,9},{10,11},{12,13},{14,15},{16,17},{18,... | collective-permute-start | bytes 442376 | tf_op jit(solution)/shard_map/ppermute | solution.py:40
  16.1 13.7 %all-to-all-start = ((bf16[32,4,192]{2,1,0:T(4,128)(2,1)}), bf16[32,4,192]{2,1,0:T(4,128)(2,1)}, u32[]{:S(2)}, u32[]{:S(2)}) async-start(bf16[32,4,192]{2,1,0:T(4,128)(2,1)} %broadcast_in_dim.8), calls=%async_computation | async-start | bytes 131072 | tf_op jit(solution)/shard_map/all_to_all | solution.py:23
  22.9 7.7 %copy-start.23 = (f32[4,128]{1,0:T(4,128)S(1)}, f32[4,128]{1,0:T(4,128)}, u32[]{:S(2)}) copy-start(f32[4,128]{1,0:T(4,128)} %param.11) | copy-start | bytes 6148
  34.3 10.3 %collective-permute-start.7 = (bf16[576,384]{1,0:T(8,128)(2,1)S(1)}, bf16[576,384]{1,0:T(8,128)(2,1)S(1)}, u32[]{:S(2)}, u32[]{:S(2)}) collective-permute-start(bf16[576,384]{1,0:T(8,128)(2,1)S(1)} %pad_maximum_fusion.9), channel_id=1, source_target_pairs={{1,0},{3,2},{5,4},{7,6},{9,8},{11,10},{13,12},{15,14},{17,16},{19,... | collective-permute-start | bytes 1327112 | tf_op jit(solution)/shard_map/ppermute | solution.py:40
  35.6 23.8 %copy-start.3 = (bf16[1,1,4,384,384]{4,3,2,1,0:T(8,128)(2,1)S(1)}, bf16[1,1,4,384,384]{4,3,2,1,0:T(8,128)(2,1)}, u32[]{:S(2)}) copy-start(bf16[1,1,4,384,384]{4,3,2,1,0:T(8,128)(2,1)} %param.8) | copy-start | bytes 3538948
  35.7 14.9 %collective-permute-start.5 = (bf16[576,384]{1,0:T(8,128)(2,1)S(1)}, bf16[576,384]{1,0:T(8,128)(2,1)S(1)}, u32[]{:S(2)}, u32[]{:S(2)}) collective-permute-start(bf16[576,384]{1,0:T(8,128)(2,1)S(1)} %pad_maximum_fusion.7), channel_id=1, source_target_pairs={{2,0},{4,2},{6,4},{8,6},{10,8},{12,10},{14,12},{16,14},{18,16},{20... | collective-permute-start | bytes 1327112 | tf_op jit(solution)/shard_map/ppermute | solution.py:40
  37.2 13.4 %collective-permute-start.6 = (bf16[576,384]{1,0:T(8,128)(2,1)S(1)}, bf16[576,384]{1,0:T(8,128)(2,1)S(1)}, u32[]{:S(2)}, u32[]{:S(2)}) collective-permute-start(bf16[576,384]{1,0:T(8,128)(2,1)S(1)} %pad_maximum_fusion.8), channel_id=1, source_target_pairs={{0,1},{2,3},{4,5},{6,7},{8,9},{10,11},{12,13},{14,15},{16,17},{18,... | collective-permute-start | bytes 1327112 | tf_op jit(solution)/shard_map/ppermute | solution.py:40
  40.3 19.1 %collective-permute-start.4 = (bf16[576,384]{1,0:T(8,128)(2,1)S(1)}, bf16[576,384]{1,0:T(8,128)(2,1)S(1)}, u32[]{:S(2)}, u32[]{:S(2)}) collective-permute-start(bf16[576,384]{1,0:T(8,128)(2,1)S(1)} %pad_maximum_fusion.6), channel_id=1, source_target_pairs={{0,2},{2,4},{4,6},{6,8},{8,10},{10,12},{12,14},{14,16},{16,18},{18... | collective-permute-start | bytes 1327112 | tf_op jit(solution)/shard_map/ppermute | solution.py:40
  44.6 15.3 %copy-start.7 = (bf16[576,384]{1,0:T(8,128)(2,1)}, bf16[576,384]{1,0:T(8,128)(2,1)S(1)}, u32[]{:S(2)}) copy-start(bf16[576,384]{1,0:T(8,128)(2,1)S(1)} %collective-permute-done.7) | copy-start | bytes 1327108
  50.6 9.4 %copy-start.9 = (bf16[576,384]{1,0:T(8,128)(2,1)}, bf16[576,384]{1,0:T(8,128)(2,1)S(1)}, u32[]{:S(2)}) copy-start(bf16[576,384]{1,0:T(8,128)(2,1)S(1)} %collective-permute-done.5) | copy-start | bytes 1327108
  50.6 9.4 %copy-start.11 = (bf16[576,384]{1,0:T(8,128)(2,1)}, bf16[576,384]{1,0:T(8,128)(2,1)S(1)}, u32[]{:S(2)}) copy-start(bf16[576,384]{1,0:T(8,128)(2,1)S(1)} %collective-permute-done.6) | copy-start | bytes 1327108
  64.9 10.3 %all-to-all-start.1 = ((bf16[32,4,192]{2,1,0:T(4,128)(2,1)}), bf16[32,4,192]{2,1,0:T(4,128)(2,1)S(1)}, u32[]{:S(2)}, u32[]{:S(2)}) async-start(bf16[32,4,192]{2,1,0:T(4,128)(2,1)} %broadcast_in_dim.9), calls=%async_computation.1 | async-start | bytes 131072 | tf_op jit(solution)/shard_map/all_to_all | solution.py:23
  77.9 14.1 %copy-start.6 = (f32[4,192,384]{2,1,0:T(8,128)S(1)}, f32[4,192,384]{2,1,0:T(8,128)}, u32[]{:S(2)}) copy-start(f32[4,192,384]{2,1,0:T(8,128)} %copy-done.5) | copy-start | bytes 3538948
  78.0 8.3 %collective-permute-start.8 = (bf16[1,192,384]{2,1,0:T(8,128)(2,1)S(1)}, bf16[1,192,384]{2,1,0:T(8,128)(2,1)S(1)}, u32[]{:S(2)}, u32[]{:S(2)}) collective-permute-start(bf16[1,192,384]{2,1,0:T(8,128)(2,1)S(1)} %get-tuple-element.9), channel_id=1, source_target_pairs={{0,2},{2,4},{4,6},{6,8},{8,10},{10,12},{12,14},{14,16},{16,18},{18... | collective-permute-start | bytes 442376 | tf_op jit(solution)/shard_map/ppermute | solution.py:12
  80.5 5.8 %collective-permute-start.11 = (bf16[1,192,384]{2,1,0:T(8,128)(2,1)S(1)}, bf16[1,192,384]{2,1,0:T(8,128)(2,1)S(1)}, u32[]{:S(2)}, u32[]{:S(2)}) collective-permute-start(bf16[1,192,384]{2,1,0:T(8,128)(2,1)S(1)} %get-tuple-element.10), channel_id=1, source_target_pairs={{1,0},{3,2},{5,4},{7,6},{9,8},{11,10},{13,12},{15,14},{17,16},{19,... | collective-permute-start | bytes 442376 | tf_op jit(solution)/shard_map/ppermute | solution.py:15
  81.8 4.5 %collective-permute-start.10 = (bf16[1,192,384]{2,1,0:T(8,128)(2,1)S(1)}, bf16[1,192,384]{2,1,0:T(8,128)(2,1)S(1)}, u32[]{:S(2)}, u32[]{:S(2)}) collective-permute-start(bf16[1,192,384]{2,1,0:T(8,128)(2,1)S(1)} %get-tuple-element.11), channel_id=1, source_target_pairs={{0,1},{2,3},{4,5},{6,7},{8,9},{10,11},{12,13},{14,15},{16,17},{18,... | collective-permute-start | bytes 442376 | tf_op jit(solution)/shard_map/ppermute | solution.py:12
  84.8 7.5 %copy-start.4 = (bf16[1,1,4,384,384]{4,3,2,1,0:T(8,128)(2,1)S(1)}, bf16[1,1,4,384,384]{4,3,2,1,0:T(8,128)(2,1)}, u32[]{:S(2)}) copy-start(bf16[1,1,4,384,384]{4,3,2,1,0:T(8,128)(2,1)} %param.8) | copy-start | bytes 3538948
  84.9 7.2 %collective-permute-start.9 = (bf16[1,192,384]{2,1,0:T(8,128)(2,1)S(1)}, bf16[1,192,384]{2,1,0:T(8,128)(2,1)S(1)}, u32[]{:S(2)}, u32[]{:S(2)}) collective-permute-start(bf16[1,192,384]{2,1,0:T(8,128)(2,1)S(1)} %get-tuple-element.12), channel_id=1, source_target_pairs={{2,0},{4,2},{6,4},{8,6},{10,8},{12,10},{14,12},{16,14},{18,16},{20... | collective-permute-start | bytes 442376 | tf_op jit(solution)/shard_map/ppermute | solution.py:15
  86.3 6.6 %copy-start.17 = (bf16[1,192,384]{2,1,0:T(8,128)(2,1)}, bf16[1,192,384]{2,1,0:T(8,128)(2,1)S(1)}, u32[]{:S(2)}) copy-start(bf16[1,192,384]{2,1,0:T(8,128)(2,1)S(1)} %collective-permute-done.8) | copy-start | bytes 442372
  (26 other events, 56.0 us)

commit v11 on v3

--- a/solution.py
+++ b/solution.py
@@ -73,38 +73,90 @@
     picks_full = picks.astype(jnp.float32)
     flags_full = flag_values.astype(jnp.float32)
 
-    def add_coarse(piece):
-        return jnp.dot(coarse_inverse, piece.astype(jnp.float32), precision=lax.Precision.HIGHEST)
+    def add_coarse(rows, piece):
+        return jnp.dot(rows, piece, precision=lax.Precision.HIGHEST)
 
-    def precondition(resid):
-        scaled = face_mul_turned(resid.astype(jnp.bfloat16), deluxe_panel).astype(jnp.bfloat16)
-        local_part = face_mul(scaled, inverse_panel)
-        extra = face_mul(local_part.astype(jnp.bfloat16), inverse_panel)
-        softened = local_part + 0.5 * flags_full[:, None, None] * extra
+    rows = loads_here.shape[1]
+    coarse_width = coarse_inverse.shape[1]
+    small = jnp.concatenate(
+        [
+            coarse_inverse,
+            jnp.pad(
+                jnp.concatenate([primal_slots, flag_values]).astype(jnp.float32)[None],
+                ((0, 0), (0, coarse_width - 2 * primal_count)),
+            ),
+        ]
+    )
+    halo, small_y = [], []
+    for axis, from_lower, face in PARTNERS:
+        payload = loads_here[face]
+        if axis == "gy":
+            payload = jnp.concatenate(
+                [payload, deluxe_panel[face], inverse_panel[face], schur_panel[face]]
+            )
+            small_y.append(from_partner(small, axis, from_lower))
+        halo.append(from_partner(payload, axis, from_lower))
+    load_partner = jnp.stack([received[:rows] for received in halo])
+    mats_y = jnp.stack([received[rows:].reshape(3, width, width) for received in halo[2:]])
+    deluxe_y, panels_y, schur_y = mats_y[:, 0], mats_y[:, 1], mats_y[:, 2]
+    small_y = jnp.stack(small_y)
+    rows_y = small_y[:, :primal_count].reshape(-1, coarse_width)
+    slots_y = small_y[:, primal_count, :primal_count].astype(jnp.int32)
+    flags_y = jnp.stack(
+        [small_y[p, primal_count, primal_count + face] for p, (_, _, face) in enumerate(PARTNERS[2:])]
+    )
+    offsets_y = jnp.array([face * width for _, _, face in PARTNERS[2:]], jnp.int32)
+    picks_y = (
+        slots_y[:, :, None]
+        == (offsets_y[:, None, None] + jnp.arange(width, dtype=jnp.int32)[None, None, :])
+    ).astype(jnp.float32)
+
+    def softened_of(resid_half, deluxe_faces, panels_faces, flags):
+        scaled = face_mul_turned(resid_half, deluxe_faces).astype(jnp.bfloat16)
+        local_part = face_mul(scaled, panels_faces)
+        extra = face_mul(local_part.astype(jnp.bfloat16), panels_faces)
+        return scaled, lax.optimization_barrier(local_part + 0.5 * flags[:, None, None] * extra)
+
+    def precondition(resid, schur_x):
+        resid_half = resid.astype(jnp.bfloat16)
+        scaled, softened = softened_of(resid_half, deluxe_panel, inverse_panel, flags_full)
+        _, softened_y = softened_of(resid_half[2:4], deluxe_y, panels_y, flags_y)
         primal = jnp.einsum(
             "kfx,frx->kr", picks_half, scaled, preferred_element_type=jnp.float32
         ).astype(jnp.bfloat16)
-        coarse = add_coarse(gather_rows(primal, ("gx", "gy")))
+        primal_all = gather_rows(primal, ("gx", "gy")).astype(jnp.float32)
+        coarse = add_coarse(coarse_inverse, primal_all)
+        coarse_y = add_coarse(rows_y, primal_all).reshape(2, primal_count, -1)
         placed = jnp.einsum("kfx,kr->frx", picks_full, coarse, precision=lax.Precision.HIGHEST)
+        placed_y = jnp.einsum("pkx,pkr->prx", picks_y, coarse_y, precision=lax.Precision.HIGHEST)
         weighted = (softened + placed).astype(jnp.bfloat16)
+        weighted_y = (softened_y + placed_y).astype(jnp.bfloat16)
         spread = face_mul(weighted, deluxe_panel).astype(jnp.bfloat16)
-        return spread.astype(jnp.float32) + face_pairs(spread).astype(jnp.float32)
+        spread_y = to_half(face_mul(weighted_y, deluxe_y))
+        received = []
+        for axis, from_lower, face in PARTNERS[:2]:
+            payload = spread[face]
+            if schur_x is None:
+                payload = jnp.concatenate([payload, schur_panel[face]])
+            received.append(from_partner(payload, axis, from_lower))
+        received = jnp.stack(received)
+        if schur_x is None:
+            schur_x = received[:, rows:]
+        partner = jnp.concatenate([received[:, :rows].astype(jnp.float32), spread_y])
+        return spread.astype(jnp.float32) + partner, schur_x
 
-    schur_partner = jnp.stack(
-        [from_partner(schur_panel[face], axis, from_lower) for axis, from_lower, face in PARTNERS]
-    )
-
-    def apply_operator(field):
+    def apply_operator(field, schur_partner):
         field_half = field.astype(jnp.bfloat16)
         bent_own = to_half(face_mul(field_half, schur_panel))
         bent_partner = to_half(face_mul(field_half, schur_partner))
         return bent_own + bent_partner
 
-    resid0 = loads_here.astype(jnp.float32) + face_pairs(loads_here).astype(jnp.float32)
-    first = precondition(resid0)
-    resid1 = resid0 - apply_operator(first)
-    second = precondition(resid1)
-    curved = apply_operator(second)
+    resid0 = loads_here.astype(jnp.float32) + load_partner.astype(jnp.float32)
+    first, schur_x = precondition(resid0, None)
+    schur_partner = jnp.concatenate([schur_x, schur_y])
+    resid1 = resid0 - apply_operator(first, schur_partner)
+    second, _ = precondition(resid1, schur_x)
+    curved = apply_operator(second, schur_partner)
     partial = jnp.stack(
         [jnp.sum(resid1 * second, axis=(0, 2)), jnp.sum(second * curved, axis=(0, 2))]
     )

time: 114 us -> 124 us (1.088)
  starting transfers between devices: 46.8 us -> 34.7 us
  matrix products: 17 us -> 28.5 us
  local copies, waits for them, and re-layouts: 6.08 us -> 12.6 us
  other arithmetic: 3.28 us -> 7.51 us
    ppermute x12 -> x0, starting transfers between devices: 26.8 us -> none  [the longest x6 18.9 us: with_halo(): lax.ppermute(lax.slice_in_dim(block, block.shape[dim] - width, None, axis...]
    ppermute x4 -> x10, waiting for transfers between devices: 8.32 us -> 22.8 us  [from_partner(): return lax.ppermute(values, axis, pairs)]
    ppermute x4 -> x10, starting transfers between devices: 10.3 us -> 23.4 us  [from_partner(): return lax.ppermute(values, axis, pairs)]
    ppermute x12 -> x0, waiting for transfers between devices: 7.61 us -> none  [the longest x6 7.6 us: with_halo(): lax.ppermute(lax.slice_in_dim(block, 0, width, axis=dim), axis, backward)]
    all_to_all x2, waiting for transfers between devices: 11.6 us -> 5.27 us  [gather_rows(): swapped = lax.all_to_all(spread, axes, 0, 0, tiled=False)]
    dot_general x8 -> x16, matrix products: 11.5 us -> 17.7 us  [face_mul(): jnp.einsum('fry,fyx->frx', vectors, matrices, preferred_element_type=jnp....]
    dot_general x2 -> x6, matrix products: 0.24 us -> 4.02 us  [the longest x4 2.92 us: add_coarse(): return jnp.dot(rows, piece, precision=lax.Precision.HIGHEST)]
    squeeze x1 -> x5, local copies, waits for them, and re-layouts: 0.12 us -> 3.68 us  [the longest x1 2.23 us: precondition(): payload = jnp.concatenate([payload, schur_panel[face]])]
  transfers between devices with their start and end apart: 18 -> 12, of which waited for: 6 -> 7; matrix products, arithmetic and copies ran while one was open for 4% -> 14% of each run, Pallas kernels for 0% -> 0%
where the time goes in v11:
time: 124 us; the launch traced here: 123 us
  starting transfers between devices  34.7 us (28%)
  matrix products  28.5 us (23%)
  waiting for transfers between devices  28.1 us (23%)
  local copies, waits for them, and re-layouts  12.6 us (10%)
  blocking collectives  11 us (9%)
  other arithmetic  7.51 us (6%)
    ppermute x10, starting transfers between devices, from_partner(): return lax.ppermute(values, axis, pairs)  23.4 us
    ppermute x10, waiting for transfers between devices, from_partner(): return lax.ppermute(values, axis, pairs)  22.8 us
    dot_general x16, matrix products, face_mul(): jnp.einsum('fry,fyx->frx', vectors, matrices, preferred_element_type=jnp....  17.7 us
    all_to_all x2, starting transfers between devices, gather_rows(): swapped = lax.all_to_all(spread, axes, 0, 0, tiled=False)  11.3 us
    all_to_all x1, blocking collectives, gather_rows(): swapped = lax.all_to_all(spread, axes, 0, 0, tiled=False)  11 us
    all_to_all x2, waiting for transfers between devices, gather_rows(): swapped = lax.all_to_all(spread, axes, 0, 0, tiled=False)  5.27 us
    unnamed x92, local copies, waits for them, and re-layouts  3.83 us
    dot_general x2, matrix products, precondition(): jnp.einsum('kfx,kr->frx', picks_full, coarse, precision=lax.Precision.HIG...  3.39 us
  transfers between devices with their start and end apart: 12, of which 7 were waited for; matrix products, arithmetic and copies ran while one was open for 14% of the time, Pallas kernels for 0%

profile of v11, /device:TPU:0, one launch (start us, length us, event | category | flops | bytes accessed | tf_op | source)
XLA Modules:
  0.0 123.1 jit_solution(16887720426482791467)
XLA Ops:
  1.9 2.2 %slice_bitcast_fusion.1 = (bf16[384,384]{1,0:T(8,128)(2,1)}, bf16[384,384]{1,0:T(8,128)(2,1)S(1)}, bf16[384,384]{1,0:T(8,128)(2,1)S(1)}, bf16[384,384]{1,0:T(8,1...) fusion(bf16[1,1,4,384,384]{4,3,2,1,0:T(8,128)(2,1)} %param.9, ...), kind=kLoop, calls=%fused_computation.89 | loop fusion | bytes 3538944 | tf_op jit(solution)/shard_map/squeeze | solution.py:140
  4.3 2.6 %collective-permute-start.2 = (bf16[1344,384]{1,0:T(8,128)(2,1)S(1)}, bf16[1344,384]{1,0:T(8,128)(2,1)S(1)}, u32[]{:S(2)}, u32[]{:S(2)}) collective-permute-start(bf16[1344,384]{1,0:T(8,128)(2,1)S(1)} %pad_maximum_fusion.1), channel_id=1, source_target_pairs={{0,1},{2,3},{4,5},{6,7},{8,9},{10,11},{12,13},{14,15},{16,17},{18,... | collective-permute-start | bytes 3096584 | tf_op jit(solution)/shard_map/ppermute | solution.py:40
  9.7 3.1 %collective-permute-start.6 = (f32[5,128]{1,0:T(8,128)S(1)}, f32[5,128]{1,0:T(8,128)S(1)}, u32[]{:S(2)}, u32[]{:S(2)}) collective-permute-start(f32[5,128]{1,0:T(8,128)S(1)} %select_maximum_fusion), channel_id=1, source_target_pairs={{0,1},{2,3},{4,5},{6,7},{8,9},{10,11},{12,13},{14,15},{16,17},{18,... | collective-permute-start | bytes 7688 | tf_op jit(solution)/shard_map/ppermute | solution.py:40
  12.8 4.2 %collective-permute-start = (bf16[192,384]{1,0:T(8,128)(2,1)S(1)}, bf16[192,384]{1,0:T(8,128)(2,1)S(1)}, u32[]{:S(2)}, u32[]{:S(2)}) collective-permute-start(bf16[192,384]{1,0:T(8,128)(2,1)S(1)} %get-tuple-element.20), channel_id=1, source_target_pairs={{0,2},{2,4},{4,6},{6,8},{8,10},{10,12},{12,14},{14,16},{16,18},{18... | collective-permute-start | bytes 442376 | tf_op jit(solution)/shard_map/ppermute | solution.py:40
  20.8 1.8 %maximum_multiply_fusion = f32[2]{0:T(128)} fusion(f32[1]{0:T(128)} %bitcast.39, f32[1]{0:T(128)} %bitcast.37), kind=kLoop, calls=%fused_computation.140 | loop fusion | flops 4 | bytes 16 | tf_op jit(solution)/shard_map/mul | solution.py:118
  27.1 1.6 %fusion.22 = f32[4,192,384]{2,1,0:T(8,128)} fusion(bf16[4,192,384]{2,1,0:T(8,128)(2,1)S(1)} %convolution_convert_fusion.3, bf16[1,1,4,384,384]{4,3,2,1,0:T(8,128)(2,1)S(1)} %copy-done), kind=kOutput, calls=%fused_computation.50 | convolution fusion | flops 226492416 | bytes 2949120 | tf_op jit(solution)/shard_map/fry,fyx->frx/dot_general | solution.py:48
  29.7 6.8 %all-to-all-start = ((bf16[32,4,192]{2,1,0:T(4,128)(2,1)}), bf16[32,4,192]{2,1,0:T(4,128)(2,1)}, u32[]{:S(2)}, u32[]{:S(2)}) async-start(bf16[32,4,192]{2,1,0:T(4,128)(2,1)} %broadcast_in_dim.8), calls=%async_computation | async-start | bytes 131072 | tf_op jit(solution)/shard_map/all_to_all | solution.py:23
  36.4 1.4 %fusion.80 = f32[2,192,384]{2,1,0:T(8,128)S(1)} fusion(bf16[2,192,384]{2,1,0:T(8,128)(2,1)} %convolution_convert_fusion.5, bf16[2,384,384]{2,1,0:T(8,128)(2,1)S(1)} %get-tuple-element.7), kind=kOutput, calls=%fused_computation.144 | convolution fusion | flops 113246208 | bytes 1474560 | tf_op jit(solution)/shard_map/fry,fyx->frx/dot_general | solution.py:48
  37.9 2.3 %fusion.5 = f32[4,192,384]{2,1,0:T(8,128)} fusion(f32[4,192,384]{2,1,0:T(8,128)S(1)} %copy-done.13, bf16[1,1,4,384,384]{4,3,2,1,0:T(8,128)(2,1)S(1)} %copy-done, f32[4]{0:T(128)} %multiply_bitcast_fusion), kind=kOutput, calls=%fused_computation.15 | convolution fusion | flops 227377152 | bytes 3538960 | tf_op jit(solution)/shard_map/fry,fyx->frx/dot_general | solution.py:48
  41.3 2.5 %all-to-all-done = bf16[32,4,192]{2,1,0:T(4,128)(2,1)} async-done(((bf16[32,4,192]{2,1,0:T(4,128)(2,1)}), bf16[32,4,192]{2,1,0:T(4,128)(2,1)}, u32[]{:S(2)}, u32[]{:S(2)}) %all-to-all-start) | async-done | bytes 49184 | tf_op jit(solution)/shard_map/all_to_all | solution.py:23
  43.8 1.5 %reshape.155 = bf16[128,192]{1,0:T(8,128)(2,1)} reshape(bf16[32,4,192]{2,1,0:T(4,128)(2,1)} %all-to-all-done) | data formatting | bytes 98304 | tf_op jit(solution)/shard_map/reshape | solution.py:24
  47.3 2.0 %fusion.8 = bf16[4,192,384]{2,1,0:T(8,128)(2,1)S(1)} fusion(f32[4,192,384]{2,1,0:T(8,128)} %fusion.5, f32[192,4,1]{0,1,2:T(4,128)S(1)} %convolution_bitcast_fusion.5, s32[4,384]{1,0:T(4,128)S(1)} %multiply_add_fusion, s32[4]{0:T(128)} %bitcast.174), kind=kOutput, calls=%fused_computation.20 | convolution fusion | flops 14751744 | bytes 1778704 | tf_op jit(solution)/shard_map/kfx,kr->frx/dot_general | solution.py:130
  50.3 1.4 %collective-permute-start.5 = (bf16[576,384]{1,0:T(8,128)(2,1)S(1)}, bf16[576,384]{1,0:T(8,128)(2,1)S(1)}, u32[]{:S(2)}, u32[]{:S(2)}) collective-permute-start(bf16[576,384]{1,0:T(8,128)(2,1)S(1)} %pad_maximum_fusion.6), channel_id=1, source_target_pairs={{2,0},{4,2},{6,4},{8,6},{10,8},{12,10},{14,12},{16,14},{18,16},{20... | collective-permute-start | bytes 1327112 | tf_op jit(solution)/shard_map/ppermute | solution.py:40
  51.8 4.6 %collective-permute-start.4 = (bf16[576,384]{1,0:T(8,128)(2,1)S(1)}, bf16[576,384]{1,0:T(8,128)(2,1)S(1)}, u32[]{:S(2)}, u32[]{:S(2)}) collective-permute-start(bf16[576,384]{1,0:T(8,128)(2,1)S(1)} %pad_maximum_fusion.5), channel_id=1, source_target_pairs={{0,2},{2,4},{4,6},{6,8},{8,10},{10,12},{12,14},{14,16},{16,18},{18... | collective-permute-start | bytes 1327112 | tf_op jit(solution)/shard_map/ppermute | solution.py:40
  57.3 8.0 %collective-permute-done.5 = bf16[576,384]{1,0:T(8,128)(2,1)S(1)} collective-permute-done((bf16[576,384]{1,0:T(8,128)(2,1)S(1)}, bf16[576,384]{1,0:T(8,128)(2,1)S(1)}, u32[]{:S(2)}, u32[]{:S(2)}) %collective-permute-start.5) | collective-permute-done | bytes 442400 | tf_op jit(solution)/shard_map/ppermute | solution.py:40
  65.4 7.7 %collective-permute-done.4 = bf16[576,384]{1,0:T(8,128)(2,1)S(1)} collective-permute-done((bf16[576,384]{1,0:T(8,128)(2,1)S(1)}, bf16[576,384]{1,0:T(8,128)(2,1)S(1)}, u32[]{:S(2)}, u32[]{:S(2)}) %collective-permute-start.4) | collective-permute-done | bytes 442400 | tf_op jit(solution)/shard_map/ppermute | solution.py:40
  76.7 1.6 %fusion.19 = f32[4,192,384]{2,1,0:T(8,128)} fusion(bf16[4,192,384]{2,1,0:T(8,128)(2,1)S(1)} %convolution_convert_fusion.1, bf16[1,1,4,384,384]{4,3,2,1,0:T(8,128)(2,1)S(1)} %copy-done), kind=kOutput, calls=%fused_computation.47 | convolution fusion | flops 226492416 | bytes 2949120 | tf_op jit(solution)/shard_map/fry,fyx->frx/dot_general | solution.py:48
  80.1 4.5 %all-to-all-start.1 = ((bf16[32,4,192]{2,1,0:T(4,128)(2,1)}), bf16[32,4,192]{2,1,0:T(4,128)(2,1)}, u32[]{:S(2)}, u32[]{:S(2)}) async-start(bf16[32,4,192]{2,1,0:T(4,128)(2,1)} %broadcast_in_dim.9), calls=%async_computation.1 | async-start | bytes 131072 | tf_op jit(solution)/shard_map/all_to_all | solution.py:23
  84.7 3.2 %fusion.2 = f32[4,192,384]{2,1,0:T(8,128)} fusion(f32[4,192,384]{2,1,0:T(8,128)} %fusion.19, bf16[1,1,4,384,384]{4,3,2,1,0:T(8,128)(2,1)S(1)} %copy-done, f32[4]{0:T(128)} %multiply_bitcast_fusion), kind=kOutput, calls=%fused_computation.9 | convolution fusion | flops 227377152 | bytes 3538960 | tf_op jit(solution)/shard_map/fry,fyx->frx/dot_general | solution.py:48
  89.1 2.8 %all-to-all-done.1 = bf16[32,4,192]{2,1,0:T(4,128)(2,1)} async-done(((bf16[32,4,192]{2,1,0:T(4,128)(2,1)}), bf16[32,4,192]{2,1,0:T(4,128)(2,1)}, u32[]{:S(2)}, u32[]{:S(2)}) %all-to-all-start.1) | async-done | bytes 49184 | tf_op jit(solution)/shard_map/all_to_all | solution.py:23
  93.7 1.4 %fusion.9 = bf16[4,192,384]{2,1,0:T(8,128)(2,1)S(1)} fusion(f32[4,192,384]{2,1,0:T(8,128)S(1)} %copy-done.12, f32[192,4,1]{0,1,2:T(4,128)S(1)} %convolution_bitcast_fusion.4, s32[4,384]{1,0:T(4,128)S(1)} %multiply_add_fusion, s32[4]{0:T(128)} %bitcast.175), kind=kOutput, calls=%fused_computation.21 | convolution fusion | flops 14751744 | bytes 1778704 | tf_op jit(solution)/shard_map/kfx,kr->frx/dot_general | solution.py:130
  95.7 2.3 %collective-permute-start.8 = (bf16[192,384]{1,0:T(8,128)(2,1)S(1)}, bf16[192,384]{1,0:T(8,128)(2,1)S(1)}, u32[]{:S(2)}, u32[]{:S(2)}) collective-permute-start(bf16[192,384]{1,0:T(8,128)(2,1)S(1)} %get-tuple-element.16), channel_id=1, source_target_pairs={{0,2},{2,4},{4,6},{6,8},{8,10},{10,12},{12,14},{14,16},{16,18},{18... | collective-permute-start | bytes 442376 | tf_op jit(solution)/shard_map/ppermute | solution.py:40
  101.4 5.2 %collective-permute-done.9 = bf16[192,384]{1,0:T(8,128)(2,1)S(1)} collective-permute-done((bf16[192,384]{1,0:T(8,128)(2,1)S(1)}, bf16[192,384]{1,0:T(8,128)(2,1)S(1)}, u32[]{:S(2)}, u32[]{:S(2)}) %collective-permute-start.9) | collective-permute-done | bytes 147488 | tf_op jit(solution)/shard_map/ppermute | solution.py:40
  110.0 11.0 %all_to_all.15 = f32[32,1,2,192]{3,2,1,0:T(2,128)} all-to-all(f32[32,1,2,192]{3,2,1,0:T(2,128)S(1)} %broadcast_in_dim.10), channel_id=1, replica_groups=mesh['gx'=16,'gy'=2] {'gx','gy'}, dimensions={0} | all-to-all | bytes 98304 | tf_op jit(solution)/shard_map/all_to_all | solution.py:23
  (158 shorter events, 36.7 us)
Async XLA Ops:
  4.3 13.3 %copy-start.40 = (s32[2]{0:T(128)S(1)}, s32[2]{0:T(128)}, u32[]{:S(2)}) copy-start(s32[2]{0:T(128)} %constant.11.clone) | copy-start | bytes 28
  4.3 18.9 %collective-permute-start.2 = (bf16[1344,384]{1,0:T(8,128)(2,1)S(1)}, bf16[1344,384]{1,0:T(8,128)(2,1)S(1)}, u32[]{:S(2)}, u32[]{:S(2)}) collective-permute-start(bf16[1344,384]{1,0:T(8,128)(2,1)S(1)} %pad_maximum_fusion.1), channel_id=1, source_target_pairs={{0,1},{2,3},{4,5},{6,7},{8,9},{10,11},{12,13},{14,15},{16,17},{18,... | collective-permute-start | bytes 3096584 | tf_op jit(solution)/shard_map/ppermute | solution.py:40
  7.0 16.3 %collective-permute-start.3 = (bf16[1344,384]{1,0:T(8,128)(2,1)S(1)}, bf16[1344,384]{1,0:T(8,128)(2,1)S(1)}, u32[]{:S(2)}, u32[]{:S(2)}) collective-permute-start(bf16[1344,384]{1,0:T(8,128)(2,1)S(1)} %pad_maximum_fusion.2), channel_id=1, source_target_pairs={{1,0},{3,2},{5,4},{7,6},{9,8},{11,10},{13,12},{15,14},{17,16},{19,... | collective-permute-start | bytes 3096584 | tf_op jit(solution)/shard_map/ppermute | solution.py:40
  8.4 9.9 %collective-permute-start.7 = (f32[5,128]{1,0:T(8,128)S(1)}, f32[5,128]{1,0:T(8,128)S(1)}, u32[]{:S(2)}, u32[]{:S(2)}) collective-permute-start(f32[5,128]{1,0:T(8,128)S(1)} %select_maximum_fusion), channel_id=1, source_target_pairs={{1,0},{3,2},{5,4},{7,6},{9,8},{11,10},{13,12},{15,14},{17,16},{19,... | collective-permute-start | bytes 7688 | tf_op jit(solution)/shard_map/ppermute | solution.py:40
  9.7 10.5 %collective-permute-start.6 = (f32[5,128]{1,0:T(8,128)S(1)}, f32[5,128]{1,0:T(8,128)S(1)}, u32[]{:S(2)}, u32[]{:S(2)}) collective-permute-start(f32[5,128]{1,0:T(8,128)S(1)} %select_maximum_fusion), channel_id=1, source_target_pairs={{0,1},{2,3},{4,5},{6,7},{8,9},{10,11},{12,13},{14,15},{16,17},{18,... | collective-permute-start | bytes 7688 | tf_op jit(solution)/shard_map/ppermute | solution.py:40
  12.8 11.7 %collective-permute-start = (bf16[192,384]{1,0:T(8,128)(2,1)S(1)}, bf16[192,384]{1,0:T(8,128)(2,1)S(1)}, u32[]{:S(2)}, u32[]{:S(2)}) collective-permute-start(bf16[192,384]{1,0:T(8,128)(2,1)S(1)} %get-tuple-element.20), channel_id=1, source_target_pairs={{0,2},{2,4},{4,6},{6,8},{8,10},{10,12},{12,14},{14,16},{16,18},{18... | collective-permute-start | bytes 442376 | tf_op jit(solution)/shard_map/ppermute | solution.py:40
  18.3 7.0 %collective-permute-start.1 = (bf16[192,384]{1,0:T(8,128)(2,1)S(1)}, bf16[192,384]{1,0:T(8,128)(2,1)S(1)}, u32[]{:S(2)}, u32[]{:S(2)}) collective-permute-start(bf16[192,384]{1,0:T(8,128)(2,1)S(1)} %get-tuple-element.21), channel_id=1, source_target_pairs={{2,0},{4,2},{6,4},{8,6},{10,8},{12,10},{14,12},{16,14},{18,16},{20... | collective-permute-start | bytes 442376 | tf_op jit(solution)/shard_map/ppermute | solution.py:40
  29.7 14.1 %all-to-all-start = ((bf16[32,4,192]{2,1,0:T(4,128)(2,1)}), bf16[32,4,192]{2,1,0:T(4,128)(2,1)}, u32[]{:S(2)}, u32[]{:S(2)}) async-start(bf16[32,4,192]{2,1,0:T(4,128)(2,1)} %broadcast_in_dim.8), calls=%async_computation | async-start | bytes 131072 | tf_op jit(solution)/shard_map/all_to_all | solution.py:23
  49.8 23.9 %copy-start.6 = (bf16[4,192,384]{2,1,0:T(8,128)(2,1)}, bf16[4,192,384]{2,1,0:T(8,128)(2,1)S(1)}, u32[]{:S(2)}) copy-start(bf16[4,192,384]{2,1,0:T(8,128)(2,1)S(1)} %convolution_convert_fusion.2) | copy-start | bytes 1769476
  49.9 6.5 %copy-start.14 = (f32[2,192,384]{2,1,0:T(8,128)S(1)}, f32[2,192,384]{2,1,0:T(8,128)}, u32[]{:S(2)}) copy-start(f32[2,192,384]{2,1,0:T(8,128)} %fusion.11) | copy-start | bytes 1769476
  49.9 6.5 %copy-start.31 = (s32[2,384]{1,0:T(2,128)S(1)}, s32[2,384]{1,0:T(2,128)}, u32[]{:S(2)}) copy-start(s32[2,384]{1,0:T(2,128)} %iota_add_fusion) | copy-start | bytes 9220
  49.9 6.5 %copy-start.34 = (s32[2,1,4]{2,1,0:T(1,128)S(1)}, s32[2,1,4]{2,1,0:T(1,128)}, u32[]{:S(2)}) copy-start(s32[2,1,4]{2,1,0:T(1,128)} %fusion.73) | copy-start | bytes 100
  50.3 15.0 %collective-permute-start.5 = (bf16[576,384]{1,0:T(8,128)(2,1)S(1)}, bf16[576,384]{1,0:T(8,128)(2,1)S(1)}, u32[]{:S(2)}, u32[]{:S(2)}) collective-permute-start(bf16[576,384]{1,0:T(8,128)(2,1)S(1)} %pad_maximum_fusion.6), channel_id=1, source_target_pairs={{2,0},{4,2},{6,4},{8,6},{10,8},{12,10},{14,12},{16,14},{18,16},{20... | collective-permute-start | bytes 1327112 | tf_op jit(solution)/shard_map/ppermute | solution.py:40
  51.8 21.2 %collective-permute-start.4 = (bf16[576,384]{1,0:T(8,128)(2,1)S(1)}, bf16[576,384]{1,0:T(8,128)(2,1)S(1)}, u32[]{:S(2)}, u32[]{:S(2)}) collective-permute-start(bf16[576,384]{1,0:T(8,128)(2,1)S(1)} %pad_maximum_fusion.5), channel_id=1, source_target_pairs={{0,2},{2,4},{4,6},{6,8},{8,10},{10,12},{12,14},{14,16},{16,18},{18... | collective-permute-start | bytes 1327112 | tf_op jit(solution)/shard_map/ppermute | solution.py:40
  57.0 16.1 %copy-start.2 = (bf16[1,1,4,384,384]{4,3,2,1,0:T(8,128)(2,1)S(1)}, bf16[1,1,4,384,384]{4,3,2,1,0:T(8,128)(2,1)}, u32[]{:S(2)}) copy-start(bf16[1,1,4,384,384]{4,3,2,1,0:T(8,128)(2,1)} %param.9) | copy-start | bytes 3538948
  57.3 16.4 %copy-start.8 = (f32[2,192,384]{2,1,0:T(8,128)}, f32[2,192,384]{2,1,0:T(8,128)S(1)}, u32[]{:S(2)}) copy-start(f32[2,192,384]{2,1,0:T(8,128)S(1)} %convolution_reduce-precision_fusion.5) | copy-start | bytes 1769476
  65.3 8.4 %copy-start.23 = (bf16[576,384]{1,0:T(8,128)(2,1)}, bf16[576,384]{1,0:T(8,128)(2,1)S(1)}, u32[]{:S(2)}) copy-start(bf16[576,384]{1,0:T(8,128)(2,1)S(1)} %collective-permute-done.5) | copy-start | bytes 1327108
  80.1 11.8 %all-to-all-start.1 = ((bf16[32,4,192]{2,1,0:T(4,128)(2,1)}), bf16[32,4,192]{2,1,0:T(4,128)(2,1)}, u32[]{:S(2)}, u32[]{:S(2)}) async-start(bf16[32,4,192]{2,1,0:T(4,128)(2,1)} %broadcast_in_dim.9), calls=%async_computation.1 | async-start | bytes 131072 | tf_op jit(solution)/shard_map/all_to_all | solution.py:23
  95.7 5.7 %collective-permute-start.8 = (bf16[192,384]{1,0:T(8,128)(2,1)S(1)}, bf16[192,384]{1,0:T(8,128)(2,1)S(1)}, u32[]{:S(2)}, u32[]{:S(2)}) collective-permute-start(bf16[192,384]{1,0:T(8,128)(2,1)S(1)} %get-tuple-element.16), channel_id=1, source_target_pairs={{0,2},{2,4},{4,6},{6,8},{8,10},{10,12},{12,14},{14,16},{16,18},{18... | collective-permute-start | bytes 442376 | tf_op jit(solution)/shard_map/ppermute | solution.py:40
  98.1 8.5 %collective-permute-start.9 = (bf16[192,384]{1,0:T(8,128)(2,1)S(1)}, bf16[192,384]{1,0:T(8,128)(2,1)S(1)}, u32[]{:S(2)}, u32[]{:S(2)}) collective-permute-start(bf16[192,384]{1,0:T(8,128)(2,1)S(1)} %get-tuple-element.17), channel_id=1, source_target_pairs={{2,0},{4,2},{6,4},{8,6},{10,8},{12,10},{14,12},{16,14},{18,16},{20... | collective-permute-start | bytes 442376 | tf_op jit(solution)/shard_map/ppermute | solution.py:40
  100.0 6.7 %copy-start.5 = (f32[4,192,384]{2,1,0:T(8,128)S(1)}, f32[4,192,384]{2,1,0:T(8,128)}, u32[]{:S(2)}) copy-start(f32[4,192,384]{2,1,0:T(8,128)} %copy-done.4) | copy-start | bytes 3538948
  109.3 12.7 %copy-start.7 = (bf16[4,192,384]{2,1,0:T(8,128)(2,1)S(1)}, bf16[4,192,384]{2,1,0:T(8,128)(2,1)}, u32[]{:S(2)}) copy-start(bf16[4,192,384]{2,1,0:T(8,128)(2,1)} %copy-done.6) | copy-start | bytes 1769476
  109.3 12.7 %copy-start.9 = (f32[2,192,384]{2,1,0:T(8,128)S(1)}, f32[2,192,384]{2,1,0:T(8,128)}, u32[]{:S(2)}) copy-start(f32[2,192,384]{2,1,0:T(8,128)} %copy-done.8) | copy-start | bytes 1769476
  109.3 12.7 %copy-start.11 = (f32[2,192,384]{2,1,0:T(8,128)S(1)}, f32[2,192,384]{2,1,0:T(8,128)}, u32[]{:S(2)}) copy-start(f32[2,192,384]{2,1,0:T(8,128)} %copy-done.10) | copy-start | bytes 1769476
  (34 other events, 74.2 us)

commit v12 on v8

--- a/solution.py
+++ b/solution.py
@@ -84,21 +84,35 @@
         primal = jnp.einsum(
             "kfx,frx->kr", picks_half, scaled, preferred_element_type=jnp.float32
         ).astype(jnp.bfloat16)
+        if schur_partner is None:
+            schur_source, primal = lax.optimization_barrier((schur_panel[0:2], primal))
+            schur_x = jnp.stack(
+                [
+                    from_partner(schur_source[face], axis, from_lower)
+                    for axis, from_lower, face in PARTNERS[:2]
+                ]
+            )
         coarse = add_coarse(gather_rows(primal, ("gx", "gy")))
         placed = jnp.einsum("kfx,kr->frx", picks_full, coarse, precision=lax.Precision.HIGHEST)
         weighted = (softened + placed).astype(jnp.bfloat16)
+        if schur_partner is None:
+            schur_x, weighted = lax.optimization_barrier((schur_x, weighted))
         spread = face_mul(weighted, deluxe_panel).astype(jnp.bfloat16)
         if schur_partner is not None:
             return spread.astype(jnp.float32) + face_pairs(spread).astype(jnp.float32), schur_partner
-        received = jnp.stack(
+        rows = spread.shape[1]
+        received_x = jnp.stack(
+            [from_partner(spread[face], axis, from_lower) for axis, from_lower, face in PARTNERS[:2]]
+        )
+        received_y = jnp.stack(
             [
                 from_partner(jnp.concatenate([spread[face], schur_panel[face]]), axis, from_lower)
-                for axis, from_lower, face in PARTNERS
+                for axis, from_lower, face in PARTNERS[2:]
             ]
         )
-        rows = spread.shape[1]
-        spread_partner = received[:, :rows]
-        return spread.astype(jnp.float32) + spread_partner.astype(jnp.float32), received[:, rows:]
+        spread_partner = jnp.concatenate([received_x, received_y[:, :rows]])
+        schur_partner = jnp.concatenate([schur_x, received_y[:, rows:]])
+        return spread.astype(jnp.float32) + spread_partner.astype(jnp.float32), schur_partner
 
     def apply_operator(field, schur_partner):
         field_half = field.astype(jnp.bfloat16)

time: 110 us -> 114 us (1.036)
  starting transfers between devices: 38.1 us -> 46.3 us
  waiting for transfers between devices: 30.7 us -> 25.2 us
  local copies, waits for them, and re-layouts: 7.7 us -> 9.31 us
  matrix products: 16.4 us -> 14.9 us
    ppermute x4 -> x6, starting transfers between devices: 10.1 us -> 14.8 us  [from_partner(): return lax.ppermute(values, axis, pairs)]
    all_to_all x2, waiting for transfers between devices: 9.4 us -> 4.72 us  [gather_rows(): swapped = lax.all_to_all(spread, axes, 0, 0, tiled=False)]
    all_to_all x2, starting transfers between devices: 9.17 us -> 12.7 us  [gather_rows(): swapped = lax.all_to_all(spread, axes, 0, 0, tiled=False)]
    dot_general x2, matrix products: 4.01 us -> 2.74 us  [precondition(): jnp.einsum('kfx,kr->frx', picks_full, coarse, precision=lax.Precision.HIG...]
    ppermute x4 -> x6, waiting for transfers between devices: 14.7 us -> 14 us  [from_partner(): return lax.ppermute(values, axis, pairs)]
    unnamed x72 -> x64, local copies, waits for them, and re-layouts: 3.06 us -> 3.17 us
  transfers between devices with their start and end apart: 14 -> 16, of which waited for: 6 -> 8; matrix products, arithmetic and copies ran while one was open for 6% -> 8% of each run, Pallas kernels for 0% -> 0%
where the time goes in v12:
time: 114 us; the launch traced here: 113 us
  starting transfers between devices  46.3 us (41%)
  waiting for transfers between devices  25.2 us (22%)
  matrix products  14.9 us (13%)
  blocking collectives  12.2 us (11%)
  local copies, waits for them, and re-layouts  9.31 us (8%)
  other arithmetic  4.39 us (4%)
    ppermute x6, starting transfers between devices, from_partner(): return lax.ppermute(values, axis, pairs)  14.8 us
    ppermute x6, waiting for transfers between devices, from_partner(): return lax.ppermute(values, axis, pairs)  14 us
    ppermute x4, starting transfers between devices, with_halo(): lax.ppermute(lax.slice_in_dim(block, block.shape[dim] - width, None, axis...  13.5 us
    all_to_all x2, starting transfers between devices, gather_rows(): swapped = lax.all_to_all(spread, axes, 0, 0, tiled=False)  12.7 us
    all_to_all x1, blocking collectives, gather_rows(): swapped = lax.all_to_all(spread, axes, 0, 0, tiled=False)  12.2 us
    dot_general x10, matrix products, face_mul(): jnp.einsum('fry,fyx->frx', vectors, matrices, preferred_element_type=jnp....  9.28 us
    ppermute x4, waiting for transfers between devices, with_halo(): lax.ppermute(lax.slice_in_dim(block, 0, width, axis=dim), axis, backward)  6.5 us
    ppermute x4, starting transfers between devices, with_halo(): lax.ppermute(lax.slice_in_dim(block, 0, width, axis=dim), axis, backward)  5.3 us
  transfers between devices with their start and end apart: 16, of which 8 were waited for; matrix products, arithmetic and copies ran while one was open for 8% of the time, Pallas kernels for 0%

profile of v12, /device:TPU:0, one launch (start us, length us, event | category | flops | bytes accessed | tf_op | source)
XLA Modules:
  0.0 112.9 jit_solution(3547803276534919831)
XLA Ops:
  0.0 1.3 %slice_bitcast_fusion.12 = (bf16[1,192,384]{2,1,0:T(8,128)(2,1)S(1)}, bf16[1,192,384]{2,1,0:T(8,128)(2,1)S(1)}, bf16[1,192,384]{2,1,0:T(8,128)(2,1)S(1)}, bf16[1,192,384]{2,1,0:T(8,128)(2,1)S(1)}) fusion(bf16[1,1,4,192,384]{4,3,2,1,0:T(8,128)(2,1)} %param.7), kind=kLoop, calls=%fused_computation.75 | loop fusion | bytes 1179648 | tf_op jit(solution)/shard_map/slice | solution.py:13
  1.3 4.9 %collective-permute-start = (bf16[1,192,384]{2,1,0:T(8,128)(2,1)S(1)}, bf16[1,192,384]{2,1,0:T(8,128)(2,1)S(1)}, u32[]{:S(2)}, u32[]{:S(2)}) collective-permute-start(bf16[1,192,384]{2,1,0:T(8,128)(2,1)S(1)} %get-tuple-element.25), channel_id=1, source_target_pairs={{0,2},{2,4},{4,6},{6,8},{8,10},{10,12},{12,14},{14,16},{16,18},{18... | collective-permute-start | bytes 442376 | tf_op jit(solution)/shard_map/ppermute | solution.py:12
  8.8 3.2 %collective-permute-start.2 = (bf16[1,192,384]{2,1,0:T(8,128)(2,1)S(1)}, bf16[1,192,384]{2,1,0:T(8,128)(2,1)S(1)}, u32[]{:S(2)}, u32[]{:S(2)}) collective-permute-start(bf16[1,192,384]{2,1,0:T(8,128)(2,1)S(1)} %get-tuple-element.28), channel_id=1, source_target_pairs={{0,1},{2,3},{4,5},{6,7},{8,9},{10,11},{12,13},{14,15},{16,17},{18,... | collective-permute-start | bytes 442376 | tf_op jit(solution)/shard_map/ppermute | solution.py:12
  17.0 6.4 %all-to-all-start = ((bf16[32,4,192]{2,1,0:T(4,128)(2,1)}), bf16[32,4,192]{2,1,0:T(4,128)(2,1)}, u32[]{:S(2)}, u32[]{:S(2)}) async-start(bf16[32,4,192]{2,1,0:T(4,128)(2,1)} %broadcast_in_dim.8), calls=%async_computation | async-start | bytes 131072 | tf_op jit(solution)/shard_map/all_to_all | solution.py:23
  23.4 4.3 %collective-permute-start.4 = (bf16[384,384]{1,0:T(8,128)(2,1)}, bf16[384,384]{1,0:T(8,128)(2,1)}, u32[]{:S(2)}, u32[]{:S(2)}) collective-permute-start(bf16[384,384]{1,0:T(8,128)(2,1)} %get-tuple-element.23), channel_id=1, source_target_pairs={{0,2},{2,4},{4,6},{6,8},{8,10},{10,12},{12,14},{14,16},{16,18},{18... | collective-permute-start | bytes 884744 | tf_op jit(solution)/shard_map/ppermute | solution.py:40
  27.7 1.4 %collective-permute-start.5 = (bf16[384,384]{1,0:T(8,128)(2,1)}, bf16[384,384]{1,0:T(8,128)(2,1)}, u32[]{:S(2)}, u32[]{:S(2)}) collective-permute-start(bf16[384,384]{1,0:T(8,128)(2,1)} %get-tuple-element.24), channel_id=1, source_target_pairs={{2,0},{4,2},{6,4},{8,6},{10,8},{12,10},{14,12},{16,14},{18,16},{20... | collective-permute-start | bytes 884744 | tf_op jit(solution)/shard_map/ppermute | solution.py:40
  30.8 1.5 %reshape.61 = bf16[128,192]{1,0:T(8,128)(2,1)} reshape(bf16[32,4,192]{2,1,0:T(4,128)(2,1)} %all-to-all-done) | data formatting | bytes 98304 | tf_op jit(solution)/shard_map/reshape | solution.py:24
  34.0 6.3 %collective-permute-done.4 = bf16[384,384]{1,0:T(8,128)(2,1)} collective-permute-done((bf16[384,384]{1,0:T(8,128)(2,1)}, bf16[384,384]{1,0:T(8,128)(2,1)}, u32[]{:S(2)}, u32[]{:S(2)}) %collective-permute-start.4) | collective-permute-done | bytes 294944 | tf_op jit(solution)/shard_map/ppermute | solution.py:40
  40.3 1.9 %collective-permute-done.5 = bf16[384,384]{1,0:T(8,128)(2,1)} collective-permute-done((bf16[384,384]{1,0:T(8,128)(2,1)}, bf16[384,384]{1,0:T(8,128)(2,1)}, u32[]{:S(2)}, u32[]{:S(2)}) %collective-permute-start.5) | collective-permute-done | bytes 294944 | tf_op jit(solution)/shard_map/ppermute | solution.py:40
  46.2 3.1 %collective-permute-start.8 = (bf16[576,384]{1,0:T(8,128)(2,1)S(1)}, bf16[576,384]{1,0:T(8,128)(2,1)S(1)}, u32[]{:S(2)}, u32[]{:S(2)}) collective-permute-start(bf16[576,384]{1,0:T(8,128)(2,1)S(1)} %pad_maximum_fusion.5), channel_id=1, source_target_pairs={{0,1},{2,3},{4,5},{6,7},{8,9},{10,11},{12,13},{14,15},{16,17},{18,... | collective-permute-start | bytes 1327112 | tf_op jit(solution)/shard_map/ppermute | solution.py:40
  49.3 3.4 %collective-permute-start.6 = (bf16[192,384]{1,0:T(8,128)(2,1)S(1)}, bf16[192,384]{1,0:T(8,128)(2,1)S(1)}, u32[]{:S(2)}, u32[]{:S(2)}) collective-permute-start(bf16[192,384]{1,0:T(8,128)(2,1)S(1)} %get-tuple-element.19), channel_id=1, source_target_pairs={{0,2},{2,4},{4,6},{6,8},{8,10},{10,12},{12,14},{14,16},{16,18},{18... | collective-permute-start | bytes 442376 | tf_op jit(solution)/shard_map/ppermute | solution.py:40
  54.0 1.3 %collective-permute-done.6 = bf16[192,384]{1,0:T(8,128)(2,1)S(1)} collective-permute-done((bf16[192,384]{1,0:T(8,128)(2,1)S(1)}, bf16[192,384]{1,0:T(8,128)(2,1)S(1)}, u32[]{:S(2)}, u32[]{:S(2)}) %collective-permute-start.6) | collective-permute-done | bytes 147488 | tf_op jit(solution)/shard_map/ppermute | solution.py:40
  55.3 4.4 %collective-permute-done.7 = bf16[192,384]{1,0:T(8,128)(2,1)S(1)} collective-permute-done((bf16[192,384]{1,0:T(8,128)(2,1)S(1)}, bf16[192,384]{1,0:T(8,128)(2,1)S(1)}, u32[]{:S(2)}, u32[]{:S(2)}) %collective-permute-start.7) | collective-permute-done | bytes 147488 | tf_op jit(solution)/shard_map/ppermute | solution.py:40
  63.3 1.6 %fusion.15 = f32[4,192,384]{2,1,0:T(8,128)} fusion(bf16[4,192,384]{2,1,0:T(8,128)(2,1)S(1)} %convolution_convert_fusion.1, bf16[1,1,4,384,384]{4,3,2,1,0:T(8,128)(2,1)S(1)} %copy-done), kind=kOutput, calls=%fused_computation.29 | convolution fusion | flops 226492416 | bytes 2949120 | tf_op jit(solution)/shard_map/fry,fyx->frx/dot_general | solution.py:48
  65.5 6.3 %all-to-all-start.1 = ((bf16[32,4,192]{2,1,0:T(4,128)(2,1)}), bf16[32,4,192]{2,1,0:T(4,128)(2,1)S(1)}, u32[]{:S(2)}, u32[]{:S(2)}) async-start(bf16[32,4,192]{2,1,0:T(4,128)(2,1)} %broadcast_in_dim.9), calls=%async_computation.1 | async-start | bytes 131072 | tf_op jit(solution)/shard_map/all_to_all | solution.py:23
  71.8 3.2 %fusion.2 = f32[4,192,384]{2,1,0:T(8,128)} fusion(f32[4,192,384]{2,1,0:T(8,128)} %fusion.15, bf16[1,1,4,384,384]{4,3,2,1,0:T(8,128)(2,1)S(1)} %copy-done, f32[4]{0:T(128)S(1)} %copy-done.22), kind=kOutput, calls=%fused_computation.5 | convolution fusion | flops 227377152 | bytes 3538960 | tf_op jit(solution)/shard_map/fry,fyx->frx/dot_general | solution.py:48
  75.0 4.2 %all-to-all-done.1 = bf16[32,4,192]{2,1,0:T(4,128)(2,1)S(1)} async-done(((bf16[32,4,192]{2,1,0:T(4,128)(2,1)}), bf16[32,4,192]{2,1,0:T(4,128)(2,1)S(1)}, u32[]{:S(2)}, u32[]{:S(2)}) %all-to-all-start.1) | async-done | bytes 49184 | tf_op jit(solution)/shard_map/all_to_all | solution.py:23
  79.4 2.0 %fusion.9 = bf16[4,192,384]{2,1,0:T(8,128)(2,1)S(1)} fusion(f32[4,192,384]{2,1,0:T(8,128)} %fusion.2, f32[192,4,1]{0,1,2:T(4,128)S(1)} %convolution_bitcast_fusion.4, s32[4,384]{1,0:T(4,128)S(1)} %multiply_add_fusion, s32[4]{0:T(128)S(1)} %bitcast.123), kind=kOutput, calls=%fused_computation.17 | convolution fusion | flops 14751744 | bytes 1778704 | tf_op jit(solution)/shard_map/kfx,kr->frx/dot_general | solution.py:96
  82.0 2.5 %collective-permute-start.10 = (bf16[1,192,384]{2,1,0:T(8,128)(2,1)S(1)}, bf16[1,192,384]{2,1,0:T(8,128)(2,1)S(1)}, u32[]{:S(2)}, u32[]{:S(2)}) collective-permute-start(bf16[1,192,384]{2,1,0:T(8,128)(2,1)S(1)} %get-tuple-element.15), channel_id=1, source_target_pairs={{0,2},{2,4},{4,6},{6,8},{8,10},{10,12},{12,14},{14,16},{16,18},{18... | collective-permute-start | bytes 442376 | tf_op jit(solution)/shard_map/ppermute | solution.py:12
  85.8 3.0 %collective-permute-start.12 = (bf16[1,192,384]{2,1,0:T(8,128)(2,1)S(1)}, bf16[1,192,384]{2,1,0:T(8,128)(2,1)S(1)}, u32[]{:S(2)}, u32[]{:S(2)}) collective-permute-start(bf16[1,192,384]{2,1,0:T(8,128)(2,1)S(1)} %get-tuple-element.17), channel_id=1, source_target_pairs={{0,1},{2,3},{4,5},{6,7},{8,9},{10,11},{12,13},{14,15},{16,17},{18,... | collective-permute-start | bytes 442376 | tf_op jit(solution)/shard_map/ppermute | solution.py:12
  88.9 1.4 %collective-permute-start.11 = (bf16[1,192,384]{2,1,0:T(8,128)(2,1)S(1)}, bf16[1,192,384]{2,1,0:T(8,128)(2,1)S(1)}, u32[]{:S(2)}, u32[]{:S(2)}) collective-permute-start(bf16[1,192,384]{2,1,0:T(8,128)(2,1)S(1)} %get-tuple-element.18), channel_id=1, source_target_pairs={{2,0},{4,2},{6,4},{8,6},{10,8},{12,10},{14,12},{16,14},{18,16},{20... | collective-permute-start | bytes 442376 | tf_op jit(solution)/shard_map/ppermute | solution.py:15
  90.3 5.7 %collective-permute-done.11 = bf16[1,192,384]{2,1,0:T(8,128)(2,1)S(1)} collective-permute-done((bf16[1,192,384]{2,1,0:T(8,128)(2,1)S(1)}, bf16[1,192,384]{2,1,0:T(8,128)(2,1)S(1)}, u32[]{:S(2)}, u32[]{:S(2)}) %collective-permute-start.11) | collective-permute-done | bytes 147488 | tf_op jit(solution)/shard_map/ppermute | solution.py:15
  98.4 12.2 %all_to_all.15 = f32[32,1,2,192]{3,2,1,0:T(2,128)S(1)} all-to-all(f32[32,1,2,192]{3,2,1,0:T(2,128)S(1)} %broadcast_in_dim.10), channel_id=1, replica_groups=mesh['gx'=16,'gy'=2] {'gx','gy'}, dimensions={0} | all-to-all | bytes 98304 | tf_op jit(solution)/shard_map/all_to_all | solution.py:23
  110.7 2.2 %fusion.32 = bf16[1,1,4,192,384]{4,3,2,1,0:T(8,128)(2,1)} fusion(bf16[4,192,384]{2,1,0:T(8,128)(2,1)S(1)} %convolution_convert_fusion, bf16[4,192,384]{2,1,0:T(8,128)(2,1)S(1)} %convolution_convert_fusion.2, f32[192]{0:T(256)S(1)} %bitcast.125, bf16[1,576,384]{2,1,0:T(8,128)(2,1)S(1)} %bitcast.109, bf16[1,576,384]{2,1,0:T(8,128)(2,1)} %bitcast.112, ...), kind=kLoop, calls=%fused_computation.51 | loop fusion | flops 6782976 | bytes 3539712 | tf_op jit(solution)/shard_map/broadcast_in_dim | solution.py:134
  (112 shorter events, 24.5 us)
Async XLA Ops:
  0.0 29.1 %copy-start = (bf16[1,1,4,384,384]{4,3,2,1,0:T(8,128)(2,1)S(1)}, bf16[1,1,4,384,384]{4,3,2,1,0:T(8,128)(2,1)}, u32[]{:S(2)}) copy-start(bf16[1,1,4,384,384]{4,3,2,1,0:T(8,128)(2,1)} %param.10) | copy-start | bytes 3538948
  0.0 12.0 %copy-start.4 = (bf16[1,1,4,384,384]{4,3,2,1,0:T(8,128)(2,1)S(1)}, bf16[1,1,4,384,384]{4,3,2,1,0:T(8,128)(2,1)}, u32[]{:S(2)}) copy-start(bf16[1,1,4,384,384]{4,3,2,1,0:T(8,128)(2,1)} %param.8) | copy-start | bytes 3538948
  1.3 12.2 %collective-permute-start = (bf16[1,192,384]{2,1,0:T(8,128)(2,1)S(1)}, bf16[1,192,384]{2,1,0:T(8,128)(2,1)S(1)}, u32[]{:S(2)}, u32[]{:S(2)}) collective-permute-start(bf16[1,192,384]{2,1,0:T(8,128)(2,1)S(1)} %get-tuple-element.25), channel_id=1, source_target_pairs={{0,2},{2,4},{4,6},{6,8},{8,10},{10,12},{12,14},{14,16},{16,18},{18... | collective-permute-start | bytes 442376 | tf_op jit(solution)/shard_map/ppermute | solution.py:12
  6.2 8.2 %collective-permute-start.1 = (bf16[1,192,384]{2,1,0:T(8,128)(2,1)S(1)}, bf16[1,192,384]{2,1,0:T(8,128)(2,1)S(1)}, u32[]{:S(2)}, u32[]{:S(2)}) collective-permute-start(bf16[1,192,384]{2,1,0:T(8,128)(2,1)S(1)} %get-tuple-element.26), channel_id=1, source_target_pairs={{2,0},{4,2},{6,4},{8,6},{10,8},{12,10},{14,12},{16,14},{18,16},{20... | collective-permute-start | bytes 442376 | tf_op jit(solution)/shard_map/ppermute | solution.py:15
  7.5 6.9 %collective-permute-start.3 = (bf16[1,192,384]{2,1,0:T(8,128)(2,1)S(1)}, bf16[1,192,384]{2,1,0:T(8,128)(2,1)S(1)}, u32[]{:S(2)}, u32[]{:S(2)}) collective-permute-start(bf16[1,192,384]{2,1,0:T(8,128)(2,1)S(1)} %get-tuple-element.27), channel_id=1, source_target_pairs={{1,0},{3,2},{5,4},{7,6},{9,8},{11,10},{13,12},{15,14},{17,16},{19,... | collective-permute-start | bytes 442376 | tf_op jit(solution)/shard_map/ppermute | solution.py:15
  8.8 5.6 %copy-start.1 = (bf16[1,1,4,384,384]{4,3,2,1,0:T(8,128)(2,1)S(1)}, bf16[1,1,4,384,384]{4,3,2,1,0:T(8,128)(2,1)}, u32[]{:S(2)}) copy-start(bf16[1,1,4,384,384]{4,3,2,1,0:T(8,128)(2,1)} %param.9) | copy-start | bytes 3538948
  8.8 5.6 %collective-permute-start.2 = (bf16[1,192,384]{2,1,0:T(8,128)(2,1)S(1)}, bf16[1,192,384]{2,1,0:T(8,128)(2,1)S(1)}, u32[]{:S(2)}, u32[]{:S(2)}) collective-permute-start(bf16[1,192,384]{2,1,0:T(8,128)(2,1)S(1)} %get-tuple-element.28), channel_id=1, source_target_pairs={{0,1},{2,3},{4,5},{6,7},{8,9},{10,11},{12,13},{14,15},{16,17},{18,... | collective-permute-start | bytes 442376 | tf_op jit(solution)/shard_map/ppermute | solution.py:12
  17.0 13.8 %all-to-all-start = ((bf16[32,4,192]{2,1,0:T(4,128)(2,1)}), bf16[32,4,192]{2,1,0:T(4,128)(2,1)}, u32[]{:S(2)}, u32[]{:S(2)}) async-start(bf16[32,4,192]{2,1,0:T(4,128)(2,1)} %broadcast_in_dim.8), calls=%async_computation | async-start | bytes 131072 | tf_op jit(solution)/shard_map/all_to_all | solution.py:23
  23.4 16.9 %collective-permute-start.4 = (bf16[384,384]{1,0:T(8,128)(2,1)}, bf16[384,384]{1,0:T(8,128)(2,1)}, u32[]{:S(2)}, u32[]{:S(2)}) collective-permute-start(bf16[384,384]{1,0:T(8,128)(2,1)} %get-tuple-element.23), channel_id=1, source_target_pairs={{0,2},{2,4},{4,6},{6,8},{8,10},{10,12},{12,14},{14,16},{16,18},{18... | collective-permute-start | bytes 884744 | tf_op jit(solution)/shard_map/ppermute | solution.py:40
  27.7 14.5 %collective-permute-start.5 = (bf16[384,384]{1,0:T(8,128)(2,1)}, bf16[384,384]{1,0:T(8,128)(2,1)}, u32[]{:S(2)}, u32[]{:S(2)}) collective-permute-start(bf16[384,384]{1,0:T(8,128)(2,1)} %get-tuple-element.24), channel_id=1, source_target_pairs={{2,0},{4,2},{6,4},{8,6},{10,8},{12,10},{14,12},{16,14},{18,16},{20... | collective-permute-start | bytes 884744 | tf_op jit(solution)/shard_map/ppermute | solution.py:40
  43.3 17.1 %copy-start.11 = (bf16[2,384,384]{2,1,0:T(8,128)(2,1)}, bf16[2,384,384]{2,1,0:T(8,128)(2,1)S(1)}, u32[]{:S(2)}) copy-start(bf16[2,384,384]{2,1,0:T(8,128)(2,1)S(1)} %pad_maximum_fusion.3) | copy-start | bytes 1769476
  43.9 15.8 %copy-start.5 = (bf16[1,1,4,384,384]{4,3,2,1,0:T(8,128)(2,1)S(1)}, bf16[1,1,4,384,384]{4,3,2,1,0:T(8,128)(2,1)}, u32[]{:S(2)}) copy-start(bf16[1,1,4,384,384]{4,3,2,1,0:T(8,128)(2,1)} %param.8) | copy-start | bytes 3538948
  44.9 14.9 %collective-permute-start.9 = (bf16[576,384]{1,0:T(8,128)(2,1)S(1)}, bf16[576,384]{1,0:T(8,128)(2,1)S(1)}, u32[]{:S(2)}, u32[]{:S(2)}) collective-permute-start(bf16[576,384]{1,0:T(8,128)(2,1)S(1)} %pad_maximum_fusion.6), channel_id=1, source_target_pairs={{1,0},{3,2},{5,4},{7,6},{9,8},{11,10},{13,12},{15,14},{17,16},{19,... | collective-permute-start | bytes 1327112 | tf_op jit(solution)/shard_map/ppermute | solution.py:40
  46.2 13.5 %collective-permute-start.8 = (bf16[576,384]{1,0:T(8,128)(2,1)S(1)}, bf16[576,384]{1,0:T(8,128)(2,1)S(1)}, u32[]{:S(2)}, u32[]{:S(2)}) collective-permute-start(bf16[576,384]{1,0:T(8,128)(2,1)S(1)} %pad_maximum_fusion.5), channel_id=1, source_target_pairs={{0,1},{2,3},{4,5},{6,7},{8,9},{10,11},{12,13},{14,15},{16,17},{18,... | collective-permute-start | bytes 1327112 | tf_op jit(solution)/shard_map/ppermute | solution.py:40
  49.3 6.0 %collective-permute-start.6 = (bf16[192,384]{1,0:T(8,128)(2,1)S(1)}, bf16[192,384]{1,0:T(8,128)(2,1)S(1)}, u32[]{:S(2)}, u32[]{:S(2)}) collective-permute-start(bf16[192,384]{1,0:T(8,128)(2,1)S(1)} %get-tuple-element.19), channel_id=1, source_target_pairs={{0,2},{2,4},{4,6},{6,8},{8,10},{10,12},{12,14},{14,16},{16,18},{18... | collective-permute-start | bytes 442376 | tf_op jit(solution)/shard_map/ppermute | solution.py:40
  52.7 7.0 %collective-permute-start.7 = (bf16[192,384]{1,0:T(8,128)(2,1)S(1)}, bf16[192,384]{1,0:T(8,128)(2,1)S(1)}, u32[]{:S(2)}, u32[]{:S(2)}) collective-permute-start(bf16[192,384]{1,0:T(8,128)(2,1)S(1)} %get-tuple-element.22), channel_id=1, source_target_pairs={{2,0},{4,2},{6,4},{8,6},{10,8},{12,10},{14,12},{16,14},{18,16},{20... | collective-permute-start | bytes 442376 | tf_op jit(solution)/shard_map/ppermute | solution.py:40
  63.3 8.5 %copy-start.22 = (f32[4]{0:T(128)S(1)}, f32[4]{0:T(128)}, u32[]{:S(2)}) copy-start(f32[4]{0:T(128)} %multiply_bitcast_fusion) | copy-start | bytes 52
  65.5 13.7 %all-to-all-start.1 = ((bf16[32,4,192]{2,1,0:T(4,128)(2,1)}), bf16[32,4,192]{2,1,0:T(4,128)(2,1)S(1)}, u32[]{:S(2)}, u32[]{:S(2)}) async-start(bf16[32,4,192]{2,1,0:T(4,128)(2,1)} %broadcast_in_dim.9), calls=%async_computation.1 | async-start | bytes 131072 | tf_op jit(solution)/shard_map/all_to_all | solution.py:23
  81.9 14.1 %copy-start.3 = (f32[4,192,384]{2,1,0:T(8,128)S(1)}, f32[4,192,384]{2,1,0:T(8,128)}, u32[]{:S(2)}) copy-start(f32[4,192,384]{2,1,0:T(8,128)} %copy-done.2) | copy-start | bytes 3538948
  82.0 8.3 %collective-permute-start.10 = (bf16[1,192,384]{2,1,0:T(8,128)(2,1)S(1)}, bf16[1,192,384]{2,1,0:T(8,128)(2,1)S(1)}, u32[]{:S(2)}, u32[]{:S(2)}) collective-permute-start(bf16[1,192,384]{2,1,0:T(8,128)(2,1)S(1)} %get-tuple-element.15), channel_id=1, source_target_pairs={{0,2},{2,4},{4,6},{6,8},{8,10},{10,12},{12,14},{14,16},{16,18},{18... | collective-permute-start | bytes 442376 | tf_op jit(solution)/shard_map/ppermute | solution.py:12
  84.5 5.8 %collective-permute-start.13 = (bf16[1,192,384]{2,1,0:T(8,128)(2,1)S(1)}, bf16[1,192,384]{2,1,0:T(8,128)(2,1)S(1)}, u32[]{:S(2)}, u32[]{:S(2)}) collective-permute-start(bf16[1,192,384]{2,1,0:T(8,128)(2,1)S(1)} %get-tuple-element.16), channel_id=1, source_target_pairs={{1,0},{3,2},{5,4},{7,6},{9,8},{11,10},{13,12},{15,14},{17,16},{19,... | collective-permute-start | bytes 442376 | tf_op jit(solution)/shard_map/ppermute | solution.py:15
  85.8 4.5 %collective-permute-start.12 = (bf16[1,192,384]{2,1,0:T(8,128)(2,1)S(1)}, bf16[1,192,384]{2,1,0:T(8,128)(2,1)S(1)}, u32[]{:S(2)}, u32[]{:S(2)}) collective-permute-start(bf16[1,192,384]{2,1,0:T(8,128)(2,1)S(1)} %get-tuple-element.17), channel_id=1, source_target_pairs={{0,1},{2,3},{4,5},{6,7},{8,9},{10,11},{12,13},{14,15},{16,17},{18,... | collective-permute-start | bytes 442376 | tf_op jit(solution)/shard_map/ppermute | solution.py:12
  88.8 7.5 %copy-start.6 = (bf16[1,1,4,384,384]{4,3,2,1,0:T(8,128)(2,1)S(1)}, bf16[1,1,4,384,384]{4,3,2,1,0:T(8,128)(2,1)}, u32[]{:S(2)}) copy-start(bf16[1,1,4,384,384]{4,3,2,1,0:T(8,128)(2,1)} %param.8) | copy-start | bytes 3538948
  88.9 7.2 %collective-permute-start.11 = (bf16[1,192,384]{2,1,0:T(8,128)(2,1)S(1)}, bf16[1,192,384]{2,1,0:T(8,128)(2,1)S(1)}, u32[]{:S(2)}, u32[]{:S(2)}) collective-permute-start(bf16[1,192,384]{2,1,0:T(8,128)(2,1)S(1)} %get-tuple-element.18), channel_id=1, source_target_pairs={{2,0},{4,2},{6,4},{8,6},{10,8},{12,10},{14,12},{16,14},{18,16},{20... | collective-permute-start | bytes 442376 | tf_op jit(solution)/shard_map/ppermute | solution.py:15
  (24 other events, 42.2 us)

commit v13 on v8

--- a/solution.py
+++ b/solution.py
@@ -73,8 +73,15 @@
     picks_full = picks.astype(jnp.float32)
     flags_full = flag_values.astype(jnp.float32)
 
+    padded_count = 8
+    devices = coarse_inverse.shape[1] // primal_count
+    coarse_padded = jnp.pad(
+        coarse_inverse.reshape(primal_count, devices, primal_count),
+        ((0, 0), (0, 0), (0, padded_count - primal_count)),
+    ).reshape(primal_count, devices * padded_count)
+
     def add_coarse(piece):
-        return jnp.dot(coarse_inverse, piece.astype(jnp.float32), precision=lax.Precision.HIGHEST)
+        return jnp.dot(coarse_padded, piece.astype(jnp.float32), precision=lax.Precision.HIGHEST)
 
     def precondition(resid, schur_partner):
         scaled = face_mul_turned(resid.astype(jnp.bfloat16), deluxe_panel).astype(jnp.bfloat16)
@@ -84,7 +91,9 @@
         primal = jnp.einsum(
             "kfx,frx->kr", picks_half, scaled, preferred_element_type=jnp.float32
         ).astype(jnp.bfloat16)
-        coarse = add_coarse(gather_rows(primal, ("gx", "gy")))
+        coarse = add_coarse(
+            gather_rows(jnp.pad(primal, ((0, padded_count - primal_count), (0, 0))), ("gx", "gy"))
+        )
         placed = jnp.einsum("kfx,kr->frx", picks_full, coarse, precision=lax.Precision.HIGHEST)
         weighted = (softened + placed).astype(jnp.bfloat16)
         spread = face_mul(weighted, deluxe_panel).astype(jnp.bfloat16)

time: 110 us -> 118 us (1.073)
  matrix products: 16.4 us -> 19.9 us
  starting transfers between devices: 38.1 us -> 41.1 us
    ppermute x4, starting transfers between devices: 13.5 us -> 15.5 us  [with_halo(): lax.ppermute(lax.slice_in_dim(block, block.shape[dim] - width, None, axis...]
    all_to_all x2, waiting for transfers between devices: 9.4 us -> 11 us  [gather_rows(): swapped = lax.all_to_all(spread, axes, 0, 0, tiled=False)]
    dot_general x2, matrix products: 1.25 us -> 2.52 us  [face_mul_turned(): jnp.einsum('fry,fxy->frx', vectors, matrices, preferred_element_type=jnp....]
    unnamed x72 -> x58, local copies, waits for them, and re-layouts: 3.06 us -> 2.88 us
  transfers between devices with their start and end apart: 14 -> 14, of which waited for: 6 -> 5; matrix products, arithmetic and copies ran while one was open for 6% -> 6% of each run, Pallas kernels for 0% -> 0%
where the time goes in v13:
time: 118 us; the launch traced here: 117 us
  starting transfers between devices  41.1 us (35%)
  waiting for transfers between devices  31.6 us (27%)
  matrix products  19.9 us (17%)
  blocking collectives  12.6 us (11%)
  local copies, waits for them, and re-layouts  7.51 us (6%)
  other arithmetic  3.52 us (3%)
    ppermute x4, starting transfers between devices, with_halo(): lax.ppermute(lax.slice_in_dim(block, block.shape[dim] - width, None, axis...  15.5 us
    ppermute x4, waiting for transfers between devices, from_partner(): return lax.ppermute(values, axis, pairs)  14.9 us
    all_to_all x1, blocking collectives, gather_rows(): swapped = lax.all_to_all(spread, axes, 0, 0, tiled=False)  12.6 us
    dot_general x10, matrix products, face_mul(): jnp.einsum('fry,fyx->frx', vectors, matrices, preferred_element_type=jnp....  11.5 us
    all_to_all x2, waiting for transfers between devices, gather_rows(): swapped = lax.all_to_all(spread, axes, 0, 0, tiled=False)  11 us
    all_to_all x2, starting transfers between devices, gather_rows(): swapped = lax.all_to_all(spread, axes, 0, 0, tiled=False)  10.3 us
    ppermute x4, starting transfers between devices, from_partner(): return lax.ppermute(values, axis, pairs)  10.1 us
    ppermute x4, waiting for transfers between devices, with_halo(): lax.ppermute(lax.slice_in_dim(block, 0, width, axis=dim), axis, backward)  5.68 us
  transfers between devices with their start and end apart: 14, of which 5 were waited for; matrix products, arithmetic and copies ran while one was open for 6% of the time, Pallas kernels for 0%

profile of v13, /device:TPU:0, one launch (start us, length us, event | category | flops | bytes accessed | tf_op | source)
XLA Modules:
  0.0 116.8 jit_solution(10057254697327244198)
XLA Ops:
  0.0 2.0 %slice_bitcast_fusion.11 = (bf16[1,192,384]{2,1,0:T(8,128)(2,1)}, bf16[1,192,384]{2,1,0:T(8,128)(2,1)S(1)}, bf16[1,192,384]{2,1,0:T(8,128)(2,1)S(1)}, bf16[1,192,384]{2,1,0:T(8,128)(2,1)S(1)}) fusion(bf16[1,1,4,192,384]{4,3,2,1,0:T(8,128)(2,1)} %param.7), kind=kLoop, calls=%fused_computation.73 | loop fusion | bytes 1179648 | tf_op jit(solution)/shard_map/slice | solution.py:13
  2.0 5.5 %collective-permute-start = (bf16[1,192,384]{2,1,0:T(8,128)(2,1)}, bf16[1,192,384]{2,1,0:T(8,128)(2,1)}, u32[]{:S(2)}, u32[]{:S(2)}) collective-permute-start(bf16[1,192,384]{2,1,0:T(8,128)(2,1)} %get-tuple-element.17), channel_id=1, source_target_pairs={{0,2},{2,4},{4,6},{6,8},{8,10},{10,12},{12,14},{14,16},{16,18},{18... | collective-permute-start | bytes 442376 | tf_op jit(solution)/shard_map/ppermute | solution.py:12
  10.1 4.4 %collective-permute-start.2 = (bf16[1,192,384]{2,1,0:T(8,128)(2,1)S(1)}, bf16[1,192,384]{2,1,0:T(8,128)(2,1)}, u32[]{:S(2)}, u32[]{:S(2)}) collective-permute-start(bf16[1,192,384]{2,1,0:T(8,128)(2,1)S(1)} %get-tuple-element.20), channel_id=1, source_target_pairs={{0,1},{2,3},{4,5},{6,7},{8,9},{10,11},{12,13},{14,15},{16,17},{18,... | collective-permute-start | bytes 442376 | tf_op jit(solution)/shard_map/ppermute | solution.py:12
  16.3 1.9 %convolution_convert_fusion.3 = bf16[4,192,384]{2,1,0:T(8,128)(2,1)S(1)} fusion(bf16[1,1,4,384,384]{4,3,2,1,0:T(8,128)(2,1)S(1)} %copy-done.1, bf16[1,1,4,192,384]{4,3,2,1,0:T(8,128)(2,1)} %param.7, bf16[1,192,384]{2,1,0:T(8,128)(2,1)} %collective-permute-done.3, bf16[1,192,384]{2,1,0:T(8,128)(2,1)} %collective-permute-done.2, ...), kind=kOutput, calls=%fused_computation.21 | convolution fusion | flops 228851712 | bytes 2949120 | tf_op jit(solution)/shard_map/fry,fxy->frx/dot_general | solution.py:52
  19.1 7.1 %all-to-all-start = ((bf16[32,8,192]{2,1,0:T(8,128)(2,1)}), bf16[32,8,192]{2,1,0:T(8,128)(2,1)}, u32[]{:S(2)}, u32[]{:S(2)}) async-start(bf16[32,8,192]{2,1,0:T(8,128)(2,1)} %broadcast_in_dim.8), calls=%async_computation | async-start | bytes 262144 | tf_op jit(solution)/shard_map/all_to_all | solution.py:23
  26.9 1.6 %fusion.5 = f32[4,192,384]{2,1,0:T(8,128)} fusion(f32[4,192,384]{2,1,0:T(8,128)S(1)} %fusion.17, bf16[1,1,4,384,384]{4,3,2,1,0:T(8,128)(2,1)S(1)} %copy-done, f32[4]{0:T(128)S(1)} %copy-done.26), kind=kOutput, calls=%fused_computation.11 | convolution fusion | flops 227377152 | bytes 3538960 | tf_op jit(solution)/shard_map/fry,fyx->frx/dot_general | solution.py:48
  28.5 6.0 %all-to-all-done = bf16[32,8,192]{2,1,0:T(8,128)(2,1)} async-done(((bf16[32,8,192]{2,1,0:T(8,128)(2,1)}), bf16[32,8,192]{2,1,0:T(8,128)(2,1)}, u32[]{:S(2)}, u32[]{:S(2)}) %all-to-all-start) | async-done | bytes 98336 | tf_op jit(solution)/shard_map/all_to_all | solution.py:23
  35.6 2.0 %fusion.8 = bf16[4,192,384]{2,1,0:T(8,128)(2,1)S(1)} fusion(f32[4,192,384]{2,1,0:T(8,128)} %fusion.5, f32[4,192,1]{1,0,2:T(4,128)S(1)} %fusion.40, s32[4,384]{1,0:T(4,128)S(1)} %multiply_add_fusion, s32[4]{0:T(128)S(1)} %bitcast.115), kind=kOutput, calls=%fused_computation.16 | convolution fusion | flops 14751744 | bytes 1778704 | tf_op jit(solution)/shard_map/kfx,kr->frx/dot_general | solution.py:97
  42.0 3.1 %collective-permute-start.6 = (bf16[576,384]{1,0:T(8,128)(2,1)S(1)}, bf16[576,384]{1,0:T(8,128)(2,1)S(1)}, u32[]{:S(2)}, u32[]{:S(2)}) collective-permute-start(bf16[576,384]{1,0:T(8,128)(2,1)S(1)} %pad_maximum_fusion.8), channel_id=1, source_target_pairs={{0,1},{2,3},{4,5},{6,7},{8,9},{10,11},{12,13},{14,15},{16,17},{18,... | collective-permute-start | bytes 1327112 | tf_op jit(solution)/shard_map/ppermute | solution.py:40
  45.2 4.3 %collective-permute-start.4 = (bf16[576,384]{1,0:T(8,128)(2,1)S(1)}, bf16[576,384]{1,0:T(8,128)(2,1)S(1)}, u32[]{:S(2)}, u32[]{:S(2)}) collective-permute-start(bf16[576,384]{1,0:T(8,128)(2,1)S(1)} %pad_maximum_fusion.6), channel_id=1, source_target_pairs={{0,2},{2,4},{4,6},{6,8},{8,10},{10,12},{12,14},{14,16},{16,18},{18... | collective-permute-start | bytes 1327112 | tf_op jit(solution)/shard_map/ppermute | solution.py:40
  49.5 5.9 %collective-permute-done.5 = bf16[576,384]{1,0:T(8,128)(2,1)S(1)} collective-permute-done((bf16[576,384]{1,0:T(8,128)(2,1)S(1)}, bf16[576,384]{1,0:T(8,128)(2,1)S(1)}, u32[]{:S(2)}, u32[]{:S(2)}) %collective-permute-start.5) | collective-permute-done | bytes 442400 | tf_op jit(solution)/shard_map/ppermute | solution.py:40
  55.4 8.9 %collective-permute-done.4 = bf16[576,384]{1,0:T(8,128)(2,1)S(1)} collective-permute-done((bf16[576,384]{1,0:T(8,128)(2,1)S(1)}, bf16[576,384]{1,0:T(8,128)(2,1)S(1)}, u32[]{:S(2)}, u32[]{:S(2)}) %collective-permute-start.4) | collective-permute-done | bytes 442400 | tf_op jit(solution)/shard_map/ppermute | solution.py:40
  65.6 1.7 %fusion.4 = f32[4,192,384]{2,1,0:T(8,128)S(1)} fusion(f32[4,192,384]{2,1,0:T(8,128)S(1)} %convolution_reduce-precision_fusion.3, bf16[1,1,4,192,384]{4,3,2,1,0:T(8,128)(2,1)S(1)} %copy-done.21, bf16[4,192,384]{2,1,0:T(8,128)(2,1)S(1)} %convolution_convert_fusion.2, bf16[1,192,384]{2,1,0:T(8,128)(2,1)} %collective-permute-done.3, ...), kind=kOutput, calls=%fused_computation.8 | convolution fusion | flops 238288896 | bytes 5898240 | tf_op jit(solution)/shard_map/fry,fyx->frx/dot_general | solution.py:48
  68.7 1.6 %fusion.14 = f32[4,192,384]{2,1,0:T(8,128)} fusion(bf16[4,192,384]{2,1,0:T(8,128)(2,1)S(1)} %convolution_convert_fusion.1, bf16[1,1,4,384,384]{4,3,2,1,0:T(8,128)(2,1)S(1)} %copy-done), kind=kOutput, calls=%fused_computation.30 | convolution fusion | flops 226492416 | bytes 2949120 | tf_op jit(solution)/shard_map/fry,fyx->frx/dot_general | solution.py:48
  70.9 3.1 %all-to-all-start.1 = ((bf16[32,8,192]{2,1,0:T(8,128)(2,1)}), bf16[32,8,192]{2,1,0:T(8,128)(2,1)S(1)}, u32[]{:S(2)}, u32[]{:S(2)}) async-start(bf16[32,8,192]{2,1,0:T(8,128)(2,1)} %broadcast_in_dim.9), calls=%async_computation.1 | async-start | bytes 262144 | tf_op jit(solution)/shard_map/all_to_all | solution.py:23
  74.1 3.2 %fusion.2 = f32[4,192,384]{2,1,0:T(8,128)} fusion(f32[4,192,384]{2,1,0:T(8,128)} %fusion.14, bf16[1,1,4,384,384]{4,3,2,1,0:T(8,128)(2,1)S(1)} %copy-done, f32[4]{0:T(128)S(1)} %copy-done.27), kind=kOutput, calls=%fused_computation.5 | convolution fusion | flops 227377152 | bytes 3538960 | tf_op jit(solution)/shard_map/fry,fyx->frx/dot_general | solution.py:48
  77.3 5.0 %all-to-all-done.1 = bf16[32,8,192]{2,1,0:T(8,128)(2,1)S(1)} async-done(((bf16[32,8,192]{2,1,0:T(8,128)(2,1)}), bf16[32,8,192]{2,1,0:T(8,128)(2,1)S(1)}, u32[]{:S(2)}, u32[]{:S(2)}) %all-to-all-start.1) | async-done | bytes 98336 | tf_op jit(solution)/shard_map/all_to_all | solution.py:23
  82.5 2.0 %fusion.9 = bf16[4,192,384]{2,1,0:T(8,128)(2,1)S(1)} fusion(f32[4,192,384]{2,1,0:T(8,128)} %fusion.2, f32[4,192,1]{1,0,2:T(4,128)S(1)} %fusion.38, s32[4,384]{1,0:T(4,128)S(1)} %multiply_add_fusion, s32[4]{0:T(128)S(1)} %bitcast.117), kind=kOutput, calls=%fused_computation.17 | convolution fusion | flops 14751744 | bytes 1778704 | tf_op jit(solution)/shard_map/kfx,kr->frx/dot_general | solution.py:97
  85.1 2.5 %collective-permute-start.8 = (bf16[1,192,384]{2,1,0:T(8,128)(2,1)S(1)}, bf16[1,192,384]{2,1,0:T(8,128)(2,1)S(1)}, u32[]{:S(2)}, u32[]{:S(2)}) collective-permute-start(bf16[1,192,384]{2,1,0:T(8,128)(2,1)S(1)} %get-tuple-element.9), channel_id=1, source_target_pairs={{0,2},{2,4},{4,6},{6,8},{8,10},{10,12},{12,14},{14,16},{16,18},{18... | collective-permute-start | bytes 442376 | tf_op jit(solution)/shard_map/ppermute | solution.py:12
  88.9 3.0 %collective-permute-start.10 = (bf16[1,192,384]{2,1,0:T(8,128)(2,1)S(1)}, bf16[1,192,384]{2,1,0:T(8,128)(2,1)S(1)}, u32[]{:S(2)}, u32[]{:S(2)}) collective-permute-start(bf16[1,192,384]{2,1,0:T(8,128)(2,1)S(1)} %get-tuple-element.11), channel_id=1, source_target_pairs={{0,1},{2,3},{4,5},{6,7},{8,9},{10,11},{12,13},{14,15},{16,17},{18,... | collective-permute-start | bytes 442376 | tf_op jit(solution)/shard_map/ppermute | solution.py:12
  92.0 1.4 %collective-permute-start.9 = (bf16[1,192,384]{2,1,0:T(8,128)(2,1)S(1)}, bf16[1,192,384]{2,1,0:T(8,128)(2,1)S(1)}, u32[]{:S(2)}, u32[]{:S(2)}) collective-permute-start(bf16[1,192,384]{2,1,0:T(8,128)(2,1)S(1)} %get-tuple-element.12), channel_id=1, source_target_pairs={{2,0},{4,2},{6,4},{8,6},{10,8},{12,10},{14,12},{16,14},{18,16},{20... | collective-permute-start | bytes 442376 | tf_op jit(solution)/shard_map/ppermute | solution.py:15
  93.5 5.7 %collective-permute-done.9 = bf16[1,192,384]{2,1,0:T(8,128)(2,1)S(1)} collective-permute-done((bf16[1,192,384]{2,1,0:T(8,128)(2,1)S(1)}, bf16[1,192,384]{2,1,0:T(8,128)(2,1)S(1)}, u32[]{:S(2)}, u32[]{:S(2)}) %collective-permute-start.9) | collective-permute-done | bytes 147488 | tf_op jit(solution)/shard_map/ppermute | solution.py:15
  101.6 12.6 %all_to_all.15 = f32[32,1,2,192]{3,2,1,0:T(2,128)S(1)} all-to-all(f32[32,1,2,192]{3,2,1,0:T(2,128)S(1)} %broadcast_in_dim.10), channel_id=1, replica_groups=mesh['gx'=16,'gy'=2] {'gx','gy'}, dimensions={0} | all-to-all | bytes 98304 | tf_op jit(solution)/shard_map/all_to_all | solution.py:23
  114.3 2.4 %fusion.31 = bf16[1,1,4,192,384]{4,3,2,1,0:T(8,128)(2,1)} fusion(bf16[4,192,384]{2,1,0:T(8,128)(2,1)S(1)} %convolution_convert_fusion, bf16[4,192,384]{2,1,0:T(8,128)(2,1)S(1)} %convolution_convert_fusion.2, f32[192]{0:T(256)S(1)} %bitcast.118, bf16[1,192,384]{2,1,0:T(8,128)(2,1)} %copy-done.18, bf16[1,192,384]{2,1,0:T(8,128)(2,1)} %copy-done.19, ...), kind=kLoop, calls=%fused_computation.50 | loop fusion | flops 6782976 | bytes 4129536 | tf_op jit(solution)/shard_map/broadcast_in_dim | solution.py:129
  (103 shorter events, 19.1 us)
Async XLA Ops:
  0.0 26.3 %copy-start = (bf16[1,1,4,384,384]{4,3,2,1,0:T(8,128)(2,1)S(1)}, bf16[1,1,4,384,384]{4,3,2,1,0:T(8,128)(2,1)}, u32[]{:S(2)}) copy-start(bf16[1,1,4,384,384]{4,3,2,1,0:T(8,128)(2,1)} %param.10) | copy-start | bytes 3538948
  0.0 14.5 %copy-start.2 = (bf16[1,1,4,384,384]{4,3,2,1,0:T(8,128)(2,1)S(1)}, bf16[1,1,4,384,384]{4,3,2,1,0:T(8,128)(2,1)}, u32[]{:S(2)}) copy-start(bf16[1,1,4,384,384]{4,3,2,1,0:T(8,128)(2,1)} %param.8) | copy-start | bytes 3538948
  2.0 14.2 %collective-permute-start = (bf16[1,192,384]{2,1,0:T(8,128)(2,1)}, bf16[1,192,384]{2,1,0:T(8,128)(2,1)}, u32[]{:S(2)}, u32[]{:S(2)}) collective-permute-start(bf16[1,192,384]{2,1,0:T(8,128)(2,1)} %get-tuple-element.17), channel_id=1, source_target_pairs={{0,2},{2,4},{4,6},{6,8},{8,10},{10,12},{12,14},{14,16},{16,18},{18... | collective-permute-start | bytes 442376 | tf_op jit(solution)/shard_map/ppermute | solution.py:12
  7.5 8.8 %collective-permute-start.1 = (bf16[1,192,384]{2,1,0:T(8,128)(2,1)S(1)}, bf16[1,192,384]{2,1,0:T(8,128)(2,1)}, u32[]{:S(2)}, u32[]{:S(2)}) collective-permute-start(bf16[1,192,384]{2,1,0:T(8,128)(2,1)S(1)} %get-tuple-element.18), channel_id=1, source_target_pairs={{2,0},{4,2},{6,4},{8,6},{10,8},{12,10},{14,12},{16,14},{18,16},{20... | collective-permute-start | bytes 442376 | tf_op jit(solution)/shard_map/ppermute | solution.py:15
  8.8 7.5 %collective-permute-start.3 = (bf16[1,192,384]{2,1,0:T(8,128)(2,1)S(1)}, bf16[1,192,384]{2,1,0:T(8,128)(2,1)}, u32[]{:S(2)}, u32[]{:S(2)}) collective-permute-start(bf16[1,192,384]{2,1,0:T(8,128)(2,1)S(1)} %get-tuple-element.19), channel_id=1, source_target_pairs={{1,0},{3,2},{5,4},{7,6},{9,8},{11,10},{13,12},{15,14},{17,16},{19,... | collective-permute-start | bytes 442376 | tf_op jit(solution)/shard_map/ppermute | solution.py:15
  10.1 6.1 %collective-permute-start.2 = (bf16[1,192,384]{2,1,0:T(8,128)(2,1)S(1)}, bf16[1,192,384]{2,1,0:T(8,128)(2,1)}, u32[]{:S(2)}, u32[]{:S(2)}) collective-permute-start(bf16[1,192,384]{2,1,0:T(8,128)(2,1)S(1)} %get-tuple-element.20), channel_id=1, source_target_pairs={{0,1},{2,3},{4,5},{6,7},{8,9},{10,11},{12,13},{14,15},{16,17},{18,... | collective-permute-start | bytes 442376 | tf_op jit(solution)/shard_map/ppermute | solution.py:12
  19.1 15.3 %all-to-all-start = ((bf16[32,8,192]{2,1,0:T(8,128)(2,1)}), bf16[32,8,192]{2,1,0:T(8,128)(2,1)}, u32[]{:S(2)}, u32[]{:S(2)}) async-start(bf16[32,8,192]{2,1,0:T(8,128)(2,1)} %broadcast_in_dim.8), calls=%async_computation | async-start | bytes 262144 | tf_op jit(solution)/shard_map/all_to_all | solution.py:23
  26.9 8.7 %copy-start.23 = (s32[1,1,4]{2,1,0:T(1,128)S(1)}, s32[1,1,4]{2,1,0:T(1,128)}, u32[]{:S(2)}) copy-start(s32[1,1,4]{2,1,0:T(1,128)} %param.12) | copy-start | bytes 52
  39.2 10.3 %collective-permute-start.7 = (bf16[576,384]{1,0:T(8,128)(2,1)S(1)}, bf16[576,384]{1,0:T(8,128)(2,1)S(1)}, u32[]{:S(2)}, u32[]{:S(2)}) collective-permute-start(bf16[576,384]{1,0:T(8,128)(2,1)S(1)} %pad_maximum_fusion.9), channel_id=1, source_target_pairs={{1,0},{3,2},{5,4},{7,6},{9,8},{11,10},{13,12},{15,14},{17,16},{19,... | collective-permute-start | bytes 1327112 | tf_op jit(solution)/shard_map/ppermute | solution.py:40
  40.5 23.9 %copy-start.3 = (bf16[1,1,4,384,384]{4,3,2,1,0:T(8,128)(2,1)S(1)}, bf16[1,1,4,384,384]{4,3,2,1,0:T(8,128)(2,1)}, u32[]{:S(2)}) copy-start(bf16[1,1,4,384,384]{4,3,2,1,0:T(8,128)(2,1)} %param.8) | copy-start | bytes 3538948
  40.5 14.9 %collective-permute-start.5 = (bf16[576,384]{1,0:T(8,128)(2,1)S(1)}, bf16[576,384]{1,0:T(8,128)(2,1)S(1)}, u32[]{:S(2)}, u32[]{:S(2)}) collective-permute-start(bf16[576,384]{1,0:T(8,128)(2,1)S(1)} %pad_maximum_fusion.7), channel_id=1, source_target_pairs={{2,0},{4,2},{6,4},{8,6},{10,8},{12,10},{14,12},{16,14},{18,16},{20... | collective-permute-start | bytes 1327112 | tf_op jit(solution)/shard_map/ppermute | solution.py:40
  42.0 13.4 %collective-permute-start.6 = (bf16[576,384]{1,0:T(8,128)(2,1)S(1)}, bf16[576,384]{1,0:T(8,128)(2,1)S(1)}, u32[]{:S(2)}, u32[]{:S(2)}) collective-permute-start(bf16[576,384]{1,0:T(8,128)(2,1)S(1)} %pad_maximum_fusion.8), channel_id=1, source_target_pairs={{0,1},{2,3},{4,5},{6,7},{8,9},{10,11},{12,13},{14,15},{16,17},{18,... | collective-permute-start | bytes 1327112 | tf_op jit(solution)/shard_map/ppermute | solution.py:40
  45.2 19.2 %collective-permute-start.4 = (bf16[576,384]{1,0:T(8,128)(2,1)S(1)}, bf16[576,384]{1,0:T(8,128)(2,1)S(1)}, u32[]{:S(2)}, u32[]{:S(2)}) collective-permute-start(bf16[576,384]{1,0:T(8,128)(2,1)S(1)} %pad_maximum_fusion.6), channel_id=1, source_target_pairs={{0,2},{2,4},{4,6},{6,8},{8,10},{10,12},{12,14},{14,16},{16,18},{18... | collective-permute-start | bytes 1327112 | tf_op jit(solution)/shard_map/ppermute | solution.py:40
  49.5 15.5 %copy-start.7 = (bf16[576,384]{1,0:T(8,128)(2,1)}, bf16[576,384]{1,0:T(8,128)(2,1)S(1)}, u32[]{:S(2)}) copy-start(bf16[576,384]{1,0:T(8,128)(2,1)S(1)} %collective-permute-done.7) | copy-start | bytes 1327108
  55.4 9.5 %copy-start.9 = (bf16[576,384]{1,0:T(8,128)(2,1)}, bf16[576,384]{1,0:T(8,128)(2,1)S(1)}, u32[]{:S(2)}) copy-start(bf16[576,384]{1,0:T(8,128)(2,1)S(1)} %collective-permute-done.5) | copy-start | bytes 1327108
  55.4 9.5 %copy-start.11 = (bf16[576,384]{1,0:T(8,128)(2,1)}, bf16[576,384]{1,0:T(8,128)(2,1)S(1)}, u32[]{:S(2)}) copy-start(bf16[576,384]{1,0:T(8,128)(2,1)S(1)} %collective-permute-done.6) | copy-start | bytes 1327108
  70.9 11.4 %all-to-all-start.1 = ((bf16[32,8,192]{2,1,0:T(8,128)(2,1)}), bf16[32,8,192]{2,1,0:T(8,128)(2,1)S(1)}, u32[]{:S(2)}, u32[]{:S(2)}) async-start(bf16[32,8,192]{2,1,0:T(8,128)(2,1)} %broadcast_in_dim.9), calls=%async_computation.1 | async-start | bytes 262144 | tf_op jit(solution)/shard_map/all_to_all | solution.py:23
  85.0 14.1 %copy-start.6 = (f32[4,192,384]{2,1,0:T(8,128)S(1)}, f32[4,192,384]{2,1,0:T(8,128)}, u32[]{:S(2)}) copy-start(f32[4,192,384]{2,1,0:T(8,128)} %copy-done.5) | copy-start | bytes 3538948
  85.1 8.3 %collective-permute-start.8 = (bf16[1,192,384]{2,1,0:T(8,128)(2,1)S(1)}, bf16[1,192,384]{2,1,0:T(8,128)(2,1)S(1)}, u32[]{:S(2)}, u32[]{:S(2)}) collective-permute-start(bf16[1,192,384]{2,1,0:T(8,128)(2,1)S(1)} %get-tuple-element.9), channel_id=1, source_target_pairs={{0,2},{2,4},{4,6},{6,8},{8,10},{10,12},{12,14},{14,16},{16,18},{18... | collective-permute-start | bytes 442376 | tf_op jit(solution)/shard_map/ppermute | solution.py:12
  87.6 5.8 %collective-permute-start.11 = (bf16[1,192,384]{2,1,0:T(8,128)(2,1)S(1)}, bf16[1,192,384]{2,1,0:T(8,128)(2,1)S(1)}, u32[]{:S(2)}, u32[]{:S(2)}) collective-permute-start(bf16[1,192,384]{2,1,0:T(8,128)(2,1)S(1)} %get-tuple-element.10), channel_id=1, source_target_pairs={{1,0},{3,2},{5,4},{7,6},{9,8},{11,10},{13,12},{15,14},{17,16},{19,... | collective-permute-start | bytes 442376 | tf_op jit(solution)/shard_map/ppermute | solution.py:15
  88.9 4.5 %collective-permute-start.10 = (bf16[1,192,384]{2,1,0:T(8,128)(2,1)S(1)}, bf16[1,192,384]{2,1,0:T(8,128)(2,1)S(1)}, u32[]{:S(2)}, u32[]{:S(2)}) collective-permute-start(bf16[1,192,384]{2,1,0:T(8,128)(2,1)S(1)} %get-tuple-element.11), channel_id=1, source_target_pairs={{0,1},{2,3},{4,5},{6,7},{8,9},{10,11},{12,13},{14,15},{16,17},{18,... | collective-permute-start | bytes 442376 | tf_op jit(solution)/shard_map/ppermute | solution.py:12
  92.0 7.5 %copy-start.4 = (bf16[1,1,4,384,384]{4,3,2,1,0:T(8,128)(2,1)S(1)}, bf16[1,1,4,384,384]{4,3,2,1,0:T(8,128)(2,1)}, u32[]{:S(2)}) copy-start(bf16[1,1,4,384,384]{4,3,2,1,0:T(8,128)(2,1)} %param.8) | copy-start | bytes 3538948
  92.0 7.2 %collective-permute-start.9 = (bf16[1,192,384]{2,1,0:T(8,128)(2,1)S(1)}, bf16[1,192,384]{2,1,0:T(8,128)(2,1)S(1)}, u32[]{:S(2)}, u32[]{:S(2)}) collective-permute-start(bf16[1,192,384]{2,1,0:T(8,128)(2,1)S(1)} %get-tuple-element.12), channel_id=1, source_target_pairs={{2,0},{4,2},{6,4},{8,6},{10,8},{12,10},{14,12},{16,14},{18,16},{20... | collective-permute-start | bytes 442376 | tf_op jit(solution)/shard_map/ppermute | solution.py:15
  93.4 6.6 %copy-start.17 = (bf16[1,192,384]{2,1,0:T(8,128)(2,1)}, bf16[1,192,384]{2,1,0:T(8,128)(2,1)S(1)}, u32[]{:S(2)}) copy-start(bf16[1,192,384]{2,1,0:T(8,128)(2,1)S(1)} %collective-permute-done.8) | copy-start | bytes 442372
  (19 other events, 51.8 us)

commit v14 on v8

--- a/solution.py
+++ b/solution.py
@@ -1,6 +1,7 @@
 import jax
 import jax.numpy as jnp
 from jax import lax
+from jax.experimental import pallas as pl
 from jax.sharding import PartitionSpec as P
 
 
@@ -52,6 +53,35 @@
     return jnp.einsum("fry,fxy->frx", vectors, matrices, preferred_element_type=jnp.float32)
 
 
+def soften_kernel(scaled_ref, panels_ref, flags_ref, out_ref):
+    local_part = jnp.dot(scaled_ref[0], panels_ref[0], preferred_element_type=jnp.float32)
+    extra = jnp.dot(
+        local_part.astype(jnp.bfloat16), panels_ref[0], preferred_element_type=jnp.float32
+    )
+    out_ref[0] = local_part + flags_ref[0, 0:1, 0:1] * extra
+
+
+def soften(scaled, panels, half_flags):
+    faces, rows, width = scaled.shape
+    flags = jnp.broadcast_to(half_flags[:, None, None], (faces, 8, 128))
+    return pl.pallas_call(
+        soften_kernel,
+        grid=(faces,),
+        in_specs=[
+            pl.BlockSpec((1, rows, width), lambda f: (f, 0, 0)),
+            pl.BlockSpec((1, width, width), lambda f: (f, 0, 0)),
+            pl.BlockSpec((1, 8, 128), lambda f: (f, 0, 0)),
+        ],
+        out_specs=pl.BlockSpec((1, rows, width), lambda f: (f, 0, 0)),
+        out_shape=jax.ShapeDtypeStruct((faces, rows, width), jnp.float32),
+        cost_estimate=pl.CostEstimate(
+            flops=4 * faces * rows * width * width,
+            transcendentals=0,
+            bytes_accessed=faces * (rows * width * 6 + width * width * 2),
+        ),
+    )(scaled, panels, flags)
+
+
 def face_pairs(values):
     along_first = with_halo(values[0:2], (("gx", 0),), 1)
     along_second = with_halo(values[2:4], (("gy", 0),), 1)
@@ -78,9 +108,7 @@
 
     def precondition(resid, schur_partner):
         scaled = face_mul_turned(resid.astype(jnp.bfloat16), deluxe_panel).astype(jnp.bfloat16)
-        local_part = face_mul(scaled, inverse_panel)
-        extra = face_mul(local_part.astype(jnp.bfloat16), inverse_panel)
-        softened = lax.optimization_barrier(local_part + 0.5 * flags_full[:, None, None] * extra)
+        softened = soften(scaled, inverse_panel, 0.5 * flags_full)
         primal = jnp.einsum(
             "kfx,frx->kr", picks_half, scaled, preferred_element_type=jnp.float32
         ).astype(jnp.bfloat16)

time: 110 us -> 109 us (level)
  Pallas kernels: 0 us -> 8.82 us
  matrix products: 16.4 us -> 9.5 us
  starting transfers between devices: 38.1 us -> 32.9 us
  local copies, waits for them, and re-layouts: 7.7 us -> 9.51 us
  waiting for transfers between devices: 30.7 us -> 32.1 us
    pallas_call x0 -> x2, Pallas kernels: none -> 8.82 us  [soften(): pl.pallas_call(soften_kernel, grid=(faces,), in_specs=[pl.BlockSpec((1, r...]
    dot_general x10 -> x6, matrix products: 10.3 us -> 3.45 us  [face_mul(): jnp.einsum('fry,fyx->frx', vectors, matrices, preferred_element_type=jnp....]
    all_to_all x2, waiting for transfers between devices: 9.4 us -> 4.6 us  [gather_rows(): swapped = lax.all_to_all(spread, axes, 0, 0, tiled=False)]
    ppermute x4, starting transfers between devices: 10.1 us -> 6.72 us  [from_partner(): return lax.ppermute(values, axis, pairs)]
    ppermute x4, starting transfers between devices: 13.5 us -> 10.8 us  [with_halo(): lax.ppermute(lax.slice_in_dim(block, block.shape[dim] - width, None, axis...]
    ppermute x4, waiting for transfers between devices: 0.01 us -> 2.72 us  [with_halo(): lax.ppermute(lax.slice_in_dim(block, block.shape[dim] - width, None, axis...]
    ppermute x4, waiting for transfers between devices: 14.7 us -> 16.6 us  [from_partner(): return lax.ppermute(values, axis, pairs)]
    ppermute x4, waiting for transfers between devices: 6.6 us -> 8.16 us  [with_halo(): lax.ppermute(lax.slice_in_dim(block, 0, width, axis=dim), axis, backward)]
  transfers between devices with their start and end apart: 14 -> 14, of which waited for: 6 -> 7; matrix products, arithmetic and copies ran while one was open for 6% -> 2% of each run, Pallas kernels for 0% -> 8%
where the time goes in v14:
time: 109 us; the launch traced here: 108 us
  starting transfers between devices  32.9 us (30%)
  waiting for transfers between devices  32.1 us (29%)
  blocking collectives  11.2 us (10%)
  local copies, waits for them, and re-layouts  9.51 us (9%)
  matrix products  9.5 us (9%)
  Pallas kernels  8.82 us (8%)
  other arithmetic  3.66 us (3%)
    ppermute x4, waiting for transfers between devices, from_partner(): return lax.ppermute(values, axis, pairs)  16.6 us
    all_to_all x1, blocking collectives, gather_rows(): swapped = lax.all_to_all(spread, axes, 0, 0, tiled=False)  11.2 us
    ppermute x4, starting transfers between devices, with_halo(): lax.ppermute(lax.slice_in_dim(block, block.shape[dim] - width, None, axis...  10.8 us
    all_to_all x2, starting transfers between devices, gather_rows(): swapped = lax.all_to_all(spread, axes, 0, 0, tiled=False)  10.1 us
    pallas_call x2, Pallas kernels, soften(): pl.pallas_call(soften_kernel, grid=(faces,), in_specs=[pl.BlockSpec((1, r...  8.82 us
    ppermute x4, waiting for transfers between devices, with_halo(): lax.ppermute(lax.slice_in_dim(block, 0, width, axis=dim), axis, backward)  8.16 us
    ppermute x4, starting transfers between devices, from_partner(): return lax.ppermute(values, axis, pairs)  6.72 us
    ppermute x4, starting transfers between devices, with_halo(): lax.ppermute(lax.slice_in_dim(block, 0, width, axis=dim), axis, backward)  5.3 us
  transfers between devices with their start and end apart: 14, of which 7 were waited for; matrix products, arithmetic and copies ran while one was open for 2% of the time, Pallas kernels for 8%

profile of v14, /device:TPU:0, one launch (start us, length us, event | category | flops | bytes accessed | tf_op | source)
XLA Modules:
  0.0 108.3 jit_solution(14877930253656366517)
XLA Ops:
  0.0 1.3 %slice_bitcast_fusion.11 = (bf16[1,192,384]{2,1,0:T(8,128)(2,1)S(1)}, bf16[1,192,384]{2,1,0:T(8,128)(2,1)S(1)}, bf16[1,192,384]{2,1,0:T(8,128)(2,1)S(1)}, bf16[1,192,384]{2,1,0:T(8,128)(2,1)S(1)}) fusion(bf16[1,1,4,192,384]{4,3,2,1,0:T(8,128)(2,1)} %param.7), kind=kLoop, calls=%fused_computation.63 | loop fusion | bytes 1179648 | tf_op jit(solution)/shard_map/slice | solution.py:14
  1.3 4.9 %collective-permute-start = (bf16[1,192,384]{2,1,0:T(8,128)(2,1)S(1)}, bf16[1,192,384]{2,1,0:T(8,128)(2,1)S(1)}, u32[]{:S(2)}, u32[]{:S(2)}) collective-permute-start(bf16[1,192,384]{2,1,0:T(8,128)(2,1)S(1)} %get-tuple-element.17), channel_id=1, source_target_pairs={{0,2},{2,4},{4,6},{6,8},{8,10},{10,12},{12,14},{14,16},{16,18},{18... | collective-permute-start | bytes 442376 | tf_op jit(solution)/shard_map/ppermute | solution.py:13
  7.5 1.5 %collective-permute-start.2 = (bf16[1,192,384]{2,1,0:T(8,128)(2,1)S(1)}, bf16[1,192,384]{2,1,0:T(8,128)(2,1)S(1)}, u32[]{:S(2)}, u32[]{:S(2)}) collective-permute-start(bf16[1,192,384]{2,1,0:T(8,128)(2,1)S(1)} %get-tuple-element.20), channel_id=1, source_target_pairs={{0,1},{2,3},{4,5},{6,7},{8,9},{10,11},{12,13},{14,15},{16,17},{18,... | collective-permute-start | bytes 442376 | tf_op jit(solution)/shard_map/ppermute | solution.py:13
  9.0 1.4 %collective-permute-start.3 = (bf16[1,192,384]{2,1,0:T(8,128)(2,1)S(1)}, bf16[1,192,384]{2,1,0:T(8,128)(2,1)S(1)}, u32[]{:S(2)}, u32[]{:S(2)}) collective-permute-start(bf16[1,192,384]{2,1,0:T(8,128)(2,1)S(1)} %get-tuple-element.19), channel_id=1, source_target_pairs={{1,0},{3,2},{5,4},{7,6},{9,8},{11,10},{13,12},{15,14},{17,16},{19,... | collective-permute-start | bytes 442376 | tf_op jit(solution)/shard_map/ppermute | solution.py:16
  11.4 3.0 %collective-permute-done.1 = bf16[1,192,384]{2,1,0:T(8,128)(2,1)S(1)} collective-permute-done((bf16[1,192,384]{2,1,0:T(8,128)(2,1)S(1)}, bf16[1,192,384]{2,1,0:T(8,128)(2,1)S(1)}, u32[]{:S(2)}, u32[]{:S(2)}) %collective-permute-start.1) | collective-permute-done | bytes 147488 | tf_op jit(solution)/shard_map/ppermute | solution.py:16
  16.1 5.8 %all-to-all-start = ((bf16[32,4,192]{2,1,0:T(4,128)(2,1)}), bf16[32,4,192]{2,1,0:T(4,128)(2,1)}, u32[]{:S(2)}, u32[]{:S(2)}) async-start(bf16[32,4,192]{2,1,0:T(4,128)(2,1)} %broadcast_in_dim.11), calls=%async_computation | async-start | bytes 131072 | tf_op jit(solution)/shard_map/all_to_all | solution.py:24
  23.2 4.4 %shard_map.73 = f32[4,192,384]{2,1,0:T(8,128)} custom-call(bf16[4,192,384]{2,1,0:T(8,128)(2,1)} %copy-done.5, bf16[4,384,384]{2,1,0:T(8,128)(2,1)} %bitcast.92, f32[4,8,128]{2,1,0:T(8,128)} %broadcast_in_dim.10.flags_ref), custom_call_target="tpu_custom_call" | custom-call | flops 452984832 | bytes 2949120 | tf_op jit(solution)/shard_map/pallas_call | solution.py:67
  27.6 1.6 %all-to-all-done = bf16[32,4,192]{2,1,0:T(4,128)(2,1)} async-done(((bf16[32,4,192]{2,1,0:T(4,128)(2,1)}), bf16[32,4,192]{2,1,0:T(4,128)(2,1)}, u32[]{:S(2)}, u32[]{:S(2)}) %all-to-all-start) | async-done | bytes 49184 | tf_op jit(solution)/shard_map/all_to_all | solution.py:24
  30.3 2.0 %fusion.6 = bf16[4,192,384]{2,1,0:T(8,128)(2,1)S(1)} fusion(f32[4,192,384]{2,1,0:T(8,128)} %shard_map.73, f32[192,4,1]{0,1,2:T(4,128)S(1)} %convolution_bitcast_fusion.5, s32[4,384]{1,0:T(4,128)S(1)} %multiply_add_fusion, s32[4]{0:T(128)S(1)} %bitcast.111), kind=kOutput, calls=%fused_computation.12 | convolution fusion | flops 14751744 | bytes 1778704 | tf_op jit(solution)/shard_map/kfx,kr->frx/dot_general | solution.py:116
  33.8 2.4 %collective-permute-start.4 = (bf16[576,384]{1,0:T(8,128)(2,1)S(1)}, bf16[576,384]{1,0:T(8,128)(2,1)S(1)}, u32[]{:S(2)}, u32[]{:S(2)}) collective-permute-start(bf16[576,384]{1,0:T(8,128)(2,1)S(1)} %pad_maximum_fusion.6), channel_id=1, source_target_pairs={{0,2},{2,4},{4,6},{6,8},{8,10},{10,12},{12,14},{14,16},{16,18},{18... | collective-permute-start | bytes 1327112 | tf_op jit(solution)/shard_map/ppermute | solution.py:41
  36.3 1.3 %collective-permute-start.5 = (bf16[576,384]{1,0:T(8,128)(2,1)S(1)}, bf16[576,384]{1,0:T(8,128)(2,1)S(1)}, u32[]{:S(2)}, u32[]{:S(2)}) collective-permute-start(bf16[576,384]{1,0:T(8,128)(2,1)S(1)} %pad_maximum_fusion.7), channel_id=1, source_target_pairs={{2,0},{4,2},{6,4},{8,6},{10,8},{12,10},{14,12},{16,14},{18,16},{20... | collective-permute-start | bytes 1327112 | tf_op jit(solution)/shard_map/ppermute | solution.py:41
  37.6 1.8 %collective-permute-start.6 = (bf16[576,384]{1,0:T(8,128)(2,1)S(1)}, bf16[576,384]{1,0:T(8,128)(2,1)S(1)}, u32[]{:S(2)}, u32[]{:S(2)}) collective-permute-start(bf16[576,384]{1,0:T(8,128)(2,1)S(1)} %pad_maximum_fusion.8), channel_id=1, source_target_pairs={{0,1},{2,3},{4,5},{6,7},{8,9},{10,11},{12,13},{14,15},{16,17},{18,... | collective-permute-start | bytes 1327112 | tf_op jit(solution)/shard_map/ppermute | solution.py:41
  40.8 14.6 %collective-permute-done.4 = bf16[576,384]{1,0:T(8,128)(2,1)S(1)} collective-permute-done((bf16[576,384]{1,0:T(8,128)(2,1)S(1)}, bf16[576,384]{1,0:T(8,128)(2,1)S(1)}, u32[]{:S(2)}, u32[]{:S(2)}) %collective-permute-start.4) | collective-permute-done | bytes 442400 | tf_op jit(solution)/shard_map/ppermute | solution.py:41
  55.3 2.0 %collective-permute-done.5 = bf16[576,384]{1,0:T(8,128)(2,1)S(1)} collective-permute-done((bf16[576,384]{1,0:T(8,128)(2,1)S(1)}, bf16[576,384]{1,0:T(8,128)(2,1)S(1)}, u32[]{:S(2)}, u32[]{:S(2)}) %collective-permute-start.5) | collective-permute-done | bytes 442400 | tf_op jit(solution)/shard_map/ppermute | solution.py:41
  61.6 4.3 %all-to-all-start.1 = ((bf16[32,4,192]{2,1,0:T(4,128)(2,1)}), bf16[32,4,192]{2,1,0:T(4,128)(2,1)}, u32[]{:S(2)}, u32[]{:S(2)}) async-start(bf16[32,4,192]{2,1,0:T(4,128)(2,1)} %broadcast_in_dim.12), calls=%async_computation.1 | async-start | bytes 131072 | tf_op jit(solution)/shard_map/all_to_all | solution.py:24
  66.0 4.4 %shard_map.74 = f32[4,192,384]{2,1,0:T(8,128)} custom-call(bf16[4,192,384]{2,1,0:T(8,128)(2,1)} %copy-done.1, bf16[4,384,384]{2,1,0:T(8,128)(2,1)} %bitcast.93, f32[4,8,128]{2,1,0:T(8,128)} %broadcast_in_dim.10.flags_ref), custom_call_target="tpu_custom_call" | custom-call | flops 452984832 | bytes 2949120 | tf_op jit(solution)/shard_map/pallas_call | solution.py:67
  70.4 3.0 %all-to-all-done.1 = bf16[32,4,192]{2,1,0:T(4,128)(2,1)} async-done(((bf16[32,4,192]{2,1,0:T(4,128)(2,1)}), bf16[32,4,192]{2,1,0:T(4,128)(2,1)}, u32[]{:S(2)}, u32[]{:S(2)}) %all-to-all-start.1) | async-done | bytes 49184 | tf_op jit(solution)/shard_map/all_to_all | solution.py:24
  74.4 2.0 %fusion.7 = bf16[4,192,384]{2,1,0:T(8,128)(2,1)S(1)} fusion(f32[4,192,384]{2,1,0:T(8,128)} %shard_map.74, f32[192,4,1]{0,1,2:T(4,128)S(1)} %convolution_bitcast_fusion.4, s32[4,384]{1,0:T(4,128)S(1)} %multiply_add_fusion, s32[4]{0:T(128)S(1)} %bitcast.113), kind=kOutput, calls=%fused_computation.13 | convolution fusion | flops 14751744 | bytes 1778704 | tf_op jit(solution)/shard_map/kfx,kr->frx/dot_general | solution.py:116
  77.0 2.2 %collective-permute-start.10 = (bf16[1,192,384]{2,1,0:T(8,128)(2,1)S(1)}, bf16[1,192,384]{2,1,0:T(8,128)(2,1)S(1)}, u32[]{:S(2)}, u32[]{:S(2)}) collective-permute-start(bf16[1,192,384]{2,1,0:T(8,128)(2,1)S(1)} %get-tuple-element.11), channel_id=1, source_target_pairs={{0,1},{2,3},{4,5},{6,7},{8,9},{10,11},{12,13},{14,15},{16,17},{18,... | collective-permute-start | bytes 442376 | tf_op jit(solution)/shard_map/ppermute | solution.py:13
  80.5 2.3 %collective-permute-start.8 = (bf16[1,192,384]{2,1,0:T(8,128)(2,1)S(1)}, bf16[1,192,384]{2,1,0:T(8,128)(2,1)S(1)}, u32[]{:S(2)}, u32[]{:S(2)}) collective-permute-start(bf16[1,192,384]{2,1,0:T(8,128)(2,1)S(1)} %get-tuple-element.9), channel_id=1, source_target_pairs={{0,2},{2,4},{4,6},{6,8},{8,10},{10,12},{12,14},{14,16},{16,18},{18... | collective-permute-start | bytes 442376 | tf_op jit(solution)/shard_map/ppermute | solution.py:13
  84.2 2.7 %collective-permute-done.8 = bf16[1,192,384]{2,1,0:T(8,128)(2,1)S(1)} collective-permute-done((bf16[1,192,384]{2,1,0:T(8,128)(2,1)S(1)}, bf16[1,192,384]{2,1,0:T(8,128)(2,1)S(1)}, u32[]{:S(2)}, u32[]{:S(2)}) %collective-permute-start.8) | collective-permute-done | bytes 147488 | tf_op jit(solution)/shard_map/ppermute | solution.py:13
  86.9 5.2 %collective-permute-done.9 = bf16[1,192,384]{2,1,0:T(8,128)(2,1)S(1)} collective-permute-done((bf16[1,192,384]{2,1,0:T(8,128)(2,1)S(1)}, bf16[1,192,384]{2,1,0:T(8,128)(2,1)S(1)}, u32[]{:S(2)}, u32[]{:S(2)}) %collective-permute-start.9) | collective-permute-done | bytes 147488 | tf_op jit(solution)/shard_map/ppermute | solution.py:16
  94.5 11.2 %all_to_all.15 = f32[32,1,2,192]{3,2,1,0:T(2,128)S(1)} all-to-all(f32[32,1,2,192]{3,2,1,0:T(2,128)S(1)} %broadcast_in_dim.13), channel_id=1, replica_groups=mesh['gx'=16,'gy'=2] {'gx','gy'}, dimensions={0} | all-to-all | bytes 98304 | tf_op jit(solution)/shard_map/all_to_all | solution.py:24
  105.8 2.4 %fusion.23 = bf16[1,1,4,192,384]{4,3,2,1,0:T(8,128)(2,1)} fusion(bf16[4,192,384]{2,1,0:T(8,128)(2,1)S(1)} %convolution_convert_fusion, bf16[4,192,384]{2,1,0:T(8,128)(2,1)S(1)} %convolution_convert_fusion.2, f32[192]{0:T(256)S(1)} %bitcast.114, bf16[1,192,384]{2,1,0:T(8,128)(2,1)} %copy-done.19, bf16[1,192,384]{2,1,0:T(8,128)(2,1)} %copy-done.18, ...), kind=kLoop, calls=%fused_computation.42 | loop fusion | flops 6782976 | bytes 4129536 | tf_op jit(solution)/shard_map/broadcast_in_dim | solution.py:148
  (110 shorter events, 20.1 us)
Async XLA Ops:
  0.0 14.4 %copy-start = (bf16[1,1,4,384,384]{4,3,2,1,0:T(8,128)(2,1)S(1)}, bf16[1,1,4,384,384]{4,3,2,1,0:T(8,128)(2,1)}, u32[]{:S(2)}) copy-start(bf16[1,1,4,384,384]{4,3,2,1,0:T(8,128)(2,1)} %param.9) | copy-start | bytes 3538948
  0.0 10.4 %copy-start.2 = (bf16[1,1,4,384,384]{4,3,2,1,0:T(8,128)(2,1)S(1)}, bf16[1,1,4,384,384]{4,3,2,1,0:T(8,128)(2,1)}, u32[]{:S(2)}) copy-start(bf16[1,1,4,384,384]{4,3,2,1,0:T(8,128)(2,1)} %param.8) | copy-start | bytes 3538948
  1.3 10.0 %collective-permute-start = (bf16[1,192,384]{2,1,0:T(8,128)(2,1)S(1)}, bf16[1,192,384]{2,1,0:T(8,128)(2,1)S(1)}, u32[]{:S(2)}, u32[]{:S(2)}) collective-permute-start(bf16[1,192,384]{2,1,0:T(8,128)(2,1)S(1)} %get-tuple-element.17), channel_id=1, source_target_pairs={{0,2},{2,4},{4,6},{6,8},{8,10},{10,12},{12,14},{14,16},{16,18},{18... | collective-permute-start | bytes 442376 | tf_op jit(solution)/shard_map/ppermute | solution.py:13
  6.2 8.2 %collective-permute-start.1 = (bf16[1,192,384]{2,1,0:T(8,128)(2,1)S(1)}, bf16[1,192,384]{2,1,0:T(8,128)(2,1)S(1)}, u32[]{:S(2)}, u32[]{:S(2)}) collective-permute-start(bf16[1,192,384]{2,1,0:T(8,128)(2,1)S(1)} %get-tuple-element.18), channel_id=1, source_target_pairs={{2,0},{4,2},{6,4},{8,6},{10,8},{12,10},{14,12},{16,14},{18,16},{20... | collective-permute-start | bytes 442376 | tf_op jit(solution)/shard_map/ppermute | solution.py:16
  7.5 6.9 %collective-permute-start.2 = (bf16[1,192,384]{2,1,0:T(8,128)(2,1)S(1)}, bf16[1,192,384]{2,1,0:T(8,128)(2,1)S(1)}, u32[]{:S(2)}, u32[]{:S(2)}) collective-permute-start(bf16[1,192,384]{2,1,0:T(8,128)(2,1)S(1)} %get-tuple-element.20), channel_id=1, source_target_pairs={{0,1},{2,3},{4,5},{6,7},{8,9},{10,11},{12,13},{14,15},{16,17},{18,... | collective-permute-start | bytes 442376 | tf_op jit(solution)/shard_map/ppermute | solution.py:13
  9.0 5.4 %collective-permute-start.3 = (bf16[1,192,384]{2,1,0:T(8,128)(2,1)S(1)}, bf16[1,192,384]{2,1,0:T(8,128)(2,1)S(1)}, u32[]{:S(2)}, u32[]{:S(2)}) collective-permute-start(bf16[1,192,384]{2,1,0:T(8,128)(2,1)S(1)} %get-tuple-element.19), channel_id=1, source_target_pairs={{1,0},{3,2},{5,4},{7,6},{9,8},{11,10},{13,12},{15,14},{17,16},{19,... | collective-permute-start | bytes 442376 | tf_op jit(solution)/shard_map/ppermute | solution.py:16
  15.2 8.1 %copy-start.5 = (bf16[4,192,384]{2,1,0:T(8,128)(2,1)}, bf16[4,192,384]{2,1,0:T(8,128)(2,1)S(1)}, u32[]{:S(2)}) copy-start(bf16[4,192,384]{2,1,0:T(8,128)(2,1)S(1)} %convolution_convert_fusion.3.scaled_ref) | copy-start | bytes 1769476
  16.1 13.2 %all-to-all-start = ((bf16[32,4,192]{2,1,0:T(4,128)(2,1)}), bf16[32,4,192]{2,1,0:T(4,128)(2,1)}, u32[]{:S(2)}, u32[]{:S(2)}) async-start(bf16[32,4,192]{2,1,0:T(4,128)(2,1)} %broadcast_in_dim.11), calls=%async_computation | async-start | bytes 131072 | tf_op jit(solution)/shard_map/all_to_all | solution.py:24
  23.2 6.9 %copy-start.24 = (f32[4,128]{1,0:T(4,128)S(1)}, f32[4,128]{1,0:T(4,128)}, u32[]{:S(2)}) copy-start(f32[4,128]{1,0:T(4,128)} %param.11) | copy-start | bytes 6148
  33.8 21.5 %collective-permute-start.4 = (bf16[576,384]{1,0:T(8,128)(2,1)S(1)}, bf16[576,384]{1,0:T(8,128)(2,1)S(1)}, u32[]{:S(2)}, u32[]{:S(2)}) collective-permute-start(bf16[576,384]{1,0:T(8,128)(2,1)S(1)} %pad_maximum_fusion.6), channel_id=1, source_target_pairs={{0,2},{2,4},{4,6},{6,8},{8,10},{10,12},{12,14},{14,16},{16,18},{18... | collective-permute-start | bytes 1327112 | tf_op jit(solution)/shard_map/ppermute | solution.py:41
  36.3 21.1 %collective-permute-start.5 = (bf16[576,384]{1,0:T(8,128)(2,1)S(1)}, bf16[576,384]{1,0:T(8,128)(2,1)S(1)}, u32[]{:S(2)}, u32[]{:S(2)}) collective-permute-start(bf16[576,384]{1,0:T(8,128)(2,1)S(1)} %pad_maximum_fusion.7), channel_id=1, source_target_pairs={{2,0},{4,2},{6,4},{8,6},{10,8},{12,10},{14,12},{16,14},{18,16},{20... | collective-permute-start | bytes 1327112 | tf_op jit(solution)/shard_map/ppermute | solution.py:41
  37.6 19.7 %collective-permute-start.6 = (bf16[576,384]{1,0:T(8,128)(2,1)S(1)}, bf16[576,384]{1,0:T(8,128)(2,1)S(1)}, u32[]{:S(2)}, u32[]{:S(2)}) collective-permute-start(bf16[576,384]{1,0:T(8,128)(2,1)S(1)} %pad_maximum_fusion.8), channel_id=1, source_target_pairs={{0,1},{2,3},{4,5},{6,7},{8,9},{10,11},{12,13},{14,15},{16,17},{18,... | collective-permute-start | bytes 1327112 | tf_op jit(solution)/shard_map/ppermute | solution.py:41
  39.5 17.9 %collective-permute-start.7 = (bf16[576,384]{1,0:T(8,128)(2,1)S(1)}, bf16[576,384]{1,0:T(8,128)(2,1)S(1)}, u32[]{:S(2)}, u32[]{:S(2)}) collective-permute-start(bf16[576,384]{1,0:T(8,128)(2,1)S(1)} %pad_maximum_fusion.9), channel_id=1, source_target_pairs={{1,0},{3,2},{5,4},{7,6},{9,8},{11,10},{13,12},{15,14},{17,16},{19,... | collective-permute-start | bytes 1327112 | tf_op jit(solution)/shard_map/ppermute | solution.py:41
  61.6 11.7 %all-to-all-start.1 = ((bf16[32,4,192]{2,1,0:T(4,128)(2,1)}), bf16[32,4,192]{2,1,0:T(4,128)(2,1)}, u32[]{:S(2)}, u32[]{:S(2)}) async-start(bf16[32,4,192]{2,1,0:T(4,128)(2,1)} %broadcast_in_dim.12), calls=%async_computation.1 | async-start | bytes 131072 | tf_op jit(solution)/shard_map/all_to_all | solution.py:24
  76.9 15.1 %copy-start.4 = (f32[4,192,384]{2,1,0:T(8,128)S(1)}, f32[4,192,384]{2,1,0:T(8,128)}, u32[]{:S(2)}) copy-start(f32[4,192,384]{2,1,0:T(8,128)} %copy-done.3) | copy-start | bytes 3538948
  77.0 7.1 %collective-permute-start.10 = (bf16[1,192,384]{2,1,0:T(8,128)(2,1)S(1)}, bf16[1,192,384]{2,1,0:T(8,128)(2,1)S(1)}, u32[]{:S(2)}, u32[]{:S(2)}) collective-permute-start(bf16[1,192,384]{2,1,0:T(8,128)(2,1)S(1)} %get-tuple-element.11), channel_id=1, source_target_pairs={{0,1},{2,3},{4,5},{6,7},{8,9},{10,11},{12,13},{14,15},{16,17},{18,... | collective-permute-start | bytes 442376 | tf_op jit(solution)/shard_map/ppermute | solution.py:13
  79.2 5.0 %collective-permute-start.11 = (bf16[1,192,384]{2,1,0:T(8,128)(2,1)S(1)}, bf16[1,192,384]{2,1,0:T(8,128)(2,1)S(1)}, u32[]{:S(2)}, u32[]{:S(2)}) collective-permute-start(bf16[1,192,384]{2,1,0:T(8,128)(2,1)S(1)} %get-tuple-element.10), channel_id=1, source_target_pairs={{1,0},{3,2},{5,4},{7,6},{9,8},{11,10},{13,12},{15,14},{17,16},{19,... | collective-permute-start | bytes 442376 | tf_op jit(solution)/shard_map/ppermute | solution.py:16
  80.5 6.4 %collective-permute-start.8 = (bf16[1,192,384]{2,1,0:T(8,128)(2,1)S(1)}, bf16[1,192,384]{2,1,0:T(8,128)(2,1)S(1)}, u32[]{:S(2)}, u32[]{:S(2)}) collective-permute-start(bf16[1,192,384]{2,1,0:T(8,128)(2,1)S(1)} %get-tuple-element.9), channel_id=1, source_target_pairs={{0,2},{2,4},{4,6},{6,8},{8,10},{10,12},{12,14},{14,16},{16,18},{18... | collective-permute-start | bytes 442376 | tf_op jit(solution)/shard_map/ppermute | solution.py:13
  82.8 9.2 %collective-permute-start.9 = (bf16[1,192,384]{2,1,0:T(8,128)(2,1)S(1)}, bf16[1,192,384]{2,1,0:T(8,128)(2,1)S(1)}, u32[]{:S(2)}, u32[]{:S(2)}) collective-permute-start(bf16[1,192,384]{2,1,0:T(8,128)(2,1)S(1)} %get-tuple-element.12), channel_id=1, source_target_pairs={{2,0},{4,2},{6,4},{8,6},{10,8},{12,10},{14,12},{16,14},{18,16},{20... | collective-permute-start | bytes 442376 | tf_op jit(solution)/shard_map/ppermute | solution.py:16
  84.1 8.8 %copy-start.18 = (bf16[1,192,384]{2,1,0:T(8,128)(2,1)}, bf16[1,192,384]{2,1,0:T(8,128)(2,1)S(1)}, u32[]{:S(2)}) copy-start(bf16[1,192,384]{2,1,0:T(8,128)(2,1)S(1)} %collective-permute-done.10) | copy-start | bytes 442372
  84.2 8.8 %copy-start.19 = (bf16[1,192,384]{2,1,0:T(8,128)(2,1)}, bf16[1,192,384]{2,1,0:T(8,128)(2,1)S(1)}, u32[]{:S(2)}) copy-start(bf16[1,192,384]{2,1,0:T(8,128)(2,1)S(1)} %collective-permute-done.11) | copy-start | bytes 442372
  86.9 6.1 %copy-start.20 = (bf16[1,192,384]{2,1,0:T(8,128)(2,1)}, bf16[1,192,384]{2,1,0:T(8,128)(2,1)S(1)}, u32[]{:S(2)}) copy-start(bf16[1,192,384]{2,1,0:T(8,128)(2,1)S(1)} %collective-permute-done.8) | copy-start | bytes 442372
  93.8 12.0 %copy-start.8 = (bf16[576,384]{1,0:T(8,128)(2,1)S(1)}, bf16[576,384]{1,0:T(8,128)(2,1)}, u32[]{:S(2)}) copy-start(bf16[576,384]{1,0:T(8,128)(2,1)} %copy-done.6) | copy-start | bytes 1327108
  93.8 12.1 %copy-start.11 = (bf16[576,384]{1,0:T(8,128)(2,1)S(1)}, bf16[576,384]{1,0:T(8,128)(2,1)}, u32[]{:S(2)}) copy-start(bf16[576,384]{1,0:T(8,128)(2,1)} %copy-done.9) | copy-start | bytes 1327108
  (24 other events, 44.7 us)

commit v15 on v14

--- a/solution.py
+++ b/solution.py
@@ -82,6 +82,42 @@
     )(scaled, panels, flags)
 
 
+def spread_kernel(softened_ref, coarse_ref, slots_ref, deluxe_ref, out_ref):
+    face = pl.program_id(0)
+    rows, width = softened_ref.shape[1], softened_ref.shape[2]
+    position = lax.broadcasted_iota(jnp.int32, (1, width), 1) + face * width
+    placed = jnp.zeros((rows, width), jnp.float32)
+    for k in range(coarse_ref.shape[1]):
+        hit = slots_ref[0:1, k:k + 1] == position
+        placed = placed + jnp.where(hit, coarse_ref[:, k:k + 1], 0.0)
+    weighted = (softened_ref[0] + placed).astype(jnp.bfloat16)
+    out_ref[0] = jnp.dot(
+        weighted, deluxe_ref[0], preferred_element_type=jnp.float32
+    ).astype(out_ref.dtype)
+
+
+def spread_of(softened, coarse, slots_block, deluxe):
+    faces, rows, width = softened.shape
+    count = coarse.shape[0]
+    return pl.pallas_call(
+        spread_kernel,
+        grid=(faces,),
+        in_specs=[
+            pl.BlockSpec((1, rows, width), lambda f: (f, 0, 0)),
+            pl.BlockSpec((rows, count), lambda f: (0, 0)),
+            pl.BlockSpec(slots_block.shape, lambda f: (0, 0)),
+            pl.BlockSpec((1, width, width), lambda f: (f, 0, 0)),
+        ],
+        out_specs=pl.BlockSpec((1, rows, width), lambda f: (f, 0, 0)),
+        out_shape=jax.ShapeDtypeStruct((faces, rows, width), jnp.bfloat16),
+        cost_estimate=pl.CostEstimate(
+            flops=2 * faces * rows * width * width,
+            transcendentals=0,
+            bytes_accessed=faces * (rows * width * 6 + width * width * 2),
+        ),
+    )(softened, coarse.T, slots_block, deluxe)
+
+
 def face_pairs(values):
     along_first = with_halo(values[0:2], (("gx", 0),), 1)
     along_second = with_halo(values[2:4], (("gy", 0),), 1)
@@ -100,7 +136,7 @@
     positions = jnp.arange(4 * width, dtype=jnp.int32)
     picks = (primal_slots[:, None] == positions[None, :]).reshape(primal_count, 4, width)
     picks_half = picks.astype(jnp.bfloat16)
-    picks_full = picks.astype(jnp.float32)
+    slots_block = jnp.zeros((8, 128), jnp.int32).at[0, :primal_count].set(primal_slots)
     flags_full = flag_values.astype(jnp.float32)
 
     def add_coarse(piece):
@@ -113,9 +149,7 @@
             "kfx,frx->kr", picks_half, scaled, preferred_element_type=jnp.float32
         ).astype(jnp.bfloat16)
         coarse = add_coarse(gather_rows(primal, ("gx", "gy")))
-        placed = jnp.einsum("kfx,kr->frx", picks_full, coarse, precision=lax.Precision.HIGHEST)
-        weighted = (softened + placed).astype(jnp.bfloat16)
-        spread = face_mul(weighted, deluxe_panel).astype(jnp.bfloat16)
+        spread = spread_of(softened, coarse, slots_block, deluxe_panel)
         if schur_partner is not None:
             return spread.astype(jnp.float32) + face_pairs(spread).astype(jnp.float32), schur_partner
         received = jnp.stack(

time: 109 us -> 115 us (1.055)
  Pallas kernels: 8.82 us -> 17.4 us
  matrix products: 9.5 us -> 6.02 us
    pallas_call x0 -> x2, Pallas kernels: none -> 8.64 us  [spread_of(): pl.pallas_call(spread_kernel, grid=(faces,), in_specs=[pl.BlockSpec((1, r...]
    dot_general x2 -> x0, matrix products: 4.01 us -> none  [precondition(): jnp.einsum('kfx,kr->frx', picks_full, coarse, precision=lax.Precision.HIG...]
    dot_general x2, matrix products: 0.24 us -> 1.81 us  [add_coarse(): jnp.dot(coarse_inverse, piece.astype(jnp.float32), precision=lax.Precisio...]
    dot_general x6 -> x4, matrix products: 3.45 us -> 2.41 us  [face_mul(): jnp.einsum('fry,fyx->frx', vectors, matrices, preferred_element_type=jnp....]
    unnamed x68 -> x58, local copies, waits for them, and re-layouts: 3.32 us -> 2.63 us
where the time goes in v15:
time: 115 us; the launch traced here: 114 us
  starting transfers between devices  33.5 us (29%)
  waiting for transfers between devices  32.1 us (28%)
  Pallas kernels  17.4 us (15%)
  blocking collectives  11.2 us (10%)
  local copies, waits for them, and re-layouts  9.99 us (9%)
  matrix products  6.02 us (5%)
  other arithmetic  3.6 us (3%)
    ppermute x4, waiting for transfers between devices, from_partner(): return lax.ppermute(values, axis, pairs)  16.4 us
    all_to_all x1, blocking collectives, gather_rows(): swapped = lax.all_to_all(spread, axes, 0, 0, tiled=False)  11.2 us
    ppermute x4, starting transfers between devices, with_halo(): lax.ppermute(lax.slice_in_dim(block, block.shape[dim] - width, None, axis...  10.7 us
    all_to_all x2, starting transfers between devices, gather_rows(): swapped = lax.all_to_all(spread, axes, 0, 0, tiled=False)  10.4 us
    ppermute x4, waiting for transfers between devices, with_halo(): lax.ppermute(lax.slice_in_dim(block, 0, width, axis=dim), axis, backward)  8.95 us
    pallas_call x2, Pallas kernels, soften(): pl.pallas_call(soften_kernel, grid=(faces,), in_specs=[pl.BlockSpec((1, r...  8.8 us
    pallas_call x2, Pallas kernels, spread_of(): pl.pallas_call(spread_kernel, grid=(faces,), in_specs=[pl.BlockSpec((1, r...  8.64 us
    ppermute x4, starting transfers between devices, from_partner(): return lax.ppermute(values, axis, pairs)  7.14 us
  transfers between devices with their start and end apart: 14, of which 7 were waited for; matrix products, arithmetic and copies ran while one was open for 2% of the time, Pallas kernels for 8%

profile of v15, /device:TPU:0, one launch (start us, length us, event | category | flops | bytes accessed | tf_op | source)
XLA Modules:
  0.0 114.4 jit_solution(8131453330920648804)
XLA Ops:
  1.3 4.9 %collective-permute-start = (bf16[1,192,384]{2,1,0:T(8,128)(2,1)S(1)}, bf16[1,192,384]{2,1,0:T(8,128)(2,1)S(1)}, u32[]{:S(2)}, u32[]{:S(2)}) collective-permute-start(bf16[1,192,384]{2,1,0:T(8,128)(2,1)S(1)} %get-tuple-element.29), channel_id=1, source_target_pairs={{0,2},{2,4},{4,6},{6,8},{8,10},{10,12},{12,14},{14,16},{16,18},{18... | collective-permute-start | bytes 442376 | tf_op jit(solution)/shard_map/ppermute | solution.py:13
  6.1 1.3 %collective-permute-start.1 = (bf16[1,192,384]{2,1,0:T(8,128)(2,1)S(1)}, bf16[1,192,384]{2,1,0:T(8,128)(2,1)S(1)}, u32[]{:S(2)}, u32[]{:S(2)}) collective-permute-start(bf16[1,192,384]{2,1,0:T(8,128)(2,1)S(1)} %get-tuple-element.30), channel_id=1, source_target_pairs={{2,0},{4,2},{6,4},{8,6},{10,8},{12,10},{14,12},{16,14},{18,16},{20... | collective-permute-start | bytes 442376 | tf_op jit(solution)/shard_map/ppermute | solution.py:16
  7.4 1.5 %collective-permute-start.2 = (bf16[1,192,384]{2,1,0:T(8,128)(2,1)S(1)}, bf16[1,192,384]{2,1,0:T(8,128)(2,1)S(1)}, u32[]{:S(2)}, u32[]{:S(2)}) collective-permute-start(bf16[1,192,384]{2,1,0:T(8,128)(2,1)S(1)} %get-tuple-element.32), channel_id=1, source_target_pairs={{0,1},{2,3},{4,5},{6,7},{8,9},{10,11},{12,13},{14,15},{16,17},{18,... | collective-permute-start | bytes 442376 | tf_op jit(solution)/shard_map/ppermute | solution.py:13
  8.9 1.4 %collective-permute-start.3 = (bf16[1,192,384]{2,1,0:T(8,128)(2,1)S(1)}, bf16[1,192,384]{2,1,0:T(8,128)(2,1)S(1)}, u32[]{:S(2)}, u32[]{:S(2)}) collective-permute-start(bf16[1,192,384]{2,1,0:T(8,128)(2,1)S(1)} %get-tuple-element.31), channel_id=1, source_target_pairs={{1,0},{3,2},{5,4},{7,6},{9,8},{11,10},{13,12},{15,14},{17,16},{19,... | collective-permute-start | bytes 442376 | tf_op jit(solution)/shard_map/ppermute | solution.py:16
  10.6 3.8 %collective-permute-done.1 = bf16[1,192,384]{2,1,0:T(8,128)(2,1)S(1)} collective-permute-done((bf16[1,192,384]{2,1,0:T(8,128)(2,1)S(1)}, bf16[1,192,384]{2,1,0:T(8,128)(2,1)S(1)}, u32[]{:S(2)}, u32[]{:S(2)}) %collective-permute-start.1) | collective-permute-done | bytes 147488 | tf_op jit(solution)/shard_map/ppermute | solution.py:16
  16.0 5.6 %all-to-all-start = ((bf16[32,4,192]{2,1,0:T(4,128)(2,1)}), bf16[32,4,192]{2,1,0:T(4,128)(2,1)S(1)}, u32[]{:S(2)}, u32[]{:S(2)}) async-start(bf16[32,4,192]{2,1,0:T(4,128)(2,1)} %broadcast_in_dim.11), calls=%async_computation | async-start | bytes 131072 | tf_op jit(solution)/shard_map/all_to_all | solution.py:24
  23.6 4.4 %shard_map.73.softened_ref = f32[4,192,384]{2,1,0:T(8,128)} custom-call(bf16[4,192,384]{2,1,0:T(8,128)(2,1)} %copy-done.7, bf16[4,384,384]{2,1,0:T(8,128)(2,1)} %bitcast.71, f32[4,8,128]{2,1,0:T(8,128)} %broadcast_in_dim.10.flags_ref), custom_call_target="tpu_custom_call" | custom-call | flops 452984832 | bytes 2949120 | tf_op jit(solution)/shard_map/pallas_call | solution.py:67
  30.0 4.3 %shard_map.74 = bf16[4,192,384]{2,1,0:T(8,128)(2,1)} custom-call(f32[4,192,384]{2,1,0:T(8,128)} %shard_map.73.softened_ref, f32[192,4]{1,0:T(8,128)} %fusion.30.coarse_ref, s32[8,128]{1,0:T(8,128)} %scatter.4.slots_ref, bf16[4,384,384]{2,1,0:T(8,128)(2,1)} %bitcast.69), custom_call_target="tpu_custom_call" | custom-call | flops 226492416 | bytes 2949120 | tf_op jit(solution)/shard_map/pallas_call | solution.py:102
  35.6 2.6 %collective-permute-start.4 = (bf16[576,384]{1,0:T(8,128)(2,1)S(1)}, bf16[576,384]{1,0:T(8,128)(2,1)S(1)}, u32[]{:S(2)}, u32[]{:S(2)}) collective-permute-start(bf16[576,384]{1,0:T(8,128)(2,1)S(1)} %pad_maximum_fusion.6), channel_id=1, source_target_pairs={{0,2},{2,4},{4,6},{6,8},{8,10},{10,12},{12,14},{14,16},{16,18},{18... | collective-permute-start | bytes 1327112 | tf_op jit(solution)/shard_map/ppermute | solution.py:41
  38.3 1.4 %collective-permute-start.5 = (bf16[576,384]{1,0:T(8,128)(2,1)S(1)}, bf16[576,384]{1,0:T(8,128)(2,1)S(1)}, u32[]{:S(2)}, u32[]{:S(2)}) collective-permute-start(bf16[576,384]{1,0:T(8,128)(2,1)S(1)} %pad_maximum_fusion.7), channel_id=1, source_target_pairs={{2,0},{4,2},{6,4},{8,6},{10,8},{12,10},{14,12},{16,14},{18,16},{20... | collective-permute-start | bytes 1327112 | tf_op jit(solution)/shard_map/ppermute | solution.py:41
  39.8 1.8 %collective-permute-start.6 = (bf16[576,384]{1,0:T(8,128)(2,1)S(1)}, bf16[576,384]{1,0:T(8,128)(2,1)S(1)}, u32[]{:S(2)}, u32[]{:S(2)}) collective-permute-start(bf16[576,384]{1,0:T(8,128)(2,1)S(1)} %pad_maximum_fusion.8), channel_id=1, source_target_pairs={{0,1},{2,3},{4,5},{6,7},{8,9},{10,11},{12,13},{14,15},{16,17},{18,... | collective-permute-start | bytes 1327112 | tf_op jit(solution)/shard_map/ppermute | solution.py:41
  41.6 1.3 %collective-permute-start.7 = (bf16[576,384]{1,0:T(8,128)(2,1)S(1)}, bf16[576,384]{1,0:T(8,128)(2,1)S(1)}, u32[]{:S(2)}, u32[]{:S(2)}) collective-permute-start(bf16[576,384]{1,0:T(8,128)(2,1)S(1)} %pad_maximum_fusion.9), channel_id=1, source_target_pairs={{1,0},{3,2},{5,4},{7,6},{9,8},{11,10},{13,12},{15,14},{17,16},{19,... | collective-permute-start | bytes 1327112 | tf_op jit(solution)/shard_map/ppermute | solution.py:41
  42.9 14.5 %collective-permute-done.4 = bf16[576,384]{1,0:T(8,128)(2,1)S(1)} collective-permute-done((bf16[576,384]{1,0:T(8,128)(2,1)S(1)}, bf16[576,384]{1,0:T(8,128)(2,1)S(1)}, u32[]{:S(2)}, u32[]{:S(2)}) %collective-permute-start.4) | collective-permute-done | bytes 442400 | tf_op jit(solution)/shard_map/ppermute | solution.py:41
  57.4 1.9 %collective-permute-done.5 = bf16[576,384]{1,0:T(8,128)(2,1)S(1)} collective-permute-done((bf16[576,384]{1,0:T(8,128)(2,1)S(1)}, bf16[576,384]{1,0:T(8,128)(2,1)S(1)}, u32[]{:S(2)}, u32[]{:S(2)}) %collective-permute-start.5) | collective-permute-done | bytes 442400 | tf_op jit(solution)/shard_map/ppermute | solution.py:41
  63.8 4.8 %all-to-all-start.1 = ((bf16[32,4,192]{2,1,0:T(4,128)(2,1)}), bf16[32,4,192]{2,1,0:T(4,128)(2,1)}, u32[]{:S(2)}, u32[]{:S(2)}) async-start(bf16[32,4,192]{2,1,0:T(4,128)(2,1)} %broadcast_in_dim.12), calls=%async_computation.1 | async-start | bytes 131072 | tf_op jit(solution)/shard_map/all_to_all | solution.py:24
  68.6 4.4 %shard_map.75.softened_ref = f32[4,192,384]{2,1,0:T(8,128)} custom-call(bf16[4,192,384]{2,1,0:T(8,128)(2,1)} %copy-done.5, bf16[4,384,384]{2,1,0:T(8,128)(2,1)} %bitcast.72, f32[4,8,128]{2,1,0:T(8,128)} %broadcast_in_dim.10.flags_ref), custom_call_target="tpu_custom_call" | custom-call | flops 452984832 | bytes 2949120 | tf_op jit(solution)/shard_map/pallas_call | solution.py:67
  73.0 3.0 %all-to-all-done.1 = bf16[32,4,192]{2,1,0:T(4,128)(2,1)} async-done(((bf16[32,4,192]{2,1,0:T(4,128)(2,1)}), bf16[32,4,192]{2,1,0:T(4,128)(2,1)}, u32[]{:S(2)}, u32[]{:S(2)}) %all-to-all-start.1) | async-done | bytes 49184 | tf_op jit(solution)/shard_map/all_to_all | solution.py:24
  77.8 4.3 %shard_map.76 = bf16[4,192,384]{2,1,0:T(8,128)(2,1)} custom-call(f32[4,192,384]{2,1,0:T(8,128)} %shard_map.75.softened_ref, f32[192,4]{1,0:T(8,128)} %fusion.31.coarse_ref, s32[8,128]{1,0:T(8,128)} %scatter.4.slots_ref, bf16[4,384,384]{2,1,0:T(8,128)(2,1)} %bitcast.70), custom_call_target="tpu_custom_call" | custom-call | flops 226492416 | bytes 2949120 | tf_op jit(solution)/shard_map/pallas_call | solution.py:102
  83.3 2.0 %collective-permute-start.10 = (bf16[1,192,384]{2,1,0:T(8,128)(2,1)S(1)}, bf16[1,192,384]{2,1,0:T(8,128)(2,1)S(1)}, u32[]{:S(2)}, u32[]{:S(2)}) collective-permute-start(bf16[1,192,384]{2,1,0:T(8,128)(2,1)S(1)} %get-tuple-element.23), channel_id=1, source_target_pairs={{0,1},{2,3},{4,5},{6,7},{8,9},{10,11},{12,13},{14,15},{16,17},{18,... | collective-permute-start | bytes 442376 | tf_op jit(solution)/shard_map/ppermute | solution.py:13
  86.7 2.3 %collective-permute-start.8 = (bf16[1,192,384]{2,1,0:T(8,128)(2,1)S(1)}, bf16[1,192,384]{2,1,0:T(8,128)(2,1)S(1)}, u32[]{:S(2)}, u32[]{:S(2)}) collective-permute-start(bf16[1,192,384]{2,1,0:T(8,128)(2,1)S(1)} %get-tuple-element.21), channel_id=1, source_target_pairs={{0,2},{2,4},{4,6},{6,8},{8,10},{10,12},{12,14},{14,16},{16,18},{18... | collective-permute-start | bytes 442376 | tf_op jit(solution)/shard_map/ppermute | solution.py:13
  90.3 2.7 %collective-permute-done.8 = bf16[1,192,384]{2,1,0:T(8,128)(2,1)S(1)} collective-permute-done((bf16[1,192,384]{2,1,0:T(8,128)(2,1)S(1)}, bf16[1,192,384]{2,1,0:T(8,128)(2,1)S(1)}, u32[]{:S(2)}, u32[]{:S(2)}) %collective-permute-start.8) | collective-permute-done | bytes 147488 | tf_op jit(solution)/shard_map/ppermute | solution.py:13
  93.1 5.2 %collective-permute-done.9 = bf16[1,192,384]{2,1,0:T(8,128)(2,1)S(1)} collective-permute-done((bf16[1,192,384]{2,1,0:T(8,128)(2,1)S(1)}, bf16[1,192,384]{2,1,0:T(8,128)(2,1)S(1)}, u32[]{:S(2)}, u32[]{:S(2)}) %collective-permute-start.9) | collective-permute-done | bytes 147488 | tf_op jit(solution)/shard_map/ppermute | solution.py:16
  100.7 11.2 %all_to_all.15 = f32[32,1,2,192]{3,2,1,0:T(2,128)S(1)} all-to-all(f32[32,1,2,192]{3,2,1,0:T(2,128)S(1)} %broadcast_in_dim.13), channel_id=1, replica_groups=mesh['gx'=16,'gy'=2] {'gx','gy'}, dimensions={0} | all-to-all | bytes 98304 | tf_op jit(solution)/shard_map/all_to_all | solution.py:24
  112.0 2.4 %fusion.15 = bf16[1,1,4,192,384]{4,3,2,1,0:T(8,128)(2,1)} fusion(bf16[4,192,384]{2,1,0:T(8,128)(2,1)S(1)} %copy-done.4, bf16[4,192,384]{2,1,0:T(8,128)(2,1)S(1)} %copy-done.3, f32[192]{0:T(256)S(1)} %bitcast.92, bf16[1,192,384]{2,1,0:T(8,128)(2,1)} %copy-done.19, bf16[1,192,384]{2,1,0:T(8,128)(2,1)} %copy-done.18, bf16[1,192,384]{2,1,0:T(8,128)(2,1)} %copy-done.21, ...), kind=kLoop, calls=%fused_computation.28 | loop fusion | flops 6782976 | bytes 4129536 | tf_op jit(solution)/shard_map/broadcast_in_dim | solution.py:182
  (99 shorter events, 20.9 us)
Async XLA Ops:
  0.0 29.1 %copy-start = (f32[4,128]{1,0:T(4,128)S(1)}, f32[4,128]{1,0:T(4,128)}, u32[]{:S(2)}) copy-start(f32[4,128]{1,0:T(4,128)} %param.13) | copy-start | bytes 6148
  0.0 10.4 %copy-start.6 = (bf16[1,1,4,384,384]{4,3,2,1,0:T(8,128)(2,1)S(1)}, bf16[1,1,4,384,384]{4,3,2,1,0:T(8,128)(2,1)}, u32[]{:S(2)}) copy-start(bf16[1,1,4,384,384]{4,3,2,1,0:T(8,128)(2,1)} %param.10) | copy-start | bytes 3538948
  1.3 9.3 %collective-permute-start = (bf16[1,192,384]{2,1,0:T(8,128)(2,1)S(1)}, bf16[1,192,384]{2,1,0:T(8,128)(2,1)S(1)}, u32[]{:S(2)}, u32[]{:S(2)}) collective-permute-start(bf16[1,192,384]{2,1,0:T(8,128)(2,1)S(1)} %get-tuple-element.29), channel_id=1, source_target_pairs={{0,2},{2,4},{4,6},{6,8},{8,10},{10,12},{12,14},{14,16},{16,18},{18... | collective-permute-start | bytes 442376 | tf_op jit(solution)/shard_map/ppermute | solution.py:13
  6.1 8.2 %collective-permute-start.1 = (bf16[1,192,384]{2,1,0:T(8,128)(2,1)S(1)}, bf16[1,192,384]{2,1,0:T(8,128)(2,1)S(1)}, u32[]{:S(2)}, u32[]{:S(2)}) collective-permute-start(bf16[1,192,384]{2,1,0:T(8,128)(2,1)S(1)} %get-tuple-element.30), channel_id=1, source_target_pairs={{2,0},{4,2},{6,4},{8,6},{10,8},{12,10},{14,12},{16,14},{18,16},{20... | collective-permute-start | bytes 442376 | tf_op jit(solution)/shard_map/ppermute | solution.py:16
  7.4 6.9 %collective-permute-start.2 = (bf16[1,192,384]{2,1,0:T(8,128)(2,1)S(1)}, bf16[1,192,384]{2,1,0:T(8,128)(2,1)S(1)}, u32[]{:S(2)}, u32[]{:S(2)}) collective-permute-start(bf16[1,192,384]{2,1,0:T(8,128)(2,1)S(1)} %get-tuple-element.32), channel_id=1, source_target_pairs={{0,1},{2,3},{4,5},{6,7},{8,9},{10,11},{12,13},{14,15},{16,17},{18,... | collective-permute-start | bytes 442376 | tf_op jit(solution)/shard_map/ppermute | solution.py:13
  8.9 5.4 %collective-permute-start.3 = (bf16[1,192,384]{2,1,0:T(8,128)(2,1)S(1)}, bf16[1,192,384]{2,1,0:T(8,128)(2,1)S(1)}, u32[]{:S(2)}, u32[]{:S(2)}) collective-permute-start(bf16[1,192,384]{2,1,0:T(8,128)(2,1)S(1)} %get-tuple-element.31), channel_id=1, source_target_pairs={{1,0},{3,2},{5,4},{7,6},{9,8},{11,10},{13,12},{15,14},{17,16},{19,... | collective-permute-start | bytes 442376 | tf_op jit(solution)/shard_map/ppermute | solution.py:16
  15.1 8.5 %copy-start.7 = (bf16[4,192,384]{2,1,0:T(8,128)(2,1)}, bf16[4,192,384]{2,1,0:T(8,128)(2,1)S(1)}, u32[]{:S(2)}) copy-start(bf16[4,192,384]{2,1,0:T(8,128)(2,1)S(1)} %convolution_convert_fusion.1.scaled_ref) | copy-start | bytes 1769476
  16.0 13.1 %all-to-all-start = ((bf16[32,4,192]{2,1,0:T(4,128)(2,1)}), bf16[32,4,192]{2,1,0:T(4,128)(2,1)S(1)}, u32[]{:S(2)}, u32[]{:S(2)}) async-start(bf16[32,4,192]{2,1,0:T(4,128)(2,1)} %broadcast_in_dim.11), calls=%async_computation | async-start | bytes 131072 | tf_op jit(solution)/shard_map/all_to_all | solution.py:24
  35.6 21.8 %collective-permute-start.4 = (bf16[576,384]{1,0:T(8,128)(2,1)S(1)}, bf16[576,384]{1,0:T(8,128)(2,1)S(1)}, u32[]{:S(2)}, u32[]{:S(2)}) collective-permute-start(bf16[576,384]{1,0:T(8,128)(2,1)S(1)} %pad_maximum_fusion.6), channel_id=1, source_target_pairs={{0,2},{2,4},{4,6},{6,8},{8,10},{10,12},{12,14},{14,16},{16,18},{18... | collective-permute-start | bytes 1327112 | tf_op jit(solution)/shard_map/ppermute | solution.py:41
  38.2 21.1 %copy-start.3 = (bf16[4,192,384]{2,1,0:T(8,128)(2,1)S(1)}, bf16[4,192,384]{2,1,0:T(8,128)(2,1)}, u32[]{:S(2)}) copy-start(bf16[4,192,384]{2,1,0:T(8,128)(2,1)} %shard_map.74) | copy-start | bytes 1769476
  38.3 21.0 %collective-permute-start.5 = (bf16[576,384]{1,0:T(8,128)(2,1)S(1)}, bf16[576,384]{1,0:T(8,128)(2,1)S(1)}, u32[]{:S(2)}, u32[]{:S(2)}) collective-permute-start(bf16[576,384]{1,0:T(8,128)(2,1)S(1)} %pad_maximum_fusion.7), channel_id=1, source_target_pairs={{2,0},{4,2},{6,4},{8,6},{10,8},{12,10},{14,12},{16,14},{18,16},{20... | collective-permute-start | bytes 1327112 | tf_op jit(solution)/shard_map/ppermute | solution.py:41
  39.8 19.5 %collective-permute-start.6 = (bf16[576,384]{1,0:T(8,128)(2,1)S(1)}, bf16[576,384]{1,0:T(8,128)(2,1)S(1)}, u32[]{:S(2)}, u32[]{:S(2)}) collective-permute-start(bf16[576,384]{1,0:T(8,128)(2,1)S(1)} %pad_maximum_fusion.8), channel_id=1, source_target_pairs={{0,1},{2,3},{4,5},{6,7},{8,9},{10,11},{12,13},{14,15},{16,17},{18,... | collective-permute-start | bytes 1327112 | tf_op jit(solution)/shard_map/ppermute | solution.py:41
  41.6 17.7 %collective-permute-start.7 = (bf16[576,384]{1,0:T(8,128)(2,1)S(1)}, bf16[576,384]{1,0:T(8,128)(2,1)S(1)}, u32[]{:S(2)}, u32[]{:S(2)}) collective-permute-start(bf16[576,384]{1,0:T(8,128)(2,1)S(1)} %pad_maximum_fusion.9), channel_id=1, source_target_pairs={{1,0},{3,2},{5,4},{7,6},{9,8},{11,10},{13,12},{15,14},{17,16},{19,... | collective-permute-start | bytes 1327112 | tf_op jit(solution)/shard_map/ppermute | solution.py:41
  63.8 12.1 %all-to-all-start.1 = ((bf16[32,4,192]{2,1,0:T(4,128)(2,1)}), bf16[32,4,192]{2,1,0:T(4,128)(2,1)}, u32[]{:S(2)}, u32[]{:S(2)}) async-start(bf16[32,4,192]{2,1,0:T(4,128)(2,1)} %broadcast_in_dim.12), calls=%async_computation.1 | async-start | bytes 131072 | tf_op jit(solution)/shard_map/all_to_all | solution.py:24
  82.1 16.2 %copy-start.4 = (bf16[4,192,384]{2,1,0:T(8,128)(2,1)S(1)}, bf16[4,192,384]{2,1,0:T(8,128)(2,1)}, u32[]{:S(2)}) copy-start(bf16[4,192,384]{2,1,0:T(8,128)(2,1)} %shard_map.76) | copy-start | bytes 1769476
  83.3 7.0 %collective-permute-start.10 = (bf16[1,192,384]{2,1,0:T(8,128)(2,1)S(1)}, bf16[1,192,384]{2,1,0:T(8,128)(2,1)S(1)}, u32[]{:S(2)}, u32[]{:S(2)}) collective-permute-start(bf16[1,192,384]{2,1,0:T(8,128)(2,1)S(1)} %get-tuple-element.23), channel_id=1, source_target_pairs={{0,1},{2,3},{4,5},{6,7},{8,9},{10,11},{12,13},{14,15},{16,17},{18,... | collective-permute-start | bytes 442376 | tf_op jit(solution)/shard_map/ppermute | solution.py:13
  85.4 5.0 %collective-permute-start.11 = (bf16[1,192,384]{2,1,0:T(8,128)(2,1)S(1)}, bf16[1,192,384]{2,1,0:T(8,128)(2,1)S(1)}, u32[]{:S(2)}, u32[]{:S(2)}) collective-permute-start(bf16[1,192,384]{2,1,0:T(8,128)(2,1)S(1)} %get-tuple-element.22), channel_id=1, source_target_pairs={{1,0},{3,2},{5,4},{7,6},{9,8},{11,10},{13,12},{15,14},{17,16},{19,... | collective-permute-start | bytes 442376 | tf_op jit(solution)/shard_map/ppermute | solution.py:16
  86.7 6.4 %collective-permute-start.8 = (bf16[1,192,384]{2,1,0:T(8,128)(2,1)S(1)}, bf16[1,192,384]{2,1,0:T(8,128)(2,1)S(1)}, u32[]{:S(2)}, u32[]{:S(2)}) collective-permute-start(bf16[1,192,384]{2,1,0:T(8,128)(2,1)S(1)} %get-tuple-element.21), channel_id=1, source_target_pairs={{0,2},{2,4},{4,6},{6,8},{8,10},{10,12},{12,14},{14,16},{16,18},{18... | collective-permute-start | bytes 442376 | tf_op jit(solution)/shard_map/ppermute | solution.py:13
  89.0 9.2 %collective-permute-start.9 = (bf16[1,192,384]{2,1,0:T(8,128)(2,1)S(1)}, bf16[1,192,384]{2,1,0:T(8,128)(2,1)S(1)}, u32[]{:S(2)}, u32[]{:S(2)}) collective-permute-start(bf16[1,192,384]{2,1,0:T(8,128)(2,1)S(1)} %get-tuple-element.24), channel_id=1, source_target_pairs={{2,0},{4,2},{6,4},{8,6},{10,8},{12,10},{14,12},{16,14},{18,16},{20... | collective-permute-start | bytes 442376 | tf_op jit(solution)/shard_map/ppermute | solution.py:16
  90.3 8.8 %copy-start.18 = (bf16[1,192,384]{2,1,0:T(8,128)(2,1)}, bf16[1,192,384]{2,1,0:T(8,128)(2,1)S(1)}, u32[]{:S(2)}) copy-start(bf16[1,192,384]{2,1,0:T(8,128)(2,1)S(1)} %collective-permute-done.10) | copy-start | bytes 442372
  90.3 8.8 %copy-start.19 = (bf16[1,192,384]{2,1,0:T(8,128)(2,1)}, bf16[1,192,384]{2,1,0:T(8,128)(2,1)S(1)}, u32[]{:S(2)}) copy-start(bf16[1,192,384]{2,1,0:T(8,128)(2,1)S(1)} %collective-permute-done.11) | copy-start | bytes 442372
  93.1 6.1 %copy-start.20 = (bf16[1,192,384]{2,1,0:T(8,128)(2,1)}, bf16[1,192,384]{2,1,0:T(8,128)(2,1)S(1)}, u32[]{:S(2)}) copy-start(bf16[1,192,384]{2,1,0:T(8,128)(2,1)S(1)} %collective-permute-done.8) | copy-start | bytes 442372
  100.0 12.0 %copy-start.14 = (bf16[576,384]{1,0:T(8,128)(2,1)S(1)}, bf16[576,384]{1,0:T(8,128)(2,1)}, u32[]{:S(2)}) copy-start(bf16[576,384]{1,0:T(8,128)(2,1)} %copy-done.12) | copy-start | bytes 1327108
  100.0 12.0 %copy-start.17 = (bf16[576,384]{1,0:T(8,128)(2,1)S(1)}, bf16[576,384]{1,0:T(8,128)(2,1)}, u32[]{:S(2)}) copy-start(bf16[576,384]{1,0:T(8,128)(2,1)} %copy-done.15) | copy-start | bytes 1327108
  (19 other events, 39.4 us)

commit v16 on v15

--- a/solution.py
+++ b/solution.py
@@ -83,17 +83,17 @@
 
 
 def spread_kernel(softened_ref, coarse_ref, slots_ref, deluxe_ref, out_ref):
-    face = pl.program_id(0)
-    rows, width = softened_ref.shape[1], softened_ref.shape[2]
-    position = lax.broadcasted_iota(jnp.int32, (1, width), 1) + face * width
-    placed = jnp.zeros((rows, width), jnp.float32)
-    for k in range(coarse_ref.shape[1]):
-        hit = slots_ref[0:1, k:k + 1] == position
-        placed = placed + jnp.where(hit, coarse_ref[:, k:k + 1], 0.0)
-    weighted = (softened_ref[0] + placed).astype(jnp.bfloat16)
-    out_ref[0] = jnp.dot(
-        weighted, deluxe_ref[0], preferred_element_type=jnp.float32
-    ).astype(out_ref.dtype)
+    faces, rows, width = softened_ref.shape
+    for face in range(faces):
+        position = lax.broadcasted_iota(jnp.int32, (1, width), 1) + face * width
+        placed = jnp.zeros((rows, width), jnp.float32)
+        for k in range(coarse_ref.shape[1]):
+            hit = slots_ref[0:1, k:k + 1] == position
+            placed = placed + jnp.where(hit, coarse_ref[:, k:k + 1], 0.0)
+        weighted = (softened_ref[face] + placed).astype(jnp.bfloat16)
+        out_ref[face] = jnp.dot(
+            weighted, deluxe_ref[face], preferred_element_type=jnp.float32
+        ).astype(out_ref.dtype)
 
 
 def spread_of(softened, coarse, slots_block, deluxe):
@@ -101,14 +101,6 @@
     count = coarse.shape[0]
     return pl.pallas_call(
         spread_kernel,
-        grid=(faces,),
-        in_specs=[
-            pl.BlockSpec((1, rows, width), lambda f: (f, 0, 0)),
-            pl.BlockSpec((rows, count), lambda f: (0, 0)),
-            pl.BlockSpec(slots_block.shape, lambda f: (0, 0)),
-            pl.BlockSpec((1, width, width), lambda f: (f, 0, 0)),
-        ],
-        out_specs=pl.BlockSpec((1, rows, width), lambda f: (f, 0, 0)),
         out_shape=jax.ShapeDtypeStruct((faces, rows, width), jnp.bfloat16),
         cost_estimate=pl.CostEstimate(
             flops=2 * faces * rows * width * width,

time: 115 us -> 113 us (0.983)
  Pallas kernels: 17.4 us -> 15.5 us
    pallas_call x2, Pallas kernels: 8.64 us -> 6.71 us  [spread_of(): pl.pallas_call(spread_kernel, out_shape=jax.ShapeDtypeStruct((faces, rows...]
where the time goes in v16:
time: 113 us; the launch traced here: 112 us
  starting transfers between devices  33.5 us (30%)
  waiting for transfers between devices  32.1 us (28%)
  Pallas kernels  15.5 us (14%)
  blocking collectives  11.2 us (10%)
  local copies, waits for them, and re-layouts  9.99 us (9%)
  matrix products  6.02 us (5%)
  other arithmetic  3.6 us (3%)
    ppermute x4, waiting for transfers between devices, from_partner(): return lax.ppermute(values, axis, pairs)  16.4 us
    all_to_all x1, blocking collectives, gather_rows(): swapped = lax.all_to_all(spread, axes, 0, 0, tiled=False)  11.2 us
    ppermute x4, starting transfers between devices, with_halo(): lax.ppermute(lax.slice_in_dim(block, block.shape[dim] - width, None, axis...  10.7 us
    all_to_all x2, starting transfers between devices, gather_rows(): swapped = lax.all_to_all(spread, axes, 0, 0, tiled=False)  10.4 us
    ppermute x4, waiting for transfers between devices, with_halo(): lax.ppermute(lax.slice_in_dim(block, 0, width, axis=dim), axis, backward)  8.95 us
    pallas_call x2, Pallas kernels, soften(): pl.pallas_call(soften_kernel, grid=(faces,), in_specs=[pl.BlockSpec((1, r...  8.8 us
    ppermute x4, starting transfers between devices, from_partner(): return lax.ppermute(values, axis, pairs)  7.14 us
    pallas_call x2, Pallas kernels, spread_of(): pl.pallas_call(spread_kernel, out_shape=jax.ShapeDtypeStruct((faces, rows...  6.71 us
  transfers between devices with their start and end apart: 14, of which 7 were waited for; matrix products, arithmetic and copies ran while one was open for 2% of the time, Pallas kernels for 8%

profile of v16, /device:TPU:0, one launch (start us, length us, event | category | flops | bytes accessed | tf_op | source)
XLA Modules:
  0.0 112.4 jit_solution(5967054865313540479)
XLA Ops:
  1.3 4.9 %collective-permute-start = (bf16[1,192,384]{2,1,0:T(8,128)(2,1)S(1)}, bf16[1,192,384]{2,1,0:T(8,128)(2,1)S(1)}, u32[]{:S(2)}, u32[]{:S(2)}) collective-permute-start(bf16[1,192,384]{2,1,0:T(8,128)(2,1)S(1)} %get-tuple-element.29), channel_id=1, source_target_pairs={{0,2},{2,4},{4,6},{6,8},{8,10},{10,12},{12,14},{14,16},{16,18},{18... | collective-permute-start | bytes 442376 | tf_op jit(solution)/shard_map/ppermute | solution.py:13
  6.1 1.3 %collective-permute-start.1 = (bf16[1,192,384]{2,1,0:T(8,128)(2,1)S(1)}, bf16[1,192,384]{2,1,0:T(8,128)(2,1)S(1)}, u32[]{:S(2)}, u32[]{:S(2)}) collective-permute-start(bf16[1,192,384]{2,1,0:T(8,128)(2,1)S(1)} %get-tuple-element.30), channel_id=1, source_target_pairs={{2,0},{4,2},{6,4},{8,6},{10,8},{12,10},{14,12},{16,14},{18,16},{20... | collective-permute-start | bytes 442376 | tf_op jit(solution)/shard_map/ppermute | solution.py:16
  7.4 1.5 %collective-permute-start.2 = (bf16[1,192,384]{2,1,0:T(8,128)(2,1)S(1)}, bf16[1,192,384]{2,1,0:T(8,128)(2,1)S(1)}, u32[]{:S(2)}, u32[]{:S(2)}) collective-permute-start(bf16[1,192,384]{2,1,0:T(8,128)(2,1)S(1)} %get-tuple-element.32), channel_id=1, source_target_pairs={{0,1},{2,3},{4,5},{6,7},{8,9},{10,11},{12,13},{14,15},{16,17},{18,... | collective-permute-start | bytes 442376 | tf_op jit(solution)/shard_map/ppermute | solution.py:13
  8.9 1.4 %collective-permute-start.3 = (bf16[1,192,384]{2,1,0:T(8,128)(2,1)S(1)}, bf16[1,192,384]{2,1,0:T(8,128)(2,1)S(1)}, u32[]{:S(2)}, u32[]{:S(2)}) collective-permute-start(bf16[1,192,384]{2,1,0:T(8,128)(2,1)S(1)} %get-tuple-element.31), channel_id=1, source_target_pairs={{1,0},{3,2},{5,4},{7,6},{9,8},{11,10},{13,12},{15,14},{17,16},{19,... | collective-permute-start | bytes 442376 | tf_op jit(solution)/shard_map/ppermute | solution.py:16
  10.6 3.8 %collective-permute-done.1 = bf16[1,192,384]{2,1,0:T(8,128)(2,1)S(1)} collective-permute-done((bf16[1,192,384]{2,1,0:T(8,128)(2,1)S(1)}, bf16[1,192,384]{2,1,0:T(8,128)(2,1)S(1)}, u32[]{:S(2)}, u32[]{:S(2)}) %collective-permute-start.1) | collective-permute-done | bytes 147488 | tf_op jit(solution)/shard_map/ppermute | solution.py:16
  16.0 5.6 %all-to-all-start = ((bf16[32,4,192]{2,1,0:T(4,128)(2,1)}), bf16[32,4,192]{2,1,0:T(4,128)(2,1)S(1)}, u32[]{:S(2)}, u32[]{:S(2)}) async-start(bf16[32,4,192]{2,1,0:T(4,128)(2,1)} %broadcast_in_dim.11), calls=%async_computation | async-start | bytes 131072 | tf_op jit(solution)/shard_map/all_to_all | solution.py:24
  23.6 4.4 %shard_map.73.softened_ref = f32[4,192,384]{2,1,0:T(8,128)} custom-call(bf16[4,192,384]{2,1,0:T(8,128)(2,1)} %copy-done.7, bf16[4,384,384]{2,1,0:T(8,128)(2,1)} %bitcast.71, f32[4,8,128]{2,1,0:T(8,128)} %broadcast_in_dim.10.flags_ref), custom_call_target="tpu_custom_call" | custom-call | flops 452984832 | bytes 2949120 | tf_op jit(solution)/shard_map/pallas_call | solution.py:67
  30.0 3.4 %shard_map.74 = bf16[4,192,384]{2,1,0:T(8,128)(2,1)} custom-call(f32[4,192,384]{2,1,0:T(8,128)} %shard_map.73.softened_ref, f32[192,4]{1,0:T(8,128)} %fusion.30.coarse_ref, s32[8,128]{1,0:T(8,128)} %scatter.4.slots_ref, bf16[4,384,384]{2,1,0:T(8,128)(2,1)} %bitcast.69), custom_call_target="tpu_custom_call" | custom-call | flops 226492416 | bytes 2949120 | tf_op jit(solution)/shard_map/pallas_call | solution.py:102
  34.6 2.6 %collective-permute-start.4 = (bf16[576,384]{1,0:T(8,128)(2,1)S(1)}, bf16[576,384]{1,0:T(8,128)(2,1)S(1)}, u32[]{:S(2)}, u32[]{:S(2)}) collective-permute-start(bf16[576,384]{1,0:T(8,128)(2,1)S(1)} %pad_maximum_fusion.6), channel_id=1, source_target_pairs={{0,2},{2,4},{4,6},{6,8},{8,10},{10,12},{12,14},{14,16},{16,18},{18... | collective-permute-start | bytes 1327112 | tf_op jit(solution)/shard_map/ppermute | solution.py:41
  37.3 1.4 %collective-permute-start.5 = (bf16[576,384]{1,0:T(8,128)(2,1)S(1)}, bf16[576,384]{1,0:T(8,128)(2,1)S(1)}, u32[]{:S(2)}, u32[]{:S(2)}) collective-permute-start(bf16[576,384]{1,0:T(8,128)(2,1)S(1)} %pad_maximum_fusion.7), channel_id=1, source_target_pairs={{2,0},{4,2},{6,4},{8,6},{10,8},{12,10},{14,12},{16,14},{18,16},{20... | collective-permute-start | bytes 1327112 | tf_op jit(solution)/shard_map/ppermute | solution.py:41
  38.8 1.8 %collective-permute-start.6 = (bf16[576,384]{1,0:T(8,128)(2,1)S(1)}, bf16[576,384]{1,0:T(8,128)(2,1)S(1)}, u32[]{:S(2)}, u32[]{:S(2)}) collective-permute-start(bf16[576,384]{1,0:T(8,128)(2,1)S(1)} %pad_maximum_fusion.8), channel_id=1, source_target_pairs={{0,1},{2,3},{4,5},{6,7},{8,9},{10,11},{12,13},{14,15},{16,17},{18,... | collective-permute-start | bytes 1327112 | tf_op jit(solution)/shard_map/ppermute | solution.py:41
  42.0 14.5 %collective-permute-done.4 = bf16[576,384]{1,0:T(8,128)(2,1)S(1)} collective-permute-done((bf16[576,384]{1,0:T(8,128)(2,1)S(1)}, bf16[576,384]{1,0:T(8,128)(2,1)S(1)}, u32[]{:S(2)}, u32[]{:S(2)}) %collective-permute-start.4) | collective-permute-done | bytes 442400 | tf_op jit(solution)/shard_map/ppermute | solution.py:41
  56.4 1.9 %collective-permute-done.5 = bf16[576,384]{1,0:T(8,128)(2,1)S(1)} collective-permute-done((bf16[576,384]{1,0:T(8,128)(2,1)S(1)}, bf16[576,384]{1,0:T(8,128)(2,1)S(1)}, u32[]{:S(2)}, u32[]{:S(2)}) %collective-permute-start.5) | collective-permute-done | bytes 442400 | tf_op jit(solution)/shard_map/ppermute | solution.py:41
  62.9 4.8 %all-to-all-start.1 = ((bf16[32,4,192]{2,1,0:T(4,128)(2,1)}), bf16[32,4,192]{2,1,0:T(4,128)(2,1)}, u32[]{:S(2)}, u32[]{:S(2)}) async-start(bf16[32,4,192]{2,1,0:T(4,128)(2,1)} %broadcast_in_dim.12), calls=%async_computation.1 | async-start | bytes 131072 | tf_op jit(solution)/shard_map/all_to_all | solution.py:24
  67.6 4.4 %shard_map.75.softened_ref = f32[4,192,384]{2,1,0:T(8,128)} custom-call(bf16[4,192,384]{2,1,0:T(8,128)(2,1)} %copy-done.5, bf16[4,384,384]{2,1,0:T(8,128)(2,1)} %bitcast.72, f32[4,8,128]{2,1,0:T(8,128)} %broadcast_in_dim.10.flags_ref), custom_call_target="tpu_custom_call" | custom-call | flops 452984832 | bytes 2949120 | tf_op jit(solution)/shard_map/pallas_call | solution.py:67
  72.0 3.0 %all-to-all-done.1 = bf16[32,4,192]{2,1,0:T(4,128)(2,1)} async-done(((bf16[32,4,192]{2,1,0:T(4,128)(2,1)}), bf16[32,4,192]{2,1,0:T(4,128)(2,1)}, u32[]{:S(2)}, u32[]{:S(2)}) %all-to-all-start.1) | async-done | bytes 49184 | tf_op jit(solution)/shard_map/all_to_all | solution.py:24
  76.8 3.4 %shard_map.76 = bf16[4,192,384]{2,1,0:T(8,128)(2,1)} custom-call(f32[4,192,384]{2,1,0:T(8,128)} %shard_map.75.softened_ref, f32[192,4]{1,0:T(8,128)} %fusion.31.coarse_ref, s32[8,128]{1,0:T(8,128)} %scatter.4.slots_ref, bf16[4,384,384]{2,1,0:T(8,128)(2,1)} %bitcast.70), custom_call_target="tpu_custom_call" | custom-call | flops 226492416 | bytes 2949120 | tf_op jit(solution)/shard_map/pallas_call | solution.py:102
  81.4 2.0 %collective-permute-start.10 = (bf16[1,192,384]{2,1,0:T(8,128)(2,1)S(1)}, bf16[1,192,384]{2,1,0:T(8,128)(2,1)S(1)}, u32[]{:S(2)}, u32[]{:S(2)}) collective-permute-start(bf16[1,192,384]{2,1,0:T(8,128)(2,1)S(1)} %get-tuple-element.23), channel_id=1, source_target_pairs={{0,1},{2,3},{4,5},{6,7},{8,9},{10,11},{12,13},{14,15},{16,17},{18,... | collective-permute-start | bytes 442376 | tf_op jit(solution)/shard_map/ppermute | solution.py:13
  84.7 2.3 %collective-permute-start.8 = (bf16[1,192,384]{2,1,0:T(8,128)(2,1)S(1)}, bf16[1,192,384]{2,1,0:T(8,128)(2,1)S(1)}, u32[]{:S(2)}, u32[]{:S(2)}) collective-permute-start(bf16[1,192,384]{2,1,0:T(8,128)(2,1)S(1)} %get-tuple-element.21), channel_id=1, source_target_pairs={{0,2},{2,4},{4,6},{6,8},{8,10},{10,12},{12,14},{14,16},{16,18},{18... | collective-permute-start | bytes 442376 | tf_op jit(solution)/shard_map/ppermute | solution.py:13
  87.1 1.3 %collective-permute-start.9 = (bf16[1,192,384]{2,1,0:T(8,128)(2,1)S(1)}, bf16[1,192,384]{2,1,0:T(8,128)(2,1)S(1)}, u32[]{:S(2)}, u32[]{:S(2)}) collective-permute-start(bf16[1,192,384]{2,1,0:T(8,128)(2,1)S(1)} %get-tuple-element.24), channel_id=1, source_target_pairs={{2,0},{4,2},{6,4},{8,6},{10,8},{12,10},{14,12},{16,14},{18,16},{20... | collective-permute-start | bytes 442376 | tf_op jit(solution)/shard_map/ppermute | solution.py:16
  88.4 2.7 %collective-permute-done.8 = bf16[1,192,384]{2,1,0:T(8,128)(2,1)S(1)} collective-permute-done((bf16[1,192,384]{2,1,0:T(8,128)(2,1)S(1)}, bf16[1,192,384]{2,1,0:T(8,128)(2,1)S(1)}, u32[]{:S(2)}, u32[]{:S(2)}) %collective-permute-start.8) | collective-permute-done | bytes 147488 | tf_op jit(solution)/shard_map/ppermute | solution.py:13
  91.1 5.2 %collective-permute-done.9 = bf16[1,192,384]{2,1,0:T(8,128)(2,1)S(1)} collective-permute-done((bf16[1,192,384]{2,1,0:T(8,128)(2,1)S(1)}, bf16[1,192,384]{2,1,0:T(8,128)(2,1)S(1)}, u32[]{:S(2)}, u32[]{:S(2)}) %collective-permute-start.9) | collective-permute-done | bytes 147488 | tf_op jit(solution)/shard_map/ppermute | solution.py:16
  98.8 11.2 %all_to_all.15 = f32[32,1,2,192]{3,2,1,0:T(2,128)S(1)} all-to-all(f32[32,1,2,192]{3,2,1,0:T(2,128)S(1)} %broadcast_in_dim.13), channel_id=1, replica_groups=mesh['gx'=16,'gy'=2] {'gx','gy'}, dimensions={0} | all-to-all | bytes 98304 | tf_op jit(solution)/shard_map/all_to_all | solution.py:24
  110.1 2.4 %fusion.15 = bf16[1,1,4,192,384]{4,3,2,1,0:T(8,128)(2,1)} fusion(bf16[4,192,384]{2,1,0:T(8,128)(2,1)S(1)} %copy-done.4, bf16[4,192,384]{2,1,0:T(8,128)(2,1)S(1)} %copy-done.3, f32[192]{0:T(256)S(1)} %bitcast.92, bf16[1,192,384]{2,1,0:T(8,128)(2,1)} %copy-done.19, bf16[1,192,384]{2,1,0:T(8,128)(2,1)} %copy-done.18, bf16[1,192,384]{2,1,0:T(8,128)(2,1)} %copy-done.21, ...), kind=kLoop, calls=%fused_computation.28 | loop fusion | flops 6782976 | bytes 4129536 | tf_op jit(solution)/shard_map/broadcast_in_dim | solution.py:174
  (99 shorter events, 20.9 us)
Async XLA Ops:
  0.0 29.1 %copy-start = (f32[4,128]{1,0:T(4,128)S(1)}, f32[4,128]{1,0:T(4,128)}, u32[]{:S(2)}) copy-start(f32[4,128]{1,0:T(4,128)} %param.13) | copy-start | bytes 6148
  0.0 10.4 %copy-start.6 = (bf16[1,1,4,384,384]{4,3,2,1,0:T(8,128)(2,1)S(1)}, bf16[1,1,4,384,384]{4,3,2,1,0:T(8,128)(2,1)}, u32[]{:S(2)}) copy-start(bf16[1,1,4,384,384]{4,3,2,1,0:T(8,128)(2,1)} %param.10) | copy-start | bytes 3538948
  1.3 9.3 %collective-permute-start = (bf16[1,192,384]{2,1,0:T(8,128)(2,1)S(1)}, bf16[1,192,384]{2,1,0:T(8,128)(2,1)S(1)}, u32[]{:S(2)}, u32[]{:S(2)}) collective-permute-start(bf16[1,192,384]{2,1,0:T(8,128)(2,1)S(1)} %get-tuple-element.29), channel_id=1, source_target_pairs={{0,2},{2,4},{4,6},{6,8},{8,10},{10,12},{12,14},{14,16},{16,18},{18... | collective-permute-start | bytes 442376 | tf_op jit(solution)/shard_map/ppermute | solution.py:13
  6.1 8.2 %collective-permute-start.1 = (bf16[1,192,384]{2,1,0:T(8,128)(2,1)S(1)}, bf16[1,192,384]{2,1,0:T(8,128)(2,1)S(1)}, u32[]{:S(2)}, u32[]{:S(2)}) collective-permute-start(bf16[1,192,384]{2,1,0:T(8,128)(2,1)S(1)} %get-tuple-element.30), channel_id=1, source_target_pairs={{2,0},{4,2},{6,4},{8,6},{10,8},{12,10},{14,12},{16,14},{18,16},{20... | collective-permute-start | bytes 442376 | tf_op jit(solution)/shard_map/ppermute | solution.py:16
  7.4 6.9 %collective-permute-start.2 = (bf16[1,192,384]{2,1,0:T(8,128)(2,1)S(1)}, bf16[1,192,384]{2,1,0:T(8,128)(2,1)S(1)}, u32[]{:S(2)}, u32[]{:S(2)}) collective-permute-start(bf16[1,192,384]{2,1,0:T(8,128)(2,1)S(1)} %get-tuple-element.32), channel_id=1, source_target_pairs={{0,1},{2,3},{4,5},{6,7},{8,9},{10,11},{12,13},{14,15},{16,17},{18,... | collective-permute-start | bytes 442376 | tf_op jit(solution)/shard_map/ppermute | solution.py:13
  8.9 5.4 %collective-permute-start.3 = (bf16[1,192,384]{2,1,0:T(8,128)(2,1)S(1)}, bf16[1,192,384]{2,1,0:T(8,128)(2,1)S(1)}, u32[]{:S(2)}, u32[]{:S(2)}) collective-permute-start(bf16[1,192,384]{2,1,0:T(8,128)(2,1)S(1)} %get-tuple-element.31), channel_id=1, source_target_pairs={{1,0},{3,2},{5,4},{7,6},{9,8},{11,10},{13,12},{15,14},{17,16},{19,... | collective-permute-start | bytes 442376 | tf_op jit(solution)/shard_map/ppermute | solution.py:16
  15.1 8.5 %copy-start.7 = (bf16[4,192,384]{2,1,0:T(8,128)(2,1)}, bf16[4,192,384]{2,1,0:T(8,128)(2,1)S(1)}, u32[]{:S(2)}) copy-start(bf16[4,192,384]{2,1,0:T(8,128)(2,1)S(1)} %convolution_convert_fusion.1.scaled_ref) | copy-start | bytes 1769476
  16.0 13.1 %all-to-all-start = ((bf16[32,4,192]{2,1,0:T(4,128)(2,1)}), bf16[32,4,192]{2,1,0:T(4,128)(2,1)S(1)}, u32[]{:S(2)}, u32[]{:S(2)}) async-start(bf16[32,4,192]{2,1,0:T(4,128)(2,1)} %broadcast_in_dim.11), calls=%async_computation | async-start | bytes 131072 | tf_op jit(solution)/shard_map/all_to_all | solution.py:24
  34.6 21.8 %collective-permute-start.4 = (bf16[576,384]{1,0:T(8,128)(2,1)S(1)}, bf16[576,384]{1,0:T(8,128)(2,1)S(1)}, u32[]{:S(2)}, u32[]{:S(2)}) collective-permute-start(bf16[576,384]{1,0:T(8,128)(2,1)S(1)} %pad_maximum_fusion.6), channel_id=1, source_target_pairs={{0,2},{2,4},{4,6},{6,8},{8,10},{10,12},{12,14},{14,16},{16,18},{18... | collective-permute-start | bytes 1327112 | tf_op jit(solution)/shard_map/ppermute | solution.py:41
  37.3 21.1 %copy-start.3 = (bf16[4,192,384]{2,1,0:T(8,128)(2,1)S(1)}, bf16[4,192,384]{2,1,0:T(8,128)(2,1)}, u32[]{:S(2)}) copy-start(bf16[4,192,384]{2,1,0:T(8,128)(2,1)} %shard_map.74) | copy-start | bytes 1769476
  37.3 21.0 %collective-permute-start.5 = (bf16[576,384]{1,0:T(8,128)(2,1)S(1)}, bf16[576,384]{1,0:T(8,128)(2,1)S(1)}, u32[]{:S(2)}, u32[]{:S(2)}) collective-permute-start(bf16[576,384]{1,0:T(8,128)(2,1)S(1)} %pad_maximum_fusion.7), channel_id=1, source_target_pairs={{2,0},{4,2},{6,4},{8,6},{10,8},{12,10},{14,12},{16,14},{18,16},{20... | collective-permute-start | bytes 1327112 | tf_op jit(solution)/shard_map/ppermute | solution.py:41
  38.8 19.5 %collective-permute-start.6 = (bf16[576,384]{1,0:T(8,128)(2,1)S(1)}, bf16[576,384]{1,0:T(8,128)(2,1)S(1)}, u32[]{:S(2)}, u32[]{:S(2)}) collective-permute-start(bf16[576,384]{1,0:T(8,128)(2,1)S(1)} %pad_maximum_fusion.8), channel_id=1, source_target_pairs={{0,1},{2,3},{4,5},{6,7},{8,9},{10,11},{12,13},{14,15},{16,17},{18,... | collective-permute-start | bytes 1327112 | tf_op jit(solution)/shard_map/ppermute | solution.py:41
  40.7 17.7 %collective-permute-start.7 = (bf16[576,384]{1,0:T(8,128)(2,1)S(1)}, bf16[576,384]{1,0:T(8,128)(2,1)S(1)}, u32[]{:S(2)}, u32[]{:S(2)}) collective-permute-start(bf16[576,384]{1,0:T(8,128)(2,1)S(1)} %pad_maximum_fusion.9), channel_id=1, source_target_pairs={{1,0},{3,2},{5,4},{7,6},{9,8},{11,10},{13,12},{15,14},{17,16},{19,... | collective-permute-start | bytes 1327112 | tf_op jit(solution)/shard_map/ppermute | solution.py:41
  62.9 12.1 %all-to-all-start.1 = ((bf16[32,4,192]{2,1,0:T(4,128)(2,1)}), bf16[32,4,192]{2,1,0:T(4,128)(2,1)}, u32[]{:S(2)}, u32[]{:S(2)}) async-start(bf16[32,4,192]{2,1,0:T(4,128)(2,1)} %broadcast_in_dim.12), calls=%async_computation.1 | async-start | bytes 131072 | tf_op jit(solution)/shard_map/all_to_all | solution.py:24
  80.1 16.2 %copy-start.4 = (bf16[4,192,384]{2,1,0:T(8,128)(2,1)S(1)}, bf16[4,192,384]{2,1,0:T(8,128)(2,1)}, u32[]{:S(2)}) copy-start(bf16[4,192,384]{2,1,0:T(8,128)(2,1)} %shard_map.76) | copy-start | bytes 1769476
  81.4 7.0 %collective-permute-start.10 = (bf16[1,192,384]{2,1,0:T(8,128)(2,1)S(1)}, bf16[1,192,384]{2,1,0:T(8,128)(2,1)S(1)}, u32[]{:S(2)}, u32[]{:S(2)}) collective-permute-start(bf16[1,192,384]{2,1,0:T(8,128)(2,1)S(1)} %get-tuple-element.23), channel_id=1, source_target_pairs={{0,1},{2,3},{4,5},{6,7},{8,9},{10,11},{12,13},{14,15},{16,17},{18,... | collective-permute-start | bytes 442376 | tf_op jit(solution)/shard_map/ppermute | solution.py:13
  83.4 5.0 %collective-permute-start.11 = (bf16[1,192,384]{2,1,0:T(8,128)(2,1)S(1)}, bf16[1,192,384]{2,1,0:T(8,128)(2,1)S(1)}, u32[]{:S(2)}, u32[]{:S(2)}) collective-permute-start(bf16[1,192,384]{2,1,0:T(8,128)(2,1)S(1)} %get-tuple-element.22), channel_id=1, source_target_pairs={{1,0},{3,2},{5,4},{7,6},{9,8},{11,10},{13,12},{15,14},{17,16},{19,... | collective-permute-start | bytes 442376 | tf_op jit(solution)/shard_map/ppermute | solution.py:16
  84.7 6.4 %collective-permute-start.8 = (bf16[1,192,384]{2,1,0:T(8,128)(2,1)S(1)}, bf16[1,192,384]{2,1,0:T(8,128)(2,1)S(1)}, u32[]{:S(2)}, u32[]{:S(2)}) collective-permute-start(bf16[1,192,384]{2,1,0:T(8,128)(2,1)S(1)} %get-tuple-element.21), channel_id=1, source_target_pairs={{0,2},{2,4},{4,6},{6,8},{8,10},{10,12},{12,14},{14,16},{16,18},{18... | collective-permute-start | bytes 442376 | tf_op jit(solution)/shard_map/ppermute | solution.py:13
  87.1 9.2 %collective-permute-start.9 = (bf16[1,192,384]{2,1,0:T(8,128)(2,1)S(1)}, bf16[1,192,384]{2,1,0:T(8,128)(2,1)S(1)}, u32[]{:S(2)}, u32[]{:S(2)}) collective-permute-start(bf16[1,192,384]{2,1,0:T(8,128)(2,1)S(1)} %get-tuple-element.24), channel_id=1, source_target_pairs={{2,0},{4,2},{6,4},{8,6},{10,8},{12,10},{14,12},{16,14},{18,16},{20... | collective-permute-start | bytes 442376 | tf_op jit(solution)/shard_map/ppermute | solution.py:16
  88.4 8.8 %copy-start.18 = (bf16[1,192,384]{2,1,0:T(8,128)(2,1)}, bf16[1,192,384]{2,1,0:T(8,128)(2,1)S(1)}, u32[]{:S(2)}) copy-start(bf16[1,192,384]{2,1,0:T(8,128)(2,1)S(1)} %collective-permute-done.10) | copy-start | bytes 442372
  88.4 8.8 %copy-start.19 = (bf16[1,192,384]{2,1,0:T(8,128)(2,1)}, bf16[1,192,384]{2,1,0:T(8,128)(2,1)S(1)}, u32[]{:S(2)}) copy-start(bf16[1,192,384]{2,1,0:T(8,128)(2,1)S(1)} %collective-permute-done.11) | copy-start | bytes 442372
  91.1 6.1 %copy-start.20 = (bf16[1,192,384]{2,1,0:T(8,128)(2,1)}, bf16[1,192,384]{2,1,0:T(8,128)(2,1)S(1)}, u32[]{:S(2)}) copy-start(bf16[1,192,384]{2,1,0:T(8,128)(2,1)S(1)} %collective-permute-done.8) | copy-start | bytes 442372
  98.0 12.0 %copy-start.14 = (bf16[576,384]{1,0:T(8,128)(2,1)S(1)}, bf16[576,384]{1,0:T(8,128)(2,1)}, u32[]{:S(2)}) copy-start(bf16[576,384]{1,0:T(8,128)(2,1)} %copy-done.12) | copy-start | bytes 1327108
  98.0 12.0 %copy-start.17 = (bf16[576,384]{1,0:T(8,128)(2,1)S(1)}, bf16[576,384]{1,0:T(8,128)(2,1)}, u32[]{:S(2)}) copy-start(bf16[576,384]{1,0:T(8,128)(2,1)} %copy-done.15) | copy-start | bytes 1327108
  (19 other events, 39.4 us)

commit v17 on v14

--- a/solution.py
+++ b/solution.py
@@ -100,7 +100,6 @@
     positions = jnp.arange(4 * width, dtype=jnp.int32)
     picks = (primal_slots[:, None] == positions[None, :]).reshape(primal_count, 4, width)
     picks_half = picks.astype(jnp.bfloat16)
-    picks_full = picks.astype(jnp.float32)
     flags_full = flag_values.astype(jnp.float32)
 
     def add_coarse(piece):
@@ -113,7 +112,9 @@
             "kfx,frx->kr", picks_half, scaled, preferred_element_type=jnp.float32
         ).astype(jnp.bfloat16)
         coarse = add_coarse(gather_rows(primal, ("gx", "gy")))
-        placed = jnp.einsum("kfx,kr->frx", picks_full, coarse, precision=lax.Precision.HIGHEST)
+        placed = jnp.zeros_like(softened)
+        for k in range(primal_count):
+            placed = placed + jnp.where(picks[k][:, None, :], coarse[k][None, :, None], 0.0)
         weighted = (softened + placed).astype(jnp.bfloat16)
         spread = face_mul(weighted, deluxe_panel).astype(jnp.bfloat16)
         if schur_partner is not None:

time: 109 us -> 116 us (1.064)
  starting transfers between devices: 32.9 us -> 39.7 us
  waiting for transfers between devices: 32.1 us -> 26.1 us
  local copies, waits for them, and re-layouts: 9.51 us -> 15.5 us
  matrix products: 9.5 us -> 8.28 us
    broadcast_in_dim x0 -> x4, local copies, waits for them, and re-layouts: none -> 4.95 us  [precondition(): jnp.where(picks[k][:, None, :], coarse[k][None, :, None], 0.0)]
    dot_general x2 -> x0, matrix products: 4.01 us -> none  [precondition(): jnp.einsum('kfx,kr->frx', picks_full, coarse, precision=lax.Precision.HIG...]
    ppermute x4, starting transfers between devices: 6.72 us -> 9.96 us  [from_partner(): return lax.ppermute(values, axis, pairs)]
    dot_general x6, matrix products: 3.45 us -> 6.24 us  [face_mul(): jnp.einsum('fry,fyx->frx', vectors, matrices, preferred_element_type=jnp....]
    ppermute x4, waiting for transfers between devices: 2.72 us -> 0.01 us  [with_halo(): lax.ppermute(lax.slice_in_dim(block, block.shape[dim] - width, None, axis...]
    ppermute x4, starting transfers between devices: 10.8 us -> 13.4 us  [with_halo(): lax.ppermute(lax.slice_in_dim(block, block.shape[dim] - width, None, axis...]
    all_to_all x2, waiting for transfers between devices: 4.6 us -> 2.93 us  [gather_rows(): swapped = lax.all_to_all(spread, axes, 0, 0, tiled=False)]
    ppermute x4, waiting for transfers between devices: 8.16 us -> 6.54 us  [with_halo(): lax.ppermute(lax.slice_in_dim(block, 0, width, axis=dim), axis, backward)]
  transfers between devices with their start and end apart: 14 -> 14, of which waited for: 7 -> 5; matrix products, arithmetic and copies ran while one was open for 2% -> 8% of each run, Pallas kernels for 8% -> 8%
where the time goes in v17:
time: 116 us; the launch traced here: 115 us
  starting transfers between devices  39.7 us (34%)
  waiting for transfers between devices  26.1 us (22%)
  local copies, waits for them, and re-layouts  15.5 us (13%)
  blocking collectives  12.2 us (11%)
  Pallas kernels  8.81 us (8%)
  matrix products  8.28 us (7%)
  other arithmetic  3.65 us (3%)
    ppermute x4, waiting for transfers between devices, from_partner(): return lax.ppermute(values, axis, pairs)  16.6 us
    ppermute x4, starting transfers between devices, with_halo(): lax.ppermute(lax.slice_in_dim(block, block.shape[dim] - width, None, axis...  13.4 us
    all_to_all x1, blocking collectives, gather_rows(): swapped = lax.all_to_all(spread, axes, 0, 0, tiled=False)  12.2 us
    all_to_all x2, starting transfers between devices, gather_rows(): swapped = lax.all_to_all(spread, axes, 0, 0, tiled=False)  11.1 us
    ppermute x4, starting transfers between devices, from_partner(): return lax.ppermute(values, axis, pairs)  9.96 us
    pallas_call x2, Pallas kernels, soften(): pl.pallas_call(soften_kernel, grid=(faces,), in_specs=[pl.BlockSpec((1, r...  8.81 us
    ppermute x4, waiting for transfers between devices, with_halo(): lax.ppermute(lax.slice_in_dim(block, 0, width, axis=dim), axis, backward)  6.54 us
    dot_general x6, matrix products, face_mul(): jnp.einsum('fry,fyx->frx', vectors, matrices, preferred_element_type=jnp....  6.24 us
  transfers between devices with their start and end apart: 14, of which 5 were waited for; matrix products, arithmetic and copies ran while one was open for 8% of the time, Pallas kernels for 8%

profile of v17, /device:TPU:0, one launch (start us, length us, event | category | flops | bytes accessed | tf_op | source)
XLA Modules:
  0.0 114.9 jit_solution(11178985601077389662)
XLA Ops:
  0.0 1.3 %slice_bitcast_fusion.11 = (bf16[1,192,384]{2,1,0:T(8,128)(2,1)S(1)}, bf16[1,192,384]{2,1,0:T(8,128)(2,1)S(1)}, bf16[1,192,384]{2,1,0:T(8,128)(2,1)S(1)}, bf16[1,192,384]{2,1,0:T(8,128)(2,1)S(1)}) fusion(bf16[1,1,4,192,384]{4,3,2,1,0:T(8,128)(2,1)} %param.7), kind=kLoop, calls=%fused_computation.77 | loop fusion | bytes 1179648 | tf_op jit(solution)/shard_map/slice | solution.py:14
  1.3 4.9 %collective-permute-start = (bf16[1,192,384]{2,1,0:T(8,128)(2,1)S(1)}, bf16[1,192,384]{2,1,0:T(8,128)(2,1)S(1)}, u32[]{:S(2)}, u32[]{:S(2)}) collective-permute-start(bf16[1,192,384]{2,1,0:T(8,128)(2,1)S(1)} %get-tuple-element.21), channel_id=1, source_target_pairs={{0,2},{2,4},{4,6},{6,8},{8,10},{10,12},{12,14},{14,16},{16,18},{18... | collective-permute-start | bytes 442376 | tf_op jit(solution)/shard_map/ppermute | solution.py:13
  6.2 1.3 %collective-permute-start.1 = (bf16[1,192,384]{2,1,0:T(8,128)(2,1)S(1)}, bf16[1,192,384]{2,1,0:T(8,128)(2,1)S(1)}, u32[]{:S(2)}, u32[]{:S(2)}) collective-permute-start(bf16[1,192,384]{2,1,0:T(8,128)(2,1)S(1)} %get-tuple-element.22), channel_id=1, source_target_pairs={{2,0},{4,2},{6,4},{8,6},{10,8},{12,10},{14,12},{16,14},{18,16},{20... | collective-permute-start | bytes 442376 | tf_op jit(solution)/shard_map/ppermute | solution.py:16
  7.5 1.3 %collective-permute-start.3 = (bf16[1,192,384]{2,1,0:T(8,128)(2,1)S(1)}, bf16[1,192,384]{2,1,0:T(8,128)(2,1)S(1)}, u32[]{:S(2)}, u32[]{:S(2)}) collective-permute-start(bf16[1,192,384]{2,1,0:T(8,128)(2,1)S(1)} %get-tuple-element.23), channel_id=1, source_target_pairs={{1,0},{3,2},{5,4},{7,6},{9,8},{11,10},{13,12},{15,14},{17,16},{19,... | collective-permute-start | bytes 442376 | tf_op jit(solution)/shard_map/ppermute | solution.py:16
  8.8 3.0 %collective-permute-start.2 = (bf16[1,192,384]{2,1,0:T(8,128)(2,1)S(1)}, bf16[1,192,384]{2,1,0:T(8,128)(2,1)S(1)}, u32[]{:S(2)}, u32[]{:S(2)}) collective-permute-start(bf16[1,192,384]{2,1,0:T(8,128)(2,1)S(1)} %get-tuple-element.24), channel_id=1, source_target_pairs={{0,1},{2,3},{4,5},{6,7},{8,9},{10,11},{12,13},{14,15},{16,17},{18,... | collective-permute-start | bytes 442376 | tf_op jit(solution)/shard_map/ppermute | solution.py:13
  16.1 6.3 %all-to-all-start = ((bf16[32,4,192]{2,1,0:T(4,128)(2,1)}), bf16[32,4,192]{2,1,0:T(4,128)(2,1)}, u32[]{:S(2)}, u32[]{:S(2)}) async-start(bf16[32,4,192]{2,1,0:T(4,128)(2,1)} %broadcast_in_dim.147), calls=%async_computation | async-start | bytes 131072 | tf_op jit(solution)/shard_map/all_to_all | solution.py:24
  28.0 1.3 %broadcast_in_dim.144.flags_ref = f32[4,8,128]{2,1,0:T(8,128)} broadcast(f32[4]{0:T(128)} %multiply_bitcast_fusion), dimensions={0} | broadcast | bytes 16400 | tf_op jit(solution)/shard_map/broadcast_in_dim | solution.py:66
  29.4 4.4 %shard_map.73 = f32[4,192,384]{2,1,0:T(8,128)} custom-call(bf16[4,192,384]{2,1,0:T(8,128)(2,1)} %copy-done.5, bf16[4,384,384]{2,1,0:T(8,128)(2,1)} %bitcast.84, f32[4,8,128]{2,1,0:T(8,128)} %broadcast_in_dim.144.flags_ref), custom_call_target="tpu_custom_call" | custom-call | flops 452984832 | bytes 2949120 | tf_op jit(solution)/shard_map/pallas_call | solution.py:67
  34.8 1.9 %convolution_convert_fusion.2 = bf16[4,192,384]{2,1,0:T(8,128)(2,1)S(1)} fusion(bf16[1,1,4,384,384]{4,3,2,1,0:T(8,128)(2,1)S(1)} %copy-done, f32[4,192,384]{2,1,0:T(8,128)} %shard_map.73, f32[192]{0:T(256)S(1)} %bitcast.113, f32[192]{0:T(256)S(1)} %bitcast.114, f32[192]{0:T(256)S(1)} %bitcast.115, f32[192]{0:T(256)S(1)} %bitcast.112, ...), kind=kOutput, calls=%fused_computation.10 | convolution fusion | flops 229441536 | bytes 2958336 | tf_op jit(solution)/shard_map/fry,fyx->frx/dot_general | solution.py:49
  37.8 1.3 %collective-permute-start.7 = (bf16[576,384]{1,0:T(8,128)(2,1)S(1)}, bf16[576,384]{1,0:T(8,128)(2,1)S(1)}, u32[]{:S(2)}, u32[]{:S(2)}) collective-permute-start(bf16[576,384]{1,0:T(8,128)(2,1)S(1)} %pad_maximum_fusion.9), channel_id=1, source_target_pairs={{1,0},{3,2},{5,4},{7,6},{9,8},{11,10},{13,12},{15,14},{17,16},{19,... | collective-permute-start | bytes 1327112 | tf_op jit(solution)/shard_map/ppermute | solution.py:41
  40.5 3.1 %collective-permute-start.6 = (bf16[576,384]{1,0:T(8,128)(2,1)S(1)}, bf16[576,384]{1,0:T(8,128)(2,1)S(1)}, u32[]{:S(2)}, u32[]{:S(2)}) collective-permute-start(bf16[576,384]{1,0:T(8,128)(2,1)S(1)} %pad_maximum_fusion.8), channel_id=1, source_target_pairs={{0,1},{2,3},{4,5},{6,7},{8,9},{10,11},{12,13},{14,15},{16,17},{18,... | collective-permute-start | bytes 1327112 | tf_op jit(solution)/shard_map/ppermute | solution.py:41
  43.6 4.3 %collective-permute-start.4 = (bf16[576,384]{1,0:T(8,128)(2,1)S(1)}, bf16[576,384]{1,0:T(8,128)(2,1)S(1)}, u32[]{:S(2)}, u32[]{:S(2)}) collective-permute-start(bf16[576,384]{1,0:T(8,128)(2,1)S(1)} %pad_maximum_fusion.6), channel_id=1, source_target_pairs={{0,2},{2,4},{4,6},{6,8},{8,10},{10,12},{12,14},{14,16},{16,18},{18... | collective-permute-start | bytes 1327112 | tf_op jit(solution)/shard_map/ppermute | solution.py:41
  48.0 5.9 %collective-permute-done.5 = bf16[576,384]{1,0:T(8,128)(2,1)S(1)} collective-permute-done((bf16[576,384]{1,0:T(8,128)(2,1)S(1)}, bf16[576,384]{1,0:T(8,128)(2,1)S(1)}, u32[]{:S(2)}, u32[]{:S(2)}) %collective-permute-start.5) | collective-permute-done | bytes 442400 | tf_op jit(solution)/shard_map/ppermute | solution.py:41
  53.9 10.7 %collective-permute-done.4 = bf16[576,384]{1,0:T(8,128)(2,1)S(1)} collective-permute-done((bf16[576,384]{1,0:T(8,128)(2,1)S(1)}, bf16[576,384]{1,0:T(8,128)(2,1)S(1)}, u32[]{:S(2)}, u32[]{:S(2)}) %collective-permute-start.4) | collective-permute-done | bytes 442400 | tf_op jit(solution)/shard_map/ppermute | solution.py:41
  68.5 4.8 %all-to-all-start.1 = ((bf16[32,4,192]{2,1,0:T(4,128)(2,1)}), bf16[32,4,192]{2,1,0:T(4,128)(2,1)}, u32[]{:S(2)}, u32[]{:S(2)}) async-start(bf16[32,4,192]{2,1,0:T(4,128)(2,1)} %broadcast_in_dim.163), calls=%async_computation.1 | async-start | bytes 131072 | tf_op jit(solution)/shard_map/all_to_all | solution.py:24
  73.4 4.4 %shard_map.74 = f32[4,192,384]{2,1,0:T(8,128)} custom-call(bf16[4,192,384]{2,1,0:T(8,128)(2,1)} %copy-done.1, bf16[4,384,384]{2,1,0:T(8,128)(2,1)} %bitcast.85, f32[4,8,128]{2,1,0:T(8,128)} %broadcast_in_dim.144.flags_ref), custom_call_target="tpu_custom_call" | custom-call | flops 452984832 | bytes 2949120 | tf_op jit(solution)/shard_map/pallas_call | solution.py:67
  77.8 2.9 %all-to-all-done.1 = bf16[32,4,192]{2,1,0:T(4,128)(2,1)} async-done(((bf16[32,4,192]{2,1,0:T(4,128)(2,1)}), bf16[32,4,192]{2,1,0:T(4,128)(2,1)}, u32[]{:S(2)}, u32[]{:S(2)}) %all-to-all-start.1) | async-done | bytes 49184 | tf_op jit(solution)/shard_map/all_to_all | solution.py:24
  81.8 1.9 %convolution_convert_fusion = bf16[4,192,384]{2,1,0:T(8,128)(2,1)S(1)} fusion(bf16[1,1,4,384,384]{4,3,2,1,0:T(8,128)(2,1)S(1)} %copy-done, f32[4,192,384]{2,1,0:T(8,128)} %shard_map.74, f32[192]{0:T(256)S(1)} %bitcast.109, f32[192]{0:T(256)S(1)} %bitcast.110, f32[192]{0:T(256)S(1)} %bitcast.111, f32[192]{0:T(256)S(1)} %bitcast.108, ...), kind=kOutput, calls=%fused_computation.8 | convolution fusion | flops 229441536 | bytes 2958336 | tf_op jit(solution)/shard_map/fry,fyx->frx/dot_general | solution.py:49
  83.8 2.5 %collective-permute-start.8 = (bf16[1,192,384]{2,1,0:T(8,128)(2,1)S(1)}, bf16[1,192,384]{2,1,0:T(8,128)(2,1)S(1)}, u32[]{:S(2)}, u32[]{:S(2)}) collective-permute-start(bf16[1,192,384]{2,1,0:T(8,128)(2,1)S(1)} %get-tuple-element.13), channel_id=1, source_target_pairs={{0,2},{2,4},{4,6},{6,8},{8,10},{10,12},{12,14},{14,16},{16,18},{18... | collective-permute-start | bytes 442376 | tf_op jit(solution)/shard_map/ppermute | solution.py:13
  87.6 3.0 %collective-permute-start.10 = (bf16[1,192,384]{2,1,0:T(8,128)(2,1)S(1)}, bf16[1,192,384]{2,1,0:T(8,128)(2,1)S(1)}, u32[]{:S(2)}, u32[]{:S(2)}) collective-permute-start(bf16[1,192,384]{2,1,0:T(8,128)(2,1)S(1)} %get-tuple-element.15), channel_id=1, source_target_pairs={{0,1},{2,3},{4,5},{6,7},{8,9},{10,11},{12,13},{14,15},{16,17},{18,... | collective-permute-start | bytes 442376 | tf_op jit(solution)/shard_map/ppermute | solution.py:13
  90.6 1.3 %collective-permute-start.9 = (bf16[1,192,384]{2,1,0:T(8,128)(2,1)S(1)}, bf16[1,192,384]{2,1,0:T(8,128)(2,1)S(1)}, u32[]{:S(2)}, u32[]{:S(2)}) collective-permute-start(bf16[1,192,384]{2,1,0:T(8,128)(2,1)S(1)} %get-tuple-element.16), channel_id=1, source_target_pairs={{2,0},{4,2},{6,4},{8,6},{10,8},{12,10},{14,12},{16,14},{18,16},{20... | collective-permute-start | bytes 442376 | tf_op jit(solution)/shard_map/ppermute | solution.py:16
  92.0 5.7 %collective-permute-done.9 = bf16[1,192,384]{2,1,0:T(8,128)(2,1)S(1)} collective-permute-done((bf16[1,192,384]{2,1,0:T(8,128)(2,1)S(1)}, bf16[1,192,384]{2,1,0:T(8,128)(2,1)S(1)}, u32[]{:S(2)}, u32[]{:S(2)}) %collective-permute-start.9) | collective-permute-done | bytes 147488 | tf_op jit(solution)/shard_map/ppermute | solution.py:16
  100.2 12.2 %all_to_all.15 = f32[32,1,2,192]{3,2,1,0:T(2,128)S(1)} all-to-all(f32[32,1,2,192]{3,2,1,0:T(2,128)S(1)} %broadcast_in_dim.172), channel_id=1, replica_groups=mesh['gx'=16,'gy'=2] {'gx','gy'}, dimensions={0} | all-to-all | bytes 98304 | tf_op jit(solution)/shard_map/all_to_all | solution.py:24
  112.4 2.4 %fusion.19 = bf16[1,1,4,192,384]{4,3,2,1,0:T(8,128)(2,1)} fusion(bf16[4,192,384]{2,1,0:T(8,128)(2,1)S(1)} %convolution_convert_fusion, bf16[4,192,384]{2,1,0:T(8,128)(2,1)S(1)} %convolution_convert_fusion.2, f32[192]{0:T(256)S(1)} %bitcast.105, bf16[1,192,384]{2,1,0:T(8,128)(2,1)} %copy-done.19, bf16[1,192,384]{2,1,0:T(8,128)(2,1)} %copy-done.20, ...), kind=kLoop, calls=%fused_computation.38 | loop fusion | flops 6782976 | bytes 4129536 | tf_op jit(solution)/shard_map/broadcast_in_dim | solution.py:149
  (126 shorter events, 22.0 us)
Async XLA Ops:
  0.0 14.4 %copy-start = (bf16[1,1,4,384,384]{4,3,2,1,0:T(8,128)(2,1)S(1)}, bf16[1,1,4,384,384]{4,3,2,1,0:T(8,128)(2,1)}, u32[]{:S(2)}) copy-start(bf16[1,1,4,384,384]{4,3,2,1,0:T(8,128)(2,1)} %param.9) | copy-start | bytes 3538948
  0.0 11.9 %copy-start.25 = (s32[1,1,4]{2,1,0:T(1,128)S(1)}, s32[1,1,4]{2,1,0:T(1,128)}, u32[]{:S(2)}) copy-start(s32[1,1,4]{2,1,0:T(1,128)} %param.12) | copy-start | bytes 52
  0.0 11.9 %copy-start.2 = (bf16[1,1,4,384,384]{4,3,2,1,0:T(8,128)(2,1)S(1)}, bf16[1,1,4,384,384]{4,3,2,1,0:T(8,128)(2,1)}, u32[]{:S(2)}) copy-start(bf16[1,1,4,384,384]{4,3,2,1,0:T(8,128)(2,1)} %param.8) | copy-start | bytes 3538948
  1.3 12.2 %collective-permute-start = (bf16[1,192,384]{2,1,0:T(8,128)(2,1)S(1)}, bf16[1,192,384]{2,1,0:T(8,128)(2,1)S(1)}, u32[]{:S(2)}, u32[]{:S(2)}) collective-permute-start(bf16[1,192,384]{2,1,0:T(8,128)(2,1)S(1)} %get-tuple-element.21), channel_id=1, source_target_pairs={{0,2},{2,4},{4,6},{6,8},{8,10},{10,12},{12,14},{14,16},{16,18},{18... | collective-permute-start | bytes 442376 | tf_op jit(solution)/shard_map/ppermute | solution.py:13
  6.2 8.2 %collective-permute-start.1 = (bf16[1,192,384]{2,1,0:T(8,128)(2,1)S(1)}, bf16[1,192,384]{2,1,0:T(8,128)(2,1)S(1)}, u32[]{:S(2)}, u32[]{:S(2)}) collective-permute-start(bf16[1,192,384]{2,1,0:T(8,128)(2,1)S(1)} %get-tuple-element.22), channel_id=1, source_target_pairs={{2,0},{4,2},{6,4},{8,6},{10,8},{12,10},{14,12},{16,14},{18,16},{20... | collective-permute-start | bytes 442376 | tf_op jit(solution)/shard_map/ppermute | solution.py:16
  7.5 6.9 %collective-permute-start.3 = (bf16[1,192,384]{2,1,0:T(8,128)(2,1)S(1)}, bf16[1,192,384]{2,1,0:T(8,128)(2,1)S(1)}, u32[]{:S(2)}, u32[]{:S(2)}) collective-permute-start(bf16[1,192,384]{2,1,0:T(8,128)(2,1)S(1)} %get-tuple-element.23), channel_id=1, source_target_pairs={{1,0},{3,2},{5,4},{7,6},{9,8},{11,10},{13,12},{15,14},{17,16},{19,... | collective-permute-start | bytes 442376 | tf_op jit(solution)/shard_map/ppermute | solution.py:16
  8.8 5.6 %collective-permute-start.2 = (bf16[1,192,384]{2,1,0:T(8,128)(2,1)S(1)}, bf16[1,192,384]{2,1,0:T(8,128)(2,1)S(1)}, u32[]{:S(2)}, u32[]{:S(2)}) collective-permute-start(bf16[1,192,384]{2,1,0:T(8,128)(2,1)S(1)} %get-tuple-element.24), channel_id=1, source_target_pairs={{0,1},{2,3},{4,5},{6,7},{8,9},{10,11},{12,13},{14,15},{16,17},{18,... | collective-permute-start | bytes 442376 | tf_op jit(solution)/shard_map/ppermute | solution.py:13
  15.2 14.2 %copy-start.5 = (bf16[4,192,384]{2,1,0:T(8,128)(2,1)}, bf16[4,192,384]{2,1,0:T(8,128)(2,1)S(1)}, u32[]{:S(2)}) copy-start(bf16[4,192,384]{2,1,0:T(8,128)(2,1)S(1)} %convolution_convert_fusion.3.scaled_ref) | copy-start | bytes 1769476
  16.1 17.7 %all-to-all-start = ((bf16[32,4,192]{2,1,0:T(4,128)(2,1)}), bf16[32,4,192]{2,1,0:T(4,128)(2,1)}, u32[]{:S(2)}, u32[]{:S(2)}) async-start(bf16[32,4,192]{2,1,0:T(4,128)(2,1)} %broadcast_in_dim.147), calls=%async_computation | async-start | bytes 131072 | tf_op jit(solution)/shard_map/all_to_all | solution.py:24
  37.8 10.2 %collective-permute-start.7 = (bf16[576,384]{1,0:T(8,128)(2,1)S(1)}, bf16[576,384]{1,0:T(8,128)(2,1)S(1)}, u32[]{:S(2)}, u32[]{:S(2)}) collective-permute-start(bf16[576,384]{1,0:T(8,128)(2,1)S(1)} %pad_maximum_fusion.9), channel_id=1, source_target_pairs={{1,0},{3,2},{5,4},{7,6},{9,8},{11,10},{13,12},{15,14},{17,16},{19,... | collective-permute-start | bytes 1327112 | tf_op jit(solution)/shard_map/ppermute | solution.py:41
  39.1 14.8 %collective-permute-start.5 = (bf16[576,384]{1,0:T(8,128)(2,1)S(1)}, bf16[576,384]{1,0:T(8,128)(2,1)S(1)}, u32[]{:S(2)}, u32[]{:S(2)}) collective-permute-start(bf16[576,384]{1,0:T(8,128)(2,1)S(1)} %pad_maximum_fusion.7), channel_id=1, source_target_pairs={{2,0},{4,2},{6,4},{8,6},{10,8},{12,10},{14,12},{16,14},{18,16},{20... | collective-permute-start | bytes 1327112 | tf_op jit(solution)/shard_map/ppermute | solution.py:41
  40.5 13.4 %collective-permute-start.6 = (bf16[576,384]{1,0:T(8,128)(2,1)S(1)}, bf16[576,384]{1,0:T(8,128)(2,1)S(1)}, u32[]{:S(2)}, u32[]{:S(2)}) collective-permute-start(bf16[576,384]{1,0:T(8,128)(2,1)S(1)} %pad_maximum_fusion.8), channel_id=1, source_target_pairs={{0,1},{2,3},{4,5},{6,7},{8,9},{10,11},{12,13},{14,15},{16,17},{18,... | collective-permute-start | bytes 1327112 | tf_op jit(solution)/shard_map/ppermute | solution.py:41
  43.6 20.9 %collective-permute-start.4 = (bf16[576,384]{1,0:T(8,128)(2,1)S(1)}, bf16[576,384]{1,0:T(8,128)(2,1)S(1)}, u32[]{:S(2)}, u32[]{:S(2)}) collective-permute-start(bf16[576,384]{1,0:T(8,128)(2,1)S(1)} %pad_maximum_fusion.6), channel_id=1, source_target_pairs={{0,2},{2,4},{4,6},{6,8},{8,10},{10,12},{12,14},{14,16},{16,18},{18... | collective-permute-start | bytes 1327112 | tf_op jit(solution)/shard_map/ppermute | solution.py:41
  47.9 17.2 %copy-start.6 = (bf16[576,384]{1,0:T(8,128)(2,1)}, bf16[576,384]{1,0:T(8,128)(2,1)S(1)}, u32[]{:S(2)}) copy-start(bf16[576,384]{1,0:T(8,128)(2,1)S(1)} %collective-permute-done.7) | copy-start | bytes 1327108
  53.9 11.3 %copy-start.9 = (bf16[576,384]{1,0:T(8,128)(2,1)}, bf16[576,384]{1,0:T(8,128)(2,1)S(1)}, u32[]{:S(2)}) copy-start(bf16[576,384]{1,0:T(8,128)(2,1)S(1)} %collective-permute-done.5) | copy-start | bytes 1327108
  53.9 11.3 %copy-start.12 = (bf16[576,384]{1,0:T(8,128)(2,1)}, bf16[576,384]{1,0:T(8,128)(2,1)S(1)}, u32[]{:S(2)}) copy-start(bf16[576,384]{1,0:T(8,128)(2,1)S(1)} %collective-permute-done.6) | copy-start | bytes 1327108
  68.5 12.2 %all-to-all-start.1 = ((bf16[32,4,192]{2,1,0:T(4,128)(2,1)}), bf16[32,4,192]{2,1,0:T(4,128)(2,1)}, u32[]{:S(2)}, u32[]{:S(2)}) async-start(bf16[32,4,192]{2,1,0:T(4,128)(2,1)} %broadcast_in_dim.163), calls=%async_computation.1 | async-start | bytes 131072 | tf_op jit(solution)/shard_map/all_to_all | solution.py:24
  83.7 14.0 %copy-start.4 = (f32[4,192,384]{2,1,0:T(8,128)S(1)}, f32[4,192,384]{2,1,0:T(8,128)}, u32[]{:S(2)}) copy-start(f32[4,192,384]{2,1,0:T(8,128)} %copy-done.3) | copy-start | bytes 3538948
  83.8 8.1 %collective-permute-start.8 = (bf16[1,192,384]{2,1,0:T(8,128)(2,1)S(1)}, bf16[1,192,384]{2,1,0:T(8,128)(2,1)S(1)}, u32[]{:S(2)}, u32[]{:S(2)}) collective-permute-start(bf16[1,192,384]{2,1,0:T(8,128)(2,1)S(1)} %get-tuple-element.13), channel_id=1, source_target_pairs={{0,2},{2,4},{4,6},{6,8},{8,10},{10,12},{12,14},{14,16},{16,18},{18... | collective-permute-start | bytes 442376 | tf_op jit(solution)/shard_map/ppermute | solution.py:13
  86.3 5.7 %collective-permute-start.11 = (bf16[1,192,384]{2,1,0:T(8,128)(2,1)S(1)}, bf16[1,192,384]{2,1,0:T(8,128)(2,1)S(1)}, u32[]{:S(2)}, u32[]{:S(2)}) collective-permute-start(bf16[1,192,384]{2,1,0:T(8,128)(2,1)S(1)} %get-tuple-element.14), channel_id=1, source_target_pairs={{1,0},{3,2},{5,4},{7,6},{9,8},{11,10},{13,12},{15,14},{17,16},{19,... | collective-permute-start | bytes 442376 | tf_op jit(solution)/shard_map/ppermute | solution.py:16
  87.6 4.4 %collective-permute-start.10 = (bf16[1,192,384]{2,1,0:T(8,128)(2,1)S(1)}, bf16[1,192,384]{2,1,0:T(8,128)(2,1)S(1)}, u32[]{:S(2)}, u32[]{:S(2)}) collective-permute-start(bf16[1,192,384]{2,1,0:T(8,128)(2,1)S(1)} %get-tuple-element.15), channel_id=1, source_target_pairs={{0,1},{2,3},{4,5},{6,7},{8,9},{10,11},{12,13},{14,15},{16,17},{18,... | collective-permute-start | bytes 442376 | tf_op jit(solution)/shard_map/ppermute | solution.py:13
  90.6 7.0 %collective-permute-start.9 = (bf16[1,192,384]{2,1,0:T(8,128)(2,1)S(1)}, bf16[1,192,384]{2,1,0:T(8,128)(2,1)S(1)}, u32[]{:S(2)}, u32[]{:S(2)}) collective-permute-start(bf16[1,192,384]{2,1,0:T(8,128)(2,1)S(1)} %get-tuple-element.16), channel_id=1, source_target_pairs={{2,0},{4,2},{6,4},{8,6},{10,8},{12,10},{14,12},{16,14},{18,16},{20... | collective-permute-start | bytes 442376 | tf_op jit(solution)/shard_map/ppermute | solution.py:16
  99.4 13.0 %copy-start.8 = (bf16[576,384]{1,0:T(8,128)(2,1)S(1)}, bf16[576,384]{1,0:T(8,128)(2,1)}, u32[]{:S(2)}) copy-start(bf16[576,384]{1,0:T(8,128)(2,1)} %copy-done.6) | copy-start | bytes 1327108
  99.4 13.1 %copy-start.11 = (bf16[576,384]{1,0:T(8,128)(2,1)S(1)}, bf16[576,384]{1,0:T(8,128)(2,1)}, u32[]{:S(2)}) copy-start(bf16[576,384]{1,0:T(8,128)(2,1)} %copy-done.9) | copy-start | bytes 1327108
  (29 other events, 81.6 us)

commit v18 on v17

--- a/solution.py
+++ b/solution.py
@@ -112,9 +112,13 @@
             "kfx,frx->kr", picks_half, scaled, preferred_element_type=jnp.float32
         ).astype(jnp.bfloat16)
         coarse = add_coarse(gather_rows(primal, ("gx", "gy")))
+        faces = softened.shape[0]
+        position = lax.broadcasted_iota(jnp.int32, softened.shape, 0) * width + lax.broadcasted_iota(
+            jnp.int32, softened.shape, 2
+        )
         placed = jnp.zeros_like(softened)
         for k in range(primal_count):
-            placed = placed + jnp.where(picks[k][:, None, :], coarse[k][None, :, None], 0.0)
+            placed = placed + jnp.where(position == primal_slots[k], coarse[k][None, :, None], 0.0)
         weighted = (softened + placed).astype(jnp.bfloat16)
         spread = face_mul(weighted, deluxe_panel).astype(jnp.bfloat16)
         if schur_partner is not None:

time: 116 us -> 115 us (level)
  local copies, waits for them, and re-layouts: 15.5 us -> 9.95 us
  matrix products: 8.28 us -> 13.3 us
    dot_general x6, matrix products: 6.24 us -> 11.3 us  [face_mul(): jnp.einsum('fry,fyx->frx', vectors, matrices, preferred_element_type=jnp....]
    broadcast_in_dim x4 -> x0, local copies, waits for them, and re-layouts: 4.95 us -> none  [precondition(): jnp.where(picks[k][:, None, :], coarse[k][None, :, None], 0.0)]
    ppermute x4, waiting for transfers between devices: 16.6 us -> 14.8 us  [from_partner(): return lax.ppermute(values, axis, pairs)]
    all_to_all x2, waiting for transfers between devices: 2.93 us -> 4.68 us  [gather_rows(): swapped = lax.all_to_all(spread, axes, 0, 0, tiled=False)]
    unnamed x78 -> x72, local copies, waits for them, and re-layouts: 3.06 us -> 3.08 us
  transfers between devices with their start and end apart: 14 -> 14, of which waited for: 5 -> 6; matrix products, arithmetic and copies ran while one was open for 8% -> 3% of each run, Pallas kernels for 8% -> 8%
where the time goes in v18:
time: 115 us; the launch traced here: 114 us
  starting transfers between devices  39.7 us (35%)
  waiting for transfers between devices  26.1 us (23%)
  matrix products  13.3 us (12%)
  blocking collectives  12.2 us (11%)
  local copies, waits for them, and re-layouts  9.95 us (9%)
  Pallas kernels  8.86 us (8%)
  other arithmetic  3.54 us (3%)
    ppermute x4, waiting for transfers between devices, from_partner(): return lax.ppermute(values, axis, pairs)  14.8 us
    ppermute x4, starting transfers between devices, with_halo(): lax.ppermute(lax.slice_in_dim(block, block.shape[dim] - width, None, axis...  13.4 us
    all_to_all x1, blocking collectives, gather_rows(): swapped = lax.all_to_all(spread, axes, 0, 0, tiled=False)  12.2 us
    dot_general x6, matrix products, face_mul(): jnp.einsum('fry,fyx->frx', vectors, matrices, preferred_element_type=jnp....  11.3 us
    all_to_all x2, starting transfers between devices, gather_rows(): swapped = lax.all_to_all(spread, axes, 0, 0, tiled=False)  11.1 us
    ppermute x4, starting transfers between devices, from_partner(): return lax.ppermute(values, axis, pairs)  9.96 us
    pallas_call x2, Pallas kernels, soften(): pl.pallas_call(soften_kernel, grid=(faces,), in_specs=[pl.BlockSpec((1, r...  8.86 us
    ppermute x4, waiting for transfers between devices, with_halo(): lax.ppermute(lax.slice_in_dim(block, 0, width, axis=dim), axis, backward)  6.56 us
  transfers between devices with their start and end apart: 14, of which 6 were waited for; matrix products, arithmetic and copies ran while one was open for 3% of the time, Pallas kernels for 8%

profile of v18, /device:TPU:0, one launch (start us, length us, event | category | flops | bytes accessed | tf_op | source)
XLA Modules:
  0.0 114.2 jit_solution(2629708341797183213)
XLA Ops:
  0.0 1.3 %slice_bitcast_fusion.11 = (bf16[1,192,384]{2,1,0:T(8,128)(2,1)S(1)}, bf16[1,192,384]{2,1,0:T(8,128)(2,1)S(1)}, bf16[1,192,384]{2,1,0:T(8,128)(2,1)S(1)}, bf16[1,192,384]{2,1,0:T(8,128)(2,1)S(1)}) fusion(bf16[1,1,4,192,384]{4,3,2,1,0:T(8,128)(2,1)} %param.7), kind=kLoop, calls=%fused_computation.84 | loop fusion | bytes 1179648 | tf_op jit(solution)/shard_map/slice | solution.py:14
  1.3 4.9 %collective-permute-start = (bf16[1,192,384]{2,1,0:T(8,128)(2,1)S(1)}, bf16[1,192,384]{2,1,0:T(8,128)(2,1)S(1)}, u32[]{:S(2)}, u32[]{:S(2)}) collective-permute-start(bf16[1,192,384]{2,1,0:T(8,128)(2,1)S(1)} %get-tuple-element.17), channel_id=1, source_target_pairs={{0,2},{2,4},{4,6},{6,8},{8,10},{10,12},{12,14},{14,16},{16,18},{18... | collective-permute-start | bytes 442376 | tf_op jit(solution)/shard_map/ppermute | solution.py:13
  6.2 1.3 %collective-permute-start.1 = (bf16[1,192,384]{2,1,0:T(8,128)(2,1)S(1)}, bf16[1,192,384]{2,1,0:T(8,128)(2,1)S(1)}, u32[]{:S(2)}, u32[]{:S(2)}) collective-permute-start(bf16[1,192,384]{2,1,0:T(8,128)(2,1)S(1)} %get-tuple-element.18), channel_id=1, source_target_pairs={{2,0},{4,2},{6,4},{8,6},{10,8},{12,10},{14,12},{16,14},{18,16},{20... | collective-permute-start | bytes 442376 | tf_op jit(solution)/shard_map/ppermute | solution.py:16
  7.5 1.3 %collective-permute-start.3 = (bf16[1,192,384]{2,1,0:T(8,128)(2,1)S(1)}, bf16[1,192,384]{2,1,0:T(8,128)(2,1)S(1)}, u32[]{:S(2)}, u32[]{:S(2)}) collective-permute-start(bf16[1,192,384]{2,1,0:T(8,128)(2,1)S(1)} %get-tuple-element.19), channel_id=1, source_target_pairs={{1,0},{3,2},{5,4},{7,6},{9,8},{11,10},{13,12},{15,14},{17,16},{19,... | collective-permute-start | bytes 442376 | tf_op jit(solution)/shard_map/ppermute | solution.py:16
  8.8 3.0 %collective-permute-start.2 = (bf16[1,192,384]{2,1,0:T(8,128)(2,1)S(1)}, bf16[1,192,384]{2,1,0:T(8,128)(2,1)S(1)}, u32[]{:S(2)}, u32[]{:S(2)}) collective-permute-start(bf16[1,192,384]{2,1,0:T(8,128)(2,1)S(1)} %get-tuple-element.20), channel_id=1, source_target_pairs={{0,1},{2,3},{4,5},{6,7},{8,9},{10,11},{12,13},{14,15},{16,17},{18,... | collective-permute-start | bytes 442376 | tf_op jit(solution)/shard_map/ppermute | solution.py:13
  16.1 6.3 %all-to-all-start = ((bf16[32,4,192]{2,1,0:T(4,128)(2,1)}), bf16[32,4,192]{2,1,0:T(4,128)(2,1)}, u32[]{:S(2)}, u32[]{:S(2)}) async-start(bf16[32,4,192]{2,1,0:T(4,128)(2,1)} %broadcast_in_dim.102), calls=%async_computation | async-start | bytes 131072 | tf_op jit(solution)/shard_map/all_to_all | solution.py:24
  23.6 4.4 %shard_map.73 = f32[4,192,384]{2,1,0:T(8,128)} custom-call(bf16[4,192,384]{2,1,0:T(8,128)(2,1)} %copy-done.5, bf16[4,384,384]{2,1,0:T(8,128)(2,1)} %bitcast.88, f32[4,8,128]{2,1,0:T(8,128)} %broadcast_in_dim.101.flags_ref), custom_call_target="tpu_custom_call" | custom-call | flops 452984832 | bytes 2949120 | tf_op jit(solution)/shard_map/pallas_call | solution.py:67
  28.0 1.8 %all-to-all-done = bf16[32,4,192]{2,1,0:T(4,128)(2,1)} async-done(((bf16[32,4,192]{2,1,0:T(4,128)(2,1)}), bf16[32,4,192]{2,1,0:T(4,128)(2,1)}, u32[]{:S(2)}, u32[]{:S(2)}) %all-to-all-start) | async-done | bytes 49184 | tf_op jit(solution)/shard_map/all_to_all | solution.py:24
  30.9 4.5 %convolution_convert_fusion.2 = bf16[4,192,384]{2,1,0:T(8,128)(2,1)S(1)} fusion(bf16[1,1,4,384,384]{4,3,2,1,0:T(8,128)(2,1)S(1)} %copy-done, f32[4,192,384]{2,1,0:T(8,128)} %shard_map.73, f32[192]{0:T(256)S(1)} %bitcast.116, s32[]{:T(128)} %bitcast.17, f32[192]{0:T(256)S(1)} %bitcast.117, s32[]{:T(128)} %bitcast.15, f32[192]{0:T(256)S(1)} %bitcast.118, ...), kind=kOutput, calls=%fused_computation.10 | convolution fusion | flops 230916096 | bytes 2952224 | tf_op jit(solution)/shard_map/fry,fyx->frx/dot_general | solution.py:49
  36.3 1.3 %collective-permute-start.7 = (bf16[576,384]{1,0:T(8,128)(2,1)S(1)}, bf16[576,384]{1,0:T(8,128)(2,1)S(1)}, u32[]{:S(2)}, u32[]{:S(2)}) collective-permute-start(bf16[576,384]{1,0:T(8,128)(2,1)S(1)} %pad_maximum_fusion.9), channel_id=1, source_target_pairs={{1,0},{3,2},{5,4},{7,6},{9,8},{11,10},{13,12},{15,14},{17,16},{19,... | collective-permute-start | bytes 1327112 | tf_op jit(solution)/shard_map/ppermute | solution.py:41
  37.7 1.3 %collective-permute-start.5 = (bf16[576,384]{1,0:T(8,128)(2,1)S(1)}, bf16[576,384]{1,0:T(8,128)(2,1)S(1)}, u32[]{:S(2)}, u32[]{:S(2)}) collective-permute-start(bf16[576,384]{1,0:T(8,128)(2,1)S(1)} %pad_maximum_fusion.7), channel_id=1, source_target_pairs={{2,0},{4,2},{6,4},{8,6},{10,8},{12,10},{14,12},{16,14},{18,16},{20... | collective-permute-start | bytes 1327112 | tf_op jit(solution)/shard_map/ppermute | solution.py:41
  39.0 3.1 %collective-permute-start.6 = (bf16[576,384]{1,0:T(8,128)(2,1)S(1)}, bf16[576,384]{1,0:T(8,128)(2,1)S(1)}, u32[]{:S(2)}, u32[]{:S(2)}) collective-permute-start(bf16[576,384]{1,0:T(8,128)(2,1)S(1)} %pad_maximum_fusion.8), channel_id=1, source_target_pairs={{0,1},{2,3},{4,5},{6,7},{8,9},{10,11},{12,13},{14,15},{16,17},{18,... | collective-permute-start | bytes 1327112 | tf_op jit(solution)/shard_map/ppermute | solution.py:41
  42.2 4.3 %collective-permute-start.4 = (bf16[576,384]{1,0:T(8,128)(2,1)S(1)}, bf16[576,384]{1,0:T(8,128)(2,1)S(1)}, u32[]{:S(2)}, u32[]{:S(2)}) collective-permute-start(bf16[576,384]{1,0:T(8,128)(2,1)S(1)} %pad_maximum_fusion.6), channel_id=1, source_target_pairs={{0,2},{2,4},{4,6},{6,8},{8,10},{10,12},{12,14},{14,16},{16,18},{18... | collective-permute-start | bytes 1327112 | tf_op jit(solution)/shard_map/ppermute | solution.py:41
  46.5 5.9 %collective-permute-done.5 = bf16[576,384]{1,0:T(8,128)(2,1)S(1)} collective-permute-done((bf16[576,384]{1,0:T(8,128)(2,1)S(1)}, bf16[576,384]{1,0:T(8,128)(2,1)S(1)}, u32[]{:S(2)}, u32[]{:S(2)}) %collective-permute-start.5) | collective-permute-done | bytes 442400 | tf_op jit(solution)/shard_map/ppermute | solution.py:41
  52.5 8.9 %collective-permute-done.4 = bf16[576,384]{1,0:T(8,128)(2,1)S(1)} collective-permute-done((bf16[576,384]{1,0:T(8,128)(2,1)S(1)}, bf16[576,384]{1,0:T(8,128)(2,1)S(1)}, u32[]{:S(2)}, u32[]{:S(2)}) %collective-permute-start.4) | collective-permute-done | bytes 442400 | tf_op jit(solution)/shard_map/ppermute | solution.py:41
  65.4 4.8 %all-to-all-start.1 = ((bf16[32,4,192]{2,1,0:T(4,128)(2,1)}), bf16[32,4,192]{2,1,0:T(4,128)(2,1)}, u32[]{:S(2)}, u32[]{:S(2)}) async-start(bf16[32,4,192]{2,1,0:T(4,128)(2,1)} %broadcast_in_dim.112), calls=%async_computation.1 | async-start | bytes 131072 | tf_op jit(solution)/shard_map/all_to_all | solution.py:24
  70.2 4.5 %shard_map.74 = f32[4,192,384]{2,1,0:T(8,128)} custom-call(bf16[4,192,384]{2,1,0:T(8,128)(2,1)} %copy-done.1, bf16[4,384,384]{2,1,0:T(8,128)(2,1)} %bitcast.89, f32[4,8,128]{2,1,0:T(8,128)} %broadcast_in_dim.101.flags_ref), custom_call_target="tpu_custom_call" | custom-call | flops 452984832 | bytes 2949120 | tf_op jit(solution)/shard_map/pallas_call | solution.py:67
  74.6 2.9 %all-to-all-done.1 = bf16[32,4,192]{2,1,0:T(4,128)(2,1)} async-done(((bf16[32,4,192]{2,1,0:T(4,128)(2,1)}), bf16[32,4,192]{2,1,0:T(4,128)(2,1)}, u32[]{:S(2)}, u32[]{:S(2)}) %all-to-all-start.1) | async-done | bytes 49184 | tf_op jit(solution)/shard_map/all_to_all | solution.py:24
  78.6 4.4 %convolution_convert_fusion = bf16[4,192,384]{2,1,0:T(8,128)(2,1)S(1)} fusion(bf16[1,1,4,384,384]{4,3,2,1,0:T(8,128)(2,1)S(1)} %copy-done, f32[4,192,384]{2,1,0:T(8,128)} %shard_map.74, f32[192]{0:T(256)S(1)} %bitcast.112, f32[192]{0:T(256)S(1)} %bitcast.113, f32[192]{0:T(256)S(1)} %bitcast.114, f32[192]{0:T(256)S(1)} %bitcast.111, s32[]{:T(128)} %bitcast.17, ...), kind=kOutput, calls=%fused_computation.8 | convolution fusion | flops 230916096 | bytes 2952224 | tf_op jit(solution)/shard_map/fry,fyx->frx/dot_general | solution.py:49
  83.1 2.5 %collective-permute-start.8 = (bf16[1,192,384]{2,1,0:T(8,128)(2,1)S(1)}, bf16[1,192,384]{2,1,0:T(8,128)(2,1)S(1)}, u32[]{:S(2)}, u32[]{:S(2)}) collective-permute-start(bf16[1,192,384]{2,1,0:T(8,128)(2,1)S(1)} %get-tuple-element.9), channel_id=1, source_target_pairs={{0,2},{2,4},{4,6},{6,8},{8,10},{10,12},{12,14},{14,16},{16,18},{18... | collective-permute-start | bytes 442376 | tf_op jit(solution)/shard_map/ppermute | solution.py:13
  86.9 3.0 %collective-permute-start.10 = (bf16[1,192,384]{2,1,0:T(8,128)(2,1)S(1)}, bf16[1,192,384]{2,1,0:T(8,128)(2,1)S(1)}, u32[]{:S(2)}, u32[]{:S(2)}) collective-permute-start(bf16[1,192,384]{2,1,0:T(8,128)(2,1)S(1)} %get-tuple-element.11), channel_id=1, source_target_pairs={{0,1},{2,3},{4,5},{6,7},{8,9},{10,11},{12,13},{14,15},{16,17},{18,... | collective-permute-start | bytes 442376 | tf_op jit(solution)/shard_map/ppermute | solution.py:13
  91.3 5.7 %collective-permute-done.9 = bf16[1,192,384]{2,1,0:T(8,128)(2,1)S(1)} collective-permute-done((bf16[1,192,384]{2,1,0:T(8,128)(2,1)S(1)}, bf16[1,192,384]{2,1,0:T(8,128)(2,1)S(1)}, u32[]{:S(2)}, u32[]{:S(2)}) %collective-permute-start.9) | collective-permute-done | bytes 147488 | tf_op jit(solution)/shard_map/ppermute | solution.py:16
  99.5 12.2 %all_to_all.15 = f32[32,1,2,192]{3,2,1,0:T(2,128)S(1)} all-to-all(f32[32,1,2,192]{3,2,1,0:T(2,128)S(1)} %broadcast_in_dim.121), channel_id=1, replica_groups=mesh['gx'=16,'gy'=2] {'gx','gy'}, dimensions={0} | all-to-all | bytes 98304 | tf_op jit(solution)/shard_map/all_to_all | solution.py:24
  111.8 2.4 %fusion.23 = bf16[1,1,4,192,384]{4,3,2,1,0:T(8,128)(2,1)} fusion(bf16[4,192,384]{2,1,0:T(8,128)(2,1)S(1)} %convolution_convert_fusion, bf16[4,192,384]{2,1,0:T(8,128)(2,1)S(1)} %convolution_convert_fusion.2, f32[192]{0:T(256)S(1)} %bitcast.108, bf16[1,192,384]{2,1,0:T(8,128)(2,1)} %copy-done.19, bf16[1,192,384]{2,1,0:T(8,128)(2,1)} %copy-done.20, ...), kind=kLoop, calls=%fused_computation.43 | loop fusion | flops 6782976 | bytes 4129536 | tf_op jit(solution)/shard_map/broadcast_in_dim | solution.py:153
  (116 shorter events, 17.6 us)
Async XLA Ops:
  0.0 14.4 %copy-start = (bf16[1,1,4,384,384]{4,3,2,1,0:T(8,128)(2,1)S(1)}, bf16[1,1,4,384,384]{4,3,2,1,0:T(8,128)(2,1)}, u32[]{:S(2)}) copy-start(bf16[1,1,4,384,384]{4,3,2,1,0:T(8,128)(2,1)} %param.9) | copy-start | bytes 3538948
  0.0 11.9 %copy-start.34 = (s32[1,1,4]{2,1,0:T(1,128)S(1)}, s32[1,1,4]{2,1,0:T(1,128)}, u32[]{:S(2)}) copy-start(s32[1,1,4]{2,1,0:T(1,128)} %param.13) | copy-start | bytes 52
  0.0 11.9 %copy-start.2 = (bf16[1,1,4,384,384]{4,3,2,1,0:T(8,128)(2,1)S(1)}, bf16[1,1,4,384,384]{4,3,2,1,0:T(8,128)(2,1)}, u32[]{:S(2)}) copy-start(bf16[1,1,4,384,384]{4,3,2,1,0:T(8,128)(2,1)} %param.8) | copy-start | bytes 3538948
  1.3 12.2 %collective-permute-start = (bf16[1,192,384]{2,1,0:T(8,128)(2,1)S(1)}, bf16[1,192,384]{2,1,0:T(8,128)(2,1)S(1)}, u32[]{:S(2)}, u32[]{:S(2)}) collective-permute-start(bf16[1,192,384]{2,1,0:T(8,128)(2,1)S(1)} %get-tuple-element.17), channel_id=1, source_target_pairs={{0,2},{2,4},{4,6},{6,8},{8,10},{10,12},{12,14},{14,16},{16,18},{18... | collective-permute-start | bytes 442376 | tf_op jit(solution)/shard_map/ppermute | solution.py:13
  6.2 8.2 %collective-permute-start.1 = (bf16[1,192,384]{2,1,0:T(8,128)(2,1)S(1)}, bf16[1,192,384]{2,1,0:T(8,128)(2,1)S(1)}, u32[]{:S(2)}, u32[]{:S(2)}) collective-permute-start(bf16[1,192,384]{2,1,0:T(8,128)(2,1)S(1)} %get-tuple-element.18), channel_id=1, source_target_pairs={{2,0},{4,2},{6,4},{8,6},{10,8},{12,10},{14,12},{16,14},{18,16},{20... | collective-permute-start | bytes 442376 | tf_op jit(solution)/shard_map/ppermute | solution.py:16
  7.5 6.9 %collective-permute-start.3 = (bf16[1,192,384]{2,1,0:T(8,128)(2,1)S(1)}, bf16[1,192,384]{2,1,0:T(8,128)(2,1)S(1)}, u32[]{:S(2)}, u32[]{:S(2)}) collective-permute-start(bf16[1,192,384]{2,1,0:T(8,128)(2,1)S(1)} %get-tuple-element.19), channel_id=1, source_target_pairs={{1,0},{3,2},{5,4},{7,6},{9,8},{11,10},{13,12},{15,14},{17,16},{19,... | collective-permute-start | bytes 442376 | tf_op jit(solution)/shard_map/ppermute | solution.py:16
  8.8 5.6 %collective-permute-start.2 = (bf16[1,192,384]{2,1,0:T(8,128)(2,1)S(1)}, bf16[1,192,384]{2,1,0:T(8,128)(2,1)S(1)}, u32[]{:S(2)}, u32[]{:S(2)}) collective-permute-start(bf16[1,192,384]{2,1,0:T(8,128)(2,1)S(1)} %get-tuple-element.20), channel_id=1, source_target_pairs={{0,1},{2,3},{4,5},{6,7},{8,9},{10,11},{12,13},{14,15},{16,17},{18,... | collective-permute-start | bytes 442376 | tf_op jit(solution)/shard_map/ppermute | solution.py:13
  15.2 8.5 %copy-start.5 = (bf16[4,192,384]{2,1,0:T(8,128)(2,1)}, bf16[4,192,384]{2,1,0:T(8,128)(2,1)S(1)}, u32[]{:S(2)}) copy-start(bf16[4,192,384]{2,1,0:T(8,128)(2,1)S(1)} %convolution_convert_fusion.3.scaled_ref) | copy-start | bytes 1769476
  16.1 13.7 %all-to-all-start = ((bf16[32,4,192]{2,1,0:T(4,128)(2,1)}), bf16[32,4,192]{2,1,0:T(4,128)(2,1)}, u32[]{:S(2)}, u32[]{:S(2)}) async-start(bf16[32,4,192]{2,1,0:T(4,128)(2,1)} %broadcast_in_dim.102), calls=%async_computation | async-start | bytes 131072 | tf_op jit(solution)/shard_map/all_to_all | solution.py:24
  36.3 10.2 %collective-permute-start.7 = (bf16[576,384]{1,0:T(8,128)(2,1)S(1)}, bf16[576,384]{1,0:T(8,128)(2,1)S(1)}, u32[]{:S(2)}, u32[]{:S(2)}) collective-permute-start(bf16[576,384]{1,0:T(8,128)(2,1)S(1)} %pad_maximum_fusion.9), channel_id=1, source_target_pairs={{1,0},{3,2},{5,4},{7,6},{9,8},{11,10},{13,12},{15,14},{17,16},{19,... | collective-permute-start | bytes 1327112 | tf_op jit(solution)/shard_map/ppermute | solution.py:41
  37.7 14.8 %collective-permute-start.5 = (bf16[576,384]{1,0:T(8,128)(2,1)S(1)}, bf16[576,384]{1,0:T(8,128)(2,1)S(1)}, u32[]{:S(2)}, u32[]{:S(2)}) collective-permute-start(bf16[576,384]{1,0:T(8,128)(2,1)S(1)} %pad_maximum_fusion.7), channel_id=1, source_target_pairs={{2,0},{4,2},{6,4},{8,6},{10,8},{12,10},{14,12},{16,14},{18,16},{20... | collective-permute-start | bytes 1327112 | tf_op jit(solution)/shard_map/ppermute | solution.py:41
  39.0 13.4 %collective-permute-start.6 = (bf16[576,384]{1,0:T(8,128)(2,1)S(1)}, bf16[576,384]{1,0:T(8,128)(2,1)S(1)}, u32[]{:S(2)}, u32[]{:S(2)}) collective-permute-start(bf16[576,384]{1,0:T(8,128)(2,1)S(1)} %pad_maximum_fusion.8), channel_id=1, source_target_pairs={{0,1},{2,3},{4,5},{6,7},{8,9},{10,11},{12,13},{14,15},{16,17},{18,... | collective-permute-start | bytes 1327112 | tf_op jit(solution)/shard_map/ppermute | solution.py:41
  42.2 19.2 %collective-permute-start.4 = (bf16[576,384]{1,0:T(8,128)(2,1)S(1)}, bf16[576,384]{1,0:T(8,128)(2,1)S(1)}, u32[]{:S(2)}, u32[]{:S(2)}) collective-permute-start(bf16[576,384]{1,0:T(8,128)(2,1)S(1)} %pad_maximum_fusion.6), channel_id=1, source_target_pairs={{0,2},{2,4},{4,6},{6,8},{8,10},{10,12},{12,14},{14,16},{16,18},{18... | collective-permute-start | bytes 1327112 | tf_op jit(solution)/shard_map/ppermute | solution.py:41
  46.5 15.4 %copy-start.6 = (bf16[576,384]{1,0:T(8,128)(2,1)}, bf16[576,384]{1,0:T(8,128)(2,1)S(1)}, u32[]{:S(2)}) copy-start(bf16[576,384]{1,0:T(8,128)(2,1)S(1)} %collective-permute-done.7) | copy-start | bytes 1327108
  52.4 9.5 %copy-start.9 = (bf16[576,384]{1,0:T(8,128)(2,1)}, bf16[576,384]{1,0:T(8,128)(2,1)S(1)}, u32[]{:S(2)}) copy-start(bf16[576,384]{1,0:T(8,128)(2,1)S(1)} %collective-permute-done.5) | copy-start | bytes 1327108
  52.5 9.5 %copy-start.12 = (bf16[576,384]{1,0:T(8,128)(2,1)}, bf16[576,384]{1,0:T(8,128)(2,1)S(1)}, u32[]{:S(2)}) copy-start(bf16[576,384]{1,0:T(8,128)(2,1)S(1)} %collective-permute-done.6) | copy-start | bytes 1327108
  65.4 12.2 %all-to-all-start.1 = ((bf16[32,4,192]{2,1,0:T(4,128)(2,1)}), bf16[32,4,192]{2,1,0:T(4,128)(2,1)}, u32[]{:S(2)}, u32[]{:S(2)}) async-start(bf16[32,4,192]{2,1,0:T(4,128)(2,1)} %broadcast_in_dim.112), calls=%async_computation.1 | async-start | bytes 131072 | tf_op jit(solution)/shard_map/all_to_all | solution.py:24
  83.1 14.0 %copy-start.4 = (f32[4,192,384]{2,1,0:T(8,128)S(1)}, f32[4,192,384]{2,1,0:T(8,128)}, u32[]{:S(2)}) copy-start(f32[4,192,384]{2,1,0:T(8,128)} %copy-done.3) | copy-start | bytes 3538948
  83.1 8.1 %collective-permute-start.8 = (bf16[1,192,384]{2,1,0:T(8,128)(2,1)S(1)}, bf16[1,192,384]{2,1,0:T(8,128)(2,1)S(1)}, u32[]{:S(2)}, u32[]{:S(2)}) collective-permute-start(bf16[1,192,384]{2,1,0:T(8,128)(2,1)S(1)} %get-tuple-element.9), channel_id=1, source_target_pairs={{0,2},{2,4},{4,6},{6,8},{8,10},{10,12},{12,14},{14,16},{16,18},{18... | collective-permute-start | bytes 442376 | tf_op jit(solution)/shard_map/ppermute | solution.py:13
  85.6 5.7 %collective-permute-start.11 = (bf16[1,192,384]{2,1,0:T(8,128)(2,1)S(1)}, bf16[1,192,384]{2,1,0:T(8,128)(2,1)S(1)}, u32[]{:S(2)}, u32[]{:S(2)}) collective-permute-start(bf16[1,192,384]{2,1,0:T(8,128)(2,1)S(1)} %get-tuple-element.10), channel_id=1, source_target_pairs={{1,0},{3,2},{5,4},{7,6},{9,8},{11,10},{13,12},{15,14},{17,16},{19,... | collective-permute-start | bytes 442376 | tf_op jit(solution)/shard_map/ppermute | solution.py:16
  86.9 4.4 %collective-permute-start.10 = (bf16[1,192,384]{2,1,0:T(8,128)(2,1)S(1)}, bf16[1,192,384]{2,1,0:T(8,128)(2,1)S(1)}, u32[]{:S(2)}, u32[]{:S(2)}) collective-permute-start(bf16[1,192,384]{2,1,0:T(8,128)(2,1)S(1)} %get-tuple-element.11), channel_id=1, source_target_pairs={{0,1},{2,3},{4,5},{6,7},{8,9},{10,11},{12,13},{14,15},{16,17},{18,... | collective-permute-start | bytes 442376 | tf_op jit(solution)/shard_map/ppermute | solution.py:13
  90.0 7.0 %collective-permute-start.9 = (bf16[1,192,384]{2,1,0:T(8,128)(2,1)S(1)}, bf16[1,192,384]{2,1,0:T(8,128)(2,1)S(1)}, u32[]{:S(2)}, u32[]{:S(2)}) collective-permute-start(bf16[1,192,384]{2,1,0:T(8,128)(2,1)S(1)} %get-tuple-element.12), channel_id=1, source_target_pairs={{2,0},{4,2},{6,4},{8,6},{10,8},{12,10},{14,12},{16,14},{18,16},{20... | collective-permute-start | bytes 442376 | tf_op jit(solution)/shard_map/ppermute | solution.py:16
  98.7 13.0 %copy-start.8 = (bf16[576,384]{1,0:T(8,128)(2,1)S(1)}, bf16[576,384]{1,0:T(8,128)(2,1)}, u32[]{:S(2)}) copy-start(bf16[576,384]{1,0:T(8,128)(2,1)} %copy-done.6) | copy-start | bytes 1327108
  98.7 13.1 %copy-start.11 = (bf16[576,384]{1,0:T(8,128)(2,1)S(1)}, bf16[576,384]{1,0:T(8,128)(2,1)}, u32[]{:S(2)}) copy-start(bf16[576,384]{1,0:T(8,128)(2,1)} %copy-done.9) | copy-start | bytes 1327108
  (26 other events, 65.5 us)
